TPU v7x, 32 devices: a whole 2x2x4 slice. The times are simulated.
32 devices in a mesh: row: 4 (over y, core), col: 8 (over z, x).
Axes of the slice: x: 2, y: 2, z: 4, core: 2. Of those that a mesh axis runs over, the one named last changes fastest.
Arguments:
- tokens: bfloat16 [512, 16384], P('col', 'row'), may hold values from -6 to 6
- gate_packed: bfloat16 [2560, 1024, 128], P('row', 'col'), may hold values from -0.0625 to 0.0625
- up_packed: bfloat16 [2560, 1024, 128], P('row', 'col'), may hold values from -0.0625 to 0.0625
- down_packed: bfloat16 [5120, 512, 128], P('col', 'row'), may hold values from -0.0546875 to 0.0546875
- gate_keep: int32 [128, 208], P('row', 'col'), may hold values from 0 to 1, as said below
- down_keep: int32 [208, 128], P('col', 'row'), may hold values from 0 to 1, as said below
Outputs:
- mixed: bfloat16 [512, 16384], P('col', 'row')
Inputs may be any that keep to these rules, and one draw needn't show every extreme that they name: `gate_keep`: in every tile of 32 x 26 blocks, at least 160 and at most 640 blocks are kept; some tile keeps exactly 640. `down_keep`: in every tile of 26 x 32 blocks, at least 160 and at most 640 blocks are kept; some tile keeps exactly 640.
All inputs are finite; a program needn't handle non-finite values.
Results may differ from a plain program's by a relative error of at most 0.02.
Values may be sent and summed in bfloat16 or wider, within the bound.
No kernel may reach another device: no remote copies, remote signals or barrier semaphores. Data moves between devices by JAX's collectives and lax.ppermute only.
A program may use at most 320 MiB of HBM per device.

v0:
```python
import functools

import jax
import jax.numpy as jnp
from jax import lax
from jax.experimental import pallas as pl
from jax.experimental.pallas import tpu as pltpu
from jax.sharding import PartitionSpec as P


def slot_tables(keep, cap):
    rows, cols = keep.shape
    flat = keep.reshape(-1).astype(jnp.int32)
    slot = (jnp.cumsum(flat) - flat).reshape(rows, cols)
    base = jnp.minimum(slot[:, 0], cap - cols)
    index = jnp.where(keep == 1, slot - base[:, None], -1)
    return base.astype(jnp.int32), index.reshape(-1).astype(jnp.int32)


def sparse_kernel(base_ref, index_ref, x_ref, *refs, n_w, group, cols, block):
    w_refs = refs[:n_w * group]
    o_refs = refs[n_w * group:n_w * group + n_w]
    acc_refs = refs[n_w * group + n_w:n_w * group + 2 * n_w]
    panel_refs = refs[n_w * group + 2 * n_w:]
    g = pl.program_id(0)

    @pl.when(g == 0)
    def _():
        for acc in acc_refs:
            acc[...] = jnp.zeros(acc.shape, acc.dtype)

    for rr in range(group):
        for c in range(cols):
            k = index_ref[(g * group + rr) * cols + c]
            for a in range(n_w):
                blk = w_refs[a * group + rr][jnp.maximum(k, 0)]
                panel_refs[a][rr * block:(rr + 1) * block, c * block:(c + 1) * block] = jnp.where(
                    k >= 0, blk, jnp.zeros_like(blk))

    x = x_ref[...]
    for panel, acc in zip(panel_refs, acc_refs):
        acc[...] += jnp.dot(x, panel[...], preferred_element_type=jnp.float32)

    @pl.when(g == pl.num_programs(0) - 1)
    def _():
        for o, acc in zip(o_refs, acc_refs):
            o[...] = acc[...].astype(o.dtype)


def sparse_matmul(x, packed, keep):
    rows, cols = keep.shape
    cap, block, _ = packed[0].shape
    t = x.shape[0]
    n_w = len(packed)
    group = next(s for s in (4, 2, 1) if rows % s == 0)
    base, index = slot_tables(keep, cap)

    def w_spec(rr):
        return pl.BlockSpec(
            (pl.Element(cols), pl.Element(block), pl.Element(block)),
            lambda g, b, i: (b[g * group + rr], 0, 0))

    kernel = functools.partial(sparse_kernel, n_w=n_w, group=group, cols=cols, block=block)
    flops = 2 * t * block * block * rows * cols * n_w
    bytes_accessed = x.size * 2 + n_w * (rows * cols * block * block * 2 + t * cols * block * 2)
    return pl.pallas_call(
        kernel,
        grid_spec=pltpu.PrefetchScalarGridSpec(
            num_scalar_prefetch=2,
            grid=(rows // group,),
            in_specs=[pl.BlockSpec((t, group * block), lambda g, b, i: (0, g))]
            + [w_spec(rr) for _ in range(n_w) for rr in range(group)],
            out_specs=[pl.BlockSpec((t, cols * block), lambda g, b, i: (0, 0))] * n_w,
            scratch_shapes=[pltpu.VMEM((t, cols * block), jnp.float32)] * n_w
            + [pltpu.VMEM((group * block, cols * block), jnp.bfloat16)] * n_w,
        ),
        out_shape=[jax.ShapeDtypeStruct((t, cols * block), jnp.bfloat16)] * n_w,
        compiler_params=pltpu.CompilerParams(dimension_semantics=("arbitrary",)),
        cost_estimate=pl.CostEstimate(flops=flops, transcendentals=0, bytes_accessed=bytes_accessed),
    )(base, index, x, *[p for p in packed for _ in range(group)])


def exchange(x, axis, n, bit):
    pairs = [(i, i ^ (1 << bit)) for i in range(n)]
    return lax.ppermute(x, axis, perm=pairs)


def halving_scatter(parts, axis, n, bits):
    me = lax.axis_index(axis)
    for bit in bits:
        half = parts[0].shape[0] // 2
        mine = (me >> bit) & 1
        keep = [lax.dynamic_slice_in_dim(p, mine * half, half, axis=0) for p in parts]
        send = [lax.dynamic_slice_in_dim(p, (1 - mine) * half, half, axis=0) for p in parts]
        got = exchange(tuple(s.astype(jnp.bfloat16) for s in send), axis, n, bit)
        parts = [k.astype(jnp.float32) + g.astype(jnp.float32) for k, g in zip(keep, got)]
    return parts


def doubling_gather(x, axis, n, bits):
    me = lax.axis_index(axis)
    for bit in bits:
        got = exchange(x, axis, n, bit)
        low = ((me >> bit) & 1) == 0
        x = jnp.where(low, jnp.concatenate([x, got], 0), jnp.concatenate([got, x], 0))
    return x


def local(tokens, gate_packed, up_packed, down_packed, gate_keep, down_keep):
    n_row = lax.axis_size("row")
    n_col = lax.axis_size("col")
    row_bits = list(range(n_row.bit_length() - 1))
    col_bits = list(range(n_col.bit_length() - 1))
    segment = doubling_gather(tokens, "col", n_col, col_bits[::-1])
    gate_rows, up_rows = sparse_matmul(segment, [gate_packed, up_packed], gate_keep)
    gate_sum, up_sum = halving_scatter([gate_rows, up_rows], "row", n_row, row_bits)
    hidden_share = (jax.nn.silu(gate_sum) * up_sum).astype(jnp.bfloat16)
    every_hidden = doubling_gather(hidden_share, "row", n_row, row_bits[::-1])
    (partial_out,) = sparse_matmul(every_hidden, [down_packed], down_keep)
    (summed,) = halving_scatter([partial_out], "col", n_col, col_bits)
    return summed.astype(jnp.bfloat16)


def solution(mesh):
    in_specs = (
        P("col", "row"),
        P("row", "col", None),
        P("row", "col", None),
        P("col", "row", None),
        P("row", "col"),
        P("col", "row"),
    )
    out_specs = P("col", "row")
    return jax.shard_map(local, mesh=mesh, in_specs=in_specs, out_specs=out_specs, check_vma=False)
```

profile of v0, /device:TPU:0, one launch (start us, length us, event | category | flops | bytes accessed | tf_op | source)
XLA Modules:
  0.0 362.7 jit_solution(3750671579352879855)
XLA Ops:
  0.0 4.0 %collective-permute-start = (bf16[64,4096]{1,0:T(8,128)(2,1)}, bf16[64,4096]{1,0:T(8,128)(2,1)S(1)}, u32[]{:S(2)}, u32[]{:S(2)}) collective-permute-start(bf16[64,4096]{1,0:T(8,128)(2,1)} %param.6), channel_id=1, source_target_pairs={{0,4},{1,5},{2,6},{3,7},{4,0},{5,1},{6,2},{7,3},{8,12},{9,13},{10,... | collective-permute-start | bytes 1572872 | tf_op jit(solution)/shard_map/ppermute | solution.py:85
  4.0 23.4 %collective-permute-done = bf16[64,4096]{1,0:T(8,128)(2,1)S(1)} collective-permute-done((bf16[64,4096]{1,0:T(8,128)(2,1)}, bf16[64,4096]{1,0:T(8,128)(2,1)S(1)}, u32[]{:S(2)}, u32[]{:S(2)}) %collective-permute-start) | collective-permute-done | bytes 524320 | tf_op jit(solution)/shard_map/ppermute | solution.py:85
  27.4 1.4 maximum_select_fusion.4
  28.8 0.9 collective-permute-start.1
  29.7 23.6 %collective-permute-done.1 = bf16[128,4096]{1,0:T(8,128)(2,1)} collective-permute-done((bf16[128,4096]{1,0:T(8,128)(2,1)S(1)}, bf16[128,4096]{1,0:T(8,128)(2,1)}, u32[]{:S(2)}, u32[]{:S(2)}) %collective-permute-start.1) | collective-permute-done | bytes 1048608 | tf_op jit(solution)/shard_map/ppermute | solution.py:85
  53.4 2.3 maximum_select_fusion.2
  55.6 1.4 collective-permute-start.2
  57.0 0.1 reshape.64
  57.1 0.3 reduce-window.24
  57.4 0.1 slice.33
  57.5 0.1 slice_reduce_fusion
  57.6 0.1 add_bitcast_fusion
  57.7 0.1 reshape.67
  57.8 0.1 fusion.base_ref
  57.9 0.1 subtract_select_fusion
  58.0 0.7 reshape.68.index_ref
  58.7 43.0 %collective-permute-done.2 = bf16[256,4096]{1,0:T(8,128)(2,1)} collective-permute-done((bf16[256,4096]{1,0:T(8,128)(2,1)S(1)}, bf16[256,4096]{1,0:T(8,128)(2,1)}, u32[]{:S(2)}, u32[]{:S(2)}) %collective-permute-start.2) | collective-permute-done | bytes 2097184 | tf_op jit(solution)/shard_map/ppermute | solution.py:85
  101.7 4.7 %maximum_select_fusion.x_ref = bf16[512,4096]{1,0:T(8,128)(2,1)} fusion(bf16[256,4096]{1,0:T(8,128)(2,1)} %collective-permute-done.2, bf16[256,4096]{1,0:T(8,128)(2,1)S(1)} %maximum_select_fusion.2, pred[]{:T(512)S(6)} %eq.33), kind=kLoop, calls=%fused_computation | loop fusion | flops 18874368 | bytes 8388609 | tf_op jit(solution)/shard_map/jit(_where)/select_n | solution.py:105
  106.4 43.3 %shard_map.64 = (bf16[512,3328]{1,0:T(8,128)(2,1)}, bf16[512,3328]{1,0:T(8,128)(2,1)}) custom-call(s32[32]{0:T(128)} %copy-done.6, s32[832]{0:T(1024)} %reshape.68.index_ref, bf16[512,4096]{1,0:T(8,128)(2,1)} %maximum_select_fusion.x_ref, bf16[640,128,128]{2,1,0:T(8,128)(2,1)} %refs_3_.1, bf16[640,128,128]{2,1,0:T(8,128)(2,1)} %refs_3_.1, ...), custom_call_target="tpu_custom_call" | custom-call | flops 27917287424 | bytes 65536000 | tf_op jit(solution)/shard_map/pallas_call | solution.py:66
  149.7 1.7 constant_dynamic-slice_fusion.2
  151.4 0.1 collective-permute-start.3
  151.5 0.7 copy-done.2
  152.1 1.4 constant_dynamic-slice_fusion.1
  153.5 1.7 collective-permute-done.3
  155.2 2.3 convert_add_fusion.2
  157.5 1.0 dynamic-slice_convert_fusion.2
  158.5 1.3 collective-permute-start.4
  159.8 1.8 convert_add_fusion.1
  161.6 1.7 copy-done.1
  163.3 1.0 dynamic-slice_convert_fusion.1
  164.3 0.7 collective-permute-start.6
  165.0 15.5 %collective-permute-done.4 = bf16[128,3328]{1,0:T(8,128)(2,1)} collective-permute-done((bf16[128,3328]{1,0:T(8,128)(2,1)}, bf16[128,3328]{1,0:T(8,128)(2,1)}, u32[]{:S(2)}, u32[]{:S(2)}) %collective-permute-start.4) | collective-permute-done | bytes 852000 | tf_op jit(solution)/shard_map/ppermute | solution.py:85
  180.6 17.5 %collective-permute-done.6 = bf16[128,3328]{1,0:T(8,128)(2,1)} collective-permute-done((bf16[128,3328]{1,0:T(8,128)(2,1)}, bf16[128,3328]{1,0:T(8,128)(2,1)}, u32[]{:S(2)}, u32[]{:S(2)}) %collective-permute-start.6) | collective-permute-done | bytes 852000 | tf_op jit(solution)/shard_map/ppermute | solution.py:85
  198.0 3.4 multiply_convert_fusion
  201.5 1.3 collective-permute-start.7
  202.8 19.1 %collective-permute-done.7 = bf16[128,3328]{1,0:T(8,128)(2,1)S(1)} collective-permute-done((bf16[128,3328]{1,0:T(8,128)(2,1)}, bf16[128,3328]{1,0:T(8,128)(2,1)S(1)}, u32[]{:S(2)}, u32[]{:S(2)}) %collective-permute-start.7) | collective-permute-done | bytes 852000 | tf_op jit(solution)/shard_map/ppermute | solution.py:85
  221.8 1.8 maximum_select_fusion.3
  223.6 0.1 collective-permute-start.8
  223.7 0.1 reshape.58
  223.8 0.3 reduce-window.16
  224.1 0.1 reshape.60
  224.2 0.1 slice.29
  224.3 0.1 slice_reduce_fusion.1
  224.4 0.1 broadcast.27
  224.5 0.1 reshape.62
  224.5 0.1 fusion.2
  224.6 0.1 fusion.1.base_ref
  224.7 0.1 subtract_select_fusion.1
  224.8 0.7 reshape.63.index_ref
  225.5 1.8 collective-permute-done.8
  227.3 2.1 maximum_select_fusion.1.x_ref
  229.4 25.6 %shard_map.65 = bf16[512,4096]{1,0:T(8,128)(2,1)} custom-call(s32[26]{0:T(128)} %copy-done.7, s32[832]{0:T(1024)} %reshape.63.index_ref, bf16[512,3328]{1,0:T(8,128)(2,1)} %maximum_select_fusion.1.x_ref, bf16[640,128,128]{2,1,0:T(8,128)(2,1)} %refs_1_.3, bf16[640,128,128]{2,1,0:T(8,128)(2,1)} %refs_1_.3), custom_call_target="tpu_custom_call" | custom-call | flops 13958643712 | bytes 34865152 | tf_op jit(solution)/shard_map/pallas_call | solution.py:66
  255.0 1.7 constant_dynamic-slice_fusion
  256.7 1.3 collective-permute-start.9
  258.1 46.5 %collective-permute-done.9 = bf16[256,4096]{1,0:T(8,128)(2,1)} collective-permute-done((bf16[256,4096]{1,0:T(8,128)(2,1)S(1)}, bf16[256,4096]{1,0:T(8,128)(2,1)}, u32[]{:S(2)}, u32[]{:S(2)}) %collective-permute-start.9) | collective-permute-done | bytes 2097184 | tf_op jit(solution)/shard_map/ppermute | solution.py:85
  304.6 2.9 convert_add_fusion
  307.6 1.9 copy-done
  309.5 0.1 dynamic-slice_convert_fusion
  309.6 2.4 collective-permute-start.10
  312.0 22.5 %collective-permute-done.10 = bf16[128,4096]{1,0:T(8,128)(2,1)S(1)} collective-permute-done((bf16[128,4096]{1,0:T(8,128)(2,1)S(1)}, bf16[128,4096]{1,0:T(8,128)(2,1)S(1)}, u32[]{:S(2)}, u32[]{:S(2)}) %collective-permute-start.10) | collective-permute-done | bytes 1048608 | tf_op jit(solution)/shard_map/ppermute | solution.py:85
  334.6 1.8 convert_add_fusion.3
  336.4 3.7 %collective-permute-start.11 = (bf16[64,4096]{1,0:T(8,128)(2,1)S(1)}, bf16[64,4096]{1,0:T(8,128)(2,1)S(1)}, u32[]{:S(2)}, u32[]{:S(2)}) collective-permute-start(bf16[64,4096]{1,0:T(8,128)(2,1)S(1)} %dynamic-slice_convert_fusion.3), channel_id=1, source_target_pairs={{0,4},{1,5},{2,6},{3,7},{4,0},{5,1},{6,2},{7,3},{8,12},{9,13},{10,... | collective-permute-start | bytes 1572872 | tf_op jit(solution)/shard_map/ppermute | solution.py:85
  340.2 21.7 %collective-permute-done.11 = bf16[64,4096]{1,0:T(8,128)(2,1)S(1)} collective-permute-done((bf16[64,4096]{1,0:T(8,128)(2,1)S(1)}, bf16[64,4096]{1,0:T(8,128)(2,1)S(1)}, u32[]{:S(2)}, u32[]{:S(2)}) %collective-permute-start.11) | collective-permute-done | bytes 524320 | tf_op jit(solution)/shard_map/ppermute | solution.py:85
  361.9 0.9 add_convert_fusion
  (21 shorter events, 0.2 us)
Async XLA Ops:
  0.0 57.0 %copy-start.4 = (s32[32,26]{1,0:T(8,128)S(1)}, s32[32,26]{1,0:T(8,128)}, u32[]{:S(2)}) copy-start(s32[32,26]{1,0:T(8,128)} %param.10) | copy-start | bytes 9988
  0.0 27.4 %collective-permute-start = (bf16[64,4096]{1,0:T(8,128)(2,1)}, bf16[64,4096]{1,0:T(8,128)(2,1)S(1)}, u32[]{:S(2)}, u32[]{:S(2)}) collective-permute-start(bf16[64,4096]{1,0:T(8,128)(2,1)} %param.6), channel_id=1, source_target_pairs={{0,4},{1,5},{2,6},{3,7},{4,0},{5,1},{6,2},{7,3},{8,12},{9,13},{10,... | collective-permute-start | bytes 1572872 | tf_op jit(solution)/shard_map/ppermute | solution.py:85
  28.8 24.5 %collective-permute-start.1 = (bf16[128,4096]{1,0:T(8,128)(2,1)S(1)}, bf16[128,4096]{1,0:T(8,128)(2,1)}, u32[]{:S(2)}, u32[]{:S(2)}) collective-permute-start(bf16[128,4096]{1,0:T(8,128)(2,1)S(1)} %maximum_select_fusion.4), channel_id=1, source_target_pairs={{0,2},{1,3},{2,0},{3,1},{4,6},{5,7},{6,4},{7,5},{8,10},{9,11},{10,... | collective-permute-start | bytes 3145736 | tf_op jit(solution)/shard_map/ppermute | solution.py:85
  55.6 46.1 %collective-permute-start.2 = (bf16[256,4096]{1,0:T(8,128)(2,1)S(1)}, bf16[256,4096]{1,0:T(8,128)(2,1)}, u32[]{:S(2)}, u32[]{:S(2)}) collective-permute-start(bf16[256,4096]{1,0:T(8,128)(2,1)S(1)} %maximum_select_fusion.2), channel_id=1, source_target_pairs={{0,1},{1,0},{2,3},{3,2},{4,5},{5,4},{6,7},{7,6},{8,9},{9,8},{10,11... | collective-permute-start | bytes 6291464 | tf_op jit(solution)/shard_map/ppermute | solution.py:85
  57.9 48.5 %copy-start.6 = (s32[32]{0:T(128)}, s32[32]{0:T(128)S(1)}, u32[]{:S(2)}) copy-start(s32[32]{0:T(128)S(1)} %fusion.base_ref) | copy-start | bytes 388
  149.7 2.5 copy-start.2
  151.4 3.8 %collective-permute-start.3 = (bf16[256,3328]{1,0:T(8,128)(2,1)S(1)}, bf16[256,3328]{1,0:T(8,128)(2,1)}, u32[]{:S(2)}, u32[]{:S(2)}) collective-permute-start(bf16[256,3328]{1,0:T(8,128)(2,1)S(1)} %constant_dynamic-slice_fusion.2), channel_id=1, source_target_pairs={{0,8},{8,0},{16,24},{24,16},{1,9},{9,1},{17,25},{25,17},{2,10},{10... | collective-permute-start | bytes 5111816 | tf_op jit(solution)/shard_map/ppermute | solution.py:85
  153.5 6.3 %collective-permute-start.5 = (bf16[256,3328]{1,0:T(8,128)(2,1)}, bf16[256,3328]{1,0:T(8,128)(2,1)}, u32[]{:S(2)}, u32[]{:S(2)}) collective-permute-start(bf16[256,3328]{1,0:T(8,128)(2,1)} %constant_dynamic-slice_fusion.1), channel_id=1, source_target_pairs={{0,8},{8,0},{16,24},{24,16},{1,9},{9,1},{17,25},{25,17},{2,10},{10... | collective-permute-start | bytes 5111816 | tf_op jit(solution)/shard_map/ppermute | solution.py:85
  153.5 6.3 %copy-start.3 = (bf16[512,3328]{1,0:T(8,128)(2,1)S(1)}, bf16[512,3328]{1,0:T(8,128)(2,1)}, u32[]{:S(2)}) copy-start(bf16[512,3328]{1,0:T(8,128)(2,1)} %get-tuple-element.8) | copy-start | bytes 10223620
  158.5 22.1 %collective-permute-start.4 = (bf16[128,3328]{1,0:T(8,128)(2,1)}, bf16[128,3328]{1,0:T(8,128)(2,1)}, u32[]{:S(2)}, u32[]{:S(2)}) collective-permute-start(bf16[128,3328]{1,0:T(8,128)(2,1)} %dynamic-slice_convert_fusion.2), channel_id=1, source_target_pairs={{0,16},{8,24},{16,0},{24,8},{1,17},{9,25},{17,1},{25,9},{2,18},{10... | collective-permute-start | bytes 2555912 | tf_op jit(solution)/shard_map/ppermute | solution.py:85
  161.6 1.7 copy-start.1
  164.3 33.7 %collective-permute-start.6 = (bf16[128,3328]{1,0:T(8,128)(2,1)}, bf16[128,3328]{1,0:T(8,128)(2,1)}, u32[]{:S(2)}, u32[]{:S(2)}) collective-permute-start(bf16[128,3328]{1,0:T(8,128)(2,1)} %dynamic-slice_convert_fusion.1), channel_id=1, source_target_pairs={{0,16},{8,24},{16,0},{24,8},{1,17},{9,25},{17,1},{25,9},{2,18},{10... | collective-permute-start | bytes 2555912 | tf_op jit(solution)/shard_map/ppermute | solution.py:85
  165.0 58.7 %copy-start.5 = (s32[26,32]{1,0:T(8,128)S(1)}, s32[26,32]{1,0:T(8,128)}, u32[]{:S(2)}) copy-start(s32[26,32]{1,0:T(8,128)} %param.11) | copy-start | bytes 9988
  201.5 20.4 %collective-permute-start.7 = (bf16[128,3328]{1,0:T(8,128)(2,1)}, bf16[128,3328]{1,0:T(8,128)(2,1)S(1)}, u32[]{:S(2)}, u32[]{:S(2)}) collective-permute-start(bf16[128,3328]{1,0:T(8,128)(2,1)} %multiply_convert_fusion), channel_id=1, source_target_pairs={{0,16},{8,24},{16,0},{24,8},{1,17},{9,25},{17,1},{25,9},{2,18},{10... | collective-permute-start | bytes 2555912 | tf_op jit(solution)/shard_map/ppermute | solution.py:85
  223.6 3.7 %collective-permute-start.8 = (bf16[256,3328]{1,0:T(8,128)(2,1)S(1)}, bf16[256,3328]{1,0:T(8,128)(2,1)S(1)}, u32[]{:S(2)}, u32[]{:S(2)}) collective-permute-start(bf16[256,3328]{1,0:T(8,128)(2,1)S(1)} %maximum_select_fusion.3), channel_id=1, source_target_pairs={{0,8},{8,0},{16,24},{24,16},{1,9},{9,1},{17,25},{25,17},{2,10},{10... | collective-permute-start | bytes 5111816 | tf_op jit(solution)/shard_map/ppermute | solution.py:85
  224.7 4.7 %copy-start.7 = (s32[26]{0:T(128)}, s32[26]{0:T(128)S(1)}, u32[]{:S(2)}) copy-start(s32[26]{0:T(128)S(1)} %fusion.1.base_ref) | copy-start | bytes 316
  256.7 47.9 %collective-permute-start.9 = (bf16[256,4096]{1,0:T(8,128)(2,1)S(1)}, bf16[256,4096]{1,0:T(8,128)(2,1)}, u32[]{:S(2)}, u32[]{:S(2)}) collective-permute-start(bf16[256,4096]{1,0:T(8,128)(2,1)S(1)} %constant_dynamic-slice_fusion), channel_id=1, source_target_pairs={{0,1},{1,0},{2,3},{3,2},{4,5},{5,4},{6,7},{7,6},{8,9},{9,8},{10,11... | collective-permute-start | bytes 6291464 | tf_op jit(solution)/shard_map/ppermute | solution.py:85
  307.6 1.9 copy-start
  309.6 25.0 %collective-permute-start.10 = (bf16[128,4096]{1,0:T(8,128)(2,1)S(1)}, bf16[128,4096]{1,0:T(8,128)(2,1)S(1)}, u32[]{:S(2)}, u32[]{:S(2)}) collective-permute-start(bf16[128,4096]{1,0:T(8,128)(2,1)S(1)} %dynamic-slice_convert_fusion), channel_id=1, source_target_pairs={{0,2},{1,3},{2,0},{3,1},{4,6},{5,7},{6,4},{7,5},{8,10},{9,11},{10,... | collective-permute-start | bytes 3145736 | tf_op jit(solution)/shard_map/ppermute | solution.py:85
  336.4 25.4 %collective-permute-start.11 = (bf16[64,4096]{1,0:T(8,128)(2,1)S(1)}, bf16[64,4096]{1,0:T(8,128)(2,1)S(1)}, u32[]{:S(2)}, u32[]{:S(2)}) collective-permute-start(bf16[64,4096]{1,0:T(8,128)(2,1)S(1)} %dynamic-slice_convert_fusion.3), channel_id=1, source_target_pairs={{0,4},{1,5},{2,6},{3,7},{4,0},{5,1},{6,2},{7,3},{8,12},{9,13},{10,... | collective-permute-start | bytes 1572872 | tf_op jit(solution)/shard_map/ppermute | solution.py:85
where the time goes:
time: 363 us
  waiting for transfers between devices  236 us (65%)
  Pallas kernels  68.8 us (19%)
  other arithmetic  26.6 us (7%)
  starting transfers between devices  17.3 us (5%)
  local copies, waits for them, and re-layouts  13.6 us (4%)
    ppermute x12, waiting for transfers between devices, exchange(): return lax.ppermute(x, axis, perm=pairs)  236 us
    pallas_call x2, Pallas kernels, sparse_matmul(): pl.pallas_call(kernel, grid_spec=pltpu.PrefetchScalarGridSpec(num_scalar_...  68.8 us
    ppermute x12, starting transfers between devices, exchange(): return lax.ppermute(x, axis, perm=pairs)  17.3 us
    select_n x5, other arithmetic, doubling_gather(): jnp.where(low, jnp.concatenate([x, got], 0), jnp.concatenate([got, x], 0))  12.3 us
    add x4, other arithmetic, halving_scatter(): k.astype(jnp.float32) + g.astype(jnp.float32)  8.82 us
  transfers between devices with their start and end apart: 12, of which 11 were waited for; matrix products, arithmetic and copies ran while one was open for 3% of the time, Pallas kernels for 0%

commit v1 on v0

--- a/solution.py
+++ b/solution.py
@@ -85,39 +85,53 @@
     return lax.ppermute(x, axis, perm=pairs)
 
 
-def halving_scatter(parts, axis, n, bits):
+def halving_scatter(streams, axis, n):
     me = lax.axis_index(axis)
-    for bit in bits:
-        half = parts[0].shape[0] // 2
-        mine = (me >> bit) & 1
-        keep = [lax.dynamic_slice_in_dim(p, mine * half, half, axis=0) for p in parts]
-        send = [lax.dynamic_slice_in_dim(p, (1 - mine) * half, half, axis=0) for p in parts]
-        got = exchange(tuple(s.astype(jnp.bfloat16) for s in send), axis, n, bit)
-        parts = [k.astype(jnp.float32) + g.astype(jnp.float32) for k, g in zip(keep, got)]
-    return parts
+    streams = [(list(parts), bits) for parts, bits in streams]
+    for step in range(len(streams[0][1])):
+        for parts, bits in streams:
+            bit = bits[step]
+            half = parts[0].shape[0] // 2
+            mine = (me >> bit) & 1
+            keep = [lax.dynamic_slice_in_dim(p, mine * half, half, axis=0) for p in parts]
+            send = [lax.dynamic_slice_in_dim(p, (1 - mine) * half, half, axis=0) for p in parts]
+            got = exchange(tuple(s.astype(jnp.bfloat16) for s in send), axis, n, bit)
+            parts[:] = [k.astype(jnp.float32) + g.astype(jnp.float32) for k, g in zip(keep, got)]
+    return [parts for parts, _ in streams]
 
 
-def doubling_gather(x, axis, n, bits):
+def doubling_gather(streams, axis, n):
     me = lax.axis_index(axis)
-    for bit in bits:
-        got = exchange(x, axis, n, bit)
-        low = ((me >> bit) & 1) == 0
-        x = jnp.where(low, jnp.concatenate([x, got], 0), jnp.concatenate([got, x], 0))
-    return x
+    xs = [x for x, _ in streams]
+    for step in range(len(streams[0][1])):
+        for p, (_, bits) in enumerate(streams):
+            bit = bits[step]
+            got = exchange(xs[p], axis, n, bit)
+            low = ((me >> bit) & 1) == 0
+            xs[p] = jnp.where(low, jnp.concatenate([xs[p], got], 0), jnp.concatenate([got, xs[p]], 0))
+    return xs
 
 
 def local(tokens, gate_packed, up_packed, down_packed, gate_keep, down_keep):
     n_row = lax.axis_size("row")
     n_col = lax.axis_size("col")
     row_bits = list(range(n_row.bit_length() - 1))
-    col_bits = list(range(n_col.bit_length() - 1))
-    segment = doubling_gather(tokens, "col", n_col, col_bits[::-1])
+    top = n_col.bit_length() - 1
+    col_orders = [list(range(top - 1, -1, -1)), [0] + list(range(top - 1, 0, -1))]
+    t_half = tokens.shape[0] // 2
+    token_parts = [tokens[:t_half], tokens[t_half:]]
+    segment = jnp.concatenate(
+        doubling_gather(list(zip(token_parts, col_orders)), "col", n_col), axis=0)
     gate_rows, up_rows = sparse_matmul(segment, [gate_packed, up_packed], gate_keep)
-    gate_sum, up_sum = halving_scatter([gate_rows, up_rows], "row", n_row, row_bits)
+    ((gate_sum, up_sum),) = halving_scatter([([gate_rows, up_rows], row_bits)], "row", n_row)
     hidden_share = (jax.nn.silu(gate_sum) * up_sum).astype(jnp.bfloat16)
-    every_hidden = doubling_gather(hidden_share, "row", n_row, row_bits[::-1])
+    (every_hidden,) = doubling_gather([(hidden_share, row_bits[::-1])], "row", n_row)
     (partial_out,) = sparse_matmul(every_hidden, [down_packed], down_keep)
-    (summed,) = halving_scatter([partial_out], "col", n_col, col_bits)
+    half_rows = partial_out.shape[0] // 2
+    out_parts = halving_scatter(
+        [([partial_out[:half_rows]], col_orders[0][::-1]), ([partial_out[half_rows:]], col_orders[1][::-1])],
+        "col", n_col)
+    summed = jnp.concatenate([parts[0] for parts in out_parts], axis=0)
     return summed.astype(jnp.bfloat16)
 
 

time: 363 us -> 294 us (0.81)
  waiting for transfers between devices: 236 us -> 161 us
  starting transfers between devices: 17.3 us -> 25.1 us
  other arithmetic: 26.6 us -> 20.3 us
  local copies, waits for them, and re-layouts: 13.6 us -> 17.5 us
    ppermute x12 -> x18, waiting for transfers between devices: 236 us -> 161 us  [exchange(): return lax.ppermute(x, axis, perm=pairs)]
    ppermute x12 -> x18, starting transfers between devices: 17.3 us -> 25.1 us  [exchange(): return lax.ppermute(x, axis, perm=pairs)]
    select_n x5 -> x8, other arithmetic: 12.3 us -> 7.29 us  [doubling_gather(): jnp.where(low, jnp.concatenate([xs[p], got], 0), jnp.concatenate([got, xs...]
    add x4 -> x6, other arithmetic: 8.82 us -> 4.95 us  [halving_scatter(): k.astype(jnp.float32) + g.astype(jnp.float32)]
    slice x1 -> x3, local copies, waits for them, and re-layouts: 0.07 us -> 3.72 us  [the longest x1 2.59 us: local(): partial_out[:half_rows]]
  transfers between devices with their start and end apart: 12 -> 18, of which waited for: 11 -> 15; matrix products, arithmetic and copies ran while one was open for 3% -> 5% of each run, Pallas kernels for 0% -> 0%
where the time goes in v1:
time: 294 us; the launch traced here: 293 us
  waiting for transfers between devices  161 us (55%)
  Pallas kernels  68.8 us (23%)
  starting transfers between devices  25.1 us (9%)
  other arithmetic  20.3 us (7%)
  local copies, waits for them, and re-layouts  17.5 us (6%)
    ppermute x18, waiting for transfers between devices, exchange(): return lax.ppermute(x, axis, perm=pairs)  161 us
    pallas_call x2, Pallas kernels, sparse_matmul(): pl.pallas_call(kernel, grid_spec=pltpu.PrefetchScalarGridSpec(num_scalar_...  68.8 us
    ppermute x18, starting transfers between devices, exchange(): return lax.ppermute(x, axis, perm=pairs)  25.1 us
    select_n x8, other arithmetic, doubling_gather(): jnp.where(low, jnp.concatenate([xs[p], got], 0), jnp.concatenate([got, xs...  7.29 us
  transfers between devices with their start and end apart: 18, of which 15 were waited for; matrix products, arithmetic and copies ran while one was open for 5% of the time, Pallas kernels for 0%

profile of v1, /device:TPU:0, one launch (start us, length us, event | category | flops | bytes accessed | tf_op | source)
XLA Modules:
  0.0 293.4 jit_solution(8156535619130207359)
XLA Ops:
  0.0 1.1 fusion.4
  1.1 4.1 %collective-permute-start = (bf16[32,4096]{1,0:T(8,128)(2,1)S(1)}, bf16[32,4096]{1,0:T(8,128)(2,1)S(1)}, u32[]{:S(2)}, u32[]{:S(2)}) collective-permute-start(bf16[32,4096]{1,0:T(8,128)(2,1)S(1)} %get-tuple-element.11), channel_id=1, source_target_pairs={{0,4},{1,5},{2,6},{3,7},{4,0},{5,1},{6,2},{7,3},{8,12},{9,13},{10,... | collective-permute-start | bytes 786440 | tf_op jit(solution)/shard_map/ppermute | solution.py:85
  5.2 1.5 collective-permute-start.3
  6.7 0.8 reshape.58
  7.4 0.8 reshape.64
  8.3 8.8 %collective-permute-done = bf16[32,4096]{1,0:T(8,128)(2,1)S(1)} collective-permute-done((bf16[32,4096]{1,0:T(8,128)(2,1)S(1)}, bf16[32,4096]{1,0:T(8,128)(2,1)S(1)}, u32[]{:S(2)}, u32[]{:S(2)}) %collective-permute-start) | collective-permute-done | bytes 262176 | tf_op jit(solution)/shard_map/ppermute | solution.py:85
  17.2 0.8 collective-permute-start.1
  18.0 0.3 reduce-window.24
  18.5 3.4 %collective-permute-start.4 = (bf16[64,4096]{1,0:T(8,128)(2,1)S(1)}, bf16[64,4096]{1,0:T(8,128)(2,1)S(1)}, u32[]{:S(2)}, u32[]{:S(2)}) collective-permute-start(bf16[64,4096]{1,0:T(8,128)(2,1)S(1)} %maximum_select_fusion.7), channel_id=1, source_target_pairs={{0,4},{1,5},{2,6},{3,7},{4,0},{5,1},{6,2},{7,3},{8,12},{9,13},{10,... | collective-permute-start | bytes 1572872 | tf_op jit(solution)/shard_map/ppermute | solution.py:85
  21.9 18.9 %collective-permute-done.1 = bf16[64,4096]{1,0:T(8,128)(2,1)S(1)} collective-permute-done((bf16[64,4096]{1,0:T(8,128)(2,1)S(1)}, bf16[64,4096]{1,0:T(8,128)(2,1)S(1)}, u32[]{:S(2)}, u32[]{:S(2)}) %collective-permute-start.1) | collective-permute-done | bytes 524320 | tf_op jit(solution)/shard_map/ppermute | solution.py:85
  40.8 0.2 maximum_select_fusion.4
  41.0 1.3 collective-permute-start.2
  42.3 0.1 slice_reduce_fusion
  42.4 2.6 collective-permute-done.4
  45.0 0.2 maximum_select_fusion.5
  45.7 0.7 reshape.68.index_ref
  46.4 18.1 %collective-permute-done.2 = bf16[128,4096]{1,0:T(8,128)(2,1)S(1)} collective-permute-done((bf16[128,4096]{1,0:T(8,128)(2,1)S(1)}, bf16[128,4096]{1,0:T(8,128)(2,1)S(1)}, u32[]{:S(2)}, u32[]{:S(2)}) %collective-permute-start.2) | collective-permute-done | bytes 1048608 | tf_op jit(solution)/shard_map/ppermute | solution.py:85
  64.5 0.5 maximum_select_fusion.1
  65.0 2.9 collective-permute-done.5
  67.9 2.3 maximum_select_fusion.2
  70.2 2.6 pad_maximum_fusion.x_ref
  72.8 43.4 %shard_map.64 = (bf16[512,3328]{1,0:T(8,128)(2,1)}, bf16[512,3328]{1,0:T(8,128)(2,1)}) custom-call(s32[32]{0:T(128)} %copy-done.7, s32[832]{0:T(1024)} %reshape.68.index_ref, bf16[512,4096]{1,0:T(8,128)(2,1)} %pad_maximum_fusion.x_ref, bf16[640,128,128]{2,1,0:T(8,128)(2,1)} %refs_3_.1, bf16[640,128,128]{2,1,0:T(8,128)(2,1)} %refs_3_.1, ...), custom_call_target="tpu_custom_call" | custom-call | flops 27917287424 | bytes 65536000 | tf_op jit(solution)/shard_map/pallas_call | solution.py:66
  116.2 1.7 constant_dynamic-slice_fusion.3
  118.0 0.7 copy-done.3
  118.7 1.4 constant_dynamic-slice_fusion.2
  120.1 1.7 collective-permute-done.6
  121.7 2.4 convert_add_fusion.1
  124.2 1.0 dynamic-slice_convert_fusion.1
  125.2 1.5 collective-permute-start.7
  126.7 1.8 convert_add_fusion
  128.5 1.7 copy-done
  130.3 1.0 dynamic-slice_convert_fusion
  131.3 0.5 collective-permute-start.9
  131.8 15.5 %collective-permute-done.7 = bf16[128,3328]{1,0:T(8,128)(2,1)} collective-permute-done((bf16[128,3328]{1,0:T(8,128)(2,1)}, bf16[128,3328]{1,0:T(8,128)(2,1)}, u32[]{:S(2)}, u32[]{:S(2)}) %collective-permute-start.7) | collective-permute-done | bytes 852000 | tf_op jit(solution)/shard_map/ppermute | solution.py:85
  147.3 17.5 %collective-permute-done.9 = bf16[128,3328]{1,0:T(8,128)(2,1)} collective-permute-done((bf16[128,3328]{1,0:T(8,128)(2,1)}, bf16[128,3328]{1,0:T(8,128)(2,1)}, u32[]{:S(2)}, u32[]{:S(2)}) %collective-permute-start.9) | collective-permute-done | bytes 852000 | tf_op jit(solution)/shard_map/ppermute | solution.py:85
  164.8 3.4 %multiply_convert_fusion = bf16[128,3328]{1,0:T(8,128)(2,1)} fusion(bf16[128,3328]{1,0:T(8,128)(2,1)} %collective-permute-done.9, f32[256,3328]{1,0:T(8,128)} %copy-done, s32[]{:T(128)S(6)} %select_n.136, bf16[128,3328]{1,0:T(8,128)(2,1)} %collective-permute-done.7, f32[256,3328]{1,0:T(8,128)S(1)} %convert_add_fusion.1), kind=kLoop, calls=%fused_computation.9 | loop fusion | flops 4259840 | bytes 5963780 | tf_op jit(solution)/shard_map/convert_element_type | solution.py:127
  168.2 1.5 collective-permute-start.10
  169.7 18.8 %collective-permute-done.10 = bf16[128,3328]{1,0:T(8,128)(2,1)S(1)} collective-permute-done((bf16[128,3328]{1,0:T(8,128)(2,1)}, bf16[128,3328]{1,0:T(8,128)(2,1)S(1)}, u32[]{:S(2)}, u32[]{:S(2)}) %collective-permute-start.10) | collective-permute-done | bytes 852000 | tf_op jit(solution)/shard_map/ppermute | solution.py:85
  188.6 1.8 maximum_select_fusion.3
  190.5 0.3 reduce-window.16
  190.9 0.1 slice_reduce_fusion.1
  191.3 0.1 fusion.1.base_ref
  191.5 0.7 reshape.63.index_ref
  192.1 1.9 collective-permute-done.11
  194.0 2.1 maximum_select_fusion.x_ref
  196.2 25.4 %shard_map.65 = bf16[512,4096]{1,0:T(8,128)(2,1)} custom-call(s32[26]{0:T(128)} %copy-done.8, s32[832]{0:T(1024)} %reshape.63.index_ref, bf16[512,3328]{1,0:T(8,128)(2,1)} %maximum_select_fusion.x_ref, bf16[640,128,128]{2,1,0:T(8,128)(2,1)} %refs_1_.3, bf16[640,128,128]{2,1,0:T(8,128)(2,1)} %refs_1_.3), custom_call_target="tpu_custom_call" | custom-call | flops 13958643712 | bytes 34865152 | tf_op jit(solution)/shard_map/pallas_call | solution.py:66
  221.6 2.6 fusion.3
  224.2 1.3 copy-done.1
  225.5 1.1 constant_dynamic-slice_fusion.1
  226.6 1.5 collective-permute-start.12
  228.2 1.9 collective-permute-start.15
  230.1 22.0 %collective-permute-done.12 = bf16[128,4096]{1,0:T(8,128)(2,1)S(1)} collective-permute-done((bf16[128,4096]{1,0:T(8,128)(2,1)}, bf16[128,4096]{1,0:T(8,128)(2,1)S(1)}, u32[]{:S(2)}, u32[]{:S(2)}) %collective-permute-start.12) | collective-permute-done | bytes 1048608 | tf_op jit(solution)/shard_map/ppermute | solution.py:85
  252.0 0.3 convert_add_fusion.3
  252.4 1.8 collective-permute-start.13
  254.1 0.2 convert_add_fusion.2
  254.5 3.0 %collective-permute-start.16 = (bf16[64,4096]{1,0:T(8,128)(2,1)S(1)}, bf16[64,4096]{1,0:T(8,128)(2,1)S(1)}, u32[]{:S(2)}, u32[]{:S(2)}) collective-permute-start(bf16[64,4096]{1,0:T(8,128)(2,1)S(1)} %dynamic-slice_convert_fusion.2), channel_id=1, source_target_pairs={{0,4},{1,5},{2,6},{3,7},{4,0},{5,1},{6,2},{7,3},{8,12},{9,13},{10,... | collective-permute-start | bytes 1572872 | tf_op jit(solution)/shard_map/ppermute | solution.py:85
  257.4 18.9 %collective-permute-done.13 = bf16[64,4096]{1,0:T(8,128)(2,1)S(1)} collective-permute-done((bf16[64,4096]{1,0:T(8,128)(2,1)S(1)}, bf16[64,4096]{1,0:T(8,128)(2,1)S(1)}, u32[]{:S(2)}, u32[]{:S(2)}) %collective-permute-start.13) | collective-permute-done | bytes 524320 | tf_op jit(solution)/shard_map/ppermute | solution.py:85
  276.5 0.5 collective-permute-start.14
  277.0 8.9 %collective-permute-done.16 = bf16[64,4096]{1,0:T(8,128)(2,1)S(1)} collective-permute-done((bf16[64,4096]{1,0:T(8,128)(2,1)S(1)}, bf16[64,4096]{1,0:T(8,128)(2,1)S(1)}, u32[]{:S(2)}, u32[]{:S(2)}) %collective-permute-start.16) | collective-permute-done | bytes 524320 | tf_op jit(solution)/shard_map/ppermute | solution.py:85
  285.9 0.1 convert_add_fusion.4
  286.1 1.6 collective-permute-start.17
  287.6 3.5 %collective-permute-done.14 = bf16[32,4096]{1,0:T(8,128)(2,1)S(1)} collective-permute-done((bf16[32,4096]{1,0:T(8,128)(2,1)S(1)}, bf16[32,4096]{1,0:T(8,128)(2,1)S(1)}, u32[]{:S(2)}, u32[]{:S(2)}) %collective-permute-start.14) | collective-permute-done | bytes 262176 | tf_op jit(solution)/shard_map/ppermute | solution.py:85
  291.1 1.4 collective-permute-done.17
  292.6 0.8 pad_maximum_fusion.1
  (47 shorter events, 1.8 us)
Async XLA Ops:
  1.1 16.0 %collective-permute-start = (bf16[32,4096]{1,0:T(8,128)(2,1)S(1)}, bf16[32,4096]{1,0:T(8,128)(2,1)S(1)}, u32[]{:S(2)}, u32[]{:S(2)}) collective-permute-start(bf16[32,4096]{1,0:T(8,128)(2,1)S(1)} %get-tuple-element.11), channel_id=1, source_target_pairs={{0,4},{1,5},{2,6},{3,7},{4,0},{5,1},{6,2},{7,3},{8,12},{9,13},{10,... | collective-permute-start | bytes 786440 | tf_op jit(solution)/shard_map/ppermute | solution.py:85
  5.2 13.2 %collective-permute-start.3 = (bf16[32,4096]{1,0:T(8,128)(2,1)S(1)}, bf16[32,4096]{1,0:T(8,128)(2,1)S(1)}, u32[]{:S(2)}, u32[]{:S(2)}) collective-permute-start(bf16[32,4096]{1,0:T(8,128)(2,1)S(1)} %get-tuple-element.12), channel_id=1, source_target_pairs={{0,1},{1,0},{2,3},{3,2},{4,5},{5,4},{6,7},{7,6},{8,9},{9,8},{10,11... | collective-permute-start | bytes 786440 | tf_op jit(solution)/shard_map/ppermute | solution.py:85
  17.2 23.6 %collective-permute-start.1 = (bf16[64,4096]{1,0:T(8,128)(2,1)S(1)}, bf16[64,4096]{1,0:T(8,128)(2,1)S(1)}, u32[]{:S(2)}, u32[]{:S(2)}) collective-permute-start(bf16[64,4096]{1,0:T(8,128)(2,1)S(1)} %maximum_select_fusion.6), channel_id=1, source_target_pairs={{0,2},{1,3},{2,0},{3,1},{4,6},{5,7},{6,4},{7,5},{8,10},{9,11},{10,... | collective-permute-start | bytes 1572872 | tf_op jit(solution)/shard_map/ppermute | solution.py:85
  18.5 27.0 %copy-start.5 = (s32[32,26]{1,0:T(8,128)S(1)}, s32[32,26]{1,0:T(8,128)}, u32[]{:S(2)}) copy-start(s32[32,26]{1,0:T(8,128)} %param.10) | copy-start | bytes 9988
  18.5 26.6 %collective-permute-start.4 = (bf16[64,4096]{1,0:T(8,128)(2,1)S(1)}, bf16[64,4096]{1,0:T(8,128)(2,1)S(1)}, u32[]{:S(2)}, u32[]{:S(2)}) collective-permute-start(bf16[64,4096]{1,0:T(8,128)(2,1)S(1)} %maximum_select_fusion.7), channel_id=1, source_target_pairs={{0,4},{1,5},{2,6},{3,7},{4,0},{5,1},{6,2},{7,3},{8,12},{9,13},{10,... | collective-permute-start | bytes 1572872 | tf_op jit(solution)/shard_map/ppermute | solution.py:85
  41.0 23.5 %collective-permute-start.2 = (bf16[128,4096]{1,0:T(8,128)(2,1)S(1)}, bf16[128,4096]{1,0:T(8,128)(2,1)S(1)}, u32[]{:S(2)}, u32[]{:S(2)}) collective-permute-start(bf16[128,4096]{1,0:T(8,128)(2,1)S(1)} %maximum_select_fusion.4), channel_id=1, source_target_pairs={{0,1},{1,0},{2,3},{3,2},{4,5},{5,4},{6,7},{7,6},{8,9},{9,8},{10,11... | collective-permute-start | bytes 3145736 | tf_op jit(solution)/shard_map/ppermute | solution.py:85
  45.2 22.7 %collective-permute-start.5 = (bf16[128,4096]{1,0:T(8,128)(2,1)S(1)}, bf16[128,4096]{1,0:T(8,128)(2,1)}, u32[]{:S(2)}, u32[]{:S(2)}) collective-permute-start(bf16[128,4096]{1,0:T(8,128)(2,1)S(1)} %maximum_select_fusion.5), channel_id=1, source_target_pairs={{0,2},{1,3},{2,0},{3,1},{4,6},{5,7},{6,4},{7,5},{8,10},{9,11},{10,... | collective-permute-start | bytes 3145736 | tf_op jit(solution)/shard_map/ppermute | solution.py:85
  45.6 19.4 %copy-start.7 = (s32[32]{0:T(128)}, s32[32]{0:T(128)S(1)}, u32[]{:S(2)}) copy-start(s32[32]{0:T(128)S(1)} %fusion.base_ref) | copy-start | bytes 388
  116.2 2.5 copy-start.3
  117.9 3.8 %collective-permute-start.6 = (bf16[256,3328]{1,0:T(8,128)(2,1)S(1)}, bf16[256,3328]{1,0:T(8,128)(2,1)}, u32[]{:S(2)}, u32[]{:S(2)}) collective-permute-start(bf16[256,3328]{1,0:T(8,128)(2,1)S(1)} %constant_dynamic-slice_fusion.3), channel_id=1, source_target_pairs={{0,8},{8,0},{16,24},{24,16},{1,9},{9,1},{17,25},{25,17},{2,10},{10... | collective-permute-start | bytes 5111816 | tf_op jit(solution)/shard_map/ppermute | solution.py:85
  120.1 6.7 %collective-permute-start.8 = (bf16[256,3328]{1,0:T(8,128)(2,1)}, bf16[256,3328]{1,0:T(8,128)(2,1)}, u32[]{:S(2)}, u32[]{:S(2)}) collective-permute-start(bf16[256,3328]{1,0:T(8,128)(2,1)} %constant_dynamic-slice_fusion.2), channel_id=1, source_target_pairs={{0,8},{8,0},{16,24},{24,16},{1,9},{9,1},{17,25},{25,17},{2,10},{10... | collective-permute-start | bytes 5111816 | tf_op jit(solution)/shard_map/ppermute | solution.py:85
  121.7 5.0 %copy-start.4 = (bf16[512,3328]{1,0:T(8,128)(2,1)S(1)}, bf16[512,3328]{1,0:T(8,128)(2,1)}, u32[]{:S(2)}) copy-start(bf16[512,3328]{1,0:T(8,128)(2,1)} %get-tuple-element.8) | copy-start | bytes 10223620
  125.2 22.1 %collective-permute-start.7 = (bf16[128,3328]{1,0:T(8,128)(2,1)}, bf16[128,3328]{1,0:T(8,128)(2,1)}, u32[]{:S(2)}, u32[]{:S(2)}) collective-permute-start(bf16[128,3328]{1,0:T(8,128)(2,1)} %dynamic-slice_convert_fusion.1), channel_id=1, source_target_pairs={{0,16},{8,24},{16,0},{24,8},{1,17},{9,25},{17,1},{25,9},{2,18},{10... | collective-permute-start | bytes 2555912 | tf_op jit(solution)/shard_map/ppermute | solution.py:85
  128.5 1.7 copy-start
  131.3 33.5 %collective-permute-start.9 = (bf16[128,3328]{1,0:T(8,128)(2,1)}, bf16[128,3328]{1,0:T(8,128)(2,1)}, u32[]{:S(2)}, u32[]{:S(2)}) collective-permute-start(bf16[128,3328]{1,0:T(8,128)(2,1)} %dynamic-slice_convert_fusion), channel_id=1, source_target_pairs={{0,16},{8,24},{16,0},{24,8},{1,17},{9,25},{17,1},{25,9},{2,18},{10... | collective-permute-start | bytes 2555912 | tf_op jit(solution)/shard_map/ppermute | solution.py:85
  168.2 23.0 %copy-start.6 = (s32[26,32]{1,0:T(8,128)S(1)}, s32[26,32]{1,0:T(8,128)}, u32[]{:S(2)}) copy-start(s32[26,32]{1,0:T(8,128)} %param.11) | copy-start | bytes 9988
  168.2 20.4 %collective-permute-start.10 = (bf16[128,3328]{1,0:T(8,128)(2,1)}, bf16[128,3328]{1,0:T(8,128)(2,1)S(1)}, u32[]{:S(2)}, u32[]{:S(2)}) collective-permute-start(bf16[128,3328]{1,0:T(8,128)(2,1)} %multiply_convert_fusion), channel_id=1, source_target_pairs={{0,16},{8,24},{16,0},{24,8},{1,17},{9,25},{17,1},{25,9},{2,18},{10... | collective-permute-start | bytes 2555912 | tf_op jit(solution)/shard_map/ppermute | solution.py:85
  190.4 3.7 %collective-permute-start.11 = (bf16[256,3328]{1,0:T(8,128)(2,1)S(1)}, bf16[256,3328]{1,0:T(8,128)(2,1)S(1)}, u32[]{:S(2)}, u32[]{:S(2)}) collective-permute-start(bf16[256,3328]{1,0:T(8,128)(2,1)S(1)} %maximum_select_fusion.3), channel_id=1, source_target_pairs={{0,8},{8,0},{16,24},{24,16},{1,9},{9,1},{17,25},{25,17},{2,10},{10... | collective-permute-start | bytes 5111816 | tf_op jit(solution)/shard_map/ppermute | solution.py:85
  191.4 4.8 %copy-start.8 = (s32[26]{0:T(128)}, s32[26]{0:T(128)S(1)}, u32[]{:S(2)}) copy-start(s32[26]{0:T(128)S(1)} %fusion.1.base_ref) | copy-start | bytes 316
  224.2 1.3 copy-start.1
  226.6 25.4 %collective-permute-start.12 = (bf16[128,4096]{1,0:T(8,128)(2,1)}, bf16[128,4096]{1,0:T(8,128)(2,1)S(1)}, u32[]{:S(2)}, u32[]{:S(2)}) collective-permute-start(bf16[128,4096]{1,0:T(8,128)(2,1)} %constant_dynamic-slice_fusion.1), channel_id=1, source_target_pairs={{0,1},{1,0},{2,3},{3,2},{4,5},{5,4},{6,7},{7,6},{8,9},{9,8},{10,11... | collective-permute-start | bytes 3145736 | tf_op jit(solution)/shard_map/ppermute | solution.py:85
  228.1 23.9 %copy-start.2 = (bf16[256,4096]{1,0:T(8,128)(2,1)S(1)}, bf16[256,4096]{1,0:T(8,128)(2,1)}, u32[]{:S(2)}) copy-start(bf16[256,4096]{1,0:T(8,128)(2,1)} %copy-done.1) | copy-start | bytes 6291460
  228.2 26.0 %collective-permute-start.15 = (bf16[128,4096]{1,0:T(8,128)(2,1)S(1)}, bf16[128,4096]{1,0:T(8,128)(2,1)S(1)}, u32[]{:S(2)}, u32[]{:S(2)}) collective-permute-start(bf16[128,4096]{1,0:T(8,128)(2,1)S(1)} %constant_dynamic-slice_fusion), channel_id=1, source_target_pairs={{0,2},{1,3},{2,0},{3,1},{4,6},{5,7},{6,4},{7,5},{8,10},{9,11},{10,... | collective-permute-start | bytes 3145736 | tf_op jit(solution)/shard_map/ppermute | solution.py:85
  252.4 23.9 %collective-permute-start.13 = (bf16[64,4096]{1,0:T(8,128)(2,1)S(1)}, bf16[64,4096]{1,0:T(8,128)(2,1)S(1)}, u32[]{:S(2)}, u32[]{:S(2)}) collective-permute-start(bf16[64,4096]{1,0:T(8,128)(2,1)S(1)} %dynamic-slice_convert_fusion.3), channel_id=1, source_target_pairs={{0,2},{1,3},{2,0},{3,1},{4,6},{5,7},{6,4},{7,5},{8,10},{9,11},{10,... | collective-permute-start | bytes 1572872 | tf_op jit(solution)/shard_map/ppermute | solution.py:85
  254.5 31.4 %collective-permute-start.16 = (bf16[64,4096]{1,0:T(8,128)(2,1)S(1)}, bf16[64,4096]{1,0:T(8,128)(2,1)S(1)}, u32[]{:S(2)}, u32[]{:S(2)}) collective-permute-start(bf16[64,4096]{1,0:T(8,128)(2,1)S(1)} %dynamic-slice_convert_fusion.2), channel_id=1, source_target_pairs={{0,4},{1,5},{2,6},{3,7},{4,0},{5,1},{6,2},{7,3},{8,12},{9,13},{10,... | collective-permute-start | bytes 1572872 | tf_op jit(solution)/shard_map/ppermute | solution.py:85
  276.5 14.6 %collective-permute-start.14 = (bf16[32,4096]{1,0:T(8,128)(2,1)S(1)}, bf16[32,4096]{1,0:T(8,128)(2,1)S(1)}, u32[]{:S(2)}, u32[]{:S(2)}) collective-permute-start(bf16[32,4096]{1,0:T(8,128)(2,1)S(1)} %dynamic-slice_convert_fusion.5), channel_id=1, source_target_pairs={{0,4},{1,5},{2,6},{3,7},{4,0},{5,1},{6,2},{7,3},{8,12},{9,13},{10,... | collective-permute-start | bytes 786440 | tf_op jit(solution)/shard_map/ppermute | solution.py:85
  286.1 6.4 %collective-permute-start.17 = (bf16[32,4096]{1,0:T(8,128)(2,1)S(1)}, bf16[32,4096]{1,0:T(8,128)(2,1)S(1)}, u32[]{:S(2)}, u32[]{:S(2)}) collective-permute-start(bf16[32,4096]{1,0:T(8,128)(2,1)S(1)} %dynamic-slice_convert_fusion.4), channel_id=1, source_target_pairs={{0,1},{1,0},{2,3},{3,2},{4,5},{5,4},{6,7},{7,6},{8,9},{9,8},{10,11... | collective-permute-start | bytes 786440 | tf_op jit(solution)/shard_map/ppermute | solution.py:85

commit v2 on v1

--- a/solution.py
+++ b/solution.py
@@ -8,16 +8,17 @@
 from jax.sharding import PartitionSpec as P
 
 
-def slot_tables(keep, cap):
-    rows, cols = keep.shape
+def slot_tables(keep, cap, r0, r1, c0, c1):
     flat = keep.reshape(-1).astype(jnp.int32)
-    slot = (jnp.cumsum(flat) - flat).reshape(rows, cols)
-    base = jnp.minimum(slot[:, 0], cap - cols)
-    index = jnp.where(keep == 1, slot - base[:, None], -1)
+    slot = (jnp.cumsum(flat) - flat).reshape(keep.shape)[r0:r1, c0:c1]
+    base = jnp.minimum(slot[:, 0], cap - (c1 - c0))
+    index = jnp.where(keep[r0:r1, c0:c1] == 1, slot - base[:, None], -1)
     return base.astype(jnp.int32), index.reshape(-1).astype(jnp.int32)
 
 
-def sparse_kernel(base_ref, index_ref, x_ref, *refs, n_w, group, cols, block):
+def sparse_kernel(base_ref, index_ref, x_ref, *refs, n_w, group, cols, block, seeded):
+    if seeded:
+        init_ref, refs = refs[0], refs[1:]
     w_refs = refs[:n_w * group]
     o_refs = refs[n_w * group:n_w * group + n_w]
     acc_refs = refs[n_w * group + n_w:n_w * group + 2 * n_w]
@@ -27,7 +28,7 @@
     @pl.when(g == 0)
     def _():
         for acc in acc_refs:
-            acc[...] = jnp.zeros(acc.shape, acc.dtype)
+            acc[...] = init_ref[...] if seeded else jnp.zeros(acc.shape, acc.dtype)
 
     for rr in range(group):
         for c in range(cols):
@@ -47,37 +48,41 @@
             o[...] = acc[...].astype(o.dtype)
 
 
-def sparse_matmul(x, packed, keep):
-    rows, cols = keep.shape
+def sparse_matmul(x, packed, keep, r0, r1, c0, c1, init=None, out_dtype=jnp.bfloat16):
+    rows, cols = r1 - r0, c1 - c0
     cap, block, _ = packed[0].shape
     t = x.shape[0]
     n_w = len(packed)
     group = next(s for s in (4, 2, 1) if rows % s == 0)
-    base, index = slot_tables(keep, cap)
+    base, index = slot_tables(keep, cap, r0, r1, c0, c1)
 
     def w_spec(rr):
         return pl.BlockSpec(
             (pl.Element(cols), pl.Element(block), pl.Element(block)),
             lambda g, b, i: (b[g * group + rr], 0, 0))
 
-    kernel = functools.partial(sparse_kernel, n_w=n_w, group=group, cols=cols, block=block)
+    seeded = init is not None
+    kernel = functools.partial(
+        sparse_kernel, n_w=n_w, group=group, cols=cols, block=block, seeded=seeded)
+    whole = pl.BlockSpec((t, cols * block), lambda g, b, i: (0, 0))
     flops = 2 * t * block * block * rows * cols * n_w
-    bytes_accessed = x.size * 2 + n_w * (rows * cols * block * block * 2 + t * cols * block * 2)
+    bytes_accessed = x.size * 2 + n_w * (rows * cols * block * block * 2 + t * cols * block * 4)
     return pl.pallas_call(
         kernel,
         grid_spec=pltpu.PrefetchScalarGridSpec(
             num_scalar_prefetch=2,
             grid=(rows // group,),
             in_specs=[pl.BlockSpec((t, group * block), lambda g, b, i: (0, g))]
+            + ([whole] if seeded else [])
             + [w_spec(rr) for _ in range(n_w) for rr in range(group)],
-            out_specs=[pl.BlockSpec((t, cols * block), lambda g, b, i: (0, 0))] * n_w,
+            out_specs=[whole] * n_w,
             scratch_shapes=[pltpu.VMEM((t, cols * block), jnp.float32)] * n_w
             + [pltpu.VMEM((group * block, cols * block), jnp.bfloat16)] * n_w,
         ),
-        out_shape=[jax.ShapeDtypeStruct((t, cols * block), jnp.bfloat16)] * n_w,
+        out_shape=[jax.ShapeDtypeStruct((t, cols * block), out_dtype)] * n_w,
         compiler_params=pltpu.CompilerParams(dimension_semantics=("arbitrary",)),
         cost_estimate=pl.CostEstimate(flops=flops, transcendentals=0, bytes_accessed=bytes_accessed),
-    )(base, index, x, *[p for p in packed for _ in range(group)])
+    )(base, index, x, *([init] if seeded else []), *[p for p in packed for _ in range(group)])
 
 
 def exchange(x, axis, n, bit):
@@ -122,11 +127,20 @@
     token_parts = [tokens[:t_half], tokens[t_half:]]
     segment = jnp.concatenate(
         doubling_gather(list(zip(token_parts, col_orders)), "col", n_col), axis=0)
-    gate_rows, up_rows = sparse_matmul(segment, [gate_packed, up_packed], gate_keep)
-    ((gate_sum, up_sum),) = halving_scatter([([gate_rows, up_rows], row_bits)], "row", n_row)
-    hidden_share = (jax.nn.silu(gate_sum) * up_sum).astype(jnp.bfloat16)
-    (every_hidden,) = doubling_gather([(hidden_share, row_bits[::-1])], "row", n_row)
-    (partial_out,) = sparse_matmul(every_hidden, [down_packed], down_keep)
+    n_in, n_hid = gate_keep.shape
+    n_out = down_keep.shape[1]
+    split = (n_hid // 2) // 4 * 4 or n_hid // 2
+    spans = [(0, split), (split, n_hid)]
+    hidden = []
+    for h0, h1 in spans:
+        gate_rows, up_rows = sparse_matmul(segment, [gate_packed, up_packed], gate_keep, 0, n_in, h0, h1)
+        ((gate_sum, up_sum),) = halving_scatter([([gate_rows, up_rows], row_bits)], "row", n_row)
+        hidden_share = (jax.nn.silu(gate_sum) * up_sum).astype(jnp.bfloat16)
+        hidden += doubling_gather([(hidden_share, row_bits[::-1])], "row", n_row)
+    (first_out,) = sparse_matmul(
+        hidden[0], [down_packed], down_keep, 0, split, 0, n_out, out_dtype=jnp.float32)
+    (partial_out,) = sparse_matmul(
+        hidden[1], [down_packed], down_keep, split, n_hid, 0, n_out, init=first_out)
     half_rows = partial_out.shape[0] // 2
     out_parts = halving_scatter(
         [([partial_out[:half_rows]], col_orders[0][::-1]), ([partial_out[half_rows:]], col_orders[1][::-1])],

time: 294 us -> 306 us (1.041)
  Pallas kernels: 68.8 us -> 83.9 us
  waiting for transfers between devices: 161 us -> 165 us
  other arithmetic: 20.3 us -> 16.4 us
    pallas_call x2 -> x4, Pallas kernels: 68.8 us -> 83.9 us  [sparse_matmul(): pl.pallas_call(kernel, grid_spec=pltpu.PrefetchScalarGridSpec(num_scalar_...]
    add x6 -> x8, other arithmetic: 4.95 us -> 1.51 us  [halving_scatter(): k.astype(jnp.float32) + g.astype(jnp.float32)]
    ppermute x18 -> x24, waiting for transfers between devices: 161 us -> 165 us  [exchange(): return lax.ppermute(x, axis, perm=pairs)]
    select_n x8 -> x10, other arithmetic: 7.29 us -> 8.72 us  [doubling_gather(): jnp.where(low, jnp.concatenate([xs[p], got], 0), jnp.concatenate([got, xs...]
    ppermute x18 -> x24, starting transfers between devices: 25.1 us -> 25.1 us  [exchange(): return lax.ppermute(x, axis, perm=pairs)]
  transfers between devices with their start and end apart: 18 -> 24, of which waited for: 15 -> 18; matrix products, arithmetic and copies ran while one was open for 5% -> 6% of each run, Pallas kernels for 0% -> 14%
where the time goes in v2:
time: 306 us; the launch traced here: 305 us
  waiting for transfers between devices  165 us (54%)
  Pallas kernels  83.9 us (27%)
  starting transfers between devices  25.1 us (8%)
  other arithmetic  16.4 us (5%)
  local copies, waits for them, and re-layouts  14.5 us (5%)
    ppermute x24, waiting for transfers between devices, exchange(): return lax.ppermute(x, axis, perm=pairs)  165 us
    pallas_call x4, Pallas kernels, sparse_matmul(): pl.pallas_call(kernel, grid_spec=pltpu.PrefetchScalarGridSpec(num_scalar_...  83.9 us
    ppermute x24, starting transfers between devices, exchange(): return lax.ppermute(x, axis, perm=pairs)  25.1 us
    select_n x10, other arithmetic, doubling_gather(): jnp.where(low, jnp.concatenate([xs[p], got], 0), jnp.concatenate([got, xs...  8.72 us
  transfers between devices with their start and end apart: 24, of which 18 were waited for; matrix products, arithmetic and copies ran while one was open for 6% of the time, Pallas kernels for 14%

profile of v2, /device:TPU:0, one launch (start us, length us, event | category | flops | bytes accessed | tf_op | source)
XLA Modules:
  0.0 304.8 jit_solution(12422326460718636239)
XLA Ops:
  0.0 1.1 fusion.10
  1.1 3.0 collective-permute-start.3
  4.1 2.6 collective-permute-start
  6.7 0.8 reshape.84
  7.5 0.8 reshape.78
  8.3 0.3 reduce-window.24
  9.0 0.7 sub.70
  9.9 0.5 collective-permute-done.3
  10.5 2.9 collective-permute-start.4
  13.5 0.3 reduce-window.16
  13.8 16.9 %collective-permute-done = bf16[32,4096]{1,0:T(8,128)(2,1)S(1)} collective-permute-done((bf16[32,4096]{1,0:T(8,128)(2,1)S(1)}, bf16[32,4096]{1,0:T(8,128)(2,1)S(1)}, u32[]{:S(2)}, u32[]{:S(2)}) %collective-permute-start) | collective-permute-done | bytes 262176 | tf_op jit(solution)/shard_map/ppermute | solution.py:90
  30.9 10.1 %collective-permute-done.4 = bf16[64,4096]{1,0:T(8,128)(2,1)} collective-permute-done((bf16[64,4096]{1,0:T(8,128)(2,1)S(1)}, bf16[64,4096]{1,0:T(8,128)(2,1)}, u32[]{:S(2)}, u32[]{:S(2)}) %collective-permute-start.4) | collective-permute-done | bytes 524320 | tf_op jit(solution)/shard_map/ppermute | solution.py:90
  41.0 1.4 maximum_select_fusion.5
  42.5 0.6 collective-permute-start.5
  43.4 0.7 reshape.88.index_ref
  44.1 8.1 %collective-permute-done.1 = bf16[64,4096]{1,0:T(8,128)(2,1)S(1)} collective-permute-done((bf16[64,4096]{1,0:T(8,128)(2,1)S(1)}, bf16[64,4096]{1,0:T(8,128)(2,1)S(1)}, u32[]{:S(2)}, u32[]{:S(2)}) %collective-permute-start.1) | collective-permute-done | bytes 524320 | tf_op jit(solution)/shard_map/ppermute | solution.py:90
  52.4 0.5 collective-permute-start.2
  53.0 0.7 reshape.90.index_ref
  53.9 20.7 %collective-permute-done.5 = bf16[128,4096]{1,0:T(8,128)(2,1)} collective-permute-done((bf16[128,4096]{1,0:T(8,128)(2,1)S(1)}, bf16[128,4096]{1,0:T(8,128)(2,1)}, u32[]{:S(2)}, u32[]{:S(2)}) %collective-permute-start.5) | collective-permute-done | bytes 1048608 | tf_op jit(solution)/shard_map/ppermute | solution.py:90
  74.7 2.3 maximum_select_fusion.1
  76.9 0.5 collective-permute-done.2
  77.4 0.5 maximum_select_fusion
  77.9 2.5 pad_maximum_fusion.x_ref
  80.4 23.1 %shard_map.65 = (bf16[512,1536]{1,0:T(8,128)(2,1)}, bf16[512,1536]{1,0:T(8,128)(2,1)}) custom-call(s32[32]{0:T(128)} %copy-done.9, s32[384]{0:T(512)} %reshape.90.index_ref, bf16[512,4096]{1,0:T(8,128)(2,1)} %pad_maximum_fusion.x_ref, bf16[640,128,128]{2,1,0:T(8,128)(2,1)} %refs_3_.4, bf16[640,128,128]{2,1,0:T(8,128)(2,1)} %refs_3_.4, ...), custom_call_target="tpu_custom_call" | custom-call | flops 12884901888 | bytes 35651584 | tf_op jit(solution)/shard_map/pallas_call | solution.py:70
  103.5 1.2 constant_dynamic-slice_fusion.2
  104.8 26.1 %shard_map.64 = (bf16[512,1792]{1,0:T(8,128)(2,1)}, bf16[512,1792]{1,0:T(8,128)(2,1)}) custom-call(s32[32]{0:T(128)} %copy-done.8, s32[448]{0:T(512)} %reshape.88.index_ref, bf16[512,4096]{1,0:T(8,128)(2,1)} %pad_maximum_fusion.x_ref, bf16[640,128,128]{2,1,0:T(8,128)(2,1)} %refs_3_.4, bf16[640,128,128]{2,1,0:T(8,128)(2,1)} %refs_3_.4, ...), custom_call_target="tpu_custom_call" | custom-call | flops 15032385536 | bytes 40894464 | tf_op jit(solution)/shard_map/pallas_call | solution.py:70
  130.8 1.4 constant_dynamic-slice_fusion.4
  132.2 0.5 collective-permute-start.8
  133.0 0.5 collective-permute-start.6
  134.0 1.6 collective-permute-start.15
  135.6 0.4 collective-permute-done.12
  136.3 1.6 collective-permute-start.13
  138.1 0.6 collective-permute-start.9
  139.0 1.6 collective-permute-start.7
  140.5 5.5 %collective-permute-done.15 = bf16[128,1536]{1,0:T(8,128)(2,1)S(1)} collective-permute-done((bf16[128,1536]{1,0:T(8,128)(2,1)S(1)}, bf16[128,1536]{1,0:T(8,128)(2,1)S(1)}, u32[]{:S(2)}, u32[]{:S(2)}) %collective-permute-start.15) | collective-permute-done | bytes 393248 | tf_op jit(solution)/shard_map/ppermute | solution.py:90
  146.0 8.4 %collective-permute-done.13 = bf16[128,1536]{1,0:T(8,128)(2,1)S(1)} collective-permute-done((bf16[128,1536]{1,0:T(8,128)(2,1)S(1)}, bf16[128,1536]{1,0:T(8,128)(2,1)S(1)}, u32[]{:S(2)}, u32[]{:S(2)}) %collective-permute-start.13) | collective-permute-done | bytes 393248 | tf_op jit(solution)/shard_map/ppermute | solution.py:90
  154.4 0.3 multiply_convert_fusion.1
  154.7 1.6 collective-permute-start.16
  156.3 8.0 %collective-permute-done.9 = bf16[128,1792]{1,0:T(8,128)(2,1)S(1)} collective-permute-done((bf16[128,1792]{1,0:T(8,128)(2,1)S(1)}, bf16[128,1792]{1,0:T(8,128)(2,1)S(1)}, u32[]{:S(2)}, u32[]{:S(2)}) %collective-permute-start.9) | collective-permute-done | bytes 458784 | tf_op jit(solution)/shard_map/ppermute | solution.py:90
  164.3 9.8 %collective-permute-done.7 = bf16[128,1792]{1,0:T(8,128)(2,1)S(1)} collective-permute-done((bf16[128,1792]{1,0:T(8,128)(2,1)S(1)}, bf16[128,1792]{1,0:T(8,128)(2,1)S(1)}, u32[]{:S(2)}, u32[]{:S(2)}) %collective-permute-start.7) | collective-permute-done | bytes 458784 | tf_op jit(solution)/shard_map/ppermute | solution.py:90
  174.1 0.3 multiply_convert_fusion
  174.4 1.6 collective-permute-start.10
  176.0 6.5 %collective-permute-done.16 = bf16[128,1536]{1,0:T(8,128)(2,1)S(1)} collective-permute-done((bf16[128,1536]{1,0:T(8,128)(2,1)S(1)}, bf16[128,1536]{1,0:T(8,128)(2,1)S(1)}, u32[]{:S(2)}, u32[]{:S(2)}) %collective-permute-start.16) | collective-permute-done | bytes 393248 | tf_op jit(solution)/shard_map/ppermute | solution.py:90
  183.0 9.0 %collective-permute-done.10 = bf16[128,1792]{1,0:T(8,128)(2,1)S(1)} collective-permute-done((bf16[128,1792]{1,0:T(8,128)(2,1)S(1)}, bf16[128,1792]{1,0:T(8,128)(2,1)S(1)}, u32[]{:S(2)}, u32[]{:S(2)}) %collective-permute-start.10) | collective-permute-done | bytes 458784 | tf_op jit(solution)/shard_map/ppermute | solution.py:90
  192.3 0.7 reshape.83.index_ref
  192.9 0.7 reshape.89.index_ref
  193.6 1.8 maximum_select_fusion.3.x_ref
  195.4 15.9 %shard_map.66.refs_0_ = f32[512,4096]{1,0:T(8,128)} custom-call(s32[12]{0:T(128)} %copy-done.11, s32[384]{0:T(512)} %reshape.89.index_ref, bf16[512,1536]{1,0:T(8,128)(2,1)} %maximum_select_fusion.3.x_ref, bf16[640,128,128]{2,1,0:T(8,128)(2,1)} %refs_2_.7, bf16[640,128,128]{2,1,0:T(8,128)(2,1)} %refs_2_.7, bf16[640,128,128]{2,1,0:T(8,128)(2,1)} %refs_2_.7, ...), custom_call_target="tpu_custom_call" | custom-call | flops 6442450944 | bytes 22544384 | tf_op jit(solution)/shard_map/pallas_call | solution.py:70
  211.3 2.0 maximum_select_fusion.2.x_ref
  213.3 18.9 %shard_map.67 = bf16[512,4096]{1,0:T(8,128)(2,1)} custom-call(s32[14]{0:T(128)} %copy-done.10, s32[448]{0:T(512)} %reshape.83.index_ref, bf16[512,1792]{1,0:T(8,128)(2,1)} %maximum_select_fusion.2.x_ref, f32[512,4096]{1,0:T(8,128)} %shard_map.66.refs_0_, bf16[640,128,128]{2,1,0:T(8,128)(2,1)} %refs_2_.7, bf16[640,128,128]{2,1,0:T(8,128)(2,1)} %refs_2_.7), custom_call_target="tpu_custom_call" | custom-call | flops 7516192768 | bytes 24903680 | tf_op jit(solution)/shard_map/pallas_call | solution.py:70
  232.1 2.6 fusion.9
  234.7 1.3 copy-done
  236.1 1.1 constant_dynamic-slice_fusion
  237.2 0.7 collective-permute-start.18
  237.9 25.0 %collective-permute-done.21 = bf16[128,4096]{1,0:T(8,128)(2,1)S(1)} collective-permute-done((bf16[128,4096]{1,0:T(8,128)(2,1)}, bf16[128,4096]{1,0:T(8,128)(2,1)S(1)}, u32[]{:S(2)}, u32[]{:S(2)}) %collective-permute-start.21) | collective-permute-done | bytes 1048608 | tf_op jit(solution)/shard_map/ppermute | solution.py:90
  263.0 0.3 convert_add_fusion
  263.3 2.3 collective-permute-start.22
  265.6 0.2 convert_add_fusion.1
  265.9 1.8 collective-permute-start.19
  267.7 21.5 %collective-permute-done.22 = bf16[64,4096]{1,0:T(8,128)(2,1)S(1)} collective-permute-done((bf16[64,4096]{1,0:T(8,128)(2,1)S(1)}, bf16[64,4096]{1,0:T(8,128)(2,1)S(1)}, u32[]{:S(2)}, u32[]{:S(2)}) %collective-permute-start.22) | collective-permute-done | bytes 524320 | tf_op jit(solution)/shard_map/ppermute | solution.py:90
  289.4 0.5 collective-permute-start.23
  290.4 6.7 %collective-permute-done.23 = bf16[32,4096]{1,0:T(8,128)(2,1)S(1)} collective-permute-done((bf16[32,4096]{1,0:T(8,128)(2,1)S(1)}, bf16[32,4096]{1,0:T(8,128)(2,1)S(1)}, u32[]{:S(2)}, u32[]{:S(2)}) %collective-permute-start.23) | collective-permute-done | bytes 262176 | tf_op jit(solution)/shard_map/ppermute | solution.py:90
  297.2 6.7 %collective-permute-done.20 = bf16[32,4096]{1,0:T(8,128)(2,1)S(1)} collective-permute-done((bf16[32,4096]{1,0:T(8,128)(2,1)S(1)}, bf16[32,4096]{1,0:T(8,128)(2,1)S(1)}, u32[]{:S(2)}, u32[]{:S(2)}) %collective-permute-start.20) | collective-permute-done | bytes 262176 | tf_op jit(solution)/shard_map/ppermute | solution.py:90
  304.0 0.8 pad_maximum_fusion.1
  (81 shorter events, 5.1 us)
Async XLA Ops:
  0.0 13.4 %copy-start.6 = (s32[32,26]{1,0:T(8,128)S(1)}, s32[32,26]{1,0:T(8,128)}, u32[]{:S(2)}) copy-start(s32[32,26]{1,0:T(8,128)} %param.10) | copy-start | bytes 9988
  1.1 9.3 %collective-permute-start.3 = (bf16[32,4096]{1,0:T(8,128)(2,1)S(1)}, bf16[32,4096]{1,0:T(8,128)(2,1)S(1)}, u32[]{:S(2)}, u32[]{:S(2)}) collective-permute-start(bf16[32,4096]{1,0:T(8,128)(2,1)S(1)} %get-tuple-element.18), channel_id=1, source_target_pairs={{0,1},{1,0},{2,3},{3,2},{4,5},{5,4},{6,7},{7,6},{8,9},{9,8},{10,11... | collective-permute-start | bytes 786440 | tf_op jit(solution)/shard_map/ppermute | solution.py:90
  4.1 26.7 %collective-permute-start = (bf16[32,4096]{1,0:T(8,128)(2,1)S(1)}, bf16[32,4096]{1,0:T(8,128)(2,1)S(1)}, u32[]{:S(2)}, u32[]{:S(2)}) collective-permute-start(bf16[32,4096]{1,0:T(8,128)(2,1)S(1)} %get-tuple-element.17), channel_id=1, source_target_pairs={{0,4},{1,5},{2,6},{3,7},{4,0},{5,1},{6,2},{7,3},{8,12},{9,13},{10,... | collective-permute-start | bytes 786440 | tf_op jit(solution)/shard_map/ppermute | solution.py:90
  9.9 32.6 %copy-start.8 = (s32[32]{0:T(128)}, s32[32]{0:T(128)S(1)}, u32[]{:S(2)}) copy-start(s32[32]{0:T(128)S(1)} %get-tuple-element.14.base_ref) | copy-start | bytes 388
  9.9 43.0 %copy-start.9 = (s32[32]{0:T(128)}, s32[32]{0:T(128)S(1)}, u32[]{:S(2)}) copy-start(s32[32]{0:T(128)S(1)} %get-tuple-element.13.base_ref) | copy-start | bytes 388
  10.5 30.6 %collective-permute-start.4 = (bf16[64,4096]{1,0:T(8,128)(2,1)S(1)}, bf16[64,4096]{1,0:T(8,128)(2,1)}, u32[]{:S(2)}, u32[]{:S(2)}) collective-permute-start(bf16[64,4096]{1,0:T(8,128)(2,1)S(1)} %maximum_select_fusion.9), channel_id=1, source_target_pairs={{0,4},{1,5},{2,6},{3,7},{4,0},{5,1},{6,2},{7,3},{8,12},{9,13},{10,... | collective-permute-start | bytes 1572872 | tf_op jit(solution)/shard_map/ppermute | solution.py:90
  30.9 22.9 %copy-start.7 = (s32[26,32]{1,0:T(8,128)S(1)}, s32[26,32]{1,0:T(8,128)}, u32[]{:S(2)}) copy-start(s32[26,32]{1,0:T(8,128)} %param.11) | copy-start | bytes 9988
  30.9 21.3 %collective-permute-start.1 = (bf16[64,4096]{1,0:T(8,128)(2,1)S(1)}, bf16[64,4096]{1,0:T(8,128)(2,1)S(1)}, u32[]{:S(2)}, u32[]{:S(2)}) collective-permute-start(bf16[64,4096]{1,0:T(8,128)(2,1)S(1)} %maximum_select_fusion.8), channel_id=1, source_target_pairs={{0,2},{1,3},{2,0},{3,1},{4,6},{5,7},{6,4},{7,5},{8,10},{9,11},{10,... | collective-permute-start | bytes 1572872 | tf_op jit(solution)/shard_map/ppermute | solution.py:90
  42.5 32.1 %collective-permute-start.5 = (bf16[128,4096]{1,0:T(8,128)(2,1)S(1)}, bf16[128,4096]{1,0:T(8,128)(2,1)}, u32[]{:S(2)}, u32[]{:S(2)}) collective-permute-start(bf16[128,4096]{1,0:T(8,128)(2,1)S(1)} %maximum_select_fusion.5), channel_id=1, source_target_pairs={{0,2},{1,3},{2,0},{3,1},{4,6},{5,7},{6,4},{7,5},{8,10},{9,11},{10,... | collective-permute-start | bytes 3145736 | tf_op jit(solution)/shard_map/ppermute | solution.py:90
  52.4 25.1 %collective-permute-start.2 = (bf16[128,4096]{1,0:T(8,128)(2,1)S(1)}, bf16[128,4096]{1,0:T(8,128)(2,1)S(1)}, u32[]{:S(2)}, u32[]{:S(2)}) collective-permute-start(bf16[128,4096]{1,0:T(8,128)(2,1)S(1)} %maximum_select_fusion.4), channel_id=1, source_target_pairs={{0,1},{1,0},{2,3},{3,2},{4,5},{5,4},{6,7},{7,6},{8,9},{9,8},{10,11... | collective-permute-start | bytes 3145736 | tf_op jit(solution)/shard_map/ppermute | solution.py:90
  53.9 129.0 %copy-start.10 = (s32[14]{0:T(128)}, s32[14]{0:T(128)S(1)}, u32[]{:S(2)}) copy-start(s32[14]{0:T(128)S(1)} %fusion.8.base_ref) | copy-start | bytes 172
  104.7 28.9 %collective-permute-start.14 = (bf16[256,1536]{1,0:T(8,128)(2,1)S(1)}, bf16[256,1536]{1,0:T(8,128)(2,1)S(1)}, u32[]{:S(2)}, u32[]{:S(2)}) collective-permute-start(bf16[256,1536]{1,0:T(8,128)(2,1)S(1)} %constant_dynamic-slice_fusion.2), channel_id=1, source_target_pairs={{0,8},{8,0},{16,24},{24,16},{1,9},{9,1},{17,25},{25,17},{2,10},{10... | collective-permute-start | bytes 2359304 | tf_op jit(solution)/shard_map/ppermute | solution.py:90
  104.7 28.0 %copy-start.4 = (bf16[512,1536]{1,0:T(8,128)(2,1)S(1)}, bf16[512,1536]{1,0:T(8,128)(2,1)}, u32[]{:S(2)}) copy-start(bf16[512,1536]{1,0:T(8,128)(2,1)} %get-tuple-element.11) | copy-start | bytes 4718596
  130.8 2.1 copy-start.2
  132.2 1.5 copy-start.5
  132.2 5.7 %collective-permute-start.8 = (bf16[256,1792]{1,0:T(8,128)(2,1)S(1)}, bf16[256,1792]{1,0:T(8,128)(2,1)S(1)}, u32[]{:S(2)}, u32[]{:S(2)}) collective-permute-start(bf16[256,1792]{1,0:T(8,128)(2,1)S(1)} %constant_dynamic-slice_fusion.4), channel_id=1, source_target_pairs={{0,8},{8,0},{16,24},{24,16},{1,9},{9,1},{17,25},{25,17},{2,10},{10... | collective-permute-start | bytes 2752520 | tf_op jit(solution)/shard_map/ppermute | solution.py:90
  132.8 3.2 %collective-permute-start.12 = (bf16[256,1536]{1,0:T(8,128)(2,1)S(1)}, bf16[256,1536]{1,0:T(8,128)(2,1)S(1)}, u32[]{:S(2)}, u32[]{:S(2)}) collective-permute-start(bf16[256,1536]{1,0:T(8,128)(2,1)S(1)} %constant_dynamic-slice_fusion.3), channel_id=1, source_target_pairs={{0,8},{8,0},{16,24},{24,16},{1,9},{9,1},{17,25},{25,17},{2,10},{10... | collective-permute-start | bytes 2359304 | tf_op jit(solution)/shard_map/ppermute | solution.py:90
  133.0 5.7 %collective-permute-start.6 = (bf16[256,1792]{1,0:T(8,128)(2,1)S(1)}, bf16[256,1792]{1,0:T(8,128)(2,1)S(1)}, u32[]{:S(2)}, u32[]{:S(2)}) collective-permute-start(bf16[256,1792]{1,0:T(8,128)(2,1)S(1)} %constant_dynamic-slice_fusion.5), channel_id=1, source_target_pairs={{0,8},{8,0},{16,24},{24,16},{1,9},{9,1},{17,25},{25,17},{2,10},{10... | collective-permute-start | bytes 2752520 | tf_op jit(solution)/shard_map/ppermute | solution.py:90
  134.0 3.9 %copy-start.3 = (bf16[512,1792]{1,0:T(8,128)(2,1)S(1)}, bf16[512,1792]{1,0:T(8,128)(2,1)}, u32[]{:S(2)}) copy-start(bf16[512,1792]{1,0:T(8,128)(2,1)} %get-tuple-element.10) | copy-start | bytes 5505028
  134.0 12.0 %collective-permute-start.15 = (bf16[128,1536]{1,0:T(8,128)(2,1)S(1)}, bf16[128,1536]{1,0:T(8,128)(2,1)S(1)}, u32[]{:S(2)}, u32[]{:S(2)}) collective-permute-start(bf16[128,1536]{1,0:T(8,128)(2,1)S(1)} %dynamic-slice_convert_fusion.4), channel_id=1, source_target_pairs={{0,16},{8,24},{16,0},{24,8},{1,17},{9,25},{17,1},{25,9},{2,18},{10... | collective-permute-start | bytes 1179656 | tf_op jit(solution)/shard_map/ppermute | solution.py:90
  136.3 18.2 %collective-permute-start.13 = (bf16[128,1536]{1,0:T(8,128)(2,1)S(1)}, bf16[128,1536]{1,0:T(8,128)(2,1)S(1)}, u32[]{:S(2)}, u32[]{:S(2)}) collective-permute-start(bf16[128,1536]{1,0:T(8,128)(2,1)S(1)} %dynamic-slice_convert_fusion.5), channel_id=1, source_target_pairs={{0,16},{8,24},{16,0},{24,8},{1,17},{9,25},{17,1},{25,9},{2,18},{10... | collective-permute-start | bytes 1179656 | tf_op jit(solution)/shard_map/ppermute | solution.py:90
  138.1 26.1 %collective-permute-start.9 = (bf16[128,1792]{1,0:T(8,128)(2,1)S(1)}, bf16[128,1792]{1,0:T(8,128)(2,1)S(1)}, u32[]{:S(2)}, u32[]{:S(2)}) collective-permute-start(bf16[128,1792]{1,0:T(8,128)(2,1)S(1)} %dynamic-slice_convert_fusion.2), channel_id=1, source_target_pairs={{0,16},{8,24},{16,0},{24,8},{1,17},{9,25},{17,1},{25,9},{2,18},{10... | collective-permute-start | bytes 1376264 | tf_op jit(solution)/shard_map/ppermute | solution.py:90
  139.0 35.1 %collective-permute-start.7 = (bf16[128,1792]{1,0:T(8,128)(2,1)S(1)}, bf16[128,1792]{1,0:T(8,128)(2,1)S(1)}, u32[]{:S(2)}, u32[]{:S(2)}) collective-permute-start(bf16[128,1792]{1,0:T(8,128)(2,1)S(1)} %dynamic-slice_convert_fusion.3), channel_id=1, source_target_pairs={{0,16},{8,24},{16,0},{24,8},{1,17},{9,25},{17,1},{25,9},{2,18},{10... | collective-permute-start | bytes 1376264 | tf_op jit(solution)/shard_map/ppermute | solution.py:90
  154.7 27.8 %collective-permute-start.16 = (bf16[128,1536]{1,0:T(8,128)(2,1)S(1)}, bf16[128,1536]{1,0:T(8,128)(2,1)S(1)}, u32[]{:S(2)}, u32[]{:S(2)}) collective-permute-start(bf16[128,1536]{1,0:T(8,128)(2,1)S(1)} %multiply_convert_fusion.1), channel_id=1, source_target_pairs={{0,16},{8,24},{16,0},{24,8},{1,17},{9,25},{17,1},{25,9},{2,18},{10... | collective-permute-start | bytes 1179656 | tf_op jit(solution)/shard_map/ppermute | solution.py:90
  174.4 17.5 %collective-permute-start.10 = (bf16[128,1792]{1,0:T(8,128)(2,1)S(1)}, bf16[128,1792]{1,0:T(8,128)(2,1)S(1)}, u32[]{:S(2)}, u32[]{:S(2)}) collective-permute-start(bf16[128,1792]{1,0:T(8,128)(2,1)S(1)} %multiply_convert_fusion), channel_id=1, source_target_pairs={{0,16},{8,24},{16,0},{24,8},{1,17},{9,25},{17,1},{25,9},{2,18},{10... | collective-permute-start | bytes 1376264 | tf_op jit(solution)/shard_map/ppermute | solution.py:90
  182.7 10.9 %collective-permute-start.17 = (bf16[256,1536]{1,0:T(8,128)(2,1)S(1)}, bf16[256,1536]{1,0:T(8,128)(2,1)S(1)}, u32[]{:S(2)}, u32[]{:S(2)}) collective-permute-start(bf16[256,1536]{1,0:T(8,128)(2,1)S(1)} %maximum_select_fusion.7), channel_id=1, source_target_pairs={{0,8},{8,0},{16,24},{24,16},{1,9},{9,1},{17,25},{25,17},{2,10},{10... | collective-permute-start | bytes 2359304 | tf_op jit(solution)/shard_map/ppermute | solution.py:90
  182.9 12.5 %copy-start.11 = (s32[12]{0:T(128)}, s32[12]{0:T(128)S(1)}, u32[]{:S(2)}) copy-start(s32[12]{0:T(128)S(1)} %fusion.6.base_ref) | copy-start | bytes 148
  192.1 19.2 %collective-permute-start.11 = (bf16[256,1792]{1,0:T(8,128)(2,1)S(1)}, bf16[256,1792]{1,0:T(8,128)(2,1)S(1)}, u32[]{:S(2)}, u32[]{:S(2)}) collective-permute-start(bf16[256,1792]{1,0:T(8,128)(2,1)S(1)} %maximum_select_fusion.6), channel_id=1, source_target_pairs={{0,8},{8,0},{16,24},{24,16},{1,9},{9,1},{17,25},{25,17},{2,10},{10... | collective-permute-start | bytes 2752520 | tf_op jit(solution)/shard_map/ppermute | solution.py:90
  234.7 1.3 copy-start
  237.1 25.9 %collective-permute-start.21 = (bf16[128,4096]{1,0:T(8,128)(2,1)}, bf16[128,4096]{1,0:T(8,128)(2,1)S(1)}, u32[]{:S(2)}, u32[]{:S(2)}) collective-permute-start(bf16[128,4096]{1,0:T(8,128)(2,1)} %constant_dynamic-slice_fusion), channel_id=1, source_target_pairs={{0,2},{1,3},{2,0},{3,1},{4,6},{5,7},{6,4},{7,5},{8,10},{9,11},{10,... | collective-permute-start | bytes 3145736 | tf_op jit(solution)/shard_map/ppermute | solution.py:90
  237.1 25.9 %copy-start.1 = (bf16[256,4096]{1,0:T(8,128)(2,1)S(1)}, bf16[256,4096]{1,0:T(8,128)(2,1)}, u32[]{:S(2)}) copy-start(bf16[256,4096]{1,0:T(8,128)(2,1)} %copy-done) | copy-start | bytes 6291460
  237.2 28.4 %collective-permute-start.18 = (bf16[128,4096]{1,0:T(8,128)(2,1)S(1)}, bf16[128,4096]{1,0:T(8,128)(2,1)S(1)}, u32[]{:S(2)}, u32[]{:S(2)}) collective-permute-start(bf16[128,4096]{1,0:T(8,128)(2,1)S(1)} %constant_dynamic-slice_fusion.1), channel_id=1, source_target_pairs={{0,1},{1,0},{2,3},{3,2},{4,5},{5,4},{6,7},{7,6},{8,9},{9,8},{10,11... | collective-permute-start | bytes 3145736 | tf_op jit(solution)/shard_map/ppermute | solution.py:90
  263.3 25.9 %collective-permute-start.22 = (bf16[64,4096]{1,0:T(8,128)(2,1)S(1)}, bf16[64,4096]{1,0:T(8,128)(2,1)S(1)}, u32[]{:S(2)}, u32[]{:S(2)}) collective-permute-start(bf16[64,4096]{1,0:T(8,128)(2,1)S(1)} %dynamic-slice_convert_fusion), channel_id=1, source_target_pairs={{0,4},{1,5},{2,6},{3,7},{4,0},{5,1},{6,2},{7,3},{8,12},{9,13},{10,... | collective-permute-start | bytes 1572872 | tf_op jit(solution)/shard_map/ppermute | solution.py:90
  265.9 24.1 %collective-permute-start.19 = (bf16[64,4096]{1,0:T(8,128)(2,1)S(1)}, bf16[64,4096]{1,0:T(8,128)(2,1)S(1)}, u32[]{:S(2)}, u32[]{:S(2)}) collective-permute-start(bf16[64,4096]{1,0:T(8,128)(2,1)S(1)} %dynamic-slice_convert_fusion.1), channel_id=1, source_target_pairs={{0,2},{1,3},{2,0},{3,1},{4,6},{5,7},{6,4},{7,5},{8,10},{9,11},{10,... | collective-permute-start | bytes 1572872 | tf_op jit(solution)/shard_map/ppermute | solution.py:90
  289.4 7.8 %collective-permute-start.23 = (bf16[32,4096]{1,0:T(8,128)(2,1)S(1)}, bf16[32,4096]{1,0:T(8,128)(2,1)S(1)}, u32[]{:S(2)}, u32[]{:S(2)}) collective-permute-start(bf16[32,4096]{1,0:T(8,128)(2,1)S(1)} %dynamic-slice_convert_fusion.6), channel_id=1, source_target_pairs={{0,1},{1,0},{2,3},{3,2},{4,5},{5,4},{6,7},{7,6},{8,9},{9,8},{10,11... | collective-permute-start | bytes 786440 | tf_op jit(solution)/shard_map/ppermute | solution.py:90
  290.2 13.7 %collective-permute-start.20 = (bf16[32,4096]{1,0:T(8,128)(2,1)S(1)}, bf16[32,4096]{1,0:T(8,128)(2,1)S(1)}, u32[]{:S(2)}, u32[]{:S(2)}) collective-permute-start(bf16[32,4096]{1,0:T(8,128)(2,1)S(1)} %dynamic-slice_convert_fusion.7), channel_id=1, source_target_pairs={{0,4},{1,5},{2,6},{3,7},{4,0},{5,1},{6,2},{7,3},{8,12},{9,13},{10,... | collective-permute-start | bytes 786440 | tf_op jit(solution)/shard_map/ppermute | solution.py:90

commit v3 on v1

--- a/solution.py
+++ b/solution.py
@@ -80,6 +80,68 @@
     )(base, index, x, *[p for p in packed for _ in range(group)])
 
 
+def densify_kernel(base_ref, index_ref, *refs, group, cols, block):
+    w_refs = refs[:group]
+    o_ref = refs[group]
+    g = pl.program_id(0)
+    for rr in range(group):
+        for c in range(cols):
+            k = index_ref[(g * group + rr) * cols + c]
+            blk = w_refs[rr][jnp.maximum(k, 0)]
+            o_ref[rr * block:(rr + 1) * block, c * block:(c + 1) * block] = jnp.where(
+                k >= 0, blk, jnp.zeros_like(blk))
+
+
+def densify(packed, keep):
+    rows, cols = keep.shape
+    cap, block, _ = packed.shape
+    group = next(s for s in (4, 2, 1) if rows % s == 0)
+    base, index = slot_tables(keep, cap)
+
+    def w_spec(rr):
+        return pl.BlockSpec(
+            (pl.Element(cols), pl.Element(block), pl.Element(block)),
+            lambda g, b, i: (b[g * group + rr], 0, 0))
+
+    kernel = functools.partial(densify_kernel, group=group, cols=cols, block=block)
+    n_bytes = 2 * rows * cols * block * block * 2
+    return pl.pallas_call(
+        kernel,
+        grid_spec=pltpu.PrefetchScalarGridSpec(
+            num_scalar_prefetch=2,
+            grid=(rows // group,),
+            in_specs=[w_spec(rr) for rr in range(group)],
+            out_specs=pl.BlockSpec((group * block, cols * block), lambda g, b, i: (g, 0)),
+        ),
+        out_shape=jax.ShapeDtypeStruct((rows * block, cols * block), packed.dtype),
+        compiler_params=pltpu.CompilerParams(dimension_semantics=("arbitrary",)),
+        cost_estimate=pl.CostEstimate(flops=0, transcendentals=0, bytes_accessed=n_bytes),
+    )(base, index, *[packed] * group)
+
+
+def dense_kernel(x_ref, *refs, n_w):
+    for w_ref, o_ref in zip(refs[:n_w], refs[n_w:]):
+        o_ref[...] = jnp.dot(x_ref[...], w_ref[...], preferred_element_type=jnp.float32).astype(o_ref.dtype)
+
+
+def dense_matmul(x, ws):
+    t, k = x.shape
+    n = ws[0].shape[1]
+    tn = next(s for s in (512, 256, 128) if n % s == 0)
+    n_w = len(ws)
+    return pl.pallas_call(
+        functools.partial(dense_kernel, n_w=n_w),
+        grid=(n // tn,),
+        in_specs=[pl.BlockSpec((t, k), lambda j: (0, 0))] + [pl.BlockSpec((k, tn), lambda j: (0, j))] * n_w,
+        out_specs=[pl.BlockSpec((t, tn), lambda j: (0, j))] * n_w,
+        out_shape=[jax.ShapeDtypeStruct((t, n), jnp.bfloat16)] * n_w,
+        compiler_params=pltpu.CompilerParams(dimension_semantics=("arbitrary",)),
+        cost_estimate=pl.CostEstimate(
+            flops=2 * t * k * n * n_w, transcendentals=0,
+            bytes_accessed=x.size * 2 + n_w * (k * n * 2 + t * n * 2)),
+    )(x, *ws)
+
+
 def exchange(x, axis, n, bit):
     pairs = [(i, i ^ (1 << bit)) for i in range(n)]
     return lax.ppermute(x, axis, perm=pairs)
@@ -122,11 +184,11 @@
     token_parts = [tokens[:t_half], tokens[t_half:]]
     segment = jnp.concatenate(
         doubling_gather(list(zip(token_parts, col_orders)), "col", n_col), axis=0)
-    gate_rows, up_rows = sparse_matmul(segment, [gate_packed, up_packed], gate_keep)
+    gate_rows, up_rows = dense_matmul(segment, [densify(gate_packed, gate_keep), densify(up_packed, gate_keep)])
     ((gate_sum, up_sum),) = halving_scatter([([gate_rows, up_rows], row_bits)], "row", n_row)
     hidden_share = (jax.nn.silu(gate_sum) * up_sum).astype(jnp.bfloat16)
     (every_hidden,) = doubling_gather([(hidden_share, row_bits[::-1])], "row", n_row)
-    (partial_out,) = sparse_matmul(every_hidden, [down_packed], down_keep)
+    (partial_out,) = dense_matmul(every_hidden, [densify(down_packed, down_keep)])
     half_rows = partial_out.shape[0] // 2
     out_parts = halving_scatter(
         [([partial_out[:half_rows]], col_orders[0][::-1]), ([partial_out[half_rows:]], col_orders[1][::-1])],

time: 294 us -> 330 us (1.12)
  Pallas kernels: 68.8 us -> 127 us
  waiting for transfers between devices: 161 us -> 140 us
    pallas_call x2 -> x5, Pallas kernels: 68.8 us -> 127 us  [the longest x3 71.2 us: densify(): pl.pallas_call(kernel, grid_spec=pltpu.PrefetchScalarGridSpec(num_scalar_...]
    ppermute x18, waiting for transfers between devices: 161 us -> 140 us  [exchange(): return lax.ppermute(x, axis, perm=pairs)]
  transfers between devices with their start and end apart: 18 -> 18, of which waited for: 15 -> 12; matrix products, arithmetic and copies ran while one was open for 5% -> 4% of each run, Pallas kernels for 0% -> 22%
where the time goes in v3:
time: 330 us; the launch traced here: 329 us
  waiting for transfers between devices  140 us (42%)
  Pallas kernels  127 us (38%)
  starting transfers between devices  24.4 us (7%)
  other arithmetic  20.2 us (6%)
  local copies, waits for them, and re-layouts  17.5 us (5%)
    ppermute x18, waiting for transfers between devices, exchange(): return lax.ppermute(x, axis, perm=pairs)  140 us
    pallas_call x3, Pallas kernels, densify(): pl.pallas_call(kernel, grid_spec=pltpu.PrefetchScalarGridSpec(num_scalar_...  71.2 us
    pallas_call x2, Pallas kernels, dense_matmul(): pl.pallas_call(functools.partial(dense_kernel, n_w=n_w), grid=(n // tn,),...  55.4 us
    ppermute x18, starting transfers between devices, exchange(): return lax.ppermute(x, axis, perm=pairs)  24.4 us
    select_n x8, other arithmetic, doubling_gather(): jnp.where(low, jnp.concatenate([xs[p], got], 0), jnp.concatenate([got, xs...  7.33 us
  transfers between devices with their start and end apart: 18, of which 12 were waited for; matrix products, arithmetic and copies ran while one was open for 4% of the time, Pallas kernels for 22%

profile of v3, /device:TPU:0, one launch (start us, length us, event | category | flops | bytes accessed | tf_op | source)
XLA Modules:
  0.0 328.8 jit_solution(7741072308059212668)
XLA Ops:
  0.0 1.1 fusion.4
  1.1 4.1 %collective-permute-start = (bf16[32,4096]{1,0:T(8,128)(2,1)S(1)}, bf16[32,4096]{1,0:T(8,128)(2,1)S(1)}, u32[]{:S(2)}, u32[]{:S(2)}) collective-permute-start(bf16[32,4096]{1,0:T(8,128)(2,1)S(1)} %get-tuple-element.11), channel_id=1, source_target_pairs={{0,4},{1,5},{2,6},{3,7},{4,0},{5,1},{6,2},{7,3},{8,12},{9,13},{10,... | collective-permute-start | bytes 786440 | tf_op jit(solution)/shard_map/ppermute | solution.py:147
  5.2 1.5 collective-permute-start.3
  6.7 0.8 reshape.61
  7.5 0.8 reshape.66
  8.3 8.8 %collective-permute-done = bf16[32,4096]{1,0:T(8,128)(2,1)S(1)} collective-permute-done((bf16[32,4096]{1,0:T(8,128)(2,1)S(1)}, bf16[32,4096]{1,0:T(8,128)(2,1)S(1)}, u32[]{:S(2)}, u32[]{:S(2)}) %collective-permute-start) | collective-permute-done | bytes 262176 | tf_op jit(solution)/shard_map/ppermute | solution.py:147
  17.2 0.8 collective-permute-start.1
  18.0 0.3 reduce-window.16
  18.5 3.4 %collective-permute-start.4 = (bf16[64,4096]{1,0:T(8,128)(2,1)S(1)}, bf16[64,4096]{1,0:T(8,128)(2,1)S(1)}, u32[]{:S(2)}, u32[]{:S(2)}) collective-permute-start(bf16[64,4096]{1,0:T(8,128)(2,1)S(1)} %maximum_select_fusion.7), channel_id=1, source_target_pairs={{0,4},{1,5},{2,6},{3,7},{4,0},{5,1},{6,2},{7,3},{8,12},{9,13},{10,... | collective-permute-start | bytes 1572872 | tf_op jit(solution)/shard_map/ppermute | solution.py:147
  21.9 18.9 %collective-permute-done.1 = bf16[64,4096]{1,0:T(8,128)(2,1)S(1)} collective-permute-done((bf16[64,4096]{1,0:T(8,128)(2,1)S(1)}, bf16[64,4096]{1,0:T(8,128)(2,1)S(1)}, u32[]{:S(2)}, u32[]{:S(2)}) %collective-permute-start.1) | collective-permute-done | bytes 524320 | tf_op jit(solution)/shard_map/ppermute | solution.py:147
  40.8 0.2 maximum_select_fusion.4
  41.0 1.3 collective-permute-start.2
  42.3 0.1 slice_reduce_fusion.1
  42.4 2.6 collective-permute-done.4
  45.0 0.2 maximum_select_fusion.5
  45.5 0.1 fusion.2.base_ref
  45.7 0.7 reshape.65.index_ref
  46.4 22.3 %shard_map.64.refs_0_ = bf16[4096,3328]{1,0:T(8,128)(2,1)} custom-call(s32[32]{0:T(128)} %copy-done.7, s32[832]{0:T(1024)} %reshape.65.index_ref, bf16[640,128,128]{2,1,0:T(8,128)(2,1)} %refs_3_.2, bf16[640,128,128]{2,1,0:T(8,128)(2,1)} %refs_3_.2, bf16[640,128,128]{2,1,0:T(8,128)(2,1)} %refs_3_.2, bf16[640,128,128]{2,1,0:T(8,128)(2,1)} %refs_3_.2), custom_call_target="tpu_custom_call" | custom-call | bytes 54525952 | tf_op jit(solution)/shard_map/pallas_call | solution.py:108
  68.7 22.4 %shard_map.65.refs_1_ = bf16[4096,3328]{1,0:T(8,128)(2,1)} custom-call(s32[32]{0:T(128)} %copy-done.7, s32[832]{0:T(1024)} %reshape.65.index_ref, bf16[640,128,128]{2,1,0:T(8,128)(2,1)} %refs_3_.3, bf16[640,128,128]{2,1,0:T(8,128)(2,1)} %refs_3_.3, bf16[640,128,128]{2,1,0:T(8,128)(2,1)} %refs_3_.3, bf16[640,128,128]{2,1,0:T(8,128)(2,1)} %refs_3_.3), custom_call_target="tpu_custom_call" | custom-call | bytes 54525952 | tf_op jit(solution)/shard_map/pallas_call | solution.py:108
  91.1 0.5 maximum_select_fusion.1
  91.6 2.3 maximum_select_fusion.2
  93.9 2.5 pad_maximum_fusion.x_ref
  96.4 35.3 %shard_map.66 = (bf16[512,3328]{1,0:T(8,128)(2,1)}, bf16[512,3328]{1,0:T(8,128)(2,1)}) custom-call(bf16[512,4096]{1,0:T(8,128)(2,1)} %pad_maximum_fusion.x_ref, bf16[4096,3328]{1,0:T(8,128)(2,1)} %shard_map.64.refs_0_, bf16[4096,3328]{1,0:T(8,128)(2,1)} %shard_map.65.refs_1_), custom_call_target="tpu_custom_call" | custom-call | flops 27917287424 | bytes 65536000 | tf_op jit(solution)/shard_map/pallas_call | solution.py:132
  131.7 1.7 constant_dynamic-slice_fusion.3
  133.5 0.7 copy-done.3
  134.2 1.3 constant_dynamic-slice_fusion.2
  135.5 1.7 collective-permute-done.6
  137.2 2.4 convert_add_fusion.1
  139.7 1.0 dynamic-slice_convert_fusion.1
  140.7 1.7 collective-permute-start.7
  142.4 1.8 convert_add_fusion
  144.2 1.7 copy-done
  145.9 1.0 dynamic-slice_convert_fusion
  146.9 0.3 collective-permute-start.9
  147.2 15.5 %collective-permute-done.7 = bf16[128,3328]{1,0:T(8,128)(2,1)} collective-permute-done((bf16[128,3328]{1,0:T(8,128)(2,1)}, bf16[128,3328]{1,0:T(8,128)(2,1)}, u32[]{:S(2)}, u32[]{:S(2)}) %collective-permute-start.7) | collective-permute-done | bytes 852000 | tf_op jit(solution)/shard_map/ppermute | solution.py:147
  162.8 17.5 %collective-permute-done.9 = bf16[128,3328]{1,0:T(8,128)(2,1)} collective-permute-done((bf16[128,3328]{1,0:T(8,128)(2,1)}, bf16[128,3328]{1,0:T(8,128)(2,1)}, u32[]{:S(2)}, u32[]{:S(2)}) %collective-permute-start.9) | collective-permute-done | bytes 852000 | tf_op jit(solution)/shard_map/ppermute | solution.py:147
  180.2 3.4 %multiply_convert_fusion = bf16[128,3328]{1,0:T(8,128)(2,1)} fusion(bf16[128,3328]{1,0:T(8,128)(2,1)} %collective-permute-done.9, f32[256,3328]{1,0:T(8,128)} %copy-done, s32[]{:T(128)S(6)} %select_n.136, bf16[128,3328]{1,0:T(8,128)(2,1)} %collective-permute-done.7, f32[256,3328]{1,0:T(8,128)S(1)} %convert_add_fusion.1), kind=kLoop, calls=%fused_computation.9 | loop fusion | flops 4259840 | bytes 5963780 | tf_op jit(solution)/shard_map/convert_element_type | solution.py:189
  183.7 1.7 collective-permute-start.10
  185.4 18.6 %collective-permute-done.10 = bf16[128,3328]{1,0:T(8,128)(2,1)S(1)} collective-permute-done((bf16[128,3328]{1,0:T(8,128)(2,1)}, bf16[128,3328]{1,0:T(8,128)(2,1)S(1)}, u32[]{:S(2)}, u32[]{:S(2)}) %collective-permute-start.10) | collective-permute-done | bytes 852000 | tf_op jit(solution)/shard_map/ppermute | solution.py:147
  204.0 1.8 maximum_select_fusion.3
  205.9 0.3 reduce-window.24
  206.4 0.1 slice_reduce_fusion
  206.7 0.1 fusion.base_ref
  206.9 0.7 reshape.71.index_ref
  207.6 26.6 %shard_map.67.refs_0_ = bf16[3328,4096]{1,0:T(8,128)(2,1)} custom-call(s32[26]{0:T(128)} %copy-done.8, s32[832]{0:T(1024)} %reshape.71.index_ref, bf16[640,128,128]{2,1,0:T(8,128)(2,1)} %refs_1_.5, bf16[640,128,128]{2,1,0:T(8,128)(2,1)} %refs_1_.5), custom_call_target="tpu_custom_call" | custom-call | bytes 54525952 | tf_op jit(solution)/shard_map/pallas_call | solution.py:108
  234.1 2.2 maximum_select_fusion.x_ref
  236.3 20.1 %shard_map.68 = bf16[512,4096]{1,0:T(8,128)(2,1)} custom-call(bf16[512,3328]{1,0:T(8,128)(2,1)} %maximum_select_fusion.x_ref, bf16[3328,4096]{1,0:T(8,128)(2,1)} %shard_map.67.refs_0_), custom_call_target="tpu_custom_call" | custom-call | flops 13958643712 | bytes 34865152 | tf_op jit(solution)/shard_map/pallas_call | solution.py:132
  256.4 2.6 fusion.3
  259.0 1.3 copy-done.1
  260.4 1.1 constant_dynamic-slice_fusion.1
  261.5 1.5 collective-permute-start.12
  263.0 2.1 collective-permute-start.15
  265.1 22.1 %collective-permute-done.12 = bf16[128,4096]{1,0:T(8,128)(2,1)S(1)} collective-permute-done((bf16[128,4096]{1,0:T(8,128)(2,1)}, bf16[128,4096]{1,0:T(8,128)(2,1)S(1)}, u32[]{:S(2)}, u32[]{:S(2)}) %collective-permute-start.12) | collective-permute-done | bytes 1048608 | tf_op jit(solution)/shard_map/ppermute | solution.py:147
  287.2 0.3 convert_add_fusion.3
  287.6 2.1 collective-permute-start.13
  289.7 0.2 convert_add_fusion.2
  290.0 1.7 collective-permute-start.16
  291.7 20.8 %collective-permute-done.13 = bf16[64,4096]{1,0:T(8,128)(2,1)S(1)} collective-permute-done((bf16[64,4096]{1,0:T(8,128)(2,1)S(1)}, bf16[64,4096]{1,0:T(8,128)(2,1)S(1)}, u32[]{:S(2)}, u32[]{:S(2)}) %collective-permute-start.13) | collective-permute-done | bytes 524320 | tf_op jit(solution)/shard_map/ppermute | solution.py:147
  312.7 8.7 %collective-permute-done.16 = bf16[64,4096]{1,0:T(8,128)(2,1)S(1)} collective-permute-done((bf16[64,4096]{1,0:T(8,128)(2,1)S(1)}, bf16[64,4096]{1,0:T(8,128)(2,1)S(1)}, u32[]{:S(2)}, u32[]{:S(2)}) %collective-permute-start.16) | collective-permute-done | bytes 524320 | tf_op jit(solution)/shard_map/ppermute | solution.py:147
  321.3 0.1 convert_add_fusion.4
  321.5 1.8 collective-permute-start.17
  323.3 3.4 %collective-permute-done.14 = bf16[32,4096]{1,0:T(8,128)(2,1)S(1)} collective-permute-done((bf16[32,4096]{1,0:T(8,128)(2,1)S(1)}, bf16[32,4096]{1,0:T(8,128)(2,1)S(1)}, u32[]{:S(2)}, u32[]{:S(2)}) %collective-permute-start.14) | collective-permute-done | bytes 262176 | tf_op jit(solution)/shard_map/ppermute | solution.py:147
  326.8 1.1 collective-permute-done.17
  328.0 0.8 pad_maximum_fusion.1
  (50 shorter events, 1.8 us)
Async XLA Ops:
  1.1 16.0 %collective-permute-start = (bf16[32,4096]{1,0:T(8,128)(2,1)S(1)}, bf16[32,4096]{1,0:T(8,128)(2,1)S(1)}, u32[]{:S(2)}, u32[]{:S(2)}) collective-permute-start(bf16[32,4096]{1,0:T(8,128)(2,1)S(1)} %get-tuple-element.11), channel_id=1, source_target_pairs={{0,4},{1,5},{2,6},{3,7},{4,0},{5,1},{6,2},{7,3},{8,12},{9,13},{10,... | collective-permute-start | bytes 786440 | tf_op jit(solution)/shard_map/ppermute | solution.py:147
  5.2 13.2 %collective-permute-start.3 = (bf16[32,4096]{1,0:T(8,128)(2,1)S(1)}, bf16[32,4096]{1,0:T(8,128)(2,1)S(1)}, u32[]{:S(2)}, u32[]{:S(2)}) collective-permute-start(bf16[32,4096]{1,0:T(8,128)(2,1)S(1)} %get-tuple-element.12), channel_id=1, source_target_pairs={{0,1},{1,0},{2,3},{3,2},{4,5},{5,4},{6,7},{7,6},{8,9},{9,8},{10,11... | collective-permute-start | bytes 786440 | tf_op jit(solution)/shard_map/ppermute | solution.py:147
  17.2 23.6 %collective-permute-start.1 = (bf16[64,4096]{1,0:T(8,128)(2,1)S(1)}, bf16[64,4096]{1,0:T(8,128)(2,1)S(1)}, u32[]{:S(2)}, u32[]{:S(2)}) collective-permute-start(bf16[64,4096]{1,0:T(8,128)(2,1)S(1)} %maximum_select_fusion.6), channel_id=1, source_target_pairs={{0,2},{1,3},{2,0},{3,1},{4,6},{5,7},{6,4},{7,5},{8,10},{9,11},{10,... | collective-permute-start | bytes 1572872 | tf_op jit(solution)/shard_map/ppermute | solution.py:147
  18.5 27.0 %copy-start.5 = (s32[32,26]{1,0:T(8,128)S(1)}, s32[32,26]{1,0:T(8,128)}, u32[]{:S(2)}) copy-start(s32[32,26]{1,0:T(8,128)} %param.10) | copy-start | bytes 9988
  18.5 26.6 %collective-permute-start.4 = (bf16[64,4096]{1,0:T(8,128)(2,1)S(1)}, bf16[64,4096]{1,0:T(8,128)(2,1)S(1)}, u32[]{:S(2)}, u32[]{:S(2)}) collective-permute-start(bf16[64,4096]{1,0:T(8,128)(2,1)S(1)} %maximum_select_fusion.7), channel_id=1, source_target_pairs={{0,4},{1,5},{2,6},{3,7},{4,0},{5,1},{6,2},{7,3},{8,12},{9,13},{10,... | collective-permute-start | bytes 1572872 | tf_op jit(solution)/shard_map/ppermute | solution.py:147
  41.0 50.1 %collective-permute-start.2 = (bf16[128,4096]{1,0:T(8,128)(2,1)S(1)}, bf16[128,4096]{1,0:T(8,128)(2,1)S(1)}, u32[]{:S(2)}, u32[]{:S(2)}) collective-permute-start(bf16[128,4096]{1,0:T(8,128)(2,1)S(1)} %maximum_select_fusion.4), channel_id=1, source_target_pairs={{0,1},{1,0},{2,3},{3,2},{4,5},{5,4},{6,7},{7,6},{8,9},{9,8},{10,11... | collective-permute-start | bytes 3145736 | tf_op jit(solution)/shard_map/ppermute | solution.py:147
  45.2 46.4 %collective-permute-start.5 = (bf16[128,4096]{1,0:T(8,128)(2,1)S(1)}, bf16[128,4096]{1,0:T(8,128)(2,1)}, u32[]{:S(2)}, u32[]{:S(2)}) collective-permute-start(bf16[128,4096]{1,0:T(8,128)(2,1)S(1)} %maximum_select_fusion.5), channel_id=1, source_target_pairs={{0,2},{1,3},{2,0},{3,1},{4,6},{5,7},{6,4},{7,5},{8,10},{9,11},{10,... | collective-permute-start | bytes 3145736 | tf_op jit(solution)/shard_map/ppermute | solution.py:147
  45.6 0.8 copy-start.7
  131.7 2.5 copy-start.3
  133.4 3.8 %collective-permute-start.6 = (bf16[256,3328]{1,0:T(8,128)(2,1)S(1)}, bf16[256,3328]{1,0:T(8,128)(2,1)}, u32[]{:S(2)}, u32[]{:S(2)}) collective-permute-start(bf16[256,3328]{1,0:T(8,128)(2,1)S(1)} %constant_dynamic-slice_fusion.3), channel_id=1, source_target_pairs={{0,8},{8,0},{16,24},{24,16},{1,9},{9,1},{17,25},{25,17},{2,10},{10... | collective-permute-start | bytes 5111816 | tf_op jit(solution)/shard_map/ppermute | solution.py:147
  135.5 6.9 %collective-permute-start.8 = (bf16[256,3328]{1,0:T(8,128)(2,1)}, bf16[256,3328]{1,0:T(8,128)(2,1)}, u32[]{:S(2)}, u32[]{:S(2)}) collective-permute-start(bf16[256,3328]{1,0:T(8,128)(2,1)} %constant_dynamic-slice_fusion.2), channel_id=1, source_target_pairs={{0,8},{8,0},{16,24},{24,16},{1,9},{9,1},{17,25},{25,17},{2,10},{10... | collective-permute-start | bytes 5111816 | tf_op jit(solution)/shard_map/ppermute | solution.py:147
  137.2 5.2 %copy-start.4 = (bf16[512,3328]{1,0:T(8,128)(2,1)S(1)}, bf16[512,3328]{1,0:T(8,128)(2,1)}, u32[]{:S(2)}) copy-start(bf16[512,3328]{1,0:T(8,128)(2,1)} %get-tuple-element.8) | copy-start | bytes 10223620
  140.7 22.1 %collective-permute-start.7 = (bf16[128,3328]{1,0:T(8,128)(2,1)}, bf16[128,3328]{1,0:T(8,128)(2,1)}, u32[]{:S(2)}, u32[]{:S(2)}) collective-permute-start(bf16[128,3328]{1,0:T(8,128)(2,1)} %dynamic-slice_convert_fusion.1), channel_id=1, source_target_pairs={{0,16},{8,24},{16,0},{24,8},{1,17},{9,25},{17,1},{25,9},{2,18},{10... | collective-permute-start | bytes 2555912 | tf_op jit(solution)/shard_map/ppermute | solution.py:147
  144.2 1.7 copy-start
  146.9 33.3 %collective-permute-start.9 = (bf16[128,3328]{1,0:T(8,128)(2,1)}, bf16[128,3328]{1,0:T(8,128)(2,1)}, u32[]{:S(2)}, u32[]{:S(2)}) collective-permute-start(bf16[128,3328]{1,0:T(8,128)(2,1)} %dynamic-slice_convert_fusion), channel_id=1, source_target_pairs={{0,16},{8,24},{16,0},{24,8},{1,17},{9,25},{17,1},{25,9},{2,18},{10... | collective-permute-start | bytes 2555912 | tf_op jit(solution)/shard_map/ppermute | solution.py:147
  183.7 23.0 %copy-start.6 = (s32[26,32]{1,0:T(8,128)S(1)}, s32[26,32]{1,0:T(8,128)}, u32[]{:S(2)}) copy-start(s32[26,32]{1,0:T(8,128)} %param.11) | copy-start | bytes 9988
  183.7 20.4 %collective-permute-start.10 = (bf16[128,3328]{1,0:T(8,128)(2,1)}, bf16[128,3328]{1,0:T(8,128)(2,1)S(1)}, u32[]{:S(2)}, u32[]{:S(2)}) collective-permute-start(bf16[128,3328]{1,0:T(8,128)(2,1)} %multiply_convert_fusion), channel_id=1, source_target_pairs={{0,16},{8,24},{16,0},{24,8},{1,17},{9,25},{17,1},{25,9},{2,18},{10... | collective-permute-start | bytes 2555912 | tf_op jit(solution)/shard_map/ppermute | solution.py:147
  205.8 28.3 %collective-permute-start.11 = (bf16[256,3328]{1,0:T(8,128)(2,1)S(1)}, bf16[256,3328]{1,0:T(8,128)(2,1)S(1)}, u32[]{:S(2)}, u32[]{:S(2)}) collective-permute-start(bf16[256,3328]{1,0:T(8,128)(2,1)S(1)} %maximum_select_fusion.3), channel_id=1, source_target_pairs={{0,8},{8,0},{16,24},{24,16},{1,9},{9,1},{17,25},{25,17},{2,10},{10... | collective-permute-start | bytes 5111816 | tf_op jit(solution)/shard_map/ppermute | solution.py:147
  206.8 0.8 copy-start.8
  259.0 1.3 copy-start.1
  261.5 25.8 %collective-permute-start.12 = (bf16[128,4096]{1,0:T(8,128)(2,1)}, bf16[128,4096]{1,0:T(8,128)(2,1)S(1)}, u32[]{:S(2)}, u32[]{:S(2)}) collective-permute-start(bf16[128,4096]{1,0:T(8,128)(2,1)} %constant_dynamic-slice_fusion.1), channel_id=1, source_target_pairs={{0,1},{1,0},{2,3},{3,2},{4,5},{5,4},{6,7},{7,6},{8,9},{9,8},{10,11... | collective-permute-start | bytes 3145736 | tf_op jit(solution)/shard_map/ppermute | solution.py:147
  263.0 24.3 %copy-start.2 = (bf16[256,4096]{1,0:T(8,128)(2,1)S(1)}, bf16[256,4096]{1,0:T(8,128)(2,1)}, u32[]{:S(2)}) copy-start(bf16[256,4096]{1,0:T(8,128)(2,1)} %copy-done.1) | copy-start | bytes 6291460
  263.0 26.6 %collective-permute-start.15 = (bf16[128,4096]{1,0:T(8,128)(2,1)S(1)}, bf16[128,4096]{1,0:T(8,128)(2,1)S(1)}, u32[]{:S(2)}, u32[]{:S(2)}) collective-permute-start(bf16[128,4096]{1,0:T(8,128)(2,1)S(1)} %constant_dynamic-slice_fusion), channel_id=1, source_target_pairs={{0,2},{1,3},{2,0},{3,1},{4,6},{5,7},{6,4},{7,5},{8,10},{9,11},{10,... | collective-permute-start | bytes 3145736 | tf_op jit(solution)/shard_map/ppermute | solution.py:147
  287.6 24.9 %collective-permute-start.13 = (bf16[64,4096]{1,0:T(8,128)(2,1)S(1)}, bf16[64,4096]{1,0:T(8,128)(2,1)S(1)}, u32[]{:S(2)}, u32[]{:S(2)}) collective-permute-start(bf16[64,4096]{1,0:T(8,128)(2,1)S(1)} %dynamic-slice_convert_fusion.3), channel_id=1, source_target_pairs={{0,2},{1,3},{2,0},{3,1},{4,6},{5,7},{6,4},{7,5},{8,10},{9,11},{10,... | collective-permute-start | bytes 1572872 | tf_op jit(solution)/shard_map/ppermute | solution.py:147
  290.0 31.3 %collective-permute-start.16 = (bf16[64,4096]{1,0:T(8,128)(2,1)S(1)}, bf16[64,4096]{1,0:T(8,128)(2,1)S(1)}, u32[]{:S(2)}, u32[]{:S(2)}) collective-permute-start(bf16[64,4096]{1,0:T(8,128)(2,1)S(1)} %dynamic-slice_convert_fusion.2), channel_id=1, source_target_pairs={{0,4},{1,5},{2,6},{3,7},{4,0},{5,1},{6,2},{7,3},{8,12},{9,13},{10,... | collective-permute-start | bytes 1572872 | tf_op jit(solution)/shard_map/ppermute | solution.py:147
  312.6 14.2 %collective-permute-start.14 = (bf16[32,4096]{1,0:T(8,128)(2,1)S(1)}, bf16[32,4096]{1,0:T(8,128)(2,1)S(1)}, u32[]{:S(2)}, u32[]{:S(2)}) collective-permute-start(bf16[32,4096]{1,0:T(8,128)(2,1)S(1)} %dynamic-slice_convert_fusion.5), channel_id=1, source_target_pairs={{0,4},{1,5},{2,6},{3,7},{4,0},{5,1},{6,2},{7,3},{8,12},{9,13},{10,... | collective-permute-start | bytes 786440 | tf_op jit(solution)/shard_map/ppermute | solution.py:147
  321.5 6.4 %collective-permute-start.17 = (bf16[32,4096]{1,0:T(8,128)(2,1)S(1)}, bf16[32,4096]{1,0:T(8,128)(2,1)S(1)}, u32[]{:S(2)}, u32[]{:S(2)}) collective-permute-start(bf16[32,4096]{1,0:T(8,128)(2,1)S(1)} %dynamic-slice_convert_fusion.4), channel_id=1, source_target_pairs={{0,1},{1,0},{2,3},{3,2},{4,5},{5,4},{6,7},{7,6},{8,9},{9,8},{10,11... | collective-permute-start | bytes 786440 | tf_op jit(solution)/shard_map/ppermute | solution.py:147

commit v4 on v1

--- a/solution.py
+++ b/solution.py
@@ -118,21 +118,29 @@
     row_bits = list(range(n_row.bit_length() - 1))
     top = n_col.bit_length() - 1
     col_orders = [list(range(top - 1, -1, -1)), [0] + list(range(top - 1, 0, -1))]
-    t_half = tokens.shape[0] // 2
-    token_parts = [tokens[:t_half], tokens[t_half:]]
-    segment = jnp.concatenate(
-        doubling_gather(list(zip(token_parts, col_orders)), "col", n_col), axis=0)
+    quarter = tokens.shape[0] // 4
+    orders = col_orders * 2
+    token_parts = [tokens[q * quarter:(q + 1) * quarter] for q in range(4)]
+    segment = jnp.concatenate(doubling_gather(list(zip(token_parts, orders)), "col", n_col), axis=0)
     gate_rows, up_rows = sparse_matmul(segment, [gate_packed, up_packed], gate_keep)
-    ((gate_sum, up_sum),) = halving_scatter([([gate_rows, up_rows], row_bits)], "row", n_row)
-    hidden_share = (jax.nn.silu(gate_sum) * up_sum).astype(jnp.bfloat16)
-    (every_hidden,) = doubling_gather([(hidden_share, row_bits[::-1])], "row", n_row)
-    (partial_out,) = sparse_matmul(every_hidden, [down_packed], down_keep)
-    half_rows = partial_out.shape[0] // 2
-    out_parts = halving_scatter(
-        [([partial_out[:half_rows]], col_orders[0][::-1]), ([partial_out[half_rows:]], col_orders[1][::-1])],
-        "col", n_col)
-    summed = jnp.concatenate([parts[0] for parts in out_parts], axis=0)
-    return summed.astype(jnp.bfloat16)
+    half = segment.shape[0] // 2
+    results = []
+    held = None
+    for h in range(2):
+        gate_h, up_h = gate_rows[h * half:(h + 1) * half], up_rows[h * half:(h + 1) * half]
+        if held is not None:
+            held, gate_h, up_h = lax.optimization_barrier((held, gate_h, up_h))
+        ((gate_sum, up_sum),) = halving_scatter([([gate_h, up_h], row_bits)], "row", n_row)
+        hidden_share = (jax.nn.silu(gate_sum) * up_sum).astype(jnp.bfloat16)
+        (hidden,) = doubling_gather([(hidden_share, row_bits[::-1])], "row", n_row)
+        held = hidden
+        (partial_out,) = sparse_matmul(hidden, [down_packed], down_keep)
+        out_parts = halving_scatter(
+            [([partial_out[:half // 2]], orders[2 * h][::-1]),
+             ([partial_out[half // 2:]], orders[2 * h + 1][::-1])],
+            "col", n_col)
+        results += [parts[0] for parts in out_parts]
+    return jnp.concatenate(results, axis=0).astype(jnp.bfloat16)
 
 
 def solution(mesh):

time: 294 us -> 307 us (1.044)
  waiting for transfers between devices: 161 us -> 141 us
  starting transfers between devices: 25.1 us -> 44.7 us
  Pallas kernels: 68.8 us -> 85.6 us
  local copies, waits for them, and re-layouts: 17.5 us -> 14.2 us
    ppermute x18 -> x36, waiting for transfers between devices: 161 us -> 141 us  [exchange(): return lax.ppermute(x, axis, perm=pairs)]
    ppermute x18 -> x36, starting transfers between devices: 25.1 us -> 44.7 us  [exchange(): return lax.ppermute(x, axis, perm=pairs)]
    pallas_call x2 -> x3, Pallas kernels: 68.8 us -> 85.6 us  [sparse_matmul(): pl.pallas_call(kernel, grid_spec=pltpu.PrefetchScalarGridSpec(num_scalar_...]
    dynamic_slice x4 -> x8, local copies, waits for them, and re-layouts: 4.22 us -> 0.42 us  [halving_scatter(): lax.dynamic_slice_in_dim(p, (1 - mine) * half, half, axis=0)]
    add x6 -> x12, other arithmetic: 4.95 us -> 1.33 us  [halving_scatter(): k.astype(jnp.float32) + g.astype(jnp.float32)]
    slice x3 -> x6, local copies, waits for them, and re-layouts: 3.72 us -> 7.11 us  [the longest x2 3.35 us: local(): partial_out[:half // 2]]
    select_n x8 -> x16, other arithmetic: 7.29 us -> 9.06 us  [doubling_gather(): jnp.where(low, jnp.concatenate([xs[p], got], 0), jnp.concatenate([got, xs...]
  transfers between devices with their start and end apart: 18 -> 36, of which waited for: 15 -> 22; matrix products, arithmetic and copies ran while one was open for 5% -> 5% of each run, Pallas kernels for 0% -> 7%
where the time goes in v4:
time: 307 us; the launch traced here: 306 us
  waiting for transfers between devices  141 us (46%)
  Pallas kernels  85.6 us (28%)
  starting transfers between devices  44.7 us (15%)
  other arithmetic  19.4 us (6%)
  local copies, waits for them, and re-layouts  14.2 us (5%)
    ppermute x36, waiting for transfers between devices, exchange(): return lax.ppermute(x, axis, perm=pairs)  141 us
    pallas_call x3, Pallas kernels, sparse_matmul(): pl.pallas_call(kernel, grid_spec=pltpu.PrefetchScalarGridSpec(num_scalar_...  85.6 us
    ppermute x36, starting transfers between devices, exchange(): return lax.ppermute(x, axis, perm=pairs)  44.7 us
    select_n x16, other arithmetic, doubling_gather(): jnp.where(low, jnp.concatenate([xs[p], got], 0), jnp.concatenate([got, xs...  9.06 us
  transfers between devices with their start and end apart: 36, of which 22 were waited for; matrix products, arithmetic and copies ran while one was open for 5% of the time, Pallas kernels for 7%

profile of v4, /device:TPU:0, one launch (start us, length us, event | category | flops | bytes accessed | tf_op | source)
XLA Modules:
  0.0 305.6 jit_solution(15526997092570366179)
XLA Ops:
  0.0 1.1 fusion.7
  1.1 4.1 %collective-permute-start = (bf16[16,4096]{1,0:T(8,128)(2,1)S(1)}, bf16[16,4096]{1,0:T(8,128)(2,1)S(1)}, u32[]{:S(2)}, u32[]{:S(2)}) collective-permute-start(bf16[16,4096]{1,0:T(8,128)(2,1)S(1)} %get-tuple-element.21), channel_id=1, source_target_pairs={{0,4},{1,5},{2,6},{3,7},{4,0},{5,1},{6,2},{7,3},{8,12},{9,13},{10,... | collective-permute-start | bytes 393224 | tf_op jit(solution)/shard_map/ppermute | solution.py:85
  5.2 1.5 collective-permute-start.3
  7.3 0.8 reshape.61
  8.1 0.8 reshape.67
  9.6 0.7 sub.27
  10.5 0.8 subtract_select_fusion
  11.3 0.7 reshape.71.index_ref
  12.0 3.2 %collective-permute-done = bf16[16,4096]{1,0:T(8,128)(2,1)S(1)} collective-permute-done((bf16[16,4096]{1,0:T(8,128)(2,1)S(1)}, bf16[16,4096]{1,0:T(8,128)(2,1)S(1)}, u32[]{:S(2)}, u32[]{:S(2)}) %collective-permute-start) | collective-permute-done | bytes 131104 | tf_op jit(solution)/shard_map/ppermute | solution.py:85
  15.4 3.4 %collective-permute-start.4 = (bf16[32,4096]{1,0:T(8,128)(2,1)S(1)}, bf16[32,4096]{1,0:T(8,128)(2,1)S(1)}, u32[]{:S(2)}, u32[]{:S(2)}) collective-permute-start(bf16[32,4096]{1,0:T(8,128)(2,1)S(1)} %maximum_select_fusion.13), channel_id=1, source_target_pairs={{0,4},{1,5},{2,6},{3,7},{4,0},{5,1},{6,2},{7,3},{8,12},{9,13},{10,... | collective-permute-start | bytes 786440 | tf_op jit(solution)/shard_map/ppermute | solution.py:85
  19.0 2.5 collective-permute-start.10
  21.5 8.6 %collective-permute-done.1 = bf16[32,4096]{1,0:T(8,128)(2,1)S(1)} collective-permute-done((bf16[32,4096]{1,0:T(8,128)(2,1)S(1)}, bf16[32,4096]{1,0:T(8,128)(2,1)S(1)}, u32[]{:S(2)}, u32[]{:S(2)}) %collective-permute-start.1) | collective-permute-done | bytes 262176 | tf_op jit(solution)/shard_map/ppermute | solution.py:85
  30.2 2.2 collective-permute-start.2
  32.6 8.7 %collective-permute-done.7 = bf16[32,4096]{1,0:T(8,128)(2,1)S(1)} collective-permute-done((bf16[32,4096]{1,0:T(8,128)(2,1)S(1)}, bf16[32,4096]{1,0:T(8,128)(2,1)S(1)}, u32[]{:S(2)}, u32[]{:S(2)}) %collective-permute-start.7) | collective-permute-done | bytes 262176 | tf_op jit(solution)/shard_map/ppermute | solution.py:85
  41.4 2.0 collective-permute-start.8
  43.8 8.8 %collective-permute-done.5 = bf16[64,4096]{1,0:T(8,128)(2,1)S(1)} collective-permute-done((bf16[64,4096]{1,0:T(8,128)(2,1)S(1)}, bf16[64,4096]{1,0:T(8,128)(2,1)S(1)}, u32[]{:S(2)}, u32[]{:S(2)}) %collective-permute-start.5) | collective-permute-done | bytes 524320 | tf_op jit(solution)/shard_map/ppermute | solution.py:85
  53.1 9.0 %collective-permute-done.11 = bf16[64,4096]{1,0:T(8,128)(2,1)S(1)} collective-permute-done((bf16[64,4096]{1,0:T(8,128)(2,1)S(1)}, bf16[64,4096]{1,0:T(8,128)(2,1)S(1)}, u32[]{:S(2)}, u32[]{:S(2)}) %collective-permute-start.11) | collective-permute-done | bytes 524320 | tf_op jit(solution)/shard_map/ppermute | solution.py:85
  62.3 2.4 pad_maximum_fusion.x_ref
  64.8 43.4 %shard_map.64 = (bf16[512,3328]{1,0:T(8,128)(2,1)}, bf16[512,3328]{1,0:T(8,128)(2,1)}) custom-call(s32[32]{0:T(128)} %copy-done.5, s32[832]{0:T(1024)} %reshape.71.index_ref, bf16[512,4096]{1,0:T(8,128)(2,1)} %pad_maximum_fusion.x_ref, bf16[640,128,128]{2,1,0:T(8,128)(2,1)} %refs_3_.1, bf16[640,128,128]{2,1,0:T(8,128)(2,1)} %refs_3_.1, ...), custom_call_target="tpu_custom_call" | custom-call | flops 27917287424 | bytes 65536000 | tf_op jit(solution)/shard_map/pallas_call | solution.py:66
  108.2 2.3 fusion.4
  111.5 1.5 collective-permute-done.12
  113.2 0.9 dynamic-slice_convert_fusion.3
  114.1 1.6 collective-permute-start.13
  115.9 0.9 dynamic-slice_convert_fusion.2
  117.6 9.4 %collective-permute-done.13 = bf16[64,3328]{1,0:T(8,128)(2,1)} collective-permute-done((bf16[64,3328]{1,0:T(8,128)(2,1)}, bf16[64,3328]{1,0:T(8,128)(2,1)}, u32[]{:S(2)}, u32[]{:S(2)}) %collective-permute-start.13) | collective-permute-done | bytes 426016 | tf_op jit(solution)/shard_map/ppermute | solution.py:85
  127.1 8.3 %collective-permute-done.15 = bf16[64,3328]{1,0:T(8,128)(2,1)} collective-permute-done((bf16[64,3328]{1,0:T(8,128)(2,1)}, bf16[64,3328]{1,0:T(8,128)(2,1)}, u32[]{:S(2)}, u32[]{:S(2)}) %collective-permute-start.15) | collective-permute-done | bytes 426016 | tf_op jit(solution)/shard_map/ppermute | solution.py:85
  135.4 2.7 multiply_convert_fusion.1
  138.1 1.6 collective-permute-start.16
  139.7 9.8 %collective-permute-done.16 = bf16[64,3328]{1,0:T(8,128)(2,1)} collective-permute-done((bf16[64,3328]{1,0:T(8,128)(2,1)}, bf16[64,3328]{1,0:T(8,128)(2,1)}, u32[]{:S(2)}, u32[]{:S(2)}) %collective-permute-start.16) | collective-permute-done | bytes 426016 | tf_op jit(solution)/shard_map/ppermute | solution.py:85
  149.5 2.5 maximum_select_fusion.6
  153.0 0.7 reshape.66.index_ref
  153.7 1.0 collective-permute-done.17
  154.7 3.5 %maximum_select_fusion.x_ref = bf16[256,3328]{1,0:T(8,128)(2,1)} fusion(bf16[128,3328]{1,0:T(8,128)(2,1)} %collective-permute-done.17, bf16[128,3328]{1,0:T(8,128)(2,1)} %maximum_select_fusion.6, pred[]{:T(512)S(6)} %eq.17), kind=kLoop, calls=%fused_computation.1 | loop fusion | flops 7667712 | bytes 3407873 | tf_op jit(solution)/shard_map/jit(_where)/select_n | solution.py:111
  158.2 21.1 %shard_map.65 = bf16[256,4096]{1,0:T(8,128)(2,1)} custom-call(s32[26]{0:T(128)} %copy-done.4, s32[832]{0:T(1024)} %reshape.66.index_ref, bf16[256,3328]{1,0:T(8,128)(2,1)} %maximum_select_fusion.x_ref, bf16[640,128,128]{2,1,0:T(8,128)(2,1)} %refs_1_.5, bf16[640,128,128]{2,1,0:T(8,128)(2,1)} %refs_1_.5), custom_call_target="tpu_custom_call" | custom-call | flops 6979321856 | bytes 31064064 | tf_op jit(solution)/shard_map/pallas_call | solution.py:66
  179.3 1.7 fusion.5
  181.1 1.6 collective-permute-start.18
  182.7 0.8 collective-permute-start.21
  184.2 10.9 %collective-permute-done.18 = bf16[64,4096]{1,0:T(8,128)(2,1)S(1)} collective-permute-done((bf16[64,4096]{1,0:T(8,128)(2,1)S(1)}, bf16[64,4096]{1,0:T(8,128)(2,1)S(1)}, u32[]{:S(2)}, u32[]{:S(2)}) %collective-permute-start.18) | collective-permute-done | bytes 524320 | tf_op jit(solution)/shard_map/ppermute | solution.py:85
  195.2 0.8 collective-permute-start.19
  196.6 3.0 collective-permute-start.22
  199.6 8.4 %collective-permute-done.19 = bf16[32,4096]{1,0:T(8,128)(2,1)S(1)} collective-permute-done((bf16[32,4096]{1,0:T(8,128)(2,1)S(1)}, bf16[32,4096]{1,0:T(8,128)(2,1)S(1)}, u32[]{:S(2)}, u32[]{:S(2)}) %collective-permute-start.19) | collective-permute-done | bytes 262176 | tf_op jit(solution)/shard_map/ppermute | solution.py:85
  208.5 1.6 collective-permute-start.25
  210.3 0.6 collective-permute-start.27
  210.9 3.1 %collective-permute-done.22 = bf16[32,4096]{1,0:T(8,128)(2,1)S(1)} collective-permute-done((bf16[32,4096]{1,0:T(8,128)(2,1)S(1)}, bf16[32,4096]{1,0:T(8,128)(2,1)S(1)}, u32[]{:S(2)}, u32[]{:S(2)}) %collective-permute-start.22) | collective-permute-done | bytes 262176 | tf_op jit(solution)/shard_map/ppermute | solution.py:85
  214.0 7.3 %collective-permute-done.25 = bf16[64,3328]{1,0:T(8,128)(2,1)S(1)} collective-permute-done((bf16[64,3328]{1,0:T(8,128)(2,1)S(1)}, bf16[64,3328]{1,0:T(8,128)(2,1)S(1)}, u32[]{:S(2)}, u32[]{:S(2)}) %collective-permute-start.25) | collective-permute-done | bytes 426016 | tf_op jit(solution)/shard_map/ppermute | solution.py:85
  221.3 6.2 %collective-permute-done.27 = bf16[64,3328]{1,0:T(8,128)(2,1)S(1)} collective-permute-done((bf16[64,3328]{1,0:T(8,128)(2,1)S(1)}, bf16[64,3328]{1,0:T(8,128)(2,1)S(1)}, u32[]{:S(2)}, u32[]{:S(2)}) %collective-permute-start.27) | collective-permute-done | bytes 426016 | tf_op jit(solution)/shard_map/ppermute | solution.py:85
  227.8 1.6 collective-permute-start.28
  229.5 1.7 collective-permute-start.23
  231.2 5.6 %collective-permute-done.28 = bf16[64,3328]{1,0:T(8,128)(2,1)S(1)} collective-permute-done((bf16[64,3328]{1,0:T(8,128)(2,1)S(1)}, bf16[64,3328]{1,0:T(8,128)(2,1)S(1)}, u32[]{:S(2)}, u32[]{:S(2)}) %collective-permute-start.28) | collective-permute-done | bytes 426016 | tf_op jit(solution)/shard_map/ppermute | solution.py:85
  237.1 2.3 collective-permute-done.29
  239.4 1.5 maximum_select_fusion.1.x_ref
  240.9 21.1 %shard_map.66 = bf16[256,4096]{1,0:T(8,128)(2,1)} custom-call(s32[26]{0:T(128)} %copy-done.4, s32[832]{0:T(1024)} %reshape.66.index_ref, bf16[256,3328]{1,0:T(8,128)(2,1)} %maximum_select_fusion.1.x_ref, bf16[640,128,128]{2,1,0:T(8,128)(2,1)} %refs_1_.5, bf16[640,128,128]{2,1,0:T(8,128)(2,1)} %refs_1_.5), custom_call_target="tpu_custom_call" | custom-call | flops 6979321856 | bytes 31064064 | tf_op jit(solution)/shard_map/pallas_call | solution.py:66
  262.0 1.7 fusion.6
  263.7 2.3 collective-permute-start.30
  266.1 2.6 collective-permute-start.33
  268.7 9.6 %collective-permute-done.30 = bf16[64,4096]{1,0:T(8,128)(2,1)S(1)} collective-permute-done((bf16[64,4096]{1,0:T(8,128)(2,1)S(1)}, bf16[64,4096]{1,0:T(8,128)(2,1)S(1)}, u32[]{:S(2)}, u32[]{:S(2)}) %collective-permute-start.30) | collective-permute-done | bytes 524320 | tf_op jit(solution)/shard_map/ppermute | solution.py:85
  278.4 2.6 collective-permute-start.31
  281.2 0.6 collective-permute-start.34
  281.8 8.6 %collective-permute-done.31 = bf16[32,4096]{1,0:T(8,128)(2,1)S(1)} collective-permute-done((bf16[32,4096]{1,0:T(8,128)(2,1)S(1)}, bf16[32,4096]{1,0:T(8,128)(2,1)S(1)}, u32[]{:S(2)}, u32[]{:S(2)}) %collective-permute-start.31) | collective-permute-done | bytes 262176 | tf_op jit(solution)/shard_map/ppermute | solution.py:85
  290.6 2.2 collective-permute-start.32
  292.7 6.9 %collective-permute-done.34 = bf16[32,4096]{1,0:T(8,128)(2,1)S(1)} collective-permute-done((bf16[32,4096]{1,0:T(8,128)(2,1)S(1)}, bf16[32,4096]{1,0:T(8,128)(2,1)S(1)}, u32[]{:S(2)}, u32[]{:S(2)}) %collective-permute-start.34) | collective-permute-done | bytes 262176 | tf_op jit(solution)/shard_map/ppermute | solution.py:85
  299.7 1.5 collective-permute-start.35
  301.2 3.5 %collective-permute-done.35 = bf16[16,4096]{1,0:T(8,128)(2,1)S(1)} collective-permute-done((bf16[16,4096]{1,0:T(8,128)(2,1)S(1)}, bf16[16,4096]{1,0:T(8,128)(2,1)S(1)}, u32[]{:S(2)}, u32[]{:S(2)}) %collective-permute-start.35) | collective-permute-done | bytes 131104 | tf_op jit(solution)/shard_map/ppermute | solution.py:85
  304.8 0.8 pad_maximum_fusion.1
  (108 shorter events, 9.7 us)
Async XLA Ops:
  1.1 14.0 %collective-permute-start = (bf16[16,4096]{1,0:T(8,128)(2,1)S(1)}, bf16[16,4096]{1,0:T(8,128)(2,1)S(1)}, u32[]{:S(2)}, u32[]{:S(2)}) collective-permute-start(bf16[16,4096]{1,0:T(8,128)(2,1)S(1)} %get-tuple-element.21), channel_id=1, source_target_pairs={{0,4},{1,5},{2,6},{3,7},{4,0},{5,1},{6,2},{7,3},{8,12},{9,13},{10,... | collective-permute-start | bytes 393224 | tf_op jit(solution)/shard_map/ppermute | solution.py:85
  5.2 10.1 %collective-permute-start.3 = (bf16[16,4096]{1,0:T(8,128)(2,1)S(1)}, bf16[16,4096]{1,0:T(8,128)(2,1)S(1)}, u32[]{:S(2)}, u32[]{:S(2)}) collective-permute-start(bf16[16,4096]{1,0:T(8,128)(2,1)S(1)} %get-tuple-element.22), channel_id=1, source_target_pairs={{0,1},{1,0},{2,3},{3,2},{4,5},{5,4},{6,7},{7,6},{8,9},{9,8},{10,11... | collective-permute-start | bytes 393224 | tf_op jit(solution)/shard_map/ppermute | solution.py:85
  6.7 12.1 %collective-permute-start.6 = (bf16[16,4096]{1,0:T(8,128)(2,1)S(1)}, bf16[16,4096]{1,0:T(8,128)(2,1)S(1)}, u32[]{:S(2)}, u32[]{:S(2)}) collective-permute-start(bf16[16,4096]{1,0:T(8,128)(2,1)S(1)} %get-tuple-element.24), channel_id=1, source_target_pairs={{0,4},{1,5},{2,6},{3,7},{4,0},{5,1},{6,2},{7,3},{8,12},{9,13},{10,... | collective-permute-start | bytes 393224 | tf_op jit(solution)/shard_map/ppermute | solution.py:85
  7.1 11.9 %collective-permute-start.9 = (bf16[16,4096]{1,0:T(8,128)(2,1)S(1)}, bf16[16,4096]{1,0:T(8,128)(2,1)S(1)}, u32[]{:S(2)}, u32[]{:S(2)}) collective-permute-start(bf16[16,4096]{1,0:T(8,128)(2,1)S(1)} %get-tuple-element.23), channel_id=1, source_target_pairs={{0,1},{1,0},{2,3},{3,2},{4,5},{5,4},{6,7},{7,6},{8,9},{9,8},{10,11... | collective-permute-start | bytes 393224 | tf_op jit(solution)/shard_map/ppermute | solution.py:85
  10.5 22.0 %copy-start.5 = (s32[32]{0:T(128)}, s32[32]{0:T(128)S(1)}, u32[]{:S(2)}) copy-start(s32[32]{0:T(128)S(1)} %fusion.base_ref) | copy-start | bytes 388
  15.2 14.9 %collective-permute-start.1 = (bf16[32,4096]{1,0:T(8,128)(2,1)S(1)}, bf16[32,4096]{1,0:T(8,128)(2,1)S(1)}, u32[]{:S(2)}, u32[]{:S(2)}) collective-permute-start(bf16[32,4096]{1,0:T(8,128)(2,1)S(1)} %maximum_select_fusion.12), channel_id=1, source_target_pairs={{0,2},{1,3},{2,0},{3,1},{4,6},{5,7},{6,4},{7,5},{8,10},{9,11},{10,... | collective-permute-start | bytes 786440 | tf_op jit(solution)/shard_map/ppermute | solution.py:85
  15.4 17.1 %collective-permute-start.4 = (bf16[32,4096]{1,0:T(8,128)(2,1)S(1)}, bf16[32,4096]{1,0:T(8,128)(2,1)S(1)}, u32[]{:S(2)}, u32[]{:S(2)}) collective-permute-start(bf16[32,4096]{1,0:T(8,128)(2,1)S(1)} %maximum_select_fusion.13), channel_id=1, source_target_pairs={{0,4},{1,5},{2,6},{3,7},{4,0},{5,1},{6,2},{7,3},{8,12},{9,13},{10,... | collective-permute-start | bytes 786440 | tf_op jit(solution)/shard_map/ppermute | solution.py:85
  18.8 22.4 %collective-permute-start.7 = (bf16[32,4096]{1,0:T(8,128)(2,1)S(1)}, bf16[32,4096]{1,0:T(8,128)(2,1)S(1)}, u32[]{:S(2)}, u32[]{:S(2)}) collective-permute-start(bf16[32,4096]{1,0:T(8,128)(2,1)S(1)} %maximum_select_fusion.14), channel_id=1, source_target_pairs={{0,2},{1,3},{2,0},{3,1},{4,6},{5,7},{6,4},{7,5},{8,10},{9,11},{10,... | collective-permute-start | bytes 786440 | tf_op jit(solution)/shard_map/ppermute | solution.py:85
  19.0 24.4 %collective-permute-start.10 = (bf16[32,4096]{1,0:T(8,128)(2,1)S(1)}, bf16[32,4096]{1,0:T(8,128)(2,1)S(1)}, u32[]{:S(2)}, u32[]{:S(2)}) collective-permute-start(bf16[32,4096]{1,0:T(8,128)(2,1)S(1)} %maximum_select_fusion.15), channel_id=1, source_target_pairs={{0,4},{1,5},{2,6},{3,7},{4,0},{5,1},{6,2},{7,3},{8,12},{9,13},{10,... | collective-permute-start | bytes 786440 | tf_op jit(solution)/shard_map/ppermute | solution.py:85
  30.2 13.4 %collective-permute-start.2 = (bf16[64,4096]{1,0:T(8,128)(2,1)S(1)}, bf16[64,4096]{1,0:T(8,128)(2,1)S(1)}, u32[]{:S(2)}, u32[]{:S(2)}) collective-permute-start(bf16[64,4096]{1,0:T(8,128)(2,1)S(1)} %maximum_select_fusion.8), channel_id=1, source_target_pairs={{0,1},{1,0},{2,3},{3,2},{4,5},{5,4},{6,7},{7,6},{8,9},{9,8},{10,11... | collective-permute-start | bytes 1572872 | tf_op jit(solution)/shard_map/ppermute | solution.py:85
  32.5 20.1 %collective-permute-start.5 = (bf16[64,4096]{1,0:T(8,128)(2,1)S(1)}, bf16[64,4096]{1,0:T(8,128)(2,1)S(1)}, u32[]{:S(2)}, u32[]{:S(2)}) collective-permute-start(bf16[64,4096]{1,0:T(8,128)(2,1)S(1)} %maximum_select_fusion.9), channel_id=1, source_target_pairs={{0,2},{1,3},{2,0},{3,1},{4,6},{5,7},{6,4},{7,5},{8,10},{9,11},{10,... | collective-permute-start | bytes 1572872 | tf_op jit(solution)/shard_map/ppermute | solution.py:85
  41.4 11.5 %collective-permute-start.8 = (bf16[64,4096]{1,0:T(8,128)(2,1)S(1)}, bf16[64,4096]{1,0:T(8,128)(2,1)S(1)}, u32[]{:S(2)}, u32[]{:S(2)}) collective-permute-start(bf16[64,4096]{1,0:T(8,128)(2,1)S(1)} %maximum_select_fusion.10), channel_id=1, source_target_pairs={{0,1},{1,0},{2,3},{3,2},{4,5},{5,4},{6,7},{7,6},{8,9},{9,8},{10,11... | collective-permute-start | bytes 1572872 | tf_op jit(solution)/shard_map/ppermute | solution.py:85
  43.5 18.6 %collective-permute-start.11 = (bf16[64,4096]{1,0:T(8,128)(2,1)S(1)}, bf16[64,4096]{1,0:T(8,128)(2,1)S(1)}, u32[]{:S(2)}, u32[]{:S(2)}) collective-permute-start(bf16[64,4096]{1,0:T(8,128)(2,1)S(1)} %maximum_select_fusion.11), channel_id=1, source_target_pairs={{0,2},{1,3},{2,0},{3,1},{4,6},{5,7},{6,4},{7,5},{8,10},{9,11},{10,... | collective-permute-start | bytes 1572872 | tf_op jit(solution)/shard_map/ppermute | solution.py:85
  108.2 3.0 copy-start.2
  110.6 2.4 collective-permute-start.12
  111.4 4.2 %collective-permute-start.14 = (bf16[128,3328]{1,0:T(8,128)(2,1)S(1)}, bf16[128,3328]{1,0:T(8,128)(2,1)S(1)}, u32[]{:S(2)}, u32[]{:S(2)}) collective-permute-start(bf16[128,3328]{1,0:T(8,128)(2,1)S(1)} %constant_dynamic-slice_fusion.6), channel_id=1, source_target_pairs={{0,8},{8,0},{16,24},{24,16},{1,9},{9,1},{17,25},{25,17},{2,10},{10... | collective-permute-start | bytes 2555912 | tf_op jit(solution)/shard_map/ppermute | solution.py:85
  113.2 2.7 copy-start
  114.1 13.0 %collective-permute-start.13 = (bf16[64,3328]{1,0:T(8,128)(2,1)}, bf16[64,3328]{1,0:T(8,128)(2,1)}, u32[]{:S(2)}, u32[]{:S(2)}) collective-permute-start(bf16[64,3328]{1,0:T(8,128)(2,1)} %dynamic-slice_convert_fusion.3), channel_id=1, source_target_pairs={{0,16},{8,24},{16,0},{24,8},{1,17},{9,25},{17,1},{25,9},{2,18},{10... | collective-permute-start | bytes 1277960 | tf_op jit(solution)/shard_map/ppermute | solution.py:85
  115.8 1.3 copy-start.1
  117.2 18.2 %collective-permute-start.15 = (bf16[64,3328]{1,0:T(8,128)(2,1)}, bf16[64,3328]{1,0:T(8,128)(2,1)}, u32[]{:S(2)}, u32[]{:S(2)}) collective-permute-start(bf16[64,3328]{1,0:T(8,128)(2,1)} %dynamic-slice_convert_fusion.2), channel_id=1, source_target_pairs={{0,16},{8,24},{16,0},{24,8},{1,17},{9,25},{17,1},{25,9},{2,18},{10... | collective-permute-start | bytes 1277960 | tf_op jit(solution)/shard_map/ppermute | solution.py:85
  117.6 35.1 %copy-start.3 = (s32[26,32]{1,0:T(8,128)S(1)}, s32[26,32]{1,0:T(8,128)}, u32[]{:S(2)}) copy-start(s32[26,32]{1,0:T(8,128)} %param.11) | copy-start | bytes 9988
  138.1 11.3 %collective-permute-start.16 = (bf16[64,3328]{1,0:T(8,128)(2,1)}, bf16[64,3328]{1,0:T(8,128)(2,1)}, u32[]{:S(2)}, u32[]{:S(2)}) collective-permute-start(bf16[64,3328]{1,0:T(8,128)(2,1)} %multiply_convert_fusion.1), channel_id=1, source_target_pairs={{0,16},{8,24},{16,0},{24,8},{1,17},{9,25},{17,1},{25,9},{2,18},{10... | collective-permute-start | bytes 1277960 | tf_op jit(solution)/shard_map/ppermute | solution.py:85
  152.0 2.7 collective-permute-start.17
  152.9 5.3 %copy-start.4 = (s32[26]{0:T(128)}, s32[26]{0:T(128)S(1)}, u32[]{:S(2)}) copy-start(s32[26]{0:T(128)S(1)} %fusion.1.base_ref) | copy-start | bytes 316
  181.1 14.0 %collective-permute-start.18 = (bf16[64,4096]{1,0:T(8,128)(2,1)S(1)}, bf16[64,4096]{1,0:T(8,128)(2,1)S(1)}, u32[]{:S(2)}, u32[]{:S(2)}) collective-permute-start(bf16[64,4096]{1,0:T(8,128)(2,1)S(1)} %constant_dynamic-slice_fusion.5), channel_id=1, source_target_pairs={{0,1},{1,0},{2,3},{3,2},{4,5},{5,4},{6,7},{7,6},{8,9},{9,8},{10,11... | collective-permute-start | bytes 1572872 | tf_op jit(solution)/shard_map/ppermute | solution.py:85
  182.7 13.8 %collective-permute-start.21 = (bf16[64,4096]{1,0:T(8,128)(2,1)S(1)}, bf16[64,4096]{1,0:T(8,128)(2,1)S(1)}, u32[]{:S(2)}, u32[]{:S(2)}) collective-permute-start(bf16[64,4096]{1,0:T(8,128)(2,1)S(1)} %constant_dynamic-slice_fusion.4), channel_id=1, source_target_pairs={{0,2},{1,3},{2,0},{3,1},{4,6},{5,7},{6,4},{7,5},{8,10},{9,11},{10,... | collective-permute-start | bytes 1572872 | tf_op jit(solution)/shard_map/ppermute | solution.py:85
  183.5 24.7 %collective-permute-start.24 = (bf16[128,3328]{1,0:T(8,128)(2,1)S(1)}, bf16[128,3328]{1,0:T(8,128)(2,1)S(1)}, u32[]{:S(2)}, u32[]{:S(2)}) collective-permute-start(bf16[128,3328]{1,0:T(8,128)(2,1)S(1)} %constant_dynamic-slice_fusion.3), channel_id=1, source_target_pairs={{0,8},{8,0},{16,24},{24,16},{1,9},{9,1},{17,25},{25,17},{2,10},{10... | collective-permute-start | bytes 2555912 | tf_op jit(solution)/shard_map/ppermute | solution.py:85
  183.7 26.4 %collective-permute-start.26 = (bf16[128,3328]{1,0:T(8,128)(2,1)S(1)}, bf16[128,3328]{1,0:T(8,128)(2,1)S(1)}, u32[]{:S(2)}, u32[]{:S(2)}) collective-permute-start(bf16[128,3328]{1,0:T(8,128)(2,1)S(1)} %constant_dynamic-slice_fusion.2), channel_id=1, source_target_pairs={{0,8},{8,0},{16,24},{24,16},{1,9},{9,1},{17,25},{25,17},{2,10},{10... | collective-permute-start | bytes 2555912 | tf_op jit(solution)/shard_map/ppermute | solution.py:85
  195.2 12.8 %collective-permute-start.19 = (bf16[32,4096]{1,0:T(8,128)(2,1)S(1)}, bf16[32,4096]{1,0:T(8,128)(2,1)S(1)}, u32[]{:S(2)}, u32[]{:S(2)}) collective-permute-start(bf16[32,4096]{1,0:T(8,128)(2,1)S(1)} %dynamic-slice_convert_fusion.7), channel_id=1, source_target_pairs={{0,2},{1,3},{2,0},{3,1},{4,6},{5,7},{6,4},{7,5},{8,10},{9,11},{10,... | collective-permute-start | bytes 786440 | tf_op jit(solution)/shard_map/ppermute | solution.py:85
  196.6 17.3 %collective-permute-start.22 = (bf16[32,4096]{1,0:T(8,128)(2,1)S(1)}, bf16[32,4096]{1,0:T(8,128)(2,1)S(1)}, u32[]{:S(2)}, u32[]{:S(2)}) collective-permute-start(bf16[32,4096]{1,0:T(8,128)(2,1)S(1)} %dynamic-slice_convert_fusion.6), channel_id=1, source_target_pairs={{0,4},{1,5},{2,6},{3,7},{4,0},{5,1},{6,2},{7,3},{8,12},{9,13},{10,... | collective-permute-start | bytes 786440 | tf_op jit(solution)/shard_map/ppermute | solution.py:85
  208.1 28.9 %collective-permute-start.20 = (bf16[16,4096]{1,0:T(8,128)(2,1)S(1)}, bf16[16,4096]{1,0:T(8,128)(2,1)S(1)}, u32[]{:S(2)}, u32[]{:S(2)}) collective-permute-start(bf16[16,4096]{1,0:T(8,128)(2,1)S(1)} %dynamic-slice_convert_fusion.11), channel_id=1, source_target_pairs={{0,4},{1,5},{2,6},{3,7},{4,0},{5,1},{6,2},{7,3},{8,12},{9,13},{10,... | collective-permute-start | bytes 393224 | tf_op jit(solution)/shard_map/ppermute | solution.py:85
  208.5 12.8 %collective-permute-start.25 = (bf16[64,3328]{1,0:T(8,128)(2,1)S(1)}, bf16[64,3328]{1,0:T(8,128)(2,1)S(1)}, u32[]{:S(2)}, u32[]{:S(2)}) collective-permute-start(bf16[64,3328]{1,0:T(8,128)(2,1)S(1)} %dynamic-slice_convert_fusion.1), channel_id=1, source_target_pairs={{0,16},{8,24},{16,0},{24,8},{1,17},{9,25},{17,1},{25,9},{2,18},{10... | collective-permute-start | bytes 1277960 | tf_op jit(solution)/shard_map/ppermute | solution.py:85
  210.3 17.2 %collective-permute-start.27 = (bf16[64,3328]{1,0:T(8,128)(2,1)S(1)}, bf16[64,3328]{1,0:T(8,128)(2,1)S(1)}, u32[]{:S(2)}, u32[]{:S(2)}) collective-permute-start(bf16[64,3328]{1,0:T(8,128)(2,1)S(1)} %dynamic-slice_convert_fusion), channel_id=1, source_target_pairs={{0,16},{8,24},{16,0},{24,8},{1,17},{9,25},{17,1},{25,9},{2,18},{10... | collective-permute-start | bytes 1277960 | tf_op jit(solution)/shard_map/ppermute | solution.py:85
  227.8 9.0 %collective-permute-start.28 = (bf16[64,3328]{1,0:T(8,128)(2,1)S(1)}, bf16[64,3328]{1,0:T(8,128)(2,1)S(1)}, u32[]{:S(2)}, u32[]{:S(2)}) collective-permute-start(bf16[64,3328]{1,0:T(8,128)(2,1)S(1)} %multiply_convert_fusion), channel_id=1, source_target_pairs={{0,16},{8,24},{16,0},{24,8},{1,17},{9,25},{17,1},{25,9},{2,18},{10... | collective-permute-start | bytes 1277960 | tf_op jit(solution)/shard_map/ppermute | solution.py:85
  229.5 36.6 %collective-permute-start.23 = (bf16[16,4096]{1,0:T(8,128)(2,1)S(1)}, bf16[16,4096]{1,0:T(8,128)(2,1)S(1)}, u32[]{:S(2)}, u32[]{:S(2)}) collective-permute-start(bf16[16,4096]{1,0:T(8,128)(2,1)S(1)} %dynamic-slice_convert_fusion.10), channel_id=1, source_target_pairs={{0,1},{1,0},{2,3},{3,2},{4,5},{5,4},{6,7},{7,6},{8,9},{9,8},{10,11... | collective-permute-start | bytes 393224 | tf_op jit(solution)/shard_map/ppermute | solution.py:85
  237.0 2.4 collective-permute-start.29
  263.7 14.5 %collective-permute-start.30 = (bf16[64,4096]{1,0:T(8,128)(2,1)S(1)}, bf16[64,4096]{1,0:T(8,128)(2,1)S(1)}, u32[]{:S(2)}, u32[]{:S(2)}) collective-permute-start(bf16[64,4096]{1,0:T(8,128)(2,1)S(1)} %constant_dynamic-slice_fusion.1), channel_id=1, source_target_pairs={{0,1},{1,0},{2,3},{3,2},{4,5},{5,4},{6,7},{7,6},{8,9},{9,8},{10,11... | collective-permute-start | bytes 1572872 | tf_op jit(solution)/shard_map/ppermute | solution.py:85
  266.1 14.9 %collective-permute-start.33 = (bf16[64,4096]{1,0:T(8,128)(2,1)S(1)}, bf16[64,4096]{1,0:T(8,128)(2,1)S(1)}, u32[]{:S(2)}, u32[]{:S(2)}) collective-permute-start(bf16[64,4096]{1,0:T(8,128)(2,1)S(1)} %constant_dynamic-slice_fusion), channel_id=1, source_target_pairs={{0,2},{1,3},{2,0},{3,1},{4,6},{5,7},{6,4},{7,5},{8,10},{9,11},{10,... | collective-permute-start | bytes 1572872 | tf_op jit(solution)/shard_map/ppermute | solution.py:85
  278.4 12.0 %collective-permute-start.31 = (bf16[32,4096]{1,0:T(8,128)(2,1)S(1)}, bf16[32,4096]{1,0:T(8,128)(2,1)S(1)}, u32[]{:S(2)}, u32[]{:S(2)}) collective-permute-start(bf16[32,4096]{1,0:T(8,128)(2,1)S(1)} %dynamic-slice_convert_fusion.5), channel_id=1, source_target_pairs={{0,2},{1,3},{2,0},{3,1},{4,6},{5,7},{6,4},{7,5},{8,10},{9,11},{10,... | collective-permute-start | bytes 786440 | tf_op jit(solution)/shard_map/ppermute | solution.py:85
  281.2 18.4 %collective-permute-start.34 = (bf16[32,4096]{1,0:T(8,128)(2,1)S(1)}, bf16[32,4096]{1,0:T(8,128)(2,1)S(1)}, u32[]{:S(2)}, u32[]{:S(2)}) collective-permute-start(bf16[32,4096]{1,0:T(8,128)(2,1)S(1)} %dynamic-slice_convert_fusion.4), channel_id=1, source_target_pairs={{0,4},{1,5},{2,6},{3,7},{4,0},{5,1},{6,2},{7,3},{8,12},{9,13},{10,... | collective-permute-start | bytes 786440 | tf_op jit(solution)/shard_map/ppermute | solution.py:85
  290.6 10.7 %collective-permute-start.32 = (bf16[16,4096]{1,0:T(8,128)(2,1)S(1)}, bf16[16,4096]{1,0:T(8,128)(2,1)S(1)}, u32[]{:S(2)}, u32[]{:S(2)}) collective-permute-start(bf16[16,4096]{1,0:T(8,128)(2,1)S(1)} %dynamic-slice_convert_fusion.9), channel_id=1, source_target_pairs={{0,4},{1,5},{2,6},{3,7},{4,0},{5,1},{6,2},{7,3},{8,12},{9,13},{10,... | collective-permute-start | bytes 393224 | tf_op jit(solution)/shard_map/ppermute | solution.py:85
  299.7 5.0 %collective-permute-start.35 = (bf16[16,4096]{1,0:T(8,128)(2,1)S(1)}, bf16[16,4096]{1,0:T(8,128)(2,1)S(1)}, u32[]{:S(2)}, u32[]{:S(2)}) collective-permute-start(bf16[16,4096]{1,0:T(8,128)(2,1)S(1)} %dynamic-slice_convert_fusion.8), channel_id=1, source_target_pairs={{0,1},{1,0},{2,3},{3,2},{4,5},{5,4},{6,7},{7,6},{8,9},{9,8},{10,11... | collective-permute-start | bytes 393224 | tf_op jit(solution)/shard_map/ppermute | solution.py:85

commit v5 on v1

--- a/solution.py
+++ b/solution.py
@@ -123,9 +123,13 @@
     segment = jnp.concatenate(
         doubling_gather(list(zip(token_parts, col_orders)), "col", n_col), axis=0)
     gate_rows, up_rows = sparse_matmul(segment, [gate_packed, up_packed], gate_keep)
-    ((gate_sum, up_sum),) = halving_scatter([([gate_rows, up_rows], row_bits)], "row", n_row)
-    hidden_share = (jax.nn.silu(gate_sum) * up_sum).astype(jnp.bfloat16)
-    (every_hidden,) = doubling_gather([(hidden_share, row_bits[::-1])], "row", n_row)
+    half = gate_rows.shape[0] // 2
+    sums = halving_scatter(
+        [([gate_rows[:half], up_rows[:half]], row_bits), ([gate_rows[half:], up_rows[half:]], row_bits)],
+        "row", n_row)
+    hidden_shares = [(jax.nn.silu(g) * u).astype(jnp.bfloat16) for g, u in sums]
+    every_hidden = jnp.concatenate(
+        doubling_gather([(h, row_bits[::-1]) for h in hidden_shares], "row", n_row), axis=0)
     (partial_out,) = sparse_matmul(every_hidden, [down_packed], down_keep)
     half_rows = partial_out.shape[0] // 2
     out_parts = halving_scatter(

time: 294 us -> 280 us (0.952)
  other arithmetic: 20.3 us -> 14 us
  waiting for transfers between devices: 161 us -> 155 us
  local copies, waits for them, and re-layouts: 17.5 us -> 13.5 us
    ppermute x18 -> x24, waiting for transfers between devices: 161 us -> 155 us  [exchange(): return lax.ppermute(x, axis, perm=pairs)]
    add x6 -> x8, other arithmetic: 4.95 us -> 1.38 us  [halving_scatter(): k.astype(jnp.float32) + g.astype(jnp.float32)]
    ppermute x18 -> x24, starting transfers between devices: 25.1 us -> 27.2 us  [exchange(): return lax.ppermute(x, axis, perm=pairs)]
    select_n x8 -> x10, other arithmetic: 7.29 us -> 5.54 us  [doubling_gather(): jnp.where(low, jnp.concatenate([xs[p], got], 0), jnp.concatenate([got, xs...]
  transfers between devices with their start and end apart: 18 -> 24, of which waited for: 15 -> 17; matrix products, arithmetic and copies ran while one was open for 5% -> 4% of each run, Pallas kernels for 0% -> 0%
where the time goes in v5:
time: 280 us; the launch traced here: 279 us
  waiting for transfers between devices  155 us (55%)
  Pallas kernels  69.2 us (25%)
  starting transfers between devices  27.2 us (10%)
  other arithmetic  14 us (5%)
  local copies, waits for them, and re-layouts  13.5 us (5%)
    ppermute x24, waiting for transfers between devices, exchange(): return lax.ppermute(x, axis, perm=pairs)  155 us
    pallas_call x2, Pallas kernels, sparse_matmul(): pl.pallas_call(kernel, grid_spec=pltpu.PrefetchScalarGridSpec(num_scalar_...  69.2 us
    ppermute x24, starting transfers between devices, exchange(): return lax.ppermute(x, axis, perm=pairs)  27.2 us
  transfers between devices with their start and end apart: 24, of which 17 were waited for; matrix products, arithmetic and copies ran while one was open for 4% of the time, Pallas kernels for 0%

profile of v5, /device:TPU:0, one launch (start us, length us, event | category | flops | bytes accessed | tf_op | source)
XLA Modules:
  0.0 279.4 jit_solution(8241323074365901720)
XLA Ops:
  0.0 1.1 fusion.6
  1.1 4.1 %collective-permute-start = (bf16[32,4096]{1,0:T(8,128)(2,1)S(1)}, bf16[32,4096]{1,0:T(8,128)(2,1)S(1)}, u32[]{:S(2)}, u32[]{:S(2)}) collective-permute-start(bf16[32,4096]{1,0:T(8,128)(2,1)S(1)} %get-tuple-element.15), channel_id=1, source_target_pairs={{0,4},{1,5},{2,6},{3,7},{4,0},{5,1},{6,2},{7,3},{8,12},{9,13},{10,... | collective-permute-start | bytes 786440 | tf_op jit(solution)/shard_map/ppermute | solution.py:85
  5.2 1.5 collective-permute-start.3
  6.7 0.8 reshape.58
  7.4 0.8 reshape.64
  8.3 0.3 reduce-window.24
  8.7 8.4 %collective-permute-done = bf16[32,4096]{1,0:T(8,128)(2,1)S(1)} collective-permute-done((bf16[32,4096]{1,0:T(8,128)(2,1)S(1)}, bf16[32,4096]{1,0:T(8,128)(2,1)S(1)}, u32[]{:S(2)}, u32[]{:S(2)}) %collective-permute-start) | collective-permute-done | bytes 262176 | tf_op jit(solution)/shard_map/ppermute | solution.py:85
  17.2 0.8 collective-permute-start.1
  18.1 3.4 %collective-permute-start.4 = (bf16[64,4096]{1,0:T(8,128)(2,1)S(1)}, bf16[64,4096]{1,0:T(8,128)(2,1)S(1)}, u32[]{:S(2)}, u32[]{:S(2)}) collective-permute-start(bf16[64,4096]{1,0:T(8,128)(2,1)S(1)} %maximum_select_fusion.9), channel_id=1, source_target_pairs={{0,4},{1,5},{2,6},{3,7},{4,0},{5,1},{6,2},{7,3},{8,12},{9,13},{10,... | collective-permute-start | bytes 1572872 | tf_op jit(solution)/shard_map/ppermute | solution.py:85
  21.6 19.7 %collective-permute-done.1 = bf16[64,4096]{1,0:T(8,128)(2,1)} collective-permute-done((bf16[64,4096]{1,0:T(8,128)(2,1)S(1)}, bf16[64,4096]{1,0:T(8,128)(2,1)}, u32[]{:S(2)}, u32[]{:S(2)}) %collective-permute-start.1) | collective-permute-done | bytes 524320 | tf_op jit(solution)/shard_map/ppermute | solution.py:85
  41.3 1.4 maximum_select_fusion.4
  42.8 1.3 collective-permute-start.2
  44.1 0.6 collective-permute-done.4
  44.6 0.2 maximum_select_fusion.5
  44.8 0.2 collective-permute-start.5
  45.1 0.3 reduce-window.16
  45.9 0.7 reshape.68.index_ref
  46.9 19.5 %collective-permute-done.2 = bf16[128,4096]{1,0:T(8,128)(2,1)} collective-permute-done((bf16[128,4096]{1,0:T(8,128)(2,1)S(1)}, bf16[128,4096]{1,0:T(8,128)(2,1)}, u32[]{:S(2)}, u32[]{:S(2)}) %collective-permute-start.2) | collective-permute-done | bytes 1048608 | tf_op jit(solution)/shard_map/ppermute | solution.py:85
  66.4 2.3 maximum_select_fusion
  68.6 0.5 maximum_select_fusion.1
  69.1 2.4 pad_maximum_fusion.x_ref
  71.6 43.6 %shard_map.64 = (bf16[512,3328]{1,0:T(8,128)(2,1)}, bf16[512,3328]{1,0:T(8,128)(2,1)}) custom-call(s32[32]{0:T(128)} %copy-done.5, s32[832]{0:T(1024)} %reshape.68.index_ref, bf16[512,4096]{1,0:T(8,128)(2,1)} %pad_maximum_fusion.x_ref, bf16[640,128,128]{2,1,0:T(8,128)(2,1)} %refs_3_.1, bf16[640,128,128]{2,1,0:T(8,128)(2,1)} %refs_3_.1, ...), custom_call_target="tpu_custom_call" | custom-call | flops 27917287424 | bytes 65536000 | tf_op jit(solution)/shard_map/pallas_call | solution.py:66
  115.2 2.3 fusion.4
  117.6 0.5 copy-done.2
  118.1 0.2 fusion.5
  118.6 0.5 collective-permute-start.12
  119.3 0.7 collective-permute-done.6
  120.2 1.0 collective-permute-start.7
  121.3 0.2 convert_add_fusion.4
  121.5 1.1 collective-permute-start.9
  122.9 1.0 collective-permute-start.13
  124.2 1.1 collective-permute-start.15
  125.3 7.7 %collective-permute-done.7 = bf16[64,3328]{1,0:T(8,128)(2,1)S(1)} collective-permute-done((bf16[64,3328]{1,0:T(8,128)(2,1)S(1)}, bf16[64,3328]{1,0:T(8,128)(2,1)S(1)}, u32[]{:S(2)}, u32[]{:S(2)}) %collective-permute-start.7) | collective-permute-done | bytes 426016 | tf_op jit(solution)/shard_map/ppermute | solution.py:85
  133.0 9.1 %collective-permute-done.9 = bf16[64,3328]{1,0:T(8,128)(2,1)S(1)} collective-permute-done((bf16[64,3328]{1,0:T(8,128)(2,1)S(1)}, bf16[64,3328]{1,0:T(8,128)(2,1)S(1)}, u32[]{:S(2)}, u32[]{:S(2)}) %collective-permute-start.9) | collective-permute-done | bytes 426016 | tf_op jit(solution)/shard_map/ppermute | solution.py:85
  142.1 0.3 multiply_convert_fusion.1
  142.4 1.0 collective-permute-start.10
  143.5 7.8 %collective-permute-done.13 = bf16[64,3328]{1,0:T(8,128)(2,1)S(1)} collective-permute-done((bf16[64,3328]{1,0:T(8,128)(2,1)S(1)}, bf16[64,3328]{1,0:T(8,128)(2,1)S(1)}, u32[]{:S(2)}, u32[]{:S(2)}) %collective-permute-start.13) | collective-permute-done | bytes 426016 | tf_op jit(solution)/shard_map/ppermute | solution.py:85
  151.2 9.1 %collective-permute-done.15 = bf16[64,3328]{1,0:T(8,128)(2,1)S(1)} collective-permute-done((bf16[64,3328]{1,0:T(8,128)(2,1)S(1)}, bf16[64,3328]{1,0:T(8,128)(2,1)S(1)}, u32[]{:S(2)}, u32[]{:S(2)}) %collective-permute-start.15) | collective-permute-done | bytes 426016 | tf_op jit(solution)/shard_map/ppermute | solution.py:85
  160.4 0.3 multiply_convert_fusion
  160.7 1.0 collective-permute-start.16
  161.7 7.8 %collective-permute-done.10 = bf16[64,3328]{1,0:T(8,128)(2,1)S(1)} collective-permute-done((bf16[64,3328]{1,0:T(8,128)(2,1)S(1)}, bf16[64,3328]{1,0:T(8,128)(2,1)S(1)}, u32[]{:S(2)}, u32[]{:S(2)}) %collective-permute-start.10) | collective-permute-done | bytes 426016 | tf_op jit(solution)/shard_map/ppermute | solution.py:85
  169.7 8.1 %collective-permute-done.16 = bf16[64,3328]{1,0:T(8,128)(2,1)S(1)} collective-permute-done((bf16[64,3328]{1,0:T(8,128)(2,1)S(1)}, bf16[64,3328]{1,0:T(8,128)(2,1)S(1)}, u32[]{:S(2)}, u32[]{:S(2)}) %collective-permute-start.16) | collective-permute-done | bytes 426016 | tf_op jit(solution)/shard_map/ppermute | solution.py:85
  178.3 0.7 reshape.63.index_ref
  179.0 0.3 maximum_select_fusion.2
  179.3 1.1 collective-permute-done.17
  180.4 0.3 maximum_select_fusion.3
  180.8 2.0 pad_maximum_fusion.1.x_ref
  182.7 25.7 %shard_map.65 = bf16[512,4096]{1,0:T(8,128)(2,1)} custom-call(s32[26]{0:T(128)} %copy-done.6, s32[832]{0:T(1024)} %reshape.63.index_ref, bf16[512,3328]{1,0:T(8,128)(2,1)} %pad_maximum_fusion.1.x_ref, bf16[640,128,128]{2,1,0:T(8,128)(2,1)} %refs_1_.3, bf16[640,128,128]{2,1,0:T(8,128)(2,1)} %refs_1_.3), custom_call_target="tpu_custom_call" | custom-call | flops 13958643712 | bytes 34865152 | tf_op jit(solution)/shard_map/pallas_call | solution.py:66
  208.4 2.6 fusion.3
  211.0 1.3 copy-done
  212.3 1.1 constant_dynamic-slice_fusion.1
  213.4 0.9 collective-permute-start.18
  214.4 1.7 collective-permute-start.21
  216.0 22.8 %collective-permute-done.18 = bf16[128,4096]{1,0:T(8,128)(2,1)S(1)} collective-permute-done((bf16[128,4096]{1,0:T(8,128)(2,1)}, bf16[128,4096]{1,0:T(8,128)(2,1)S(1)}, u32[]{:S(2)}, u32[]{:S(2)}) %collective-permute-start.18) | collective-permute-done | bytes 1048608 | tf_op jit(solution)/shard_map/ppermute | solution.py:85
  238.8 0.3 convert_add_fusion.1
  239.1 1.0 collective-permute-start.19
  240.1 0.2 convert_add_fusion
  240.4 3.1 %collective-permute-start.22 = (bf16[64,4096]{1,0:T(8,128)(2,1)S(1)}, bf16[64,4096]{1,0:T(8,128)(2,1)S(1)}, u32[]{:S(2)}, u32[]{:S(2)}) collective-permute-start(bf16[64,4096]{1,0:T(8,128)(2,1)S(1)} %dynamic-slice_convert_fusion), channel_id=1, source_target_pairs={{0,4},{1,5},{2,6},{3,7},{4,0},{5,1},{6,2},{7,3},{8,12},{9,13},{10,... | collective-permute-start | bytes 1572872 | tf_op jit(solution)/shard_map/ppermute | solution.py:85
  243.5 19.4 %collective-permute-done.19 = bf16[64,4096]{1,0:T(8,128)(2,1)S(1)} collective-permute-done((bf16[64,4096]{1,0:T(8,128)(2,1)S(1)}, bf16[64,4096]{1,0:T(8,128)(2,1)S(1)}, u32[]{:S(2)}, u32[]{:S(2)}) %collective-permute-start.19) | collective-permute-done | bytes 524320 | tf_op jit(solution)/shard_map/ppermute | solution.py:85
  263.2 8.7 %collective-permute-done.22 = bf16[64,4096]{1,0:T(8,128)(2,1)S(1)} collective-permute-done((bf16[64,4096]{1,0:T(8,128)(2,1)S(1)}, bf16[64,4096]{1,0:T(8,128)(2,1)S(1)}, u32[]{:S(2)}, u32[]{:S(2)}) %collective-permute-start.22) | collective-permute-done | bytes 524320 | tf_op jit(solution)/shard_map/ppermute | solution.py:85
  272.0 1.8 collective-permute-start.23
  273.8 3.1 %collective-permute-done.20 = bf16[32,4096]{1,0:T(8,128)(2,1)S(1)} collective-permute-done((bf16[32,4096]{1,0:T(8,128)(2,1)S(1)}, bf16[32,4096]{1,0:T(8,128)(2,1)S(1)}, u32[]{:S(2)}, u32[]{:S(2)}) %collective-permute-start.20) | collective-permute-done | bytes 262176 | tf_op jit(solution)/shard_map/ppermute | solution.py:85
  277.0 1.5 collective-permute-done.23
  278.5 0.8 pad_maximum_fusion.2
  (67 shorter events, 3.8 us)
Async XLA Ops:
  1.1 16.0 %collective-permute-start = (bf16[32,4096]{1,0:T(8,128)(2,1)S(1)}, bf16[32,4096]{1,0:T(8,128)(2,1)S(1)}, u32[]{:S(2)}, u32[]{:S(2)}) collective-permute-start(bf16[32,4096]{1,0:T(8,128)(2,1)S(1)} %get-tuple-element.15), channel_id=1, source_target_pairs={{0,4},{1,5},{2,6},{3,7},{4,0},{5,1},{6,2},{7,3},{8,12},{9,13},{10,... | collective-permute-start | bytes 786440 | tf_op jit(solution)/shard_map/ppermute | solution.py:85
  5.2 12.8 %collective-permute-start.3 = (bf16[32,4096]{1,0:T(8,128)(2,1)S(1)}, bf16[32,4096]{1,0:T(8,128)(2,1)S(1)}, u32[]{:S(2)}, u32[]{:S(2)}) collective-permute-start(bf16[32,4096]{1,0:T(8,128)(2,1)S(1)} %get-tuple-element.16), channel_id=1, source_target_pairs={{0,1},{1,0},{2,3},{3,2},{4,5},{5,4},{6,7},{7,6},{8,9},{9,8},{10,11... | collective-permute-start | bytes 786440 | tf_op jit(solution)/shard_map/ppermute | solution.py:85
  17.2 24.1 %collective-permute-start.1 = (bf16[64,4096]{1,0:T(8,128)(2,1)S(1)}, bf16[64,4096]{1,0:T(8,128)(2,1)}, u32[]{:S(2)}, u32[]{:S(2)}) collective-permute-start(bf16[64,4096]{1,0:T(8,128)(2,1)S(1)} %maximum_select_fusion.8), channel_id=1, source_target_pairs={{0,2},{1,3},{2,0},{3,1},{4,6},{5,7},{6,4},{7,5},{8,10},{9,11},{10,... | collective-permute-start | bytes 1572872 | tf_op jit(solution)/shard_map/ppermute | solution.py:85
  18.1 26.6 %collective-permute-start.4 = (bf16[64,4096]{1,0:T(8,128)(2,1)S(1)}, bf16[64,4096]{1,0:T(8,128)(2,1)S(1)}, u32[]{:S(2)}, u32[]{:S(2)}) collective-permute-start(bf16[64,4096]{1,0:T(8,128)(2,1)S(1)} %maximum_select_fusion.9), channel_id=1, source_target_pairs={{0,4},{1,5},{2,6},{3,7},{4,0},{5,1},{6,2},{7,3},{8,12},{9,13},{10,... | collective-permute-start | bytes 1572872 | tf_op jit(solution)/shard_map/ppermute | solution.py:85
  21.6 24.1 %copy-start.3 = (s32[32,26]{1,0:T(8,128)S(1)}, s32[32,26]{1,0:T(8,128)}, u32[]{:S(2)}) copy-start(s32[32,26]{1,0:T(8,128)} %param.10) | copy-start | bytes 9988
  42.8 23.6 %collective-permute-start.2 = (bf16[128,4096]{1,0:T(8,128)(2,1)S(1)}, bf16[128,4096]{1,0:T(8,128)(2,1)}, u32[]{:S(2)}, u32[]{:S(2)}) collective-permute-start(bf16[128,4096]{1,0:T(8,128)(2,1)S(1)} %maximum_select_fusion.4), channel_id=1, source_target_pairs={{0,1},{1,0},{2,3},{3,2},{4,5},{5,4},{6,7},{7,6},{8,9},{9,8},{10,11... | collective-permute-start | bytes 3145736 | tf_op jit(solution)/shard_map/ppermute | solution.py:85
  44.8 23.8 %collective-permute-start.5 = (bf16[128,4096]{1,0:T(8,128)(2,1)S(1)}, bf16[128,4096]{1,0:T(8,128)(2,1)S(1)}, u32[]{:S(2)}, u32[]{:S(2)}) collective-permute-start(bf16[128,4096]{1,0:T(8,128)(2,1)S(1)} %maximum_select_fusion.5), channel_id=1, source_target_pairs={{0,2},{1,3},{2,0},{3,1},{4,6},{5,7},{6,4},{7,5},{8,10},{9,11},{10,... | collective-permute-start | bytes 3145736 | tf_op jit(solution)/shard_map/ppermute | solution.py:85
  45.8 22.8 %copy-start.5 = (s32[32]{0:T(128)}, s32[32]{0:T(128)S(1)}, u32[]{:S(2)}) copy-start(s32[32]{0:T(128)S(1)} %fusion.base_ref) | copy-start | bytes 388
  115.2 3.0 %copy-start.2 = (bf16[512,3328]{1,0:T(8,128)(2,1)S(1)}, bf16[512,3328]{1,0:T(8,128)(2,1)}, u32[]{:S(2)}) copy-start(bf16[512,3328]{1,0:T(8,128)(2,1)} %get-tuple-element.8) | copy-start | bytes 10223620
  117.6 2.4 collective-permute-start.6
  118.4 2.9 %collective-permute-start.8 = (bf16[128,3328]{1,0:T(8,128)(2,1)S(1)}, bf16[128,3328]{1,0:T(8,128)(2,1)S(1)}, u32[]{:S(2)}, u32[]{:S(2)}) collective-permute-start(bf16[128,3328]{1,0:T(8,128)(2,1)S(1)} %constant_dynamic-slice_fusion.4), channel_id=1, source_target_pairs={{0,8},{8,0},{16,24},{24,16},{1,9},{9,1},{17,25},{25,17},{2,10},{10... | collective-permute-start | bytes 2555912 | tf_op jit(solution)/shard_map/ppermute | solution.py:85
  118.6 4.1 %collective-permute-start.12 = (bf16[128,3328]{1,0:T(8,128)(2,1)S(1)}, bf16[128,3328]{1,0:T(8,128)(2,1)S(1)}, u32[]{:S(2)}, u32[]{:S(2)}) collective-permute-start(bf16[128,3328]{1,0:T(8,128)(2,1)S(1)} %constant_dynamic-slice_fusion.3), channel_id=1, source_target_pairs={{0,8},{8,0},{16,24},{24,16},{1,9},{9,1},{17,25},{25,17},{2,10},{10... | collective-permute-start | bytes 2555912 | tf_op jit(solution)/shard_map/ppermute | solution.py:85
  119.2 4.7 %collective-permute-start.14 = (bf16[128,3328]{1,0:T(8,128)(2,1)S(1)}, bf16[128,3328]{1,0:T(8,128)(2,1)S(1)}, u32[]{:S(2)}, u32[]{:S(2)}) collective-permute-start(bf16[128,3328]{1,0:T(8,128)(2,1)S(1)} %constant_dynamic-slice_fusion.2), channel_id=1, source_target_pairs={{0,8},{8,0},{16,24},{24,16},{1,9},{9,1},{17,25},{25,17},{2,10},{10... | collective-permute-start | bytes 2555912 | tf_op jit(solution)/shard_map/ppermute | solution.py:85
  120.2 12.7 %collective-permute-start.7 = (bf16[64,3328]{1,0:T(8,128)(2,1)S(1)}, bf16[64,3328]{1,0:T(8,128)(2,1)S(1)}, u32[]{:S(2)}, u32[]{:S(2)}) collective-permute-start(bf16[64,3328]{1,0:T(8,128)(2,1)S(1)} %dynamic-slice_convert_fusion.5), channel_id=1, source_target_pairs={{0,16},{8,24},{16,0},{24,8},{1,17},{9,25},{17,1},{25,9},{2,18},{10... | collective-permute-start | bytes 1277960 | tf_op jit(solution)/shard_map/ppermute | solution.py:85
  121.5 20.6 %collective-permute-start.9 = (bf16[64,3328]{1,0:T(8,128)(2,1)S(1)}, bf16[64,3328]{1,0:T(8,128)(2,1)S(1)}, u32[]{:S(2)}, u32[]{:S(2)}) collective-permute-start(bf16[64,3328]{1,0:T(8,128)(2,1)S(1)} %dynamic-slice_convert_fusion.4), channel_id=1, source_target_pairs={{0,16},{8,24},{16,0},{24,8},{1,17},{9,25},{17,1},{25,9},{2,18},{10... | collective-permute-start | bytes 1277960 | tf_op jit(solution)/shard_map/ppermute | solution.py:85
  122.9 28.3 %collective-permute-start.13 = (bf16[64,3328]{1,0:T(8,128)(2,1)S(1)}, bf16[64,3328]{1,0:T(8,128)(2,1)S(1)}, u32[]{:S(2)}, u32[]{:S(2)}) collective-permute-start(bf16[64,3328]{1,0:T(8,128)(2,1)S(1)} %dynamic-slice_convert_fusion.3), channel_id=1, source_target_pairs={{0,16},{8,24},{16,0},{24,8},{1,17},{9,25},{17,1},{25,9},{2,18},{10... | collective-permute-start | bytes 1277960 | tf_op jit(solution)/shard_map/ppermute | solution.py:85
  124.2 36.2 %collective-permute-start.15 = (bf16[64,3328]{1,0:T(8,128)(2,1)S(1)}, bf16[64,3328]{1,0:T(8,128)(2,1)S(1)}, u32[]{:S(2)}, u32[]{:S(2)}) collective-permute-start(bf16[64,3328]{1,0:T(8,128)(2,1)S(1)} %dynamic-slice_convert_fusion.2), channel_id=1, source_target_pairs={{0,16},{8,24},{16,0},{24,8},{1,17},{9,25},{17,1},{25,9},{2,18},{10... | collective-permute-start | bytes 1277960 | tf_op jit(solution)/shard_map/ppermute | solution.py:85
  142.4 27.1 %collective-permute-start.10 = (bf16[64,3328]{1,0:T(8,128)(2,1)S(1)}, bf16[64,3328]{1,0:T(8,128)(2,1)S(1)}, u32[]{:S(2)}, u32[]{:S(2)}) collective-permute-start(bf16[64,3328]{1,0:T(8,128)(2,1)S(1)} %multiply_convert_fusion.1), channel_id=1, source_target_pairs={{0,16},{8,24},{16,0},{24,8},{1,17},{9,25},{17,1},{25,9},{2,18},{10... | collective-permute-start | bytes 1277960 | tf_op jit(solution)/shard_map/ppermute | solution.py:85
  160.7 17.4 %copy-start.4 = (s32[26,32]{1,0:T(8,128)S(1)}, s32[26,32]{1,0:T(8,128)}, u32[]{:S(2)}) copy-start(s32[26,32]{1,0:T(8,128)} %param.11) | copy-start | bytes 9988
  160.7 17.1 %collective-permute-start.16 = (bf16[64,3328]{1,0:T(8,128)(2,1)S(1)}, bf16[64,3328]{1,0:T(8,128)(2,1)S(1)}, u32[]{:S(2)}, u32[]{:S(2)}) collective-permute-start(bf16[64,3328]{1,0:T(8,128)(2,1)S(1)} %multiply_convert_fusion), channel_id=1, source_target_pairs={{0,16},{8,24},{16,0},{24,8},{1,17},{9,25},{17,1},{25,9},{2,18},{10... | collective-permute-start | bytes 1277960 | tf_op jit(solution)/shard_map/ppermute | solution.py:85
  169.7 9.3 %collective-permute-start.11 = (bf16[128,3328]{1,0:T(8,128)(2,1)S(1)}, bf16[128,3328]{1,0:T(8,128)(2,1)S(1)}, u32[]{:S(2)}, u32[]{:S(2)}) collective-permute-start(bf16[128,3328]{1,0:T(8,128)(2,1)S(1)} %maximum_select_fusion.6), channel_id=1, source_target_pairs={{0,8},{8,0},{16,24},{24,16},{1,9},{9,1},{17,25},{25,17},{2,10},{10... | collective-permute-start | bytes 2555912 | tf_op jit(solution)/shard_map/ppermute | solution.py:85
  178.0 2.4 collective-permute-start.17
  178.2 2.5 copy-start.6
  211.0 1.3 copy-start
  213.4 25.4 %collective-permute-start.18 = (bf16[128,4096]{1,0:T(8,128)(2,1)}, bf16[128,4096]{1,0:T(8,128)(2,1)S(1)}, u32[]{:S(2)}, u32[]{:S(2)}) collective-permute-start(bf16[128,4096]{1,0:T(8,128)(2,1)} %constant_dynamic-slice_fusion.1), channel_id=1, source_target_pairs={{0,1},{1,0},{2,3},{3,2},{4,5},{5,4},{6,7},{7,6},{8,9},{9,8},{10,11... | collective-permute-start | bytes 3145736 | tf_op jit(solution)/shard_map/ppermute | solution.py:85
  214.3 24.5 %copy-start.1 = (bf16[256,4096]{1,0:T(8,128)(2,1)S(1)}, bf16[256,4096]{1,0:T(8,128)(2,1)}, u32[]{:S(2)}) copy-start(bf16[256,4096]{1,0:T(8,128)(2,1)} %copy-done) | copy-start | bytes 6291460
  214.4 25.7 %collective-permute-start.21 = (bf16[128,4096]{1,0:T(8,128)(2,1)S(1)}, bf16[128,4096]{1,0:T(8,128)(2,1)S(1)}, u32[]{:S(2)}, u32[]{:S(2)}) collective-permute-start(bf16[128,4096]{1,0:T(8,128)(2,1)S(1)} %constant_dynamic-slice_fusion), channel_id=1, source_target_pairs={{0,2},{1,3},{2,0},{3,1},{4,6},{5,7},{6,4},{7,5},{8,10},{9,11},{10,... | collective-permute-start | bytes 3145736 | tf_op jit(solution)/shard_map/ppermute | solution.py:85
  239.1 23.8 %collective-permute-start.19 = (bf16[64,4096]{1,0:T(8,128)(2,1)S(1)}, bf16[64,4096]{1,0:T(8,128)(2,1)S(1)}, u32[]{:S(2)}, u32[]{:S(2)}) collective-permute-start(bf16[64,4096]{1,0:T(8,128)(2,1)S(1)} %dynamic-slice_convert_fusion.1), channel_id=1, source_target_pairs={{0,2},{1,3},{2,0},{3,1},{4,6},{5,7},{6,4},{7,5},{8,10},{9,11},{10,... | collective-permute-start | bytes 1572872 | tf_op jit(solution)/shard_map/ppermute | solution.py:85
  240.4 31.4 %collective-permute-start.22 = (bf16[64,4096]{1,0:T(8,128)(2,1)S(1)}, bf16[64,4096]{1,0:T(8,128)(2,1)S(1)}, u32[]{:S(2)}, u32[]{:S(2)}) collective-permute-start(bf16[64,4096]{1,0:T(8,128)(2,1)S(1)} %dynamic-slice_convert_fusion), channel_id=1, source_target_pairs={{0,4},{1,5},{2,6},{3,7},{4,0},{5,1},{6,2},{7,3},{8,12},{9,13},{10,... | collective-permute-start | bytes 1572872 | tf_op jit(solution)/shard_map/ppermute | solution.py:85
  263.1 13.8 %collective-permute-start.20 = (bf16[32,4096]{1,0:T(8,128)(2,1)S(1)}, bf16[32,4096]{1,0:T(8,128)(2,1)S(1)}, u32[]{:S(2)}, u32[]{:S(2)}) collective-permute-start(bf16[32,4096]{1,0:T(8,128)(2,1)S(1)} %dynamic-slice_convert_fusion.7), channel_id=1, source_target_pairs={{0,4},{1,5},{2,6},{3,7},{4,0},{5,1},{6,2},{7,3},{8,12},{9,13},{10,... | collective-permute-start | bytes 786440 | tf_op jit(solution)/shard_map/ppermute | solution.py:85
  272.0 6.4 %collective-permute-start.23 = (bf16[32,4096]{1,0:T(8,128)(2,1)S(1)}, bf16[32,4096]{1,0:T(8,128)(2,1)S(1)}, u32[]{:S(2)}, u32[]{:S(2)}) collective-permute-start(bf16[32,4096]{1,0:T(8,128)(2,1)S(1)} %dynamic-slice_convert_fusion.6), channel_id=1, source_target_pairs={{0,1},{1,0},{2,3},{3,2},{4,5},{5,4},{6,7},{7,6},{8,9},{9,8},{10,11... | collective-permute-start | bytes 786440 | tf_op jit(solution)/shard_map/ppermute | solution.py:85

commit v6 on v5

--- a/solution.py
+++ b/solution.py
@@ -118,10 +118,10 @@
     row_bits = list(range(n_row.bit_length() - 1))
     top = n_col.bit_length() - 1
     col_orders = [list(range(top - 1, -1, -1)), [0] + list(range(top - 1, 0, -1))]
-    t_half = tokens.shape[0] // 2
-    token_parts = [tokens[:t_half], tokens[t_half:]]
-    segment = jnp.concatenate(
-        doubling_gather(list(zip(token_parts, col_orders)), "col", n_col), axis=0)
+    quarter = tokens.shape[0] // 4
+    orders = col_orders * 2
+    token_parts = [tokens[q * quarter:(q + 1) * quarter] for q in range(4)]
+    segment = jnp.concatenate(doubling_gather(list(zip(token_parts, orders)), "col", n_col), axis=0)
     gate_rows, up_rows = sparse_matmul(segment, [gate_packed, up_packed], gate_keep)
     half = gate_rows.shape[0] // 2
     sums = halving_scatter(
@@ -131,10 +131,9 @@
     every_hidden = jnp.concatenate(
         doubling_gather([(h, row_bits[::-1]) for h in hidden_shares], "row", n_row), axis=0)
     (partial_out,) = sparse_matmul(every_hidden, [down_packed], down_keep)
-    half_rows = partial_out.shape[0] // 2
+    rows_q = partial_out.shape[0] // 4
     out_parts = halving_scatter(
-        [([partial_out[:half_rows]], col_orders[0][::-1]), ([partial_out[half_rows:]], col_orders[1][::-1])],
-        "col", n_col)
+        [([partial_out[q * rows_q:(q + 1) * rows_q]], orders[q][::-1]) for q in range(4)], "col", n_col)
     summed = jnp.concatenate([parts[0] for parts in out_parts], axis=0)
     return summed.astype(jnp.bfloat16)
 

time: 280 us -> 268 us (0.957)
  waiting for transfers between devices: 155 us -> 123 us
  starting transfers between devices: 27.2 us -> 50.5 us
    ppermute x24 -> x36, waiting for transfers between devices: 155 us -> 123 us  [exchange(): return lax.ppermute(x, axis, perm=pairs)]
    ppermute x24 -> x36, starting transfers between devices: 27.2 us -> 50.5 us  [exchange(): return lax.ppermute(x, axis, perm=pairs)]
    select_n x10 -> x16, other arithmetic: 5.54 us -> 2.32 us  [doubling_gather(): jnp.where(low, jnp.concatenate([xs[p], got], 0), jnp.concatenate([got, xs...]
  transfers between devices with their start and end apart: 24 -> 36, of which waited for: 17 -> 21; matrix products, arithmetic and copies ran while one was open for 4% -> 4% of each run, Pallas kernels for 0% -> 0%
where the time goes in v6:
time: 268 us; the launch traced here: 267 us
  waiting for transfers between devices  123 us (46%)
  Pallas kernels  69.1 us (26%)
  starting transfers between devices  50.5 us (19%)
  other arithmetic  12.2 us (5%)
  local copies, waits for them, and re-layouts  11.4 us (4%)
    ppermute x36, waiting for transfers between devices, exchange(): return lax.ppermute(x, axis, perm=pairs)  123 us
    pallas_call x2, Pallas kernels, sparse_matmul(): pl.pallas_call(kernel, grid_spec=pltpu.PrefetchScalarGridSpec(num_scalar_...  69.1 us
    ppermute x36, starting transfers between devices, exchange(): return lax.ppermute(x, axis, perm=pairs)  50.5 us
  transfers between devices with their start and end apart: 36, of which 21 were waited for; matrix products, arithmetic and copies ran while one was open for 4% of the time, Pallas kernels for 0%

profile of v6, /device:TPU:0, one launch (start us, length us, event | category | flops | bytes accessed | tf_op | source)
XLA Modules:
  0.0 267.1 jit_solution(5024920009546903772)
XLA Ops:
  0.0 1.1 fusion.6
  1.1 4.1 %collective-permute-start = (bf16[16,4096]{1,0:T(8,128)(2,1)S(1)}, bf16[16,4096]{1,0:T(8,128)(2,1)S(1)}, u32[]{:S(2)}, u32[]{:S(2)}) collective-permute-start(bf16[16,4096]{1,0:T(8,128)(2,1)S(1)} %get-tuple-element.17), channel_id=1, source_target_pairs={{0,4},{1,5},{2,6},{3,7},{4,0},{5,1},{6,2},{7,3},{8,12},{9,13},{10,... | collective-permute-start | bytes 393224 | tf_op jit(solution)/shard_map/ppermute | solution.py:85
  5.2 1.5 collective-permute-start.3
  6.7 0.3 collective-permute-start.6
  7.3 0.8 reshape.58
  8.1 0.8 reshape.64
  9.6 0.7 sub.27
  10.5 0.8 subtract_select_fusion
  11.7 0.7 reshape.68.index_ref
  12.7 2.5 collective-permute-done
  15.4 3.4 %collective-permute-start.4 = (bf16[32,4096]{1,0:T(8,128)(2,1)S(1)}, bf16[32,4096]{1,0:T(8,128)(2,1)S(1)}, u32[]{:S(2)}, u32[]{:S(2)}) collective-permute-start(bf16[32,4096]{1,0:T(8,128)(2,1)S(1)} %maximum_select_fusion.13), channel_id=1, source_target_pairs={{0,4},{1,5},{2,6},{3,7},{4,0},{5,1},{6,2},{7,3},{8,12},{9,13},{10,... | collective-permute-start | bytes 786440 | tf_op jit(solution)/shard_map/ppermute | solution.py:85
  19.0 2.5 collective-permute-start.10
  21.5 8.6 %collective-permute-done.1 = bf16[32,4096]{1,0:T(8,128)(2,1)S(1)} collective-permute-done((bf16[32,4096]{1,0:T(8,128)(2,1)S(1)}, bf16[32,4096]{1,0:T(8,128)(2,1)S(1)}, u32[]{:S(2)}, u32[]{:S(2)}) %collective-permute-start.1) | collective-permute-done | bytes 262176 | tf_op jit(solution)/shard_map/ppermute | solution.py:85
  30.2 2.2 collective-permute-start.2
  32.6 8.7 %collective-permute-done.7 = bf16[32,4096]{1,0:T(8,128)(2,1)S(1)} collective-permute-done((bf16[32,4096]{1,0:T(8,128)(2,1)S(1)}, bf16[32,4096]{1,0:T(8,128)(2,1)S(1)}, u32[]{:S(2)}, u32[]{:S(2)}) %collective-permute-start.7) | collective-permute-done | bytes 262176 | tf_op jit(solution)/shard_map/ppermute | solution.py:85
  41.4 2.0 collective-permute-start.8
  43.8 8.8 %collective-permute-done.5 = bf16[64,4096]{1,0:T(8,128)(2,1)S(1)} collective-permute-done((bf16[64,4096]{1,0:T(8,128)(2,1)S(1)}, bf16[64,4096]{1,0:T(8,128)(2,1)S(1)}, u32[]{:S(2)}, u32[]{:S(2)}) %collective-permute-start.5) | collective-permute-done | bytes 524320 | tf_op jit(solution)/shard_map/ppermute | solution.py:85
  53.1 9.0 %collective-permute-done.11 = bf16[64,4096]{1,0:T(8,128)(2,1)S(1)} collective-permute-done((bf16[64,4096]{1,0:T(8,128)(2,1)S(1)}, bf16[64,4096]{1,0:T(8,128)(2,1)S(1)}, u32[]{:S(2)}, u32[]{:S(2)}) %collective-permute-start.11) | collective-permute-done | bytes 524320 | tf_op jit(solution)/shard_map/ppermute | solution.py:85
  62.3 2.5 pad_maximum_fusion.x_ref
  64.8 43.4 %shard_map.64 = (bf16[512,3328]{1,0:T(8,128)(2,1)}, bf16[512,3328]{1,0:T(8,128)(2,1)}) custom-call(s32[32]{0:T(128)} %copy-done.2, s32[832]{0:T(1024)} %reshape.68.index_ref, bf16[512,4096]{1,0:T(8,128)(2,1)} %pad_maximum_fusion.x_ref, bf16[640,128,128]{2,1,0:T(8,128)(2,1)} %refs_3_.1, bf16[640,128,128]{2,1,0:T(8,128)(2,1)} %refs_3_.1, ...), custom_call_target="tpu_custom_call" | custom-call | flops 27917287424 | bytes 65536000 | tf_op jit(solution)/shard_map/pallas_call | solution.py:66
  108.2 2.3 fusion.4
  110.7 0.5 copy-done
  111.6 0.5 collective-permute-start.18
  112.3 0.7 collective-permute-done.12
  113.3 1.6 collective-permute-start.13
  115.2 1.0 collective-permute-start.15
  116.4 1.2 collective-permute-start.19
  117.8 1.0 collective-permute-start.21
  118.8 7.2 %collective-permute-done.13 = bf16[64,3328]{1,0:T(8,128)(2,1)S(1)} collective-permute-done((bf16[64,3328]{1,0:T(8,128)(2,1)S(1)}, bf16[64,3328]{1,0:T(8,128)(2,1)S(1)}, u32[]{:S(2)}, u32[]{:S(2)}) %collective-permute-start.13) | collective-permute-done | bytes 426016 | tf_op jit(solution)/shard_map/ppermute | solution.py:85
  126.0 9.1 %collective-permute-done.15 = bf16[64,3328]{1,0:T(8,128)(2,1)S(1)} collective-permute-done((bf16[64,3328]{1,0:T(8,128)(2,1)S(1)}, bf16[64,3328]{1,0:T(8,128)(2,1)S(1)}, u32[]{:S(2)}, u32[]{:S(2)}) %collective-permute-start.15) | collective-permute-done | bytes 426016 | tf_op jit(solution)/shard_map/ppermute | solution.py:85
  135.1 0.3 multiply_convert_fusion.1
  135.5 1.6 collective-permute-start.16
  137.1 7.2 %collective-permute-done.19 = bf16[64,3328]{1,0:T(8,128)(2,1)S(1)} collective-permute-done((bf16[64,3328]{1,0:T(8,128)(2,1)S(1)}, bf16[64,3328]{1,0:T(8,128)(2,1)S(1)}, u32[]{:S(2)}, u32[]{:S(2)}) %collective-permute-start.19) | collective-permute-done | bytes 426016 | tf_op jit(solution)/shard_map/ppermute | solution.py:85
  144.3 9.1 %collective-permute-done.21 = bf16[64,3328]{1,0:T(8,128)(2,1)S(1)} collective-permute-done((bf16[64,3328]{1,0:T(8,128)(2,1)S(1)}, bf16[64,3328]{1,0:T(8,128)(2,1)S(1)}, u32[]{:S(2)}, u32[]{:S(2)}) %collective-permute-start.21) | collective-permute-done | bytes 426016 | tf_op jit(solution)/shard_map/ppermute | solution.py:85
  153.7 1.6 collective-permute-start.22
  155.4 7.2 %collective-permute-done.16 = bf16[64,3328]{1,0:T(8,128)(2,1)S(1)} collective-permute-done((bf16[64,3328]{1,0:T(8,128)(2,1)S(1)}, bf16[64,3328]{1,0:T(8,128)(2,1)S(1)}, u32[]{:S(2)}, u32[]{:S(2)}) %collective-permute-start.16) | collective-permute-done | bytes 426016 | tf_op jit(solution)/shard_map/ppermute | solution.py:85
  162.8 8.1 %collective-permute-done.22 = bf16[64,3328]{1,0:T(8,128)(2,1)S(1)} collective-permute-done((bf16[64,3328]{1,0:T(8,128)(2,1)S(1)}, bf16[64,3328]{1,0:T(8,128)(2,1)S(1)}, u32[]{:S(2)}, u32[]{:S(2)}) %collective-permute-start.22) | collective-permute-done | bytes 426016 | tf_op jit(solution)/shard_map/ppermute | solution.py:85
  171.4 0.7 reshape.63.index_ref
  172.0 0.3 maximum_select_fusion
  172.4 1.1 collective-permute-done.23
  173.8 1.9 pad_maximum_fusion.1.x_ref
  175.7 25.7 %shard_map.65 = bf16[512,4096]{1,0:T(8,128)(2,1)} custom-call(s32[26]{0:T(128)} %copy-done.3, s32[832]{0:T(1024)} %reshape.63.index_ref, bf16[512,3328]{1,0:T(8,128)(2,1)} %pad_maximum_fusion.1.x_ref, bf16[640,128,128]{2,1,0:T(8,128)(2,1)} %refs_1_.3, bf16[640,128,128]{2,1,0:T(8,128)(2,1)} %refs_1_.3), custom_call_target="tpu_custom_call" | custom-call | flops 13958643712 | bytes 34865152 | tf_op jit(solution)/shard_map/pallas_call | solution.py:66
  201.4 2.7 fusion.3
  204.1 1.6 collective-permute-start.24
  205.8 0.7 collective-permute-start.27
  206.5 0.6 collective-permute-start.30
  207.1 1.5 collective-permute-start.33
  208.6 10.4 %collective-permute-done.24 = bf16[64,4096]{1,0:T(8,128)(2,1)S(1)} collective-permute-done((bf16[64,4096]{1,0:T(8,128)(2,1)S(1)}, bf16[64,4096]{1,0:T(8,128)(2,1)S(1)}, u32[]{:S(2)}, u32[]{:S(2)}) %collective-permute-start.24) | collective-permute-done | bytes 524320 | tf_op jit(solution)/shard_map/ppermute | solution.py:85
  219.1 0.7 collective-permute-start.25
  219.8 0.8 collective-permute-done.27
  220.8 2.6 collective-permute-start.28
  223.4 5.9 %collective-permute-done.30 = bf16[64,4096]{1,0:T(8,128)(2,1)S(1)} collective-permute-done((bf16[64,4096]{1,0:T(8,128)(2,1)S(1)}, bf16[64,4096]{1,0:T(8,128)(2,1)S(1)}, u32[]{:S(2)}, u32[]{:S(2)}) %collective-permute-start.30) | collective-permute-done | bytes 524320 | tf_op jit(solution)/shard_map/ppermute | solution.py:85
  229.5 0.8 collective-permute-start.31
  230.3 7.2 %collective-permute-done.33 = bf16[64,4096]{1,0:T(8,128)(2,1)S(1)} collective-permute-done((bf16[64,4096]{1,0:T(8,128)(2,1)S(1)}, bf16[64,4096]{1,0:T(8,128)(2,1)S(1)}, u32[]{:S(2)}, u32[]{:S(2)}) %collective-permute-start.33) | collective-permute-done | bytes 524320 | tf_op jit(solution)/shard_map/ppermute | solution.py:85
  237.7 1.5 collective-permute-start.34
  239.2 4.8 %collective-permute-done.25 = bf16[32,4096]{1,0:T(8,128)(2,1)S(1)} collective-permute-done((bf16[32,4096]{1,0:T(8,128)(2,1)S(1)}, bf16[32,4096]{1,0:T(8,128)(2,1)S(1)}, u32[]{:S(2)}, u32[]{:S(2)}) %collective-permute-start.25) | collective-permute-done | bytes 262176 | tf_op jit(solution)/shard_map/ppermute | solution.py:85
  244.0 6.4 %collective-permute-start.26 = (bf16[16,4096]{1,0:T(8,128)(2,1)S(1)}, bf16[16,4096]{1,0:T(8,128)(2,1)S(1)}, u32[]{:S(2)}, u32[]{:S(2)}) collective-permute-start(bf16[16,4096]{1,0:T(8,128)(2,1)S(1)} %dynamic-slice_convert_fusion.11), channel_id=1, source_target_pairs={{0,4},{1,5},{2,6},{3,7},{4,0},{5,1},{6,2},{7,3},{8,12},{9,13},{10,... | collective-permute-start | bytes 393224 | tf_op jit(solution)/shard_map/ppermute | solution.py:85
  250.5 0.6 collective-permute-start.29
  251.1 2.3 collective-permute-done.31
  253.5 1.4 collective-permute-start.32
  255.0 6.5 %collective-permute-start.35 = (bf16[16,4096]{1,0:T(8,128)(2,1)S(1)}, bf16[16,4096]{1,0:T(8,128)(2,1)S(1)}, u32[]{:S(2)}, u32[]{:S(2)}) collective-permute-start(bf16[16,4096]{1,0:T(8,128)(2,1)S(1)} %dynamic-slice_convert_fusion.8), channel_id=1, source_target_pairs={{0,1},{1,0},{2,3},{3,2},{4,5},{5,4},{6,7},{7,6},{8,9},{9,8},{10,11... | collective-permute-start | bytes 393224 | tf_op jit(solution)/shard_map/ppermute | solution.py:85
  261.5 2.1 collective-permute-done.26
  263.6 2.5 collective-permute-done.32
  266.2 0.8 pad_maximum_fusion.2
  (103 shorter events, 7.6 us)
Async XLA Ops:
  1.1 14.0 %collective-permute-start = (bf16[16,4096]{1,0:T(8,128)(2,1)S(1)}, bf16[16,4096]{1,0:T(8,128)(2,1)S(1)}, u32[]{:S(2)}, u32[]{:S(2)}) collective-permute-start(bf16[16,4096]{1,0:T(8,128)(2,1)S(1)} %get-tuple-element.17), channel_id=1, source_target_pairs={{0,4},{1,5},{2,6},{3,7},{4,0},{5,1},{6,2},{7,3},{8,12},{9,13},{10,... | collective-permute-start | bytes 393224 | tf_op jit(solution)/shard_map/ppermute | solution.py:85
  5.2 10.1 %collective-permute-start.3 = (bf16[16,4096]{1,0:T(8,128)(2,1)S(1)}, bf16[16,4096]{1,0:T(8,128)(2,1)S(1)}, u32[]{:S(2)}, u32[]{:S(2)}) collective-permute-start(bf16[16,4096]{1,0:T(8,128)(2,1)S(1)} %get-tuple-element.18), channel_id=1, source_target_pairs={{0,1},{1,0},{2,3},{3,2},{4,5},{5,4},{6,7},{7,6},{8,9},{9,8},{10,11... | collective-permute-start | bytes 393224 | tf_op jit(solution)/shard_map/ppermute | solution.py:85
  6.7 12.1 %collective-permute-start.6 = (bf16[16,4096]{1,0:T(8,128)(2,1)S(1)}, bf16[16,4096]{1,0:T(8,128)(2,1)S(1)}, u32[]{:S(2)}, u32[]{:S(2)}) collective-permute-start(bf16[16,4096]{1,0:T(8,128)(2,1)S(1)} %get-tuple-element.20), channel_id=1, source_target_pairs={{0,4},{1,5},{2,6},{3,7},{4,0},{5,1},{6,2},{7,3},{8,12},{9,13},{10,... | collective-permute-start | bytes 393224 | tf_op jit(solution)/shard_map/ppermute | solution.py:85
  7.1 11.9 %collective-permute-start.9 = (bf16[16,4096]{1,0:T(8,128)(2,1)S(1)}, bf16[16,4096]{1,0:T(8,128)(2,1)S(1)}, u32[]{:S(2)}, u32[]{:S(2)}) collective-permute-start(bf16[16,4096]{1,0:T(8,128)(2,1)S(1)} %get-tuple-element.19), channel_id=1, source_target_pairs={{0,1},{1,0},{2,3},{3,2},{4,5},{5,4},{6,7},{7,6},{8,9},{9,8},{10,11... | collective-permute-start | bytes 393224 | tf_op jit(solution)/shard_map/ppermute | solution.py:85
  10.5 22.0 %copy-start.2 = (s32[32]{0:T(128)}, s32[32]{0:T(128)S(1)}, u32[]{:S(2)}) copy-start(s32[32]{0:T(128)S(1)} %fusion.base_ref) | copy-start | bytes 388
  15.2 14.9 %collective-permute-start.1 = (bf16[32,4096]{1,0:T(8,128)(2,1)S(1)}, bf16[32,4096]{1,0:T(8,128)(2,1)S(1)}, u32[]{:S(2)}, u32[]{:S(2)}) collective-permute-start(bf16[32,4096]{1,0:T(8,128)(2,1)S(1)} %maximum_select_fusion.12), channel_id=1, source_target_pairs={{0,2},{1,3},{2,0},{3,1},{4,6},{5,7},{6,4},{7,5},{8,10},{9,11},{10,... | collective-permute-start | bytes 786440 | tf_op jit(solution)/shard_map/ppermute | solution.py:85
  15.4 17.1 %collective-permute-start.4 = (bf16[32,4096]{1,0:T(8,128)(2,1)S(1)}, bf16[32,4096]{1,0:T(8,128)(2,1)S(1)}, u32[]{:S(2)}, u32[]{:S(2)}) collective-permute-start(bf16[32,4096]{1,0:T(8,128)(2,1)S(1)} %maximum_select_fusion.13), channel_id=1, source_target_pairs={{0,4},{1,5},{2,6},{3,7},{4,0},{5,1},{6,2},{7,3},{8,12},{9,13},{10,... | collective-permute-start | bytes 786440 | tf_op jit(solution)/shard_map/ppermute | solution.py:85
  18.8 22.4 %collective-permute-start.7 = (bf16[32,4096]{1,0:T(8,128)(2,1)S(1)}, bf16[32,4096]{1,0:T(8,128)(2,1)S(1)}, u32[]{:S(2)}, u32[]{:S(2)}) collective-permute-start(bf16[32,4096]{1,0:T(8,128)(2,1)S(1)} %maximum_select_fusion.14), channel_id=1, source_target_pairs={{0,2},{1,3},{2,0},{3,1},{4,6},{5,7},{6,4},{7,5},{8,10},{9,11},{10,... | collective-permute-start | bytes 786440 | tf_op jit(solution)/shard_map/ppermute | solution.py:85
  19.0 24.4 %collective-permute-start.10 = (bf16[32,4096]{1,0:T(8,128)(2,1)S(1)}, bf16[32,4096]{1,0:T(8,128)(2,1)S(1)}, u32[]{:S(2)}, u32[]{:S(2)}) collective-permute-start(bf16[32,4096]{1,0:T(8,128)(2,1)S(1)} %maximum_select_fusion.15), channel_id=1, source_target_pairs={{0,4},{1,5},{2,6},{3,7},{4,0},{5,1},{6,2},{7,3},{8,12},{9,13},{10,... | collective-permute-start | bytes 786440 | tf_op jit(solution)/shard_map/ppermute | solution.py:85
  30.2 13.4 %collective-permute-start.2 = (bf16[64,4096]{1,0:T(8,128)(2,1)S(1)}, bf16[64,4096]{1,0:T(8,128)(2,1)S(1)}, u32[]{:S(2)}, u32[]{:S(2)}) collective-permute-start(bf16[64,4096]{1,0:T(8,128)(2,1)S(1)} %maximum_select_fusion.8), channel_id=1, source_target_pairs={{0,1},{1,0},{2,3},{3,2},{4,5},{5,4},{6,7},{7,6},{8,9},{9,8},{10,11... | collective-permute-start | bytes 1572872 | tf_op jit(solution)/shard_map/ppermute | solution.py:85
  32.5 20.1 %collective-permute-start.5 = (bf16[64,4096]{1,0:T(8,128)(2,1)S(1)}, bf16[64,4096]{1,0:T(8,128)(2,1)S(1)}, u32[]{:S(2)}, u32[]{:S(2)}) collective-permute-start(bf16[64,4096]{1,0:T(8,128)(2,1)S(1)} %maximum_select_fusion.9), channel_id=1, source_target_pairs={{0,2},{1,3},{2,0},{3,1},{4,6},{5,7},{6,4},{7,5},{8,10},{9,11},{10,... | collective-permute-start | bytes 1572872 | tf_op jit(solution)/shard_map/ppermute | solution.py:85
  41.4 11.5 %collective-permute-start.8 = (bf16[64,4096]{1,0:T(8,128)(2,1)S(1)}, bf16[64,4096]{1,0:T(8,128)(2,1)S(1)}, u32[]{:S(2)}, u32[]{:S(2)}) collective-permute-start(bf16[64,4096]{1,0:T(8,128)(2,1)S(1)} %maximum_select_fusion.10), channel_id=1, source_target_pairs={{0,1},{1,0},{2,3},{3,2},{4,5},{5,4},{6,7},{7,6},{8,9},{9,8},{10,11... | collective-permute-start | bytes 1572872 | tf_op jit(solution)/shard_map/ppermute | solution.py:85
  43.5 18.6 %collective-permute-start.11 = (bf16[64,4096]{1,0:T(8,128)(2,1)S(1)}, bf16[64,4096]{1,0:T(8,128)(2,1)S(1)}, u32[]{:S(2)}, u32[]{:S(2)}) collective-permute-start(bf16[64,4096]{1,0:T(8,128)(2,1)S(1)} %maximum_select_fusion.11), channel_id=1, source_target_pairs={{0,2},{1,3},{2,0},{3,1},{4,6},{5,7},{6,4},{7,5},{8,10},{9,11},{10,... | collective-permute-start | bytes 1572872 | tf_op jit(solution)/shard_map/ppermute | solution.py:85
  108.2 3.0 %copy-start = (bf16[512,3328]{1,0:T(8,128)(2,1)S(1)}, bf16[512,3328]{1,0:T(8,128)(2,1)}, u32[]{:S(2)}) copy-start(bf16[512,3328]{1,0:T(8,128)(2,1)} %get-tuple-element.8) | copy-start | bytes 10223620
  110.6 2.4 collective-permute-start.12
  111.5 3.4 %collective-permute-start.14 = (bf16[128,3328]{1,0:T(8,128)(2,1)S(1)}, bf16[128,3328]{1,0:T(8,128)(2,1)S(1)}, u32[]{:S(2)}, u32[]{:S(2)}) collective-permute-start(bf16[128,3328]{1,0:T(8,128)(2,1)S(1)} %constant_dynamic-slice_fusion.6), channel_id=1, source_target_pairs={{0,8},{8,0},{16,24},{24,16},{1,9},{9,1},{17,25},{25,17},{2,10},{10... | collective-permute-start | bytes 2555912 | tf_op jit(solution)/shard_map/ppermute | solution.py:85
  111.6 4.5 %collective-permute-start.18 = (bf16[128,3328]{1,0:T(8,128)(2,1)S(1)}, bf16[128,3328]{1,0:T(8,128)(2,1)S(1)}, u32[]{:S(2)}, u32[]{:S(2)}) collective-permute-start(bf16[128,3328]{1,0:T(8,128)(2,1)S(1)} %constant_dynamic-slice_fusion.5), channel_id=1, source_target_pairs={{0,8},{8,0},{16,24},{24,16},{1,9},{9,1},{17,25},{25,17},{2,10},{10... | collective-permute-start | bytes 2555912 | tf_op jit(solution)/shard_map/ppermute | solution.py:85
  112.2 5.3 %collective-permute-start.20 = (bf16[128,3328]{1,0:T(8,128)(2,1)S(1)}, bf16[128,3328]{1,0:T(8,128)(2,1)S(1)}, u32[]{:S(2)}, u32[]{:S(2)}) collective-permute-start(bf16[128,3328]{1,0:T(8,128)(2,1)S(1)} %constant_dynamic-slice_fusion.4), channel_id=1, source_target_pairs={{0,8},{8,0},{16,24},{24,16},{1,9},{9,1},{17,25},{25,17},{2,10},{10... | collective-permute-start | bytes 2555912 | tf_op jit(solution)/shard_map/ppermute | solution.py:85
  113.3 12.7 %collective-permute-start.13 = (bf16[64,3328]{1,0:T(8,128)(2,1)S(1)}, bf16[64,3328]{1,0:T(8,128)(2,1)S(1)}, u32[]{:S(2)}, u32[]{:S(2)}) collective-permute-start(bf16[64,3328]{1,0:T(8,128)(2,1)S(1)} %dynamic-slice_convert_fusion.3), channel_id=1, source_target_pairs={{0,16},{8,24},{16,0},{24,8},{1,17},{9,25},{17,1},{25,9},{2,18},{10... | collective-permute-start | bytes 1277960 | tf_op jit(solution)/shard_map/ppermute | solution.py:85
  115.2 20.0 %collective-permute-start.15 = (bf16[64,3328]{1,0:T(8,128)(2,1)S(1)}, bf16[64,3328]{1,0:T(8,128)(2,1)S(1)}, u32[]{:S(2)}, u32[]{:S(2)}) collective-permute-start(bf16[64,3328]{1,0:T(8,128)(2,1)S(1)} %dynamic-slice_convert_fusion.2), channel_id=1, source_target_pairs={{0,16},{8,24},{16,0},{24,8},{1,17},{9,25},{17,1},{25,9},{2,18},{10... | collective-permute-start | bytes 1277960 | tf_op jit(solution)/shard_map/ppermute | solution.py:85
  116.4 27.9 %collective-permute-start.19 = (bf16[64,3328]{1,0:T(8,128)(2,1)S(1)}, bf16[64,3328]{1,0:T(8,128)(2,1)S(1)}, u32[]{:S(2)}, u32[]{:S(2)}) collective-permute-start(bf16[64,3328]{1,0:T(8,128)(2,1)S(1)} %dynamic-slice_convert_fusion.1), channel_id=1, source_target_pairs={{0,16},{8,24},{16,0},{24,8},{1,17},{9,25},{17,1},{25,9},{2,18},{10... | collective-permute-start | bytes 1277960 | tf_op jit(solution)/shard_map/ppermute | solution.py:85
  117.8 35.6 %collective-permute-start.21 = (bf16[64,3328]{1,0:T(8,128)(2,1)S(1)}, bf16[64,3328]{1,0:T(8,128)(2,1)S(1)}, u32[]{:S(2)}, u32[]{:S(2)}) collective-permute-start(bf16[64,3328]{1,0:T(8,128)(2,1)S(1)} %dynamic-slice_convert_fusion), channel_id=1, source_target_pairs={{0,16},{8,24},{16,0},{24,8},{1,17},{9,25},{17,1},{25,9},{2,18},{10... | collective-permute-start | bytes 1277960 | tf_op jit(solution)/shard_map/ppermute | solution.py:85
  135.5 27.1 %collective-permute-start.16 = (bf16[64,3328]{1,0:T(8,128)(2,1)S(1)}, bf16[64,3328]{1,0:T(8,128)(2,1)S(1)}, u32[]{:S(2)}, u32[]{:S(2)}) collective-permute-start(bf16[64,3328]{1,0:T(8,128)(2,1)S(1)} %multiply_convert_fusion.1), channel_id=1, source_target_pairs={{0,16},{8,24},{16,0},{24,8},{1,17},{9,25},{17,1},{25,9},{2,18},{10... | collective-permute-start | bytes 1277960 | tf_op jit(solution)/shard_map/ppermute | solution.py:85
  153.7 17.4 %copy-start.1 = (s32[26,32]{1,0:T(8,128)S(1)}, s32[26,32]{1,0:T(8,128)}, u32[]{:S(2)}) copy-start(s32[26,32]{1,0:T(8,128)} %param.11) | copy-start | bytes 9988
  153.7 17.1 %collective-permute-start.22 = (bf16[64,3328]{1,0:T(8,128)(2,1)S(1)}, bf16[64,3328]{1,0:T(8,128)(2,1)S(1)}, u32[]{:S(2)}, u32[]{:S(2)}) collective-permute-start(bf16[64,3328]{1,0:T(8,128)(2,1)S(1)} %multiply_convert_fusion), channel_id=1, source_target_pairs={{0,16},{8,24},{16,0},{24,8},{1,17},{9,25},{17,1},{25,9},{2,18},{10... | collective-permute-start | bytes 1277960 | tf_op jit(solution)/shard_map/ppermute | solution.py:85
  162.7 9.3 %collective-permute-start.17 = (bf16[128,3328]{1,0:T(8,128)(2,1)S(1)}, bf16[128,3328]{1,0:T(8,128)(2,1)S(1)}, u32[]{:S(2)}, u32[]{:S(2)}) collective-permute-start(bf16[128,3328]{1,0:T(8,128)(2,1)S(1)} %maximum_select_fusion.6), channel_id=1, source_target_pairs={{0,8},{8,0},{16,24},{24,16},{1,9},{9,1},{17,25},{25,17},{2,10},{10... | collective-permute-start | bytes 2555912 | tf_op jit(solution)/shard_map/ppermute | solution.py:85
  171.0 2.4 collective-permute-start.23
  171.3 1.1 copy-start.3
  204.1 14.8 %collective-permute-start.24 = (bf16[64,4096]{1,0:T(8,128)(2,1)S(1)}, bf16[64,4096]{1,0:T(8,128)(2,1)S(1)}, u32[]{:S(2)}, u32[]{:S(2)}) collective-permute-start(bf16[64,4096]{1,0:T(8,128)(2,1)S(1)} %constant_dynamic-slice_fusion.3), channel_id=1, source_target_pairs={{0,1},{1,0},{2,3},{3,2},{4,5},{5,4},{6,7},{7,6},{8,9},{9,8},{10,11... | collective-permute-start | bytes 1572872 | tf_op jit(solution)/shard_map/ppermute | solution.py:85
  205.8 14.9 %collective-permute-start.27 = (bf16[64,4096]{1,0:T(8,128)(2,1)S(1)}, bf16[64,4096]{1,0:T(8,128)(2,1)S(1)}, u32[]{:S(2)}, u32[]{:S(2)}) collective-permute-start(bf16[64,4096]{1,0:T(8,128)(2,1)S(1)} %constant_dynamic-slice_fusion.2), channel_id=1, source_target_pairs={{0,2},{1,3},{2,0},{3,1},{4,6},{5,7},{6,4},{7,5},{8,10},{9,11},{10,... | collective-permute-start | bytes 1572872 | tf_op jit(solution)/shard_map/ppermute | solution.py:85
  206.5 22.8 %collective-permute-start.30 = (bf16[64,4096]{1,0:T(8,128)(2,1)S(1)}, bf16[64,4096]{1,0:T(8,128)(2,1)S(1)}, u32[]{:S(2)}, u32[]{:S(2)}) collective-permute-start(bf16[64,4096]{1,0:T(8,128)(2,1)S(1)} %constant_dynamic-slice_fusion.1), channel_id=1, source_target_pairs={{0,1},{1,0},{2,3},{3,2},{4,5},{5,4},{6,7},{7,6},{8,9},{9,8},{10,11... | collective-permute-start | bytes 1572872 | tf_op jit(solution)/shard_map/ppermute | solution.py:85
  207.1 30.4 %collective-permute-start.33 = (bf16[64,4096]{1,0:T(8,128)(2,1)S(1)}, bf16[64,4096]{1,0:T(8,128)(2,1)S(1)}, u32[]{:S(2)}, u32[]{:S(2)}) collective-permute-start(bf16[64,4096]{1,0:T(8,128)(2,1)S(1)} %constant_dynamic-slice_fusion), channel_id=1, source_target_pairs={{0,2},{1,3},{2,0},{3,1},{4,6},{5,7},{6,4},{7,5},{8,10},{9,11},{10,... | collective-permute-start | bytes 1572872 | tf_op jit(solution)/shard_map/ppermute | solution.py:85
  219.1 24.8 %collective-permute-start.25 = (bf16[32,4096]{1,0:T(8,128)(2,1)S(1)}, bf16[32,4096]{1,0:T(8,128)(2,1)S(1)}, u32[]{:S(2)}, u32[]{:S(2)}) collective-permute-start(bf16[32,4096]{1,0:T(8,128)(2,1)S(1)} %dynamic-slice_convert_fusion.7), channel_id=1, source_target_pairs={{0,2},{1,3},{2,0},{3,1},{4,6},{5,7},{6,4},{7,5},{8,10},{9,11},{10,... | collective-permute-start | bytes 786440 | tf_op jit(solution)/shard_map/ppermute | solution.py:85
  220.8 29.6 %collective-permute-start.28 = (bf16[32,4096]{1,0:T(8,128)(2,1)S(1)}, bf16[32,4096]{1,0:T(8,128)(2,1)S(1)}, u32[]{:S(2)}, u32[]{:S(2)}) collective-permute-start(bf16[32,4096]{1,0:T(8,128)(2,1)S(1)} %dynamic-slice_convert_fusion.6), channel_id=1, source_target_pairs={{0,4},{1,5},{2,6},{3,7},{4,0},{5,1},{6,2},{7,3},{8,12},{9,13},{10,... | collective-permute-start | bytes 786440 | tf_op jit(solution)/shard_map/ppermute | solution.py:85
  229.5 23.9 %collective-permute-start.31 = (bf16[32,4096]{1,0:T(8,128)(2,1)S(1)}, bf16[32,4096]{1,0:T(8,128)(2,1)S(1)}, u32[]{:S(2)}, u32[]{:S(2)}) collective-permute-start(bf16[32,4096]{1,0:T(8,128)(2,1)S(1)} %dynamic-slice_convert_fusion.5), channel_id=1, source_target_pairs={{0,2},{1,3},{2,0},{3,1},{4,6},{5,7},{6,4},{7,5},{8,10},{9,11},{10,... | collective-permute-start | bytes 786440 | tf_op jit(solution)/shard_map/ppermute | solution.py:85
  237.7 17.2 %collective-permute-start.34 = (bf16[32,4096]{1,0:T(8,128)(2,1)S(1)}, bf16[32,4096]{1,0:T(8,128)(2,1)S(1)}, u32[]{:S(2)}, u32[]{:S(2)}) collective-permute-start(bf16[32,4096]{1,0:T(8,128)(2,1)S(1)} %dynamic-slice_convert_fusion.4), channel_id=1, source_target_pairs={{0,4},{1,5},{2,6},{3,7},{4,0},{5,1},{6,2},{7,3},{8,12},{9,13},{10,... | collective-permute-start | bytes 786440 | tf_op jit(solution)/shard_map/ppermute | solution.py:85
  244.0 19.6 %collective-permute-start.26 = (bf16[16,4096]{1,0:T(8,128)(2,1)S(1)}, bf16[16,4096]{1,0:T(8,128)(2,1)S(1)}, u32[]{:S(2)}, u32[]{:S(2)}) collective-permute-start(bf16[16,4096]{1,0:T(8,128)(2,1)S(1)} %dynamic-slice_convert_fusion.11), channel_id=1, source_target_pairs={{0,4},{1,5},{2,6},{3,7},{4,0},{5,1},{6,2},{7,3},{8,12},{9,13},{10,... | collective-permute-start | bytes 393224 | tf_op jit(solution)/shard_map/ppermute | solution.py:85
  250.5 15.6 %collective-permute-start.29 = (bf16[16,4096]{1,0:T(8,128)(2,1)S(1)}, bf16[16,4096]{1,0:T(8,128)(2,1)S(1)}, u32[]{:S(2)}, u32[]{:S(2)}) collective-permute-start(bf16[16,4096]{1,0:T(8,128)(2,1)S(1)} %dynamic-slice_convert_fusion.10), channel_id=1, source_target_pairs={{0,1},{1,0},{2,3},{3,2},{4,5},{5,4},{6,7},{7,6},{8,9},{9,8},{10,11... | collective-permute-start | bytes 393224 | tf_op jit(solution)/shard_map/ppermute | solution.py:85
  253.5 12.6 %collective-permute-start.32 = (bf16[16,4096]{1,0:T(8,128)(2,1)S(1)}, bf16[16,4096]{1,0:T(8,128)(2,1)S(1)}, u32[]{:S(2)}, u32[]{:S(2)}) collective-permute-start(bf16[16,4096]{1,0:T(8,128)(2,1)S(1)} %dynamic-slice_convert_fusion.9), channel_id=1, source_target_pairs={{0,4},{1,5},{2,6},{3,7},{4,0},{5,1},{6,2},{7,3},{8,12},{9,13},{10,... | collective-permute-start | bytes 393224 | tf_op jit(solution)/shard_map/ppermute | solution.py:85
  255.0 11.2 %collective-permute-start.35 = (bf16[16,4096]{1,0:T(8,128)(2,1)S(1)}, bf16[16,4096]{1,0:T(8,128)(2,1)S(1)}, u32[]{:S(2)}, u32[]{:S(2)}) collective-permute-start(bf16[16,4096]{1,0:T(8,128)(2,1)S(1)} %dynamic-slice_convert_fusion.8), channel_id=1, source_target_pairs={{0,1},{1,0},{2,3},{3,2},{4,5},{5,4},{6,7},{7,6},{8,9},{9,8},{10,11... | collective-permute-start | bytes 393224 | tf_op jit(solution)/shard_map/ppermute | solution.py:85

commit v7 on v6

--- a/solution.py
+++ b/solution.py
@@ -123,9 +123,9 @@
     token_parts = [tokens[q * quarter:(q + 1) * quarter] for q in range(4)]
     segment = jnp.concatenate(doubling_gather(list(zip(token_parts, orders)), "col", n_col), axis=0)
     gate_rows, up_rows = sparse_matmul(segment, [gate_packed, up_packed], gate_keep)
-    half = gate_rows.shape[0] // 2
+    rq = gate_rows.shape[0] // 4
     sums = halving_scatter(
-        [([gate_rows[:half], up_rows[:half]], row_bits), ([gate_rows[half:], up_rows[half:]], row_bits)],
+        [([gate_rows[q * rq:(q + 1) * rq], up_rows[q * rq:(q + 1) * rq]], row_bits) for q in range(4)],
         "row", n_row)
     hidden_shares = [(jax.nn.silu(g) * u).astype(jnp.bfloat16) for g, u in sums]
     every_hidden = jnp.concatenate(

time: 268 us -> 268 us (level)
  waiting for transfers between devices: 123 us -> 116 us
  starting transfers between devices: 50.5 us -> 57 us
    ppermute x36 -> x48, waiting for transfers between devices: 123 us -> 116 us  [exchange(): return lax.ppermute(x, axis, perm=pairs)]
    ppermute x36 -> x48, starting transfers between devices: 50.5 us -> 57 us  [exchange(): return lax.ppermute(x, axis, perm=pairs)]
  transfers between devices with their start and end apart: 36 -> 48, of which waited for: 21 -> 28; matrix products, arithmetic and copies ran while one was open for 4% -> 5% of each run, Pallas kernels for 0% -> 0%
where the time goes in v7:
time: 268 us; the launch traced here: 267 us
  waiting for transfers between devices  116 us (43%)
  Pallas kernels  69 us (26%)
  starting transfers between devices  57 us (21%)
  other arithmetic  13.5 us (5%)
  local copies, waits for them, and re-layouts  11.5 us (4%)
    ppermute x48, waiting for transfers between devices, exchange(): return lax.ppermute(x, axis, perm=pairs)  116 us
    pallas_call x2, Pallas kernels, sparse_matmul(): pl.pallas_call(kernel, grid_spec=pltpu.PrefetchScalarGridSpec(num_scalar_...  69 us
    ppermute x48, starting transfers between devices, exchange(): return lax.ppermute(x, axis, perm=pairs)  57 us
  transfers between devices with their start and end apart: 48, of which 28 were waited for; matrix products, arithmetic and copies ran while one was open for 5% of the time, Pallas kernels for 0%

profile of v7, /device:TPU:0, one launch (start us, length us, event | category | flops | bytes accessed | tf_op | source)
XLA Modules:
  0.0 267.3 jit_solution(5983744670647760289)
XLA Ops:
  0.0 1.1 fusion.6
  1.1 4.1 %collective-permute-start = (bf16[16,4096]{1,0:T(8,128)(2,1)S(1)}, bf16[16,4096]{1,0:T(8,128)(2,1)S(1)}, u32[]{:S(2)}, u32[]{:S(2)}) collective-permute-start(bf16[16,4096]{1,0:T(8,128)(2,1)S(1)} %get-tuple-element.21), channel_id=1, source_target_pairs={{0,4},{1,5},{2,6},{3,7},{4,0},{5,1},{6,2},{7,3},{8,12},{9,13},{10,... | collective-permute-start | bytes 393224 | tf_op jit(solution)/shard_map/ppermute | solution.py:85
  5.2 1.5 collective-permute-start.3
  7.3 0.8 reshape.58
  8.1 0.8 reshape.64
  10.9 0.8 subtract_select_fusion
  12.7 0.8 fusion.2
  13.6 0.8 subtract_select_fusion.1
  15.2 1.8 collective-permute-start.1
  17.1 2.7 collective-permute-start.4
  20.3 1.2 collective-permute-start.10
  21.5 10.1 %collective-permute-done.1 = bf16[32,4096]{1,0:T(8,128)(2,1)S(1)} collective-permute-done((bf16[32,4096]{1,0:T(8,128)(2,1)S(1)}, bf16[32,4096]{1,0:T(8,128)(2,1)S(1)}, u32[]{:S(2)}, u32[]{:S(2)}) %collective-permute-start.1) | collective-permute-done | bytes 262176 | tf_op jit(solution)/shard_map/ppermute | solution.py:85
  31.7 2.2 collective-permute-start.2
  34.1 7.3 %collective-permute-done.7 = bf16[32,4096]{1,0:T(8,128)(2,1)S(1)} collective-permute-done((bf16[32,4096]{1,0:T(8,128)(2,1)S(1)}, bf16[32,4096]{1,0:T(8,128)(2,1)S(1)}, u32[]{:S(2)}, u32[]{:S(2)}) %collective-permute-start.7) | collective-permute-done | bytes 262176 | tf_op jit(solution)/shard_map/ppermute | solution.py:85
  41.5 1.9 collective-permute-start.8
  43.5 0.9 collective-permute-start.11
  44.6 8.0 %collective-permute-done.5 = bf16[64,4096]{1,0:T(8,128)(2,1)S(1)} collective-permute-done((bf16[64,4096]{1,0:T(8,128)(2,1)S(1)}, bf16[64,4096]{1,0:T(8,128)(2,1)S(1)}, u32[]{:S(2)}, u32[]{:S(2)}) %collective-permute-start.5) | collective-permute-done | bytes 524320 | tf_op jit(solution)/shard_map/ppermute | solution.py:85
  53.1 9.0 %collective-permute-done.11 = bf16[64,4096]{1,0:T(8,128)(2,1)S(1)} collective-permute-done((bf16[64,4096]{1,0:T(8,128)(2,1)S(1)}, bf16[64,4096]{1,0:T(8,128)(2,1)S(1)}, u32[]{:S(2)}, u32[]{:S(2)}) %collective-permute-start.11) | collective-permute-done | bytes 524320 | tf_op jit(solution)/shard_map/ppermute | solution.py:85
  62.3 2.5 pad_maximum_fusion.x_ref
  64.8 43.4 %shard_map.64 = (bf16[512,3328]{1,0:T(8,128)(2,1)}, bf16[512,3328]{1,0:T(8,128)(2,1)}) custom-call(s32[32]{0:T(128)} %copy-done.1, s32[832]{0:T(1024)} %reshape.68.index_ref, bf16[512,4096]{1,0:T(8,128)(2,1)} %pad_maximum_fusion.x_ref, bf16[640,128,128]{2,1,0:T(8,128)(2,1)} %refs_3_.1, bf16[640,128,128]{2,1,0:T(8,128)(2,1)} %refs_3_.1, ...), custom_call_target="tpu_custom_call" | custom-call | flops 27917287424 | bytes 65536000 | tf_op jit(solution)/shard_map/pallas_call | solution.py:66
  108.2 2.3 fusion.4
  114.5 1.6 collective-permute-start.13
  116.9 1.6 collective-permute-start.19
  119.3 1.6 collective-permute-start.25
  121.1 1.5 collective-permute-done.13
  122.6 1.6 collective-permute-start.27
  124.2 3.0 %collective-permute-done.15 = bf16[32,3328]{1,0:T(8,128)(2,1)S(1)} collective-permute-done((bf16[32,3328]{1,0:T(8,128)(2,1)S(1)}, bf16[32,3328]{1,0:T(8,128)(2,1)S(1)}, u32[]{:S(2)}, u32[]{:S(2)}) %collective-permute-start.15) | collective-permute-done | bytes 213024 | tf_op jit(solution)/shard_map/ppermute | solution.py:85
  127.2 1.6 collective-permute-start.31
  128.9 2.8 %collective-permute-done.19 = bf16[32,3328]{1,0:T(8,128)(2,1)S(1)} collective-permute-done((bf16[32,3328]{1,0:T(8,128)(2,1)S(1)}, bf16[32,3328]{1,0:T(8,128)(2,1)S(1)}, u32[]{:S(2)}, u32[]{:S(2)}) %collective-permute-start.19) | collective-permute-done | bytes 213024 | tf_op jit(solution)/shard_map/ppermute | solution.py:85
  131.7 1.6 collective-permute-start.33
  133.3 3.0 %collective-permute-done.21 = bf16[32,3328]{1,0:T(8,128)(2,1)S(1)} collective-permute-done((bf16[32,3328]{1,0:T(8,128)(2,1)S(1)}, bf16[32,3328]{1,0:T(8,128)(2,1)S(1)}, u32[]{:S(2)}, u32[]{:S(2)}) %collective-permute-start.21) | collective-permute-done | bytes 213024 | tf_op jit(solution)/shard_map/ppermute | solution.py:85
  136.3 1.6 collective-permute-start.16
  138.0 2.8 %collective-permute-done.25 = bf16[32,3328]{1,0:T(8,128)(2,1)S(1)} collective-permute-done((bf16[32,3328]{1,0:T(8,128)(2,1)S(1)}, bf16[32,3328]{1,0:T(8,128)(2,1)S(1)}, u32[]{:S(2)}, u32[]{:S(2)}) %collective-permute-start.25) | collective-permute-done | bytes 213024 | tf_op jit(solution)/shard_map/ppermute | solution.py:85
  140.8 1.6 collective-permute-start.22
  142.4 3.0 %collective-permute-done.27 = bf16[32,3328]{1,0:T(8,128)(2,1)S(1)} collective-permute-done((bf16[32,3328]{1,0:T(8,128)(2,1)S(1)}, bf16[32,3328]{1,0:T(8,128)(2,1)S(1)}, u32[]{:S(2)}, u32[]{:S(2)}) %collective-permute-start.27) | collective-permute-done | bytes 213024 | tf_op jit(solution)/shard_map/ppermute | solution.py:85
  145.6 1.6 collective-permute-start.28
  147.2 2.8 %collective-permute-done.31 = bf16[32,3328]{1,0:T(8,128)(2,1)S(1)} collective-permute-done((bf16[32,3328]{1,0:T(8,128)(2,1)S(1)}, bf16[32,3328]{1,0:T(8,128)(2,1)S(1)}, u32[]{:S(2)}, u32[]{:S(2)}) %collective-permute-start.31) | collective-permute-done | bytes 213024 | tf_op jit(solution)/shard_map/ppermute | solution.py:85
  150.0 4.6 %collective-permute-done.33 = bf16[32,3328]{1,0:T(8,128)(2,1)S(1)} collective-permute-done((bf16[32,3328]{1,0:T(8,128)(2,1)S(1)}, bf16[32,3328]{1,0:T(8,128)(2,1)S(1)}, u32[]{:S(2)}, u32[]{:S(2)}) %collective-permute-start.33) | collective-permute-done | bytes 213024 | tf_op jit(solution)/shard_map/ppermute | solution.py:85
  154.7 1.6 collective-permute-start.34
  156.3 2.8 %collective-permute-done.16 = bf16[32,3328]{1,0:T(8,128)(2,1)S(1)} collective-permute-done((bf16[32,3328]{1,0:T(8,128)(2,1)S(1)}, bf16[32,3328]{1,0:T(8,128)(2,1)S(1)}, u32[]{:S(2)}, u32[]{:S(2)}) %collective-permute-start.16) | collective-permute-done | bytes 213024 | tf_op jit(solution)/shard_map/ppermute | solution.py:85
  159.3 4.4 %collective-permute-done.22 = bf16[32,3328]{1,0:T(8,128)(2,1)S(1)} collective-permute-done((bf16[32,3328]{1,0:T(8,128)(2,1)S(1)}, bf16[32,3328]{1,0:T(8,128)(2,1)S(1)}, u32[]{:S(2)}, u32[]{:S(2)}) %collective-permute-start.22) | collective-permute-done | bytes 213024 | tf_op jit(solution)/shard_map/ppermute | solution.py:85
  163.8 4.4 %collective-permute-done.28 = bf16[32,3328]{1,0:T(8,128)(2,1)S(1)} collective-permute-done((bf16[32,3328]{1,0:T(8,128)(2,1)S(1)}, bf16[32,3328]{1,0:T(8,128)(2,1)S(1)}, u32[]{:S(2)}, u32[]{:S(2)}) %collective-permute-start.28) | collective-permute-done | bytes 213024 | tf_op jit(solution)/shard_map/ppermute | solution.py:85
  168.4 3.6 %collective-permute-done.34 = bf16[32,3328]{1,0:T(8,128)(2,1)S(1)} collective-permute-done((bf16[32,3328]{1,0:T(8,128)(2,1)S(1)}, bf16[32,3328]{1,0:T(8,128)(2,1)S(1)}, u32[]{:S(2)}, u32[]{:S(2)}) %collective-permute-start.34) | collective-permute-done | bytes 213024 | tf_op jit(solution)/shard_map/ppermute | solution.py:85
  172.7 1.3 collective-permute-done.35
  174.1 1.9 pad_maximum_fusion.1.x_ref
  175.9 25.6 %shard_map.65 = bf16[512,4096]{1,0:T(8,128)(2,1)} custom-call(s32[26]{0:T(128)} %copy-done.2, s32[832]{0:T(1024)} %reshape.63.index_ref, bf16[512,3328]{1,0:T(8,128)(2,1)} %pad_maximum_fusion.1.x_ref, bf16[640,128,128]{2,1,0:T(8,128)(2,1)} %refs_1_.3, bf16[640,128,128]{2,1,0:T(8,128)(2,1)} %refs_1_.3), custom_call_target="tpu_custom_call" | custom-call | flops 13958643712 | bytes 34865152 | tf_op jit(solution)/shard_map/pallas_call | solution.py:66
  201.6 2.7 fusion.3
  204.3 1.6 collective-permute-start.36
  206.0 1.3 collective-permute-start.39
  208.0 0.7 collective-permute-start.45
  208.7 10.4 %collective-permute-done.36 = bf16[64,4096]{1,0:T(8,128)(2,1)S(1)} collective-permute-done((bf16[64,4096]{1,0:T(8,128)(2,1)S(1)}, bf16[64,4096]{1,0:T(8,128)(2,1)S(1)}, u32[]{:S(2)}, u32[]{:S(2)}) %collective-permute-start.36) | collective-permute-done | bytes 524320 | tf_op jit(solution)/shard_map/ppermute | solution.py:85
  219.3 1.5 collective-permute-start.37
  221.0 2.7 %collective-permute-start.40 = (bf16[32,4096]{1,0:T(8,128)(2,1)S(1)}, bf16[32,4096]{1,0:T(8,128)(2,1)S(1)}, u32[]{:S(2)}, u32[]{:S(2)}) collective-permute-start(bf16[32,4096]{1,0:T(8,128)(2,1)S(1)} %dynamic-slice_convert_fusion.2), channel_id=1, source_target_pairs={{0,4},{1,5},{2,6},{3,7},{4,0},{5,1},{6,2},{7,3},{8,12},{9,13},{10,... | collective-permute-start | bytes 786440 | tf_op jit(solution)/shard_map/ppermute | solution.py:85
  223.7 6.0 %collective-permute-done.42 = bf16[64,4096]{1,0:T(8,128)(2,1)S(1)} collective-permute-done((bf16[64,4096]{1,0:T(8,128)(2,1)S(1)}, bf16[64,4096]{1,0:T(8,128)(2,1)S(1)}, u32[]{:S(2)}, u32[]{:S(2)}) %collective-permute-start.42) | collective-permute-done | bytes 524320 | tf_op jit(solution)/shard_map/ppermute | solution.py:85
  229.9 1.2 collective-permute-start.43
  231.1 6.6 %collective-permute-done.45 = bf16[64,4096]{1,0:T(8,128)(2,1)S(1)} collective-permute-done((bf16[64,4096]{1,0:T(8,128)(2,1)S(1)}, bf16[64,4096]{1,0:T(8,128)(2,1)S(1)}, u32[]{:S(2)}, u32[]{:S(2)}) %collective-permute-start.45) | collective-permute-done | bytes 524320 | tf_op jit(solution)/shard_map/ppermute | solution.py:85
  237.8 1.6 collective-permute-start.46
  239.5 4.6 %collective-permute-done.37 = bf16[32,4096]{1,0:T(8,128)(2,1)S(1)} collective-permute-done((bf16[32,4096]{1,0:T(8,128)(2,1)S(1)}, bf16[32,4096]{1,0:T(8,128)(2,1)S(1)}, u32[]{:S(2)}, u32[]{:S(2)}) %collective-permute-start.37) | collective-permute-done | bytes 262176 | tf_op jit(solution)/shard_map/ppermute | solution.py:85
  244.2 6.4 %collective-permute-start.38 = (bf16[16,4096]{1,0:T(8,128)(2,1)S(1)}, bf16[16,4096]{1,0:T(8,128)(2,1)S(1)}, u32[]{:S(2)}, u32[]{:S(2)}) collective-permute-start(bf16[16,4096]{1,0:T(8,128)(2,1)S(1)} %dynamic-slice_convert_fusion.15), channel_id=1, source_target_pairs={{0,4},{1,5},{2,6},{3,7},{4,0},{5,1},{6,2},{7,3},{8,12},{9,13},{10,... | collective-permute-start | bytes 393224 | tf_op jit(solution)/shard_map/ppermute | solution.py:85
  251.1 2.5 collective-permute-done.43
  253.7 1.5 collective-permute-start.44
  256.0 7.8 %collective-permute-done.38 = bf16[16,4096]{1,0:T(8,128)(2,1)S(1)} collective-permute-done((bf16[16,4096]{1,0:T(8,128)(2,1)S(1)}, bf16[16,4096]{1,0:T(8,128)(2,1)S(1)}, u32[]{:S(2)}, u32[]{:S(2)}) %collective-permute-start.38) | collective-permute-done | bytes 131104 | tf_op jit(solution)/shard_map/ppermute | solution.py:85
  263.8 2.5 collective-permute-done.44
  266.4 0.8 pad_maximum_fusion.2
  (143 shorter events, 16.8 us)
Async XLA Ops:
  1.1 14.0 %collective-permute-start = (bf16[16,4096]{1,0:T(8,128)(2,1)S(1)}, bf16[16,4096]{1,0:T(8,128)(2,1)S(1)}, u32[]{:S(2)}, u32[]{:S(2)}) collective-permute-start(bf16[16,4096]{1,0:T(8,128)(2,1)S(1)} %get-tuple-element.21), channel_id=1, source_target_pairs={{0,4},{1,5},{2,6},{3,7},{4,0},{5,1},{6,2},{7,3},{8,12},{9,13},{10,... | collective-permute-start | bytes 393224 | tf_op jit(solution)/shard_map/ppermute | solution.py:85
  5.2 11.8 %collective-permute-start.3 = (bf16[16,4096]{1,0:T(8,128)(2,1)S(1)}, bf16[16,4096]{1,0:T(8,128)(2,1)S(1)}, u32[]{:S(2)}, u32[]{:S(2)}) collective-permute-start(bf16[16,4096]{1,0:T(8,128)(2,1)S(1)} %get-tuple-element.22), channel_id=1, source_target_pairs={{0,1},{1,0},{2,3},{3,2},{4,5},{5,4},{6,7},{7,6},{8,9},{9,8},{10,11... | collective-permute-start | bytes 393224 | tf_op jit(solution)/shard_map/ppermute | solution.py:85
  6.7 13.0 %collective-permute-start.6 = (bf16[16,4096]{1,0:T(8,128)(2,1)S(1)}, bf16[16,4096]{1,0:T(8,128)(2,1)S(1)}, u32[]{:S(2)}, u32[]{:S(2)}) collective-permute-start(bf16[16,4096]{1,0:T(8,128)(2,1)S(1)} %get-tuple-element.24), channel_id=1, source_target_pairs={{0,4},{1,5},{2,6},{3,7},{4,0},{5,1},{6,2},{7,3},{8,12},{9,13},{10,... | collective-permute-start | bytes 393224 | tf_op jit(solution)/shard_map/ppermute | solution.py:85
  7.1 13.2 %collective-permute-start.9 = (bf16[16,4096]{1,0:T(8,128)(2,1)S(1)}, bf16[16,4096]{1,0:T(8,128)(2,1)S(1)}, u32[]{:S(2)}, u32[]{:S(2)}) collective-permute-start(bf16[16,4096]{1,0:T(8,128)(2,1)S(1)} %get-tuple-element.23), channel_id=1, source_target_pairs={{0,1},{1,0},{2,3},{3,2},{4,5},{5,4},{6,7},{7,6},{8,9},{9,8},{10,11... | collective-permute-start | bytes 393224 | tf_op jit(solution)/shard_map/ppermute | solution.py:85
  10.9 23.1 %copy-start.1 = (s32[32]{0:T(128)}, s32[32]{0:T(128)S(1)}, u32[]{:S(2)}) copy-start(s32[32]{0:T(128)S(1)} %fusion.base_ref) | copy-start | bytes 388
  13.6 20.4 %copy-start.2 = (s32[26]{0:T(128)}, s32[26]{0:T(128)S(1)}, u32[]{:S(2)}) copy-start(s32[26]{0:T(128)S(1)} %fusion.1.base_ref) | copy-start | bytes 316
  15.2 16.3 %collective-permute-start.1 = (bf16[32,4096]{1,0:T(8,128)(2,1)S(1)}, bf16[32,4096]{1,0:T(8,128)(2,1)S(1)}, u32[]{:S(2)}, u32[]{:S(2)}) collective-permute-start(bf16[32,4096]{1,0:T(8,128)(2,1)S(1)} %maximum_select_fusion.16), channel_id=1, source_target_pairs={{0,2},{1,3},{2,0},{3,1},{4,6},{5,7},{6,4},{7,5},{8,10},{9,11},{10,... | collective-permute-start | bytes 786440 | tf_op jit(solution)/shard_map/ppermute | solution.py:85
  17.1 16.8 %collective-permute-start.4 = (bf16[32,4096]{1,0:T(8,128)(2,1)S(1)}, bf16[32,4096]{1,0:T(8,128)(2,1)S(1)}, u32[]{:S(2)}, u32[]{:S(2)}) collective-permute-start(bf16[32,4096]{1,0:T(8,128)(2,1)S(1)} %maximum_select_fusion.17), channel_id=1, source_target_pairs={{0,4},{1,5},{2,6},{3,7},{4,0},{5,1},{6,2},{7,3},{8,12},{9,13},{10,... | collective-permute-start | bytes 786440 | tf_op jit(solution)/shard_map/ppermute | solution.py:85
  19.8 21.6 %collective-permute-start.7 = (bf16[32,4096]{1,0:T(8,128)(2,1)S(1)}, bf16[32,4096]{1,0:T(8,128)(2,1)S(1)}, u32[]{:S(2)}, u32[]{:S(2)}) collective-permute-start(bf16[32,4096]{1,0:T(8,128)(2,1)S(1)} %maximum_select_fusion.18), channel_id=1, source_target_pairs={{0,2},{1,3},{2,0},{3,1},{4,6},{5,7},{6,4},{7,5},{8,10},{9,11},{10,... | collective-permute-start | bytes 786440 | tf_op jit(solution)/shard_map/ppermute | solution.py:85
  20.3 23.0 %collective-permute-start.10 = (bf16[32,4096]{1,0:T(8,128)(2,1)S(1)}, bf16[32,4096]{1,0:T(8,128)(2,1)S(1)}, u32[]{:S(2)}, u32[]{:S(2)}) collective-permute-start(bf16[32,4096]{1,0:T(8,128)(2,1)S(1)} %maximum_select_fusion.19), channel_id=1, source_target_pairs={{0,4},{1,5},{2,6},{3,7},{4,0},{5,1},{6,2},{7,3},{8,12},{9,13},{10,... | collective-permute-start | bytes 786440 | tf_op jit(solution)/shard_map/ppermute | solution.py:85
  31.7 12.7 %collective-permute-start.2 = (bf16[64,4096]{1,0:T(8,128)(2,1)S(1)}, bf16[64,4096]{1,0:T(8,128)(2,1)S(1)}, u32[]{:S(2)}, u32[]{:S(2)}) collective-permute-start(bf16[64,4096]{1,0:T(8,128)(2,1)S(1)} %maximum_select_fusion.8), channel_id=1, source_target_pairs={{0,1},{1,0},{2,3},{3,2},{4,5},{5,4},{6,7},{7,6},{8,9},{9,8},{10,11... | collective-permute-start | bytes 1572872 | tf_op jit(solution)/shard_map/ppermute | solution.py:85
  34.0 18.6 %collective-permute-start.5 = (bf16[64,4096]{1,0:T(8,128)(2,1)S(1)}, bf16[64,4096]{1,0:T(8,128)(2,1)S(1)}, u32[]{:S(2)}, u32[]{:S(2)}) collective-permute-start(bf16[64,4096]{1,0:T(8,128)(2,1)S(1)} %maximum_select_fusion.9), channel_id=1, source_target_pairs={{0,2},{1,3},{2,0},{3,1},{4,6},{5,7},{6,4},{7,5},{8,10},{9,11},{10,... | collective-permute-start | bytes 1572872 | tf_op jit(solution)/shard_map/ppermute | solution.py:85
  41.5 11.4 %collective-permute-start.8 = (bf16[64,4096]{1,0:T(8,128)(2,1)S(1)}, bf16[64,4096]{1,0:T(8,128)(2,1)S(1)}, u32[]{:S(2)}, u32[]{:S(2)}) collective-permute-start(bf16[64,4096]{1,0:T(8,128)(2,1)S(1)} %maximum_select_fusion.10), channel_id=1, source_target_pairs={{0,1},{1,0},{2,3},{3,2},{4,5},{5,4},{6,7},{7,6},{8,9},{9,8},{10,11... | collective-permute-start | bytes 1572872 | tf_op jit(solution)/shard_map/ppermute | solution.py:85
  43.5 18.6 %collective-permute-start.11 = (bf16[64,4096]{1,0:T(8,128)(2,1)S(1)}, bf16[64,4096]{1,0:T(8,128)(2,1)S(1)}, u32[]{:S(2)}, u32[]{:S(2)}) collective-permute-start(bf16[64,4096]{1,0:T(8,128)(2,1)S(1)} %maximum_select_fusion.11), channel_id=1, source_target_pairs={{0,2},{1,3},{2,0},{3,1},{4,6},{5,7},{6,4},{7,5},{8,10},{9,11},{10,... | collective-permute-start | bytes 1572872 | tf_op jit(solution)/shard_map/ppermute | solution.py:85
  108.2 3.0 %copy-start = (bf16[512,3328]{1,0:T(8,128)(2,1)S(1)}, bf16[512,3328]{1,0:T(8,128)(2,1)}, u32[]{:S(2)}) copy-start(bf16[512,3328]{1,0:T(8,128)(2,1)} %get-tuple-element.8) | copy-start | bytes 10223620
  110.5 2.4 collective-permute-start.12
  111.4 1.8 collective-permute-start.14
  111.6 2.3 collective-permute-start.18
  112.1 2.3 collective-permute-start.20
  112.3 3.9 %collective-permute-start.24 = (bf16[64,3328]{1,0:T(8,128)(2,1)S(1)}, bf16[64,3328]{1,0:T(8,128)(2,1)S(1)}, u32[]{:S(2)}, u32[]{:S(2)}) collective-permute-start(bf16[64,3328]{1,0:T(8,128)(2,1)S(1)} %constant_dynamic-slice_fusion.7), channel_id=1, source_target_pairs={{0,8},{8,0},{16,24},{24,16},{1,9},{9,1},{17,25},{25,17},{2,10},{10... | collective-permute-start | bytes 1277960 | tf_op jit(solution)/shard_map/ppermute | solution.py:85
  112.9 3.9 %collective-permute-start.26 = (bf16[64,3328]{1,0:T(8,128)(2,1)S(1)}, bf16[64,3328]{1,0:T(8,128)(2,1)S(1)}, u32[]{:S(2)}, u32[]{:S(2)}) collective-permute-start(bf16[64,3328]{1,0:T(8,128)(2,1)S(1)} %constant_dynamic-slice_fusion.6), channel_id=1, source_target_pairs={{0,8},{8,0},{16,24},{24,16},{1,9},{9,1},{17,25},{25,17},{2,10},{10... | collective-permute-start | bytes 1277960 | tf_op jit(solution)/shard_map/ppermute | solution.py:85
  113.3 5.4 %collective-permute-start.30 = (bf16[64,3328]{1,0:T(8,128)(2,1)S(1)}, bf16[64,3328]{1,0:T(8,128)(2,1)S(1)}, u32[]{:S(2)}, u32[]{:S(2)}) collective-permute-start(bf16[64,3328]{1,0:T(8,128)(2,1)S(1)} %constant_dynamic-slice_fusion.5), channel_id=1, source_target_pairs={{0,8},{8,0},{16,24},{24,16},{1,9},{9,1},{17,25},{25,17},{2,10},{10... | collective-permute-start | bytes 1277960 | tf_op jit(solution)/shard_map/ppermute | solution.py:85
  113.9 5.4 %collective-permute-start.32 = (bf16[64,3328]{1,0:T(8,128)(2,1)S(1)}, bf16[64,3328]{1,0:T(8,128)(2,1)S(1)}, u32[]{:S(2)}, u32[]{:S(2)}) collective-permute-start(bf16[64,3328]{1,0:T(8,128)(2,1)S(1)} %constant_dynamic-slice_fusion.4), channel_id=1, source_target_pairs={{0,8},{8,0},{16,24},{24,16},{1,9},{9,1},{17,25},{25,17},{2,10},{10... | collective-permute-start | bytes 1277960 | tf_op jit(solution)/shard_map/ppermute | solution.py:85
  114.5 8.1 %collective-permute-start.13 = (bf16[32,3328]{1,0:T(8,128)(2,1)S(1)}, bf16[32,3328]{1,0:T(8,128)(2,1)S(1)}, u32[]{:S(2)}, u32[]{:S(2)}) collective-permute-start(bf16[32,3328]{1,0:T(8,128)(2,1)S(1)} %dynamic-slice_convert_fusion.11), channel_id=1, source_target_pairs={{0,16},{8,24},{16,0},{24,8},{1,17},{9,25},{17,1},{25,9},{2,18},{10... | collective-permute-start | bytes 638984 | tf_op jit(solution)/shard_map/ppermute | solution.py:85
  116.2 10.9 %collective-permute-start.15 = (bf16[32,3328]{1,0:T(8,128)(2,1)S(1)}, bf16[32,3328]{1,0:T(8,128)(2,1)S(1)}, u32[]{:S(2)}, u32[]{:S(2)}) collective-permute-start(bf16[32,3328]{1,0:T(8,128)(2,1)S(1)} %dynamic-slice_convert_fusion.10), channel_id=1, source_target_pairs={{0,16},{8,24},{16,0},{24,8},{1,17},{9,25},{17,1},{25,9},{2,18},{10... | collective-permute-start | bytes 638984 | tf_op jit(solution)/shard_map/ppermute | solution.py:85
  116.9 14.8 %collective-permute-start.19 = (bf16[32,3328]{1,0:T(8,128)(2,1)S(1)}, bf16[32,3328]{1,0:T(8,128)(2,1)S(1)}, u32[]{:S(2)}, u32[]{:S(2)}) collective-permute-start(bf16[32,3328]{1,0:T(8,128)(2,1)S(1)} %dynamic-slice_convert_fusion.9), channel_id=1, source_target_pairs={{0,16},{8,24},{16,0},{24,8},{1,17},{9,25},{17,1},{25,9},{2,18},{10... | collective-permute-start | bytes 638984 | tf_op jit(solution)/shard_map/ppermute | solution.py:85
  118.6 17.6 %collective-permute-start.21 = (bf16[32,3328]{1,0:T(8,128)(2,1)S(1)}, bf16[32,3328]{1,0:T(8,128)(2,1)S(1)}, u32[]{:S(2)}, u32[]{:S(2)}) collective-permute-start(bf16[32,3328]{1,0:T(8,128)(2,1)S(1)} %dynamic-slice_convert_fusion.8), channel_id=1, source_target_pairs={{0,16},{8,24},{16,0},{24,8},{1,17},{9,25},{17,1},{25,9},{2,18},{10... | collective-permute-start | bytes 638984 | tf_op jit(solution)/shard_map/ppermute | solution.py:85
  119.3 21.5 %collective-permute-start.25 = (bf16[32,3328]{1,0:T(8,128)(2,1)S(1)}, bf16[32,3328]{1,0:T(8,128)(2,1)S(1)}, u32[]{:S(2)}, u32[]{:S(2)}) collective-permute-start(bf16[32,3328]{1,0:T(8,128)(2,1)S(1)} %dynamic-slice_convert_fusion.7), channel_id=1, source_target_pairs={{0,16},{8,24},{16,0},{24,8},{1,17},{9,25},{17,1},{25,9},{2,18},{10... | collective-permute-start | bytes 638984 | tf_op jit(solution)/shard_map/ppermute | solution.py:85
  122.6 22.8 %collective-permute-start.27 = (bf16[32,3328]{1,0:T(8,128)(2,1)S(1)}, bf16[32,3328]{1,0:T(8,128)(2,1)S(1)}, u32[]{:S(2)}, u32[]{:S(2)}) collective-permute-start(bf16[32,3328]{1,0:T(8,128)(2,1)S(1)} %dynamic-slice_convert_fusion.6), channel_id=1, source_target_pairs={{0,16},{8,24},{16,0},{24,8},{1,17},{9,25},{17,1},{25,9},{2,18},{10... | collective-permute-start | bytes 638984 | tf_op jit(solution)/shard_map/ppermute | solution.py:85
  127.2 22.8 %collective-permute-start.31 = (bf16[32,3328]{1,0:T(8,128)(2,1)S(1)}, bf16[32,3328]{1,0:T(8,128)(2,1)S(1)}, u32[]{:S(2)}, u32[]{:S(2)}) collective-permute-start(bf16[32,3328]{1,0:T(8,128)(2,1)S(1)} %dynamic-slice_convert_fusion.5), channel_id=1, source_target_pairs={{0,16},{8,24},{16,0},{24,8},{1,17},{9,25},{17,1},{25,9},{2,18},{10... | collective-permute-start | bytes 638984 | tf_op jit(solution)/shard_map/ppermute | solution.py:85
  131.7 22.8 %collective-permute-start.33 = (bf16[32,3328]{1,0:T(8,128)(2,1)S(1)}, bf16[32,3328]{1,0:T(8,128)(2,1)S(1)}, u32[]{:S(2)}, u32[]{:S(2)}) collective-permute-start(bf16[32,3328]{1,0:T(8,128)(2,1)S(1)} %dynamic-slice_convert_fusion.4), channel_id=1, source_target_pairs={{0,16},{8,24},{16,0},{24,8},{1,17},{9,25},{17,1},{25,9},{2,18},{10... | collective-permute-start | bytes 638984 | tf_op jit(solution)/shard_map/ppermute | solution.py:85
  136.3 22.8 %collective-permute-start.16 = (bf16[32,3328]{1,0:T(8,128)(2,1)S(1)}, bf16[32,3328]{1,0:T(8,128)(2,1)S(1)}, u32[]{:S(2)}, u32[]{:S(2)}) collective-permute-start(bf16[32,3328]{1,0:T(8,128)(2,1)S(1)} %multiply_convert_fusion.3), channel_id=1, source_target_pairs={{0,16},{8,24},{16,0},{24,8},{1,17},{9,25},{17,1},{25,9},{2,18},{10... | collective-permute-start | bytes 638984 | tf_op jit(solution)/shard_map/ppermute | solution.py:85
  140.8 22.8 %collective-permute-start.22 = (bf16[32,3328]{1,0:T(8,128)(2,1)S(1)}, bf16[32,3328]{1,0:T(8,128)(2,1)S(1)}, u32[]{:S(2)}, u32[]{:S(2)}) collective-permute-start(bf16[32,3328]{1,0:T(8,128)(2,1)S(1)} %multiply_convert_fusion.2), channel_id=1, source_target_pairs={{0,16},{8,24},{16,0},{24,8},{1,17},{9,25},{17,1},{25,9},{2,18},{10... | collective-permute-start | bytes 638984 | tf_op jit(solution)/shard_map/ppermute | solution.py:85
  145.6 22.7 %collective-permute-start.28 = (bf16[32,3328]{1,0:T(8,128)(2,1)S(1)}, bf16[32,3328]{1,0:T(8,128)(2,1)S(1)}, u32[]{:S(2)}, u32[]{:S(2)}) collective-permute-start(bf16[32,3328]{1,0:T(8,128)(2,1)S(1)} %multiply_convert_fusion.1), channel_id=1, source_target_pairs={{0,16},{8,24},{16,0},{24,8},{1,17},{9,25},{17,1},{25,9},{2,18},{10... | collective-permute-start | bytes 638984 | tf_op jit(solution)/shard_map/ppermute | solution.py:85
  154.7 17.3 %collective-permute-start.34 = (bf16[32,3328]{1,0:T(8,128)(2,1)S(1)}, bf16[32,3328]{1,0:T(8,128)(2,1)S(1)}, u32[]{:S(2)}, u32[]{:S(2)}) collective-permute-start(bf16[32,3328]{1,0:T(8,128)(2,1)S(1)} %multiply_convert_fusion), channel_id=1, source_target_pairs={{0,16},{8,24},{16,0},{24,8},{1,17},{9,25},{17,1},{25,9},{2,18},{10... | collective-permute-start | bytes 638984 | tf_op jit(solution)/shard_map/ppermute | solution.py:85
  159.2 13.0 %collective-permute-start.17 = (bf16[64,3328]{1,0:T(8,128)(2,1)S(1)}, bf16[64,3328]{1,0:T(8,128)(2,1)S(1)}, u32[]{:S(2)}, u32[]{:S(2)}) collective-permute-start(bf16[64,3328]{1,0:T(8,128)(2,1)S(1)} %maximum_select_fusion.12), channel_id=1, source_target_pairs={{0,8},{8,0},{16,24},{24,16},{1,9},{9,1},{17,25},{25,17},{2,10},{10... | collective-permute-start | bytes 1277960 | tf_op jit(solution)/shard_map/ppermute | solution.py:85
  163.7 8.6 %collective-permute-start.23 = (bf16[64,3328]{1,0:T(8,128)(2,1)S(1)}, bf16[64,3328]{1,0:T(8,128)(2,1)S(1)}, u32[]{:S(2)}, u32[]{:S(2)}) collective-permute-start(bf16[64,3328]{1,0:T(8,128)(2,1)S(1)} %maximum_select_fusion.13), channel_id=1, source_target_pairs={{0,8},{8,0},{16,24},{24,16},{1,9},{9,1},{17,25},{25,17},{2,10},{10... | collective-permute-start | bytes 1277960 | tf_op jit(solution)/shard_map/ppermute | solution.py:85
  168.3 4.2 %collective-permute-start.29 = (bf16[64,3328]{1,0:T(8,128)(2,1)S(1)}, bf16[64,3328]{1,0:T(8,128)(2,1)S(1)}, u32[]{:S(2)}, u32[]{:S(2)}) collective-permute-start(bf16[64,3328]{1,0:T(8,128)(2,1)S(1)} %maximum_select_fusion.14), channel_id=1, source_target_pairs={{0,8},{8,0},{16,24},{24,16},{1,9},{9,1},{17,25},{25,17},{2,10},{10... | collective-permute-start | bytes 1277960 | tf_op jit(solution)/shard_map/ppermute | solution.py:85
  172.1 1.8 collective-permute-start.35
  204.3 14.8 %collective-permute-start.36 = (bf16[64,4096]{1,0:T(8,128)(2,1)S(1)}, bf16[64,4096]{1,0:T(8,128)(2,1)S(1)}, u32[]{:S(2)}, u32[]{:S(2)}) collective-permute-start(bf16[64,4096]{1,0:T(8,128)(2,1)S(1)} %constant_dynamic-slice_fusion.3), channel_id=1, source_target_pairs={{0,1},{1,0},{2,3},{3,2},{4,5},{5,4},{6,7},{7,6},{8,9},{9,8},{10,11... | collective-permute-start | bytes 1572872 | tf_op jit(solution)/shard_map/ppermute | solution.py:85
  206.0 14.9 %collective-permute-start.39 = (bf16[64,4096]{1,0:T(8,128)(2,1)S(1)}, bf16[64,4096]{1,0:T(8,128)(2,1)S(1)}, u32[]{:S(2)}, u32[]{:S(2)}) collective-permute-start(bf16[64,4096]{1,0:T(8,128)(2,1)S(1)} %constant_dynamic-slice_fusion.2), channel_id=1, source_target_pairs={{0,2},{1,3},{2,0},{3,1},{4,6},{5,7},{6,4},{7,5},{8,10},{9,11},{10,... | collective-permute-start | bytes 1572872 | tf_op jit(solution)/shard_map/ppermute | solution.py:85
  207.3 22.4 %collective-permute-start.42 = (bf16[64,4096]{1,0:T(8,128)(2,1)S(1)}, bf16[64,4096]{1,0:T(8,128)(2,1)S(1)}, u32[]{:S(2)}, u32[]{:S(2)}) collective-permute-start(bf16[64,4096]{1,0:T(8,128)(2,1)S(1)} %constant_dynamic-slice_fusion.1), channel_id=1, source_target_pairs={{0,1},{1,0},{2,3},{3,2},{4,5},{5,4},{6,7},{7,6},{8,9},{9,8},{10,11... | collective-permute-start | bytes 1572872 | tf_op jit(solution)/shard_map/ppermute | solution.py:85
  208.0 29.7 %collective-permute-start.45 = (bf16[64,4096]{1,0:T(8,128)(2,1)S(1)}, bf16[64,4096]{1,0:T(8,128)(2,1)S(1)}, u32[]{:S(2)}, u32[]{:S(2)}) collective-permute-start(bf16[64,4096]{1,0:T(8,128)(2,1)S(1)} %constant_dynamic-slice_fusion), channel_id=1, source_target_pairs={{0,2},{1,3},{2,0},{3,1},{4,6},{5,7},{6,4},{7,5},{8,10},{9,11},{10,... | collective-permute-start | bytes 1572872 | tf_op jit(solution)/shard_map/ppermute | solution.py:85
  219.3 24.8 %collective-permute-start.37 = (bf16[32,4096]{1,0:T(8,128)(2,1)S(1)}, bf16[32,4096]{1,0:T(8,128)(2,1)S(1)}, u32[]{:S(2)}, u32[]{:S(2)}) collective-permute-start(bf16[32,4096]{1,0:T(8,128)(2,1)S(1)} %dynamic-slice_convert_fusion.3), channel_id=1, source_target_pairs={{0,2},{1,3},{2,0},{3,1},{4,6},{5,7},{6,4},{7,5},{8,10},{9,11},{10,... | collective-permute-start | bytes 786440 | tf_op jit(solution)/shard_map/ppermute | solution.py:85
  221.0 29.6 %collective-permute-start.40 = (bf16[32,4096]{1,0:T(8,128)(2,1)S(1)}, bf16[32,4096]{1,0:T(8,128)(2,1)S(1)}, u32[]{:S(2)}, u32[]{:S(2)}) collective-permute-start(bf16[32,4096]{1,0:T(8,128)(2,1)S(1)} %dynamic-slice_convert_fusion.2), channel_id=1, source_target_pairs={{0,4},{1,5},{2,6},{3,7},{4,0},{5,1},{6,2},{7,3},{8,12},{9,13},{10,... | collective-permute-start | bytes 786440 | tf_op jit(solution)/shard_map/ppermute | solution.py:85
  229.9 23.7 %collective-permute-start.43 = (bf16[32,4096]{1,0:T(8,128)(2,1)S(1)}, bf16[32,4096]{1,0:T(8,128)(2,1)S(1)}, u32[]{:S(2)}, u32[]{:S(2)}) collective-permute-start(bf16[32,4096]{1,0:T(8,128)(2,1)S(1)} %dynamic-slice_convert_fusion.1), channel_id=1, source_target_pairs={{0,2},{1,3},{2,0},{3,1},{4,6},{5,7},{6,4},{7,5},{8,10},{9,11},{10,... | collective-permute-start | bytes 786440 | tf_op jit(solution)/shard_map/ppermute | solution.py:85
  237.8 17.3 %collective-permute-start.46 = (bf16[32,4096]{1,0:T(8,128)(2,1)S(1)}, bf16[32,4096]{1,0:T(8,128)(2,1)S(1)}, u32[]{:S(2)}, u32[]{:S(2)}) collective-permute-start(bf16[32,4096]{1,0:T(8,128)(2,1)S(1)} %dynamic-slice_convert_fusion), channel_id=1, source_target_pairs={{0,4},{1,5},{2,6},{3,7},{4,0},{5,1},{6,2},{7,3},{8,12},{9,13},{10,... | collective-permute-start | bytes 786440 | tf_op jit(solution)/shard_map/ppermute | solution.py:85
  244.2 19.6 %collective-permute-start.38 = (bf16[16,4096]{1,0:T(8,128)(2,1)S(1)}, bf16[16,4096]{1,0:T(8,128)(2,1)S(1)}, u32[]{:S(2)}, u32[]{:S(2)}) collective-permute-start(bf16[16,4096]{1,0:T(8,128)(2,1)S(1)} %dynamic-slice_convert_fusion.15), channel_id=1, source_target_pairs={{0,4},{1,5},{2,6},{3,7},{4,0},{5,1},{6,2},{7,3},{8,12},{9,13},{10,... | collective-permute-start | bytes 393224 | tf_op jit(solution)/shard_map/ppermute | solution.py:85
  250.6 15.7 %collective-permute-start.41 = (bf16[16,4096]{1,0:T(8,128)(2,1)S(1)}, bf16[16,4096]{1,0:T(8,128)(2,1)S(1)}, u32[]{:S(2)}, u32[]{:S(2)}) collective-permute-start(bf16[16,4096]{1,0:T(8,128)(2,1)S(1)} %dynamic-slice_convert_fusion.14), channel_id=1, source_target_pairs={{0,1},{1,0},{2,3},{3,2},{4,5},{5,4},{6,7},{7,6},{8,9},{9,8},{10,11... | collective-permute-start | bytes 393224 | tf_op jit(solution)/shard_map/ppermute | solution.py:85
  253.7 12.6 %collective-permute-start.44 = (bf16[16,4096]{1,0:T(8,128)(2,1)S(1)}, bf16[16,4096]{1,0:T(8,128)(2,1)S(1)}, u32[]{:S(2)}, u32[]{:S(2)}) collective-permute-start(bf16[16,4096]{1,0:T(8,128)(2,1)S(1)} %dynamic-slice_convert_fusion.13), channel_id=1, source_target_pairs={{0,4},{1,5},{2,6},{3,7},{4,0},{5,1},{6,2},{7,3},{8,12},{9,13},{10,... | collective-permute-start | bytes 393224 | tf_op jit(solution)/shard_map/ppermute | solution.py:85
  255.3 11.1 %collective-permute-start.47 = (bf16[16,4096]{1,0:T(8,128)(2,1)S(1)}, bf16[16,4096]{1,0:T(8,128)(2,1)S(1)}, u32[]{:S(2)}, u32[]{:S(2)}) collective-permute-start(bf16[16,4096]{1,0:T(8,128)(2,1)S(1)} %dynamic-slice_convert_fusion.12), channel_id=1, source_target_pairs={{0,1},{1,0},{2,3},{3,2},{4,5},{5,4},{6,7},{7,6},{8,9},{9,8},{10,11... | collective-permute-start | bytes 393224 | tf_op jit(solution)/shard_map/ppermute | solution.py:85

commit v8 on v2

--- a/solution.py
+++ b/solution.py
@@ -123,30 +123,29 @@
     row_bits = list(range(n_row.bit_length() - 1))
     top = n_col.bit_length() - 1
     col_orders = [list(range(top - 1, -1, -1)), [0] + list(range(top - 1, 0, -1))]
-    t_half = tokens.shape[0] // 2
-    token_parts = [tokens[:t_half], tokens[t_half:]]
-    segment = jnp.concatenate(
-        doubling_gather(list(zip(token_parts, col_orders)), "col", n_col), axis=0)
+    quarter = tokens.shape[0] // 4
+    orders = col_orders * 2
+    token_parts = [tokens[q * quarter:(q + 1) * quarter] for q in range(4)]
+    segment = jnp.concatenate(doubling_gather(list(zip(token_parts, orders)), "col", n_col), axis=0)
     n_in, n_hid = gate_keep.shape
+    gate_rows, up_rows = sparse_matmul(segment, [gate_packed, up_packed], gate_keep, 0, n_in, 0, n_hid)
+    half = gate_rows.shape[0] // 2
+    sums = halving_scatter(
+        [([gate_rows[:half], up_rows[:half]], row_bits), ([gate_rows[half:], up_rows[half:]], row_bits)],
+        "row", n_row)
+    hidden_shares = [(jax.nn.silu(g) * u).astype(jnp.bfloat16) for g, u in sums]
+    every_hidden = jnp.concatenate(
+        doubling_gather([(h, row_bits[::-1]) for h in hidden_shares], "row", n_row), axis=0)
     n_out = down_keep.shape[1]
-    split = (n_hid // 2) // 4 * 4 or n_hid // 2
-    spans = [(0, split), (split, n_hid)]
-    hidden = []
-    for h0, h1 in spans:
-        gate_rows, up_rows = sparse_matmul(segment, [gate_packed, up_packed], gate_keep, 0, n_in, h0, h1)
-        ((gate_sum, up_sum),) = halving_scatter([([gate_rows, up_rows], row_bits)], "row", n_row)
-        hidden_share = (jax.nn.silu(gate_sum) * up_sum).astype(jnp.bfloat16)
-        hidden += doubling_gather([(hidden_share, row_bits[::-1])], "row", n_row)
-    (first_out,) = sparse_matmul(
-        hidden[0], [down_packed], down_keep, 0, split, 0, n_out, out_dtype=jnp.float32)
-    (partial_out,) = sparse_matmul(
-        hidden[1], [down_packed], down_keep, split, n_hid, 0, n_out, init=first_out)
-    half_rows = partial_out.shape[0] // 2
-    out_parts = halving_scatter(
-        [([partial_out[:half_rows]], col_orders[0][::-1]), ([partial_out[half_rows:]], col_orders[1][::-1])],
-        "col", n_col)
-    summed = jnp.concatenate([parts[0] for parts in out_parts], axis=0)
-    return summed.astype(jnp.bfloat16)
+    out_half = n_out // 2
+    pieces = []
+    for o0, o1 in ((0, out_half), (out_half, n_out)):
+        (partial_out,) = sparse_matmul(every_hidden, [down_packed], down_keep, 0, n_hid, o0, o1)
+        rows_q = partial_out.shape[0] // 4
+        out_parts = halving_scatter(
+            [([partial_out[q * rows_q:(q + 1) * rows_q]], orders[q][::-1]) for q in range(4)], "col", n_col)
+        pieces.append(jnp.concatenate([parts[0] for parts in out_parts], axis=0))
+    return jnp.concatenate(pieces, axis=1).astype(jnp.bfloat16)
 
 
 def solution(mesh):

time: 306 us -> 274 us (0.90)
  waiting for transfers between devices: 165 us -> 108 us
  starting transfers between devices: 25.1 us -> 57.9 us
  Pallas kernels: 83.9 us -> 78.8 us
    ppermute x24 -> x48, waiting for transfers between devices: 165 us -> 108 us  [exchange(): return lax.ppermute(x, axis, perm=pairs)]
    ppermute x24 -> x48, starting transfers between devices: 25.1 us -> 57.9 us  [exchange(): return lax.ppermute(x, axis, perm=pairs)]
    select_n x10 -> x16, other arithmetic: 8.72 us -> 2.3 us  [doubling_gather(): jnp.where(low, jnp.concatenate([xs[p], got], 0), jnp.concatenate([got, xs...]
    pallas_call x4 -> x3, Pallas kernels: 83.9 us -> 78.8 us  [sparse_matmul(): pl.pallas_call(kernel, grid_spec=pltpu.PrefetchScalarGridSpec(num_scalar_...]
    dynamic_slice x6 -> x12, local copies, waits for them, and re-layouts: 3.81 us -> 0.43 us  [halving_scatter(): lax.dynamic_slice_in_dim(p, (1 - mine) * half, half, axis=0)]
    slice x3 -> x6, local copies, waits for them, and re-layouts: 3.74 us -> 7.06 us  [the longest x2 3.3 us: local(): partial_out[q * rows_q:(q + 1) * rows_q]]
  transfers between devices with their start and end apart: 24 -> 48, of which waited for: 18 -> 22; matrix products, arithmetic and copies ran while one was open for 6% -> 6% of each run, Pallas kernels for 14% -> 6%
where the time goes in v8:
time: 274 us; the launch traced here: 273 us
  waiting for transfers between devices  108 us (39%)
  Pallas kernels  78.8 us (29%)
  starting transfers between devices  57.9 us (21%)
  other arithmetic  15.1 us (6%)
  local copies, waits for them, and re-layouts  12.8 us (5%)
    ppermute x48, waiting for transfers between devices, exchange(): return lax.ppermute(x, axis, perm=pairs)  108 us
    pallas_call x3, Pallas kernels, sparse_matmul(): pl.pallas_call(kernel, grid_spec=pltpu.PrefetchScalarGridSpec(num_scalar_...  78.8 us
    ppermute x48, starting transfers between devices, exchange(): return lax.ppermute(x, axis, perm=pairs)  57.9 us
  transfers between devices with their start and end apart: 48, of which 22 were waited for; matrix products, arithmetic and copies ran while one was open for 6% of the time, Pallas kernels for 6%

profile of v8, /device:TPU:0, one launch (start us, length us, event | category | flops | bytes accessed | tf_op | source)
XLA Modules:
  0.0 273.0 jit_solution(3257484158099486405)
XLA Ops:
  0.0 1.1 fusion.10
  1.1 4.1 %collective-permute-start = (bf16[16,4096]{1,0:T(8,128)(2,1)S(1)}, bf16[16,4096]{1,0:T(8,128)(2,1)S(1)}, u32[]{:S(2)}, u32[]{:S(2)}) collective-permute-start(bf16[16,4096]{1,0:T(8,128)(2,1)S(1)} %get-tuple-element.23), channel_id=1, source_target_pairs={{0,4},{1,5},{2,6},{3,7},{4,0},{5,1},{6,2},{7,3},{8,12},{9,13},{10,... | collective-permute-start | bytes 393224 | tf_op jit(solution)/shard_map/ppermute | solution.py:90
  5.2 1.5 collective-permute-start.3
  7.3 0.8 reshape.65
  8.1 0.8 reshape.71
  9.6 0.7 sub.31
  10.5 0.8 subtract_select_fusion
  12.7 2.5 collective-permute-done
  15.4 3.4 %collective-permute-start.4 = (bf16[32,4096]{1,0:T(8,128)(2,1)S(1)}, bf16[32,4096]{1,0:T(8,128)(2,1)S(1)}, u32[]{:S(2)}, u32[]{:S(2)}) collective-permute-start(bf16[32,4096]{1,0:T(8,128)(2,1)S(1)} %maximum_select_fusion.13), channel_id=1, source_target_pairs={{0,4},{1,5},{2,6},{3,7},{4,0},{5,1},{6,2},{7,3},{8,12},{9,13},{10,... | collective-permute-start | bytes 786440 | tf_op jit(solution)/shard_map/ppermute | solution.py:90
  19.0 2.5 collective-permute-start.10
  21.5 8.6 %collective-permute-done.1 = bf16[32,4096]{1,0:T(8,128)(2,1)S(1)} collective-permute-done((bf16[32,4096]{1,0:T(8,128)(2,1)S(1)}, bf16[32,4096]{1,0:T(8,128)(2,1)S(1)}, u32[]{:S(2)}, u32[]{:S(2)}) %collective-permute-start.1) | collective-permute-done | bytes 262176 | tf_op jit(solution)/shard_map/ppermute | solution.py:90
  30.2 2.2 collective-permute-start.2
  32.6 8.7 %collective-permute-done.7 = bf16[32,4096]{1,0:T(8,128)(2,1)S(1)} collective-permute-done((bf16[32,4096]{1,0:T(8,128)(2,1)S(1)}, bf16[32,4096]{1,0:T(8,128)(2,1)S(1)}, u32[]{:S(2)}, u32[]{:S(2)}) %collective-permute-start.7) | collective-permute-done | bytes 262176 | tf_op jit(solution)/shard_map/ppermute | solution.py:90
  41.4 2.0 collective-permute-start.8
  43.8 8.8 %collective-permute-done.5 = bf16[64,4096]{1,0:T(8,128)(2,1)S(1)} collective-permute-done((bf16[64,4096]{1,0:T(8,128)(2,1)S(1)}, bf16[64,4096]{1,0:T(8,128)(2,1)S(1)}, u32[]{:S(2)}, u32[]{:S(2)}) %collective-permute-start.5) | collective-permute-done | bytes 524320 | tf_op jit(solution)/shard_map/ppermute | solution.py:90
  53.1 9.0 %collective-permute-done.11 = bf16[64,4096]{1,0:T(8,128)(2,1)S(1)} collective-permute-done((bf16[64,4096]{1,0:T(8,128)(2,1)S(1)}, bf16[64,4096]{1,0:T(8,128)(2,1)S(1)}, u32[]{:S(2)}, u32[]{:S(2)}) %collective-permute-start.11) | collective-permute-done | bytes 524320 | tf_op jit(solution)/shard_map/ppermute | solution.py:90
  62.3 2.5 pad_maximum_fusion.x_ref
  64.8 43.4 %shard_map.64 = (bf16[512,3328]{1,0:T(8,128)(2,1)}, bf16[512,3328]{1,0:T(8,128)(2,1)}) custom-call(s32[32]{0:T(128)} %copy-done.4, s32[832]{0:T(1024)} %reshape.75.index_ref, bf16[512,4096]{1,0:T(8,128)(2,1)} %pad_maximum_fusion.x_ref, bf16[640,128,128]{2,1,0:T(8,128)(2,1)} %refs_3_.1, bf16[640,128,128]{2,1,0:T(8,128)(2,1)} %refs_3_.1, ...), custom_call_target="tpu_custom_call" | custom-call | flops 27917287424 | bytes 72351744 | tf_op jit(solution)/shard_map/pallas_call | solution.py:70
  108.2 2.3 fusion.6
  113.3 1.6 collective-permute-start.13
  115.2 1.0 collective-permute-start.15
  116.4 1.2 collective-permute-start.19
  117.8 1.0 collective-permute-start.21
  118.8 7.2 %collective-permute-done.13 = bf16[64,3328]{1,0:T(8,128)(2,1)S(1)} collective-permute-done((bf16[64,3328]{1,0:T(8,128)(2,1)S(1)}, bf16[64,3328]{1,0:T(8,128)(2,1)S(1)}, u32[]{:S(2)}, u32[]{:S(2)}) %collective-permute-start.13) | collective-permute-done | bytes 426016 | tf_op jit(solution)/shard_map/ppermute | solution.py:90
  126.0 9.1 %collective-permute-done.15 = bf16[64,3328]{1,0:T(8,128)(2,1)S(1)} collective-permute-done((bf16[64,3328]{1,0:T(8,128)(2,1)S(1)}, bf16[64,3328]{1,0:T(8,128)(2,1)S(1)}, u32[]{:S(2)}, u32[]{:S(2)}) %collective-permute-start.15) | collective-permute-done | bytes 426016 | tf_op jit(solution)/shard_map/ppermute | solution.py:90
  135.4 1.6 collective-permute-start.16
  137.1 7.2 %collective-permute-done.19 = bf16[64,3328]{1,0:T(8,128)(2,1)S(1)} collective-permute-done((bf16[64,3328]{1,0:T(8,128)(2,1)S(1)}, bf16[64,3328]{1,0:T(8,128)(2,1)S(1)}, u32[]{:S(2)}, u32[]{:S(2)}) %collective-permute-start.19) | collective-permute-done | bytes 426016 | tf_op jit(solution)/shard_map/ppermute | solution.py:90
  144.3 9.1 %collective-permute-done.21 = bf16[64,3328]{1,0:T(8,128)(2,1)S(1)} collective-permute-done((bf16[64,3328]{1,0:T(8,128)(2,1)S(1)}, bf16[64,3328]{1,0:T(8,128)(2,1)S(1)}, u32[]{:S(2)}, u32[]{:S(2)}) %collective-permute-start.21) | collective-permute-done | bytes 426016 | tf_op jit(solution)/shard_map/ppermute | solution.py:90
  153.7 1.6 collective-permute-start.22
  155.3 7.2 %collective-permute-done.16 = bf16[64,3328]{1,0:T(8,128)(2,1)S(1)} collective-permute-done((bf16[64,3328]{1,0:T(8,128)(2,1)S(1)}, bf16[64,3328]{1,0:T(8,128)(2,1)S(1)}, u32[]{:S(2)}, u32[]{:S(2)}) %collective-permute-start.16) | collective-permute-done | bytes 426016 | tf_op jit(solution)/shard_map/ppermute | solution.py:90
  162.7 8.1 %collective-permute-done.22 = bf16[64,3328]{1,0:T(8,128)(2,1)S(1)} collective-permute-done((bf16[64,3328]{1,0:T(8,128)(2,1)S(1)}, bf16[64,3328]{1,0:T(8,128)(2,1)S(1)}, u32[]{:S(2)}, u32[]{:S(2)}) %collective-permute-start.22) | collective-permute-done | bytes 426016 | tf_op jit(solution)/shard_map/ppermute | solution.py:90
  173.8 1.9 pad_maximum_fusion.1.x_ref
  175.7 17.7 %shard_map.65 = bf16[512,2048]{1,0:T(8,128)(2,1)} custom-call(s32[26]{0:T(128)} %copy-done.3, s32[416]{0:T(512)} %reshape.70.index_ref, bf16[512,3328]{1,0:T(8,128)(2,1)} %pad_maximum_fusion.1.x_ref, bf16[640,128,128]{2,1,0:T(8,128)(2,1)} %refs_1_.5, bf16[640,128,128]{2,1,0:T(8,128)(2,1)} %refs_1_.5), custom_call_target="tpu_custom_call" | custom-call | flops 6979321856 | bytes 21233664 | tf_op jit(solution)/shard_map/pallas_call | solution.py:70
  193.4 1.7 fusion.8
  195.1 1.6 collective-permute-start.24
  198.1 1.4 collective-permute-start.33
  199.5 17.7 %shard_map.66 = bf16[512,2048]{1,0:T(8,128)(2,1)} custom-call(s32[26]{0:T(128)} %copy-done.2, s32[416]{0:T(512)} %reshape.76.index_ref, bf16[512,3328]{1,0:T(8,128)(2,1)} %pad_maximum_fusion.1.x_ref, bf16[640,128,128]{2,1,0:T(8,128)(2,1)} %refs_1_.5, bf16[640,128,128]{2,1,0:T(8,128)(2,1)} %refs_1_.5), custom_call_target="tpu_custom_call" | custom-call | flops 6979321856 | bytes 21233664 | tf_op jit(solution)/shard_map/pallas_call | solution.py:70
  217.2 1.7 fusion.9
  218.9 1.6 collective-permute-start.36
  220.6 0.7 collective-permute-start.39
  221.3 1.0 convert_add_fusion.11
  222.9 1.0 convert_add_fusion.9
  223.9 1.4 collective-permute-start.45
  225.3 1.0 convert_add_fusion.10
  226.4 0.8 collective-permute-start.25
  227.2 0.9 collective-permute-done.36
  228.2 3.1 %collective-permute-start.28 = (bf16[32,2048]{1,0:T(8,128)(2,1)S(1)}, bf16[32,2048]{1,0:T(8,128)(2,1)S(1)}, u32[]{:S(2)}, u32[]{:S(2)}) collective-permute-start(bf16[32,2048]{1,0:T(8,128)(2,1)S(1)} %dynamic-slice_convert_fusion.10), channel_id=1, source_target_pairs={{0,4},{1,5},{2,6},{3,7},{4,0},{5,1},{6,2},{7,3},{8,12},{9,13},{10,... | collective-permute-start | bytes 393224 | tf_op jit(solution)/shard_map/ppermute | solution.py:90
  231.4 1.6 collective-permute-start.31
  233.2 2.4 collective-permute-start.34
  235.7 5.5 %collective-permute-done.45 = bf16[64,2048]{1,0:T(8,128)(2,1)S(1)} collective-permute-done((bf16[64,2048]{1,0:T(8,128)(2,1)S(1)}, bf16[64,2048]{1,0:T(8,128)(2,1)S(1)}, u32[]{:S(2)}, u32[]{:S(2)}) %collective-permute-start.45) | collective-permute-done | bytes 262176 | tf_op jit(solution)/shard_map/ppermute | solution.py:90
  241.2 4.1 %collective-permute-done.25 = bf16[32,2048]{1,0:T(8,128)(2,1)S(1)} collective-permute-done((bf16[32,2048]{1,0:T(8,128)(2,1)S(1)}, bf16[32,2048]{1,0:T(8,128)(2,1)S(1)}, u32[]{:S(2)}, u32[]{:S(2)}) %collective-permute-start.25) | collective-permute-done | bytes 131104 | tf_op jit(solution)/shard_map/ppermute | solution.py:90
  245.3 1.6 collective-permute-start.40
  246.9 1.3 collective-permute-done.31
  248.3 1.2 collective-permute-start.43
  249.6 4.9 %collective-permute-start.46 = (bf16[32,2048]{1,0:T(8,128)(2,1)S(1)}, bf16[32,2048]{1,0:T(8,128)(2,1)S(1)}, u32[]{:S(2)}, u32[]{:S(2)}) collective-permute-start(bf16[32,2048]{1,0:T(8,128)(2,1)S(1)} %dynamic-slice_convert_fusion.4), channel_id=1, source_target_pairs={{0,4},{1,5},{2,6},{3,7},{4,0},{5,1},{6,2},{7,3},{8,12},{9,13},{10,... | collective-permute-start | bytes 393224 | tf_op jit(solution)/shard_map/ppermute | solution.py:90
  255.4 1.7 collective-permute-done.40
  257.1 1.3 collective-permute-start.32
  258.4 1.5 collective-permute-start.35
  260.0 3.8 %collective-permute-done.46 = bf16[32,2048]{1,0:T(8,128)(2,1)S(1)} collective-permute-done((bf16[32,2048]{1,0:T(8,128)(2,1)S(1)}, bf16[32,2048]{1,0:T(8,128)(2,1)S(1)}, u32[]{:S(2)}, u32[]{:S(2)}) %collective-permute-start.46) | collective-permute-done | bytes 131104 | tf_op jit(solution)/shard_map/ppermute | solution.py:90
  264.5 1.3 collective-permute-start.41
  265.9 1.9 collective-permute-start.44
  267.8 1.3 collective-permute-start.47
  269.2 2.5 collective-permute-done.44
  272.1 0.8 maximum_maximum_fusion
  (156 shorter events, 16.4 us)
Async XLA Ops:
  1.1 14.0 %collective-permute-start = (bf16[16,4096]{1,0:T(8,128)(2,1)S(1)}, bf16[16,4096]{1,0:T(8,128)(2,1)S(1)}, u32[]{:S(2)}, u32[]{:S(2)}) collective-permute-start(bf16[16,4096]{1,0:T(8,128)(2,1)S(1)} %get-tuple-element.23), channel_id=1, source_target_pairs={{0,4},{1,5},{2,6},{3,7},{4,0},{5,1},{6,2},{7,3},{8,12},{9,13},{10,... | collective-permute-start | bytes 393224 | tf_op jit(solution)/shard_map/ppermute | solution.py:90
  5.2 10.1 %collective-permute-start.3 = (bf16[16,4096]{1,0:T(8,128)(2,1)S(1)}, bf16[16,4096]{1,0:T(8,128)(2,1)S(1)}, u32[]{:S(2)}, u32[]{:S(2)}) collective-permute-start(bf16[16,4096]{1,0:T(8,128)(2,1)S(1)} %get-tuple-element.24), channel_id=1, source_target_pairs={{0,1},{1,0},{2,3},{3,2},{4,5},{5,4},{6,7},{7,6},{8,9},{9,8},{10,11... | collective-permute-start | bytes 393224 | tf_op jit(solution)/shard_map/ppermute | solution.py:90
  6.7 12.1 %collective-permute-start.6 = (bf16[16,4096]{1,0:T(8,128)(2,1)S(1)}, bf16[16,4096]{1,0:T(8,128)(2,1)S(1)}, u32[]{:S(2)}, u32[]{:S(2)}) collective-permute-start(bf16[16,4096]{1,0:T(8,128)(2,1)S(1)} %get-tuple-element.26), channel_id=1, source_target_pairs={{0,4},{1,5},{2,6},{3,7},{4,0},{5,1},{6,2},{7,3},{8,12},{9,13},{10,... | collective-permute-start | bytes 393224 | tf_op jit(solution)/shard_map/ppermute | solution.py:90
  7.1 11.9 %collective-permute-start.9 = (bf16[16,4096]{1,0:T(8,128)(2,1)S(1)}, bf16[16,4096]{1,0:T(8,128)(2,1)S(1)}, u32[]{:S(2)}, u32[]{:S(2)}) collective-permute-start(bf16[16,4096]{1,0:T(8,128)(2,1)S(1)} %get-tuple-element.25), channel_id=1, source_target_pairs={{0,1},{1,0},{2,3},{3,2},{4,5},{5,4},{6,7},{7,6},{8,9},{9,8},{10,11... | collective-permute-start | bytes 393224 | tf_op jit(solution)/shard_map/ppermute | solution.py:90
  10.5 22.0 %copy-start.4 = (s32[32]{0:T(128)}, s32[32]{0:T(128)S(1)}, u32[]{:S(2)}) copy-start(s32[32]{0:T(128)S(1)} %fusion.2.base_ref) | copy-start | bytes 388
  15.2 14.9 %collective-permute-start.1 = (bf16[32,4096]{1,0:T(8,128)(2,1)S(1)}, bf16[32,4096]{1,0:T(8,128)(2,1)S(1)}, u32[]{:S(2)}, u32[]{:S(2)}) collective-permute-start(bf16[32,4096]{1,0:T(8,128)(2,1)S(1)} %maximum_select_fusion.12), channel_id=1, source_target_pairs={{0,2},{1,3},{2,0},{3,1},{4,6},{5,7},{6,4},{7,5},{8,10},{9,11},{10,... | collective-permute-start | bytes 786440 | tf_op jit(solution)/shard_map/ppermute | solution.py:90
  15.4 17.1 %collective-permute-start.4 = (bf16[32,4096]{1,0:T(8,128)(2,1)S(1)}, bf16[32,4096]{1,0:T(8,128)(2,1)S(1)}, u32[]{:S(2)}, u32[]{:S(2)}) collective-permute-start(bf16[32,4096]{1,0:T(8,128)(2,1)S(1)} %maximum_select_fusion.13), channel_id=1, source_target_pairs={{0,4},{1,5},{2,6},{3,7},{4,0},{5,1},{6,2},{7,3},{8,12},{9,13},{10,... | collective-permute-start | bytes 786440 | tf_op jit(solution)/shard_map/ppermute | solution.py:90
  18.8 22.4 %collective-permute-start.7 = (bf16[32,4096]{1,0:T(8,128)(2,1)S(1)}, bf16[32,4096]{1,0:T(8,128)(2,1)S(1)}, u32[]{:S(2)}, u32[]{:S(2)}) collective-permute-start(bf16[32,4096]{1,0:T(8,128)(2,1)S(1)} %maximum_select_fusion.14), channel_id=1, source_target_pairs={{0,2},{1,3},{2,0},{3,1},{4,6},{5,7},{6,4},{7,5},{8,10},{9,11},{10,... | collective-permute-start | bytes 786440 | tf_op jit(solution)/shard_map/ppermute | solution.py:90
  19.0 24.4 %collective-permute-start.10 = (bf16[32,4096]{1,0:T(8,128)(2,1)S(1)}, bf16[32,4096]{1,0:T(8,128)(2,1)S(1)}, u32[]{:S(2)}, u32[]{:S(2)}) collective-permute-start(bf16[32,4096]{1,0:T(8,128)(2,1)S(1)} %maximum_select_fusion.15), channel_id=1, source_target_pairs={{0,4},{1,5},{2,6},{3,7},{4,0},{5,1},{6,2},{7,3},{8,12},{9,13},{10,... | collective-permute-start | bytes 786440 | tf_op jit(solution)/shard_map/ppermute | solution.py:90
  30.2 13.4 %collective-permute-start.2 = (bf16[64,4096]{1,0:T(8,128)(2,1)S(1)}, bf16[64,4096]{1,0:T(8,128)(2,1)S(1)}, u32[]{:S(2)}, u32[]{:S(2)}) collective-permute-start(bf16[64,4096]{1,0:T(8,128)(2,1)S(1)} %maximum_select_fusion.8), channel_id=1, source_target_pairs={{0,1},{1,0},{2,3},{3,2},{4,5},{5,4},{6,7},{7,6},{8,9},{9,8},{10,11... | collective-permute-start | bytes 1572872 | tf_op jit(solution)/shard_map/ppermute | solution.py:90
  32.5 20.1 %collective-permute-start.5 = (bf16[64,4096]{1,0:T(8,128)(2,1)S(1)}, bf16[64,4096]{1,0:T(8,128)(2,1)S(1)}, u32[]{:S(2)}, u32[]{:S(2)}) collective-permute-start(bf16[64,4096]{1,0:T(8,128)(2,1)S(1)} %maximum_select_fusion.9), channel_id=1, source_target_pairs={{0,2},{1,3},{2,0},{3,1},{4,6},{5,7},{6,4},{7,5},{8,10},{9,11},{10,... | collective-permute-start | bytes 1572872 | tf_op jit(solution)/shard_map/ppermute | solution.py:90
  41.4 11.5 %collective-permute-start.8 = (bf16[64,4096]{1,0:T(8,128)(2,1)S(1)}, bf16[64,4096]{1,0:T(8,128)(2,1)S(1)}, u32[]{:S(2)}, u32[]{:S(2)}) collective-permute-start(bf16[64,4096]{1,0:T(8,128)(2,1)S(1)} %maximum_select_fusion.10), channel_id=1, source_target_pairs={{0,1},{1,0},{2,3},{3,2},{4,5},{5,4},{6,7},{7,6},{8,9},{9,8},{10,11... | collective-permute-start | bytes 1572872 | tf_op jit(solution)/shard_map/ppermute | solution.py:90
  43.5 18.6 %collective-permute-start.11 = (bf16[64,4096]{1,0:T(8,128)(2,1)S(1)}, bf16[64,4096]{1,0:T(8,128)(2,1)S(1)}, u32[]{:S(2)}, u32[]{:S(2)}) collective-permute-start(bf16[64,4096]{1,0:T(8,128)(2,1)S(1)} %maximum_select_fusion.11), channel_id=1, source_target_pairs={{0,2},{1,3},{2,0},{3,1},{4,6},{5,7},{6,4},{7,5},{8,10},{9,11},{10,... | collective-permute-start | bytes 1572872 | tf_op jit(solution)/shard_map/ppermute | solution.py:90
  108.2 3.0 %copy-start = (bf16[512,3328]{1,0:T(8,128)(2,1)S(1)}, bf16[512,3328]{1,0:T(8,128)(2,1)}, u32[]{:S(2)}) copy-start(bf16[512,3328]{1,0:T(8,128)(2,1)} %get-tuple-element.8) | copy-start | bytes 10223620
  110.6 2.4 collective-permute-start.12
  111.5 3.4 %collective-permute-start.14 = (bf16[128,3328]{1,0:T(8,128)(2,1)S(1)}, bf16[128,3328]{1,0:T(8,128)(2,1)S(1)}, u32[]{:S(2)}, u32[]{:S(2)}) collective-permute-start(bf16[128,3328]{1,0:T(8,128)(2,1)S(1)} %constant_dynamic-slice_fusion.10), channel_id=1, source_target_pairs={{0,8},{8,0},{16,24},{24,16},{1,9},{9,1},{17,25},{25,17},{2,10},{10... | collective-permute-start | bytes 2555912 | tf_op jit(solution)/shard_map/ppermute | solution.py:90
  111.6 4.5 %collective-permute-start.18 = (bf16[128,3328]{1,0:T(8,128)(2,1)S(1)}, bf16[128,3328]{1,0:T(8,128)(2,1)S(1)}, u32[]{:S(2)}, u32[]{:S(2)}) collective-permute-start(bf16[128,3328]{1,0:T(8,128)(2,1)S(1)} %constant_dynamic-slice_fusion.9), channel_id=1, source_target_pairs={{0,8},{8,0},{16,24},{24,16},{1,9},{9,1},{17,25},{25,17},{2,10},{10... | collective-permute-start | bytes 2555912 | tf_op jit(solution)/shard_map/ppermute | solution.py:90
  112.2 5.3 %collective-permute-start.20 = (bf16[128,3328]{1,0:T(8,128)(2,1)S(1)}, bf16[128,3328]{1,0:T(8,128)(2,1)S(1)}, u32[]{:S(2)}, u32[]{:S(2)}) collective-permute-start(bf16[128,3328]{1,0:T(8,128)(2,1)S(1)} %constant_dynamic-slice_fusion.8), channel_id=1, source_target_pairs={{0,8},{8,0},{16,24},{24,16},{1,9},{9,1},{17,25},{25,17},{2,10},{10... | collective-permute-start | bytes 2555912 | tf_op jit(solution)/shard_map/ppermute | solution.py:90
  113.3 12.7 %collective-permute-start.13 = (bf16[64,3328]{1,0:T(8,128)(2,1)S(1)}, bf16[64,3328]{1,0:T(8,128)(2,1)S(1)}, u32[]{:S(2)}, u32[]{:S(2)}) collective-permute-start(bf16[64,3328]{1,0:T(8,128)(2,1)S(1)} %dynamic-slice_convert_fusion.3), channel_id=1, source_target_pairs={{0,16},{8,24},{16,0},{24,8},{1,17},{9,25},{17,1},{25,9},{2,18},{10... | collective-permute-start | bytes 1277960 | tf_op jit(solution)/shard_map/ppermute | solution.py:90
  115.2 20.0 %collective-permute-start.15 = (bf16[64,3328]{1,0:T(8,128)(2,1)S(1)}, bf16[64,3328]{1,0:T(8,128)(2,1)S(1)}, u32[]{:S(2)}, u32[]{:S(2)}) collective-permute-start(bf16[64,3328]{1,0:T(8,128)(2,1)S(1)} %dynamic-slice_convert_fusion.2), channel_id=1, source_target_pairs={{0,16},{8,24},{16,0},{24,8},{1,17},{9,25},{17,1},{25,9},{2,18},{10... | collective-permute-start | bytes 1277960 | tf_op jit(solution)/shard_map/ppermute | solution.py:90
  116.4 27.9 %collective-permute-start.19 = (bf16[64,3328]{1,0:T(8,128)(2,1)S(1)}, bf16[64,3328]{1,0:T(8,128)(2,1)S(1)}, u32[]{:S(2)}, u32[]{:S(2)}) collective-permute-start(bf16[64,3328]{1,0:T(8,128)(2,1)S(1)} %dynamic-slice_convert_fusion.1), channel_id=1, source_target_pairs={{0,16},{8,24},{16,0},{24,8},{1,17},{9,25},{17,1},{25,9},{2,18},{10... | collective-permute-start | bytes 1277960 | tf_op jit(solution)/shard_map/ppermute | solution.py:90
  117.8 35.6 %collective-permute-start.21 = (bf16[64,3328]{1,0:T(8,128)(2,1)S(1)}, bf16[64,3328]{1,0:T(8,128)(2,1)S(1)}, u32[]{:S(2)}, u32[]{:S(2)}) collective-permute-start(bf16[64,3328]{1,0:T(8,128)(2,1)S(1)} %dynamic-slice_convert_fusion), channel_id=1, source_target_pairs={{0,16},{8,24},{16,0},{24,8},{1,17},{9,25},{17,1},{25,9},{2,18},{10... | collective-permute-start | bytes 1277960 | tf_op jit(solution)/shard_map/ppermute | solution.py:90
  135.4 27.1 %collective-permute-start.16 = (bf16[64,3328]{1,0:T(8,128)(2,1)S(1)}, bf16[64,3328]{1,0:T(8,128)(2,1)S(1)}, u32[]{:S(2)}, u32[]{:S(2)}) collective-permute-start(bf16[64,3328]{1,0:T(8,128)(2,1)S(1)} %multiply_convert_fusion.1), channel_id=1, source_target_pairs={{0,16},{8,24},{16,0},{24,8},{1,17},{9,25},{17,1},{25,9},{2,18},{10... | collective-permute-start | bytes 1277960 | tf_op jit(solution)/shard_map/ppermute | solution.py:90
  153.7 17.4 %copy-start.1 = (s32[26,32]{1,0:T(8,128)S(1)}, s32[26,32]{1,0:T(8,128)}, u32[]{:S(2)}) copy-start(s32[26,32]{1,0:T(8,128)} %param.11) | copy-start | bytes 9988
  153.7 17.1 %collective-permute-start.22 = (bf16[64,3328]{1,0:T(8,128)(2,1)S(1)}, bf16[64,3328]{1,0:T(8,128)(2,1)S(1)}, u32[]{:S(2)}, u32[]{:S(2)}) collective-permute-start(bf16[64,3328]{1,0:T(8,128)(2,1)S(1)} %multiply_convert_fusion), channel_id=1, source_target_pairs={{0,16},{8,24},{16,0},{24,8},{1,17},{9,25},{17,1},{25,9},{2,18},{10... | collective-permute-start | bytes 1277960 | tf_op jit(solution)/shard_map/ppermute | solution.py:90
  162.7 10.1 %collective-permute-start.17 = (bf16[128,3328]{1,0:T(8,128)(2,1)S(1)}, bf16[128,3328]{1,0:T(8,128)(2,1)S(1)}, u32[]{:S(2)}, u32[]{:S(2)}) collective-permute-start(bf16[128,3328]{1,0:T(8,128)(2,1)S(1)} %maximum_select_fusion.6), channel_id=1, source_target_pairs={{0,8},{8,0},{16,24},{24,16},{1,9},{9,1},{17,25},{25,17},{2,10},{10... | collective-permute-start | bytes 2555912 | tf_op jit(solution)/shard_map/ppermute | solution.py:90
  171.0 2.4 collective-permute-start.23
  171.3 1.8 copy-start.2
  171.3 1.8 copy-start.3
  195.1 25.5 %collective-permute-start.24 = (bf16[64,2048]{1,0:T(8,128)(2,1)S(1)}, bf16[64,2048]{1,0:T(8,128)(2,1)}, u32[]{:S(2)}, u32[]{:S(2)}) collective-permute-start(bf16[64,2048]{1,0:T(8,128)(2,1)S(1)} %constant_dynamic-slice_fusion.7), channel_id=1, source_target_pairs={{0,1},{1,0},{2,3},{3,2},{4,5},{5,4},{6,7},{7,6},{8,9},{9,8},{10,11... | collective-permute-start | bytes 786440 | tf_op jit(solution)/shard_map/ppermute | solution.py:90
  196.7 27.2 %collective-permute-start.27 = (bf16[64,2048]{1,0:T(8,128)(2,1)S(1)}, bf16[64,2048]{1,0:T(8,128)(2,1)}, u32[]{:S(2)}, u32[]{:S(2)}) collective-permute-start(bf16[64,2048]{1,0:T(8,128)(2,1)S(1)} %constant_dynamic-slice_fusion.6), channel_id=1, source_target_pairs={{0,2},{1,3},{2,0},{3,1},{4,6},{5,7},{6,4},{7,5},{8,10},{9,11},{10,... | collective-permute-start | bytes 786440 | tf_op jit(solution)/shard_map/ppermute | solution.py:90
  197.5 24.8 %collective-permute-start.30 = (bf16[64,2048]{1,0:T(8,128)(2,1)S(1)}, bf16[64,2048]{1,0:T(8,128)(2,1)}, u32[]{:S(2)}, u32[]{:S(2)}) collective-permute-start(bf16[64,2048]{1,0:T(8,128)(2,1)S(1)} %constant_dynamic-slice_fusion.5), channel_id=1, source_target_pairs={{0,1},{1,0},{2,3},{3,2},{4,5},{5,4},{6,7},{7,6},{8,9},{9,8},{10,11... | collective-permute-start | bytes 786440 | tf_op jit(solution)/shard_map/ppermute | solution.py:90
  198.1 28.3 %collective-permute-start.33 = (bf16[64,2048]{1,0:T(8,128)(2,1)S(1)}, bf16[64,2048]{1,0:T(8,128)(2,1)S(1)}, u32[]{:S(2)}, u32[]{:S(2)}) collective-permute-start(bf16[64,2048]{1,0:T(8,128)(2,1)S(1)} %constant_dynamic-slice_fusion.4), channel_id=1, source_target_pairs={{0,2},{1,3},{2,0},{3,1},{4,6},{5,7},{6,4},{7,5},{8,10},{9,11},{10,... | collective-permute-start | bytes 786440 | tf_op jit(solution)/shard_map/ppermute | solution.py:90
  218.9 9.3 %collective-permute-start.36 = (bf16[64,2048]{1,0:T(8,128)(2,1)S(1)}, bf16[64,2048]{1,0:T(8,128)(2,1)S(1)}, u32[]{:S(2)}, u32[]{:S(2)}) collective-permute-start(bf16[64,2048]{1,0:T(8,128)(2,1)S(1)} %constant_dynamic-slice_fusion.3), channel_id=1, source_target_pairs={{0,1},{1,0},{2,3},{3,2},{4,5},{5,4},{6,7},{7,6},{8,9},{9,8},{10,11... | collective-permute-start | bytes 786440 | tf_op jit(solution)/shard_map/ppermute | solution.py:90
  220.6 10.8 %collective-permute-start.39 = (bf16[64,2048]{1,0:T(8,128)(2,1)S(1)}, bf16[64,2048]{1,0:T(8,128)(2,1)S(1)}, u32[]{:S(2)}, u32[]{:S(2)}) collective-permute-start(bf16[64,2048]{1,0:T(8,128)(2,1)S(1)} %constant_dynamic-slice_fusion.2), channel_id=1, source_target_pairs={{0,2},{1,3},{2,0},{3,1},{4,6},{5,7},{6,4},{7,5},{8,10},{9,11},{10,... | collective-permute-start | bytes 786440 | tf_op jit(solution)/shard_map/ppermute | solution.py:90
  222.3 10.8 %collective-permute-start.42 = (bf16[64,2048]{1,0:T(8,128)(2,1)S(1)}, bf16[64,2048]{1,0:T(8,128)(2,1)S(1)}, u32[]{:S(2)}, u32[]{:S(2)}) collective-permute-start(bf16[64,2048]{1,0:T(8,128)(2,1)S(1)} %constant_dynamic-slice_fusion.1), channel_id=1, source_target_pairs={{0,1},{1,0},{2,3},{3,2},{4,5},{5,4},{6,7},{7,6},{8,9},{9,8},{10,11... | collective-permute-start | bytes 786440 | tf_op jit(solution)/shard_map/ppermute | solution.py:90
  223.9 17.2 %collective-permute-start.45 = (bf16[64,2048]{1,0:T(8,128)(2,1)S(1)}, bf16[64,2048]{1,0:T(8,128)(2,1)S(1)}, u32[]{:S(2)}, u32[]{:S(2)}) collective-permute-start(bf16[64,2048]{1,0:T(8,128)(2,1)S(1)} %constant_dynamic-slice_fusion), channel_id=1, source_target_pairs={{0,2},{1,3},{2,0},{3,1},{4,6},{5,7},{6,4},{7,5},{8,10},{9,11},{10,... | collective-permute-start | bytes 786440 | tf_op jit(solution)/shard_map/ppermute | solution.py:90
  226.4 19.0 %collective-permute-start.25 = (bf16[32,2048]{1,0:T(8,128)(2,1)S(1)}, bf16[32,2048]{1,0:T(8,128)(2,1)S(1)}, u32[]{:S(2)}, u32[]{:S(2)}) collective-permute-start(bf16[32,2048]{1,0:T(8,128)(2,1)S(1)} %dynamic-slice_convert_fusion.11), channel_id=1, source_target_pairs={{0,2},{1,3},{2,0},{3,1},{4,6},{5,7},{6,4},{7,5},{8,10},{9,11},{10,... | collective-permute-start | bytes 393224 | tf_op jit(solution)/shard_map/ppermute | solution.py:90
  228.2 21.4 %collective-permute-start.28 = (bf16[32,2048]{1,0:T(8,128)(2,1)S(1)}, bf16[32,2048]{1,0:T(8,128)(2,1)S(1)}, u32[]{:S(2)}, u32[]{:S(2)}) collective-permute-start(bf16[32,2048]{1,0:T(8,128)(2,1)S(1)} %dynamic-slice_convert_fusion.10), channel_id=1, source_target_pairs={{0,4},{1,5},{2,6},{3,7},{4,0},{5,1},{6,2},{7,3},{8,12},{9,13},{10,... | collective-permute-start | bytes 393224 | tf_op jit(solution)/shard_map/ppermute | solution.py:90
  231.4 16.9 %collective-permute-start.31 = (bf16[32,2048]{1,0:T(8,128)(2,1)S(1)}, bf16[32,2048]{1,0:T(8,128)(2,1)S(1)}, u32[]{:S(2)}, u32[]{:S(2)}) collective-permute-start(bf16[32,2048]{1,0:T(8,128)(2,1)S(1)} %dynamic-slice_convert_fusion.9), channel_id=1, source_target_pairs={{0,2},{1,3},{2,0},{3,1},{4,6},{5,7},{6,4},{7,5},{8,10},{9,11},{10,... | collective-permute-start | bytes 393224 | tf_op jit(solution)/shard_map/ppermute | solution.py:90
  233.2 21.3 %collective-permute-start.34 = (bf16[32,2048]{1,0:T(8,128)(2,1)S(1)}, bf16[32,2048]{1,0:T(8,128)(2,1)S(1)}, u32[]{:S(2)}, u32[]{:S(2)}) collective-permute-start(bf16[32,2048]{1,0:T(8,128)(2,1)S(1)} %dynamic-slice_convert_fusion.8), channel_id=1, source_target_pairs={{0,4},{1,5},{2,6},{3,7},{4,0},{5,1},{6,2},{7,3},{8,12},{9,13},{10,... | collective-permute-start | bytes 393224 | tf_op jit(solution)/shard_map/ppermute | solution.py:90
  241.1 13.5 %collective-permute-start.37 = (bf16[32,2048]{1,0:T(8,128)(2,1)S(1)}, bf16[32,2048]{1,0:T(8,128)(2,1)S(1)}, u32[]{:S(2)}, u32[]{:S(2)}) collective-permute-start(bf16[32,2048]{1,0:T(8,128)(2,1)S(1)} %dynamic-slice_convert_fusion.7), channel_id=1, source_target_pairs={{0,2},{1,3},{2,0},{3,1},{4,6},{5,7},{6,4},{7,5},{8,10},{9,11},{10,... | collective-permute-start | bytes 393224 | tf_op jit(solution)/shard_map/ppermute | solution.py:90
  245.3 11.7 %collective-permute-start.40 = (bf16[32,2048]{1,0:T(8,128)(2,1)S(1)}, bf16[32,2048]{1,0:T(8,128)(2,1)S(1)}, u32[]{:S(2)}, u32[]{:S(2)}) collective-permute-start(bf16[32,2048]{1,0:T(8,128)(2,1)S(1)} %dynamic-slice_convert_fusion.6), channel_id=1, source_target_pairs={{0,4},{1,5},{2,6},{3,7},{4,0},{5,1},{6,2},{7,3},{8,12},{9,13},{10,... | collective-permute-start | bytes 393224 | tf_op jit(solution)/shard_map/ppermute | solution.py:90
  248.3 10.1 %collective-permute-start.43 = (bf16[32,2048]{1,0:T(8,128)(2,1)S(1)}, bf16[32,2048]{1,0:T(8,128)(2,1)S(1)}, u32[]{:S(2)}, u32[]{:S(2)}) collective-permute-start(bf16[32,2048]{1,0:T(8,128)(2,1)S(1)} %dynamic-slice_convert_fusion.5), channel_id=1, source_target_pairs={{0,2},{1,3},{2,0},{3,1},{4,6},{5,7},{6,4},{7,5},{8,10},{9,11},{10,... | collective-permute-start | bytes 393224 | tf_op jit(solution)/shard_map/ppermute | solution.py:90
  249.6 14.3 %collective-permute-start.46 = (bf16[32,2048]{1,0:T(8,128)(2,1)S(1)}, bf16[32,2048]{1,0:T(8,128)(2,1)S(1)}, u32[]{:S(2)}, u32[]{:S(2)}) collective-permute-start(bf16[32,2048]{1,0:T(8,128)(2,1)S(1)} %dynamic-slice_convert_fusion.4), channel_id=1, source_target_pairs={{0,4},{1,5},{2,6},{3,7},{4,0},{5,1},{6,2},{7,3},{8,12},{9,13},{10,... | collective-permute-start | bytes 393224 | tf_op jit(solution)/shard_map/ppermute | solution.py:90
  254.5 10.0 %collective-permute-start.26 = (bf16[16,2048]{1,0:T(8,128)(2,1)S(1)}, bf16[16,2048]{1,0:T(8,128)(2,1)S(1)}, u32[]{:S(2)}, u32[]{:S(2)}) collective-permute-start(bf16[16,2048]{1,0:T(8,128)(2,1)S(1)} %dynamic-slice_convert_fusion.19), channel_id=1, source_target_pairs={{0,4},{1,5},{2,6},{3,7},{4,0},{5,1},{6,2},{7,3},{8,12},{9,13},{10,... | collective-permute-start | bytes 196616 | tf_op jit(solution)/shard_map/ppermute | solution.py:90
  254.7 13.1 %collective-permute-start.29 = (bf16[16,2048]{1,0:T(8,128)(2,1)S(1)}, bf16[16,2048]{1,0:T(8,128)(2,1)S(1)}, u32[]{:S(2)}, u32[]{:S(2)}) collective-permute-start(bf16[16,2048]{1,0:T(8,128)(2,1)S(1)} %dynamic-slice_convert_fusion.18), channel_id=1, source_target_pairs={{0,1},{1,0},{2,3},{3,2},{4,5},{5,4},{6,7},{7,6},{8,9},{9,8},{10,11... | collective-permute-start | bytes 196616 | tf_op jit(solution)/shard_map/ppermute | solution.py:90
  257.1 8.8 %collective-permute-start.32 = (bf16[16,2048]{1,0:T(8,128)(2,1)S(1)}, bf16[16,2048]{1,0:T(8,128)(2,1)S(1)}, u32[]{:S(2)}, u32[]{:S(2)}) collective-permute-start(bf16[16,2048]{1,0:T(8,128)(2,1)S(1)} %dynamic-slice_convert_fusion.17), channel_id=1, source_target_pairs={{0,4},{1,5},{2,6},{3,7},{4,0},{5,1},{6,2},{7,3},{8,12},{9,13},{10,... | collective-permute-start | bytes 196616 | tf_op jit(solution)/shard_map/ppermute | solution.py:90
  258.4 10.7 %collective-permute-start.35 = (bf16[16,2048]{1,0:T(8,128)(2,1)S(1)}, bf16[16,2048]{1,0:T(8,128)(2,1)S(1)}, u32[]{:S(2)}, u32[]{:S(2)}) collective-permute-start(bf16[16,2048]{1,0:T(8,128)(2,1)S(1)} %dynamic-slice_convert_fusion.16), channel_id=1, source_target_pairs={{0,1},{1,0},{2,3},{3,2},{4,5},{5,4},{6,7},{7,6},{8,9},{9,8},{10,11... | collective-permute-start | bytes 196616 | tf_op jit(solution)/shard_map/ppermute | solution.py:90
  263.8 5.3 %collective-permute-start.38 = (bf16[16,2048]{1,0:T(8,128)(2,1)S(1)}, bf16[16,2048]{1,0:T(8,128)(2,1)S(1)}, u32[]{:S(2)}, u32[]{:S(2)}) collective-permute-start(bf16[16,2048]{1,0:T(8,128)(2,1)S(1)} %dynamic-slice_convert_fusion.15), channel_id=1, source_target_pairs={{0,4},{1,5},{2,6},{3,7},{4,0},{5,1},{6,2},{7,3},{8,12},{9,13},{10,... | collective-permute-start | bytes 196616 | tf_op jit(solution)/shard_map/ppermute | solution.py:90
  264.5 4.7 %collective-permute-start.41 = (bf16[16,2048]{1,0:T(8,128)(2,1)S(1)}, bf16[16,2048]{1,0:T(8,128)(2,1)S(1)}, u32[]{:S(2)}, u32[]{:S(2)}) collective-permute-start(bf16[16,2048]{1,0:T(8,128)(2,1)S(1)} %dynamic-slice_convert_fusion.14), channel_id=1, source_target_pairs={{0,1},{1,0},{2,3},{3,2},{4,5},{5,4},{6,7},{7,6},{8,9},{9,8},{10,11... | collective-permute-start | bytes 196616 | tf_op jit(solution)/shard_map/ppermute | solution.py:90
  265.9 5.9 %collective-permute-start.44 = (bf16[16,2048]{1,0:T(8,128)(2,1)S(1)}, bf16[16,2048]{1,0:T(8,128)(2,1)S(1)}, u32[]{:S(2)}, u32[]{:S(2)}) collective-permute-start(bf16[16,2048]{1,0:T(8,128)(2,1)S(1)} %dynamic-slice_convert_fusion.13), channel_id=1, source_target_pairs={{0,4},{1,5},{2,6},{3,7},{4,0},{5,1},{6,2},{7,3},{8,12},{9,13},{10,... | collective-permute-start | bytes 196616 | tf_op jit(solution)/shard_map/ppermute | solution.py:90
  267.8 4.3 %collective-permute-start.47 = (bf16[16,2048]{1,0:T(8,128)(2,1)S(1)}, bf16[16,2048]{1,0:T(8,128)(2,1)S(1)}, u32[]{:S(2)}, u32[]{:S(2)}) collective-permute-start(bf16[16,2048]{1,0:T(8,128)(2,1)S(1)} %dynamic-slice_convert_fusion.12), channel_id=1, source_target_pairs={{0,1},{1,0},{2,3},{3,2},{4,5},{5,4},{6,7},{7,6},{8,9},{9,8},{10,11... | collective-permute-start | bytes 196616 | tf_op jit(solution)/shard_map/ppermute | solution.py:90

commit v9 on v6

--- a/solution.py
+++ b/solution.py
@@ -52,7 +52,8 @@
     cap, block, _ = packed[0].shape
     t = x.shape[0]
     n_w = len(packed)
-    group = next(s for s in (4, 2, 1) if rows % s == 0)
+    sizes = (8, 4, 2, 1) if n_w == 1 else (4, 2, 1)
+    group = next(s for s in sizes if rows % s == 0)
     base, index = slot_tables(keep, cap)
 
     def w_spec(rr):
@@ -122,7 +123,8 @@
     orders = col_orders * 2
     token_parts = [tokens[q * quarter:(q + 1) * quarter] for q in range(4)]
     segment = jnp.concatenate(doubling_gather(list(zip(token_parts, orders)), "col", n_col), axis=0)
-    gate_rows, up_rows = sparse_matmul(segment, [gate_packed, up_packed], gate_keep)
+    (gate_rows,) = sparse_matmul(segment, [gate_packed], gate_keep)
+    (up_rows,) = sparse_matmul(segment, [up_packed], gate_keep)
     half = gate_rows.shape[0] // 2
     sums = halving_scatter(
         [([gate_rows[:half], up_rows[:half]], row_bits), ([gate_rows[half:], up_rows[half:]], row_bits)],

time: 268 us -> 276 us (1.030)
  waiting for transfers between devices: 123 us -> 141 us
  starting transfers between devices: 50.5 us -> 33 us
  Pallas kernels: 69.1 us -> 73.6 us
    ppermute x36, waiting for transfers between devices: 123 us -> 141 us  [exchange(): return lax.ppermute(x, axis, perm=pairs)]
    ppermute x36, starting transfers between devices: 50.5 us -> 33 us  [exchange(): return lax.ppermute(x, axis, perm=pairs)]
    pallas_call x2 -> x3, Pallas kernels: 69.1 us -> 73.6 us  [sparse_matmul(): pl.pallas_call(kernel, grid_spec=pltpu.PrefetchScalarGridSpec(num_scalar_...]
  transfers between devices with their start and end apart: 36 -> 36, of which waited for: 21 -> 22; matrix products, arithmetic and copies ran while one was open for 4% -> 5% of each run, Pallas kernels for 0% -> 9%
where the time goes in v9:
time: 276 us; the launch traced here: 275 us
  waiting for transfers between devices  141 us (51%)
  Pallas kernels  73.6 us (27%)
  starting transfers between devices  33 us (12%)
  local copies, waits for them, and re-layouts  13.7 us (5%)
  other arithmetic  13.3 us (5%)
    ppermute x36, waiting for transfers between devices, exchange(): return lax.ppermute(x, axis, perm=pairs)  141 us
    pallas_call x3, Pallas kernels, sparse_matmul(): pl.pallas_call(kernel, grid_spec=pltpu.PrefetchScalarGridSpec(num_scalar_...  73.6 us
    ppermute x36, starting transfers between devices, exchange(): return lax.ppermute(x, axis, perm=pairs)  33 us
  transfers between devices with their start and end apart: 36, of which 22 were waited for; matrix products, arithmetic and copies ran while one was open for 5% of the time, Pallas kernels for 9%

profile of v9, /device:TPU:0, one launch (start us, length us, event | category | flops | bytes accessed | tf_op | source)
XLA Modules:
  0.0 275.3 jit_solution(13991668205080670984)
XLA Ops:
  0.0 1.1 fusion.6
  1.1 4.1 %collective-permute-start = (bf16[16,4096]{1,0:T(8,128)(2,1)S(1)}, bf16[16,4096]{1,0:T(8,128)(2,1)S(1)}, u32[]{:S(2)}, u32[]{:S(2)}) collective-permute-start(bf16[16,4096]{1,0:T(8,128)(2,1)S(1)} %get-tuple-element.13), channel_id=1, source_target_pairs={{0,4},{1,5},{2,6},{3,7},{4,0},{5,1},{6,2},{7,3},{8,12},{9,13},{10,... | collective-permute-start | bytes 393224 | tf_op jit(solution)/shard_map/ppermute | solution.py:86
  5.2 1.5 collective-permute-start.3
  6.7 0.3 collective-permute-start.6
  7.1 0.3 collective-permute-start.9
  7.3 0.8 reshape.61
  8.1 0.8 reshape.67
  9.0 0.3 reduce-window.24
  9.6 0.7 sub.27
  10.5 0.8 subtract_select_fusion
  11.3 0.3 reduce-window.16
  11.7 0.7 reshape.71.index_ref
  12.7 2.5 collective-permute-done
  15.4 3.4 %collective-permute-start.4 = (bf16[32,4096]{1,0:T(8,128)(2,1)S(1)}, bf16[32,4096]{1,0:T(8,128)(2,1)S(1)}, u32[]{:S(2)}, u32[]{:S(2)}) collective-permute-start(bf16[32,4096]{1,0:T(8,128)(2,1)S(1)} %maximum_select_fusion.13), channel_id=1, source_target_pairs={{0,4},{1,5},{2,6},{3,7},{4,0},{5,1},{6,2},{7,3},{8,12},{9,13},{10,... | collective-permute-start | bytes 786440 | tf_op jit(solution)/shard_map/ppermute | solution.py:86
  19.0 2.5 collective-permute-start.10
  21.5 8.6 %collective-permute-done.1 = bf16[32,4096]{1,0:T(8,128)(2,1)S(1)} collective-permute-done((bf16[32,4096]{1,0:T(8,128)(2,1)S(1)}, bf16[32,4096]{1,0:T(8,128)(2,1)S(1)}, u32[]{:S(2)}, u32[]{:S(2)}) %collective-permute-start.1) | collective-permute-done | bytes 262176 | tf_op jit(solution)/shard_map/ppermute | solution.py:86
  30.2 2.2 collective-permute-start.2
  32.6 8.7 %collective-permute-done.7 = bf16[32,4096]{1,0:T(8,128)(2,1)S(1)} collective-permute-done((bf16[32,4096]{1,0:T(8,128)(2,1)S(1)}, bf16[32,4096]{1,0:T(8,128)(2,1)S(1)}, u32[]{:S(2)}, u32[]{:S(2)}) %collective-permute-start.7) | collective-permute-done | bytes 262176 | tf_op jit(solution)/shard_map/ppermute | solution.py:86
  41.4 2.0 collective-permute-start.8
  43.8 8.8 %collective-permute-done.5 = bf16[64,4096]{1,0:T(8,128)(2,1)S(1)} collective-permute-done((bf16[64,4096]{1,0:T(8,128)(2,1)S(1)}, bf16[64,4096]{1,0:T(8,128)(2,1)S(1)}, u32[]{:S(2)}, u32[]{:S(2)}) %collective-permute-start.5) | collective-permute-done | bytes 524320 | tf_op jit(solution)/shard_map/ppermute | solution.py:86
  53.1 9.0 %collective-permute-done.11 = bf16[64,4096]{1,0:T(8,128)(2,1)S(1)} collective-permute-done((bf16[64,4096]{1,0:T(8,128)(2,1)S(1)}, bf16[64,4096]{1,0:T(8,128)(2,1)S(1)}, u32[]{:S(2)}, u32[]{:S(2)}) %collective-permute-start.11) | collective-permute-done | bytes 524320 | tf_op jit(solution)/shard_map/ppermute | solution.py:86
  62.3 2.5 pad_maximum_fusion.x_ref
  64.8 24.1 %shard_map.64 = bf16[512,3328]{1,0:T(8,128)(2,1)} custom-call(s32[32]{0:T(128)} %copy-done.1, s32[832]{0:T(1024)} %reshape.71.index_ref, bf16[512,4096]{1,0:T(8,128)(2,1)} %pad_maximum_fusion.x_ref, bf16[640,128,128]{2,1,0:T(8,128)(2,1)} %refs_7_.2, bf16[640,128,128]{2,1,0:T(8,128)(2,1)} %refs_7_.2, bf16[640,128,128]{2,1,0:T(8,128)(2,1)} %refs_7_.2, ...), custom_call_target="tpu_custom_call" | custom-call | flops 13958643712 | bytes 34865152 | tf_op jit(solution)/shard_map/pallas_call | solution.py:67
  88.9 2.2 fusion.4
  91.1 1.1 constant_dynamic-slice_fusion.7
  92.2 24.1 %shard_map.65 = bf16[512,3328]{1,0:T(8,128)(2,1)} custom-call(s32[32]{0:T(128)} %copy-done.1, s32[832]{0:T(1024)} %reshape.71.index_ref, bf16[512,4096]{1,0:T(8,128)(2,1)} %pad_maximum_fusion.x_ref, bf16[640,128,128]{2,1,0:T(8,128)(2,1)} %refs_7_.3, bf16[640,128,128]{2,1,0:T(8,128)(2,1)} %refs_7_.3, bf16[640,128,128]{2,1,0:T(8,128)(2,1)} %refs_7_.3, ...), custom_call_target="tpu_custom_call" | custom-call | flops 13958643712 | bytes 34865152 | tf_op jit(solution)/shard_map/pallas_call | solution.py:67
  116.3 2.2 fusion.5
  118.5 0.6 collective-permute-start.14
  119.3 0.5 collective-permute-start.20
  119.9 1.3 convert_add_fusion.3
  121.3 1.6 collective-permute-start.13
  123.1 0.5 collective-permute-start.15
  123.9 1.6 collective-permute-start.19
  125.8 0.5 collective-permute-start.21
  126.3 7.7 %collective-permute-done.13 = bf16[64,3328]{1,0:T(8,128)(2,1)S(1)} collective-permute-done((bf16[64,3328]{1,0:T(8,128)(2,1)S(1)}, bf16[64,3328]{1,0:T(8,128)(2,1)S(1)}, u32[]{:S(2)}, u32[]{:S(2)}) %collective-permute-start.13) | collective-permute-done | bytes 426016 | tf_op jit(solution)/shard_map/ppermute | solution.py:86
  134.0 9.1 %collective-permute-done.15 = bf16[64,3328]{1,0:T(8,128)(2,1)S(1)} collective-permute-done((bf16[64,3328]{1,0:T(8,128)(2,1)S(1)}, bf16[64,3328]{1,0:T(8,128)(2,1)S(1)}, u32[]{:S(2)}, u32[]{:S(2)}) %collective-permute-start.15) | collective-permute-done | bytes 426016 | tf_op jit(solution)/shard_map/ppermute | solution.py:86
  143.1 0.3 multiply_convert_fusion.1
  143.4 1.6 collective-permute-start.16
  145.1 7.2 %collective-permute-done.19 = bf16[64,3328]{1,0:T(8,128)(2,1)S(1)} collective-permute-done((bf16[64,3328]{1,0:T(8,128)(2,1)S(1)}, bf16[64,3328]{1,0:T(8,128)(2,1)S(1)}, u32[]{:S(2)}, u32[]{:S(2)}) %collective-permute-start.19) | collective-permute-done | bytes 426016 | tf_op jit(solution)/shard_map/ppermute | solution.py:86
  152.3 9.1 %collective-permute-done.21 = bf16[64,3328]{1,0:T(8,128)(2,1)S(1)} collective-permute-done((bf16[64,3328]{1,0:T(8,128)(2,1)S(1)}, bf16[64,3328]{1,0:T(8,128)(2,1)S(1)}, u32[]{:S(2)}, u32[]{:S(2)}) %collective-permute-start.21) | collective-permute-done | bytes 426016 | tf_op jit(solution)/shard_map/ppermute | solution.py:86
  161.4 0.3 multiply_convert_fusion
  161.7 1.6 collective-permute-start.22
  163.3 7.2 %collective-permute-done.16 = bf16[64,3328]{1,0:T(8,128)(2,1)S(1)} collective-permute-done((bf16[64,3328]{1,0:T(8,128)(2,1)S(1)}, bf16[64,3328]{1,0:T(8,128)(2,1)S(1)}, u32[]{:S(2)}, u32[]{:S(2)}) %collective-permute-start.16) | collective-permute-done | bytes 426016 | tf_op jit(solution)/shard_map/ppermute | solution.py:86
  170.8 8.0 %collective-permute-done.22 = bf16[64,3328]{1,0:T(8,128)(2,1)S(1)} collective-permute-done((bf16[64,3328]{1,0:T(8,128)(2,1)S(1)}, bf16[64,3328]{1,0:T(8,128)(2,1)S(1)}, u32[]{:S(2)}, u32[]{:S(2)}) %collective-permute-start.22) | collective-permute-done | bytes 426016 | tf_op jit(solution)/shard_map/ppermute | solution.py:86
  179.2 0.7 reshape.66.index_ref
  179.9 0.3 maximum_select_fusion
  180.3 1.1 collective-permute-done.23
  181.3 0.3 maximum_select_fusion.1
  181.7 2.0 pad_maximum_fusion.1.x_ref
  183.6 25.4 %shard_map.66 = bf16[512,4096]{1,0:T(8,128)(2,1)} custom-call(s32[26]{0:T(128)} %copy-done.2, s32[832]{0:T(1024)} %reshape.66.index_ref, bf16[512,3328]{1,0:T(8,128)(2,1)} %pad_maximum_fusion.1.x_ref, bf16[640,128,128]{2,1,0:T(8,128)(2,1)} %refs_1_.5, bf16[640,128,128]{2,1,0:T(8,128)(2,1)} %refs_1_.5), custom_call_target="tpu_custom_call" | custom-call | flops 13958643712 | bytes 34865152 | tf_op jit(solution)/shard_map/pallas_call | solution.py:67
  209.0 2.7 fusion.3
  211.7 3.6 %collective-permute-start.24 = (bf16[64,4096]{1,0:T(8,128)(2,1)S(1)}, bf16[64,4096]{1,0:T(8,128)(2,1)S(1)}, u32[]{:S(2)}, u32[]{:S(2)}) collective-permute-start(bf16[64,4096]{1,0:T(8,128)(2,1)S(1)} %constant_dynamic-slice_fusion.3), channel_id=1, source_target_pairs={{0,1},{1,0},{2,3},{3,2},{4,5},{5,4},{6,7},{7,6},{8,9},{9,8},{10,11... | collective-permute-start | bytes 1572872 | tf_op jit(solution)/shard_map/ppermute | solution.py:86
  215.7 2.1 collective-permute-start.33
  217.7 10.4 %collective-permute-done.24 = bf16[64,4096]{1,0:T(8,128)(2,1)S(1)} collective-permute-done((bf16[64,4096]{1,0:T(8,128)(2,1)S(1)}, bf16[64,4096]{1,0:T(8,128)(2,1)S(1)}, u32[]{:S(2)}, u32[]{:S(2)}) %collective-permute-start.24) | collective-permute-done | bytes 524320 | tf_op jit(solution)/shard_map/ppermute | solution.py:86
  228.3 2.0 collective-permute-done.27
  230.5 0.8 collective-permute-start.28
  231.3 7.4 %collective-permute-done.30 = bf16[64,4096]{1,0:T(8,128)(2,1)S(1)} collective-permute-done((bf16[64,4096]{1,0:T(8,128)(2,1)S(1)}, bf16[64,4096]{1,0:T(8,128)(2,1)S(1)}, u32[]{:S(2)}, u32[]{:S(2)}) %collective-permute-start.30) | collective-permute-done | bytes 524320 | tf_op jit(solution)/shard_map/ppermute | solution.py:86
  238.9 8.2 %collective-permute-done.33 = bf16[64,4096]{1,0:T(8,128)(2,1)S(1)} collective-permute-done((bf16[64,4096]{1,0:T(8,128)(2,1)S(1)}, bf16[64,4096]{1,0:T(8,128)(2,1)S(1)}, u32[]{:S(2)}, u32[]{:S(2)}) %collective-permute-start.33) | collective-permute-done | bytes 524320 | tf_op jit(solution)/shard_map/ppermute | solution.py:86
  247.4 10.9 %collective-permute-done.25 = bf16[32,4096]{1,0:T(8,128)(2,1)S(1)} collective-permute-done((bf16[32,4096]{1,0:T(8,128)(2,1)S(1)}, bf16[32,4096]{1,0:T(8,128)(2,1)S(1)}, u32[]{:S(2)}, u32[]{:S(2)}) %collective-permute-start.25) | collective-permute-done | bytes 262176 | tf_op jit(solution)/shard_map/ppermute | solution.py:86
  258.7 4.1 %collective-permute-done.31 = bf16[32,4096]{1,0:T(8,128)(2,1)S(1)} collective-permute-done((bf16[32,4096]{1,0:T(8,128)(2,1)S(1)}, bf16[32,4096]{1,0:T(8,128)(2,1)S(1)}, u32[]{:S(2)}, u32[]{:S(2)}) %collective-permute-start.31) | collective-permute-done | bytes 262176 | tf_op jit(solution)/shard_map/ppermute | solution.py:86
  263.0 6.3 %collective-permute-done.34 = bf16[32,4096]{1,0:T(8,128)(2,1)S(1)} collective-permute-done((bf16[32,4096]{1,0:T(8,128)(2,1)S(1)}, bf16[32,4096]{1,0:T(8,128)(2,1)S(1)}, u32[]{:S(2)}, u32[]{:S(2)}) %collective-permute-start.34) | collective-permute-done | bytes 262176 | tf_op jit(solution)/shard_map/ppermute | solution.py:86
  269.6 2.5 collective-permute-done.26
  272.1 2.0 collective-permute-done.32
  274.4 0.8 pad_maximum_fusion.2
  (102 shorter events, 6.5 us)
Async XLA Ops:
  1.1 14.0 %collective-permute-start = (bf16[16,4096]{1,0:T(8,128)(2,1)S(1)}, bf16[16,4096]{1,0:T(8,128)(2,1)S(1)}, u32[]{:S(2)}, u32[]{:S(2)}) collective-permute-start(bf16[16,4096]{1,0:T(8,128)(2,1)S(1)} %get-tuple-element.13), channel_id=1, source_target_pairs={{0,4},{1,5},{2,6},{3,7},{4,0},{5,1},{6,2},{7,3},{8,12},{9,13},{10,... | collective-permute-start | bytes 393224 | tf_op jit(solution)/shard_map/ppermute | solution.py:86
  5.2 10.1 %collective-permute-start.3 = (bf16[16,4096]{1,0:T(8,128)(2,1)S(1)}, bf16[16,4096]{1,0:T(8,128)(2,1)S(1)}, u32[]{:S(2)}, u32[]{:S(2)}) collective-permute-start(bf16[16,4096]{1,0:T(8,128)(2,1)S(1)} %get-tuple-element.14), channel_id=1, source_target_pairs={{0,1},{1,0},{2,3},{3,2},{4,5},{5,4},{6,7},{7,6},{8,9},{9,8},{10,11... | collective-permute-start | bytes 393224 | tf_op jit(solution)/shard_map/ppermute | solution.py:86
  6.7 12.1 %collective-permute-start.6 = (bf16[16,4096]{1,0:T(8,128)(2,1)S(1)}, bf16[16,4096]{1,0:T(8,128)(2,1)S(1)}, u32[]{:S(2)}, u32[]{:S(2)}) collective-permute-start(bf16[16,4096]{1,0:T(8,128)(2,1)S(1)} %get-tuple-element.16), channel_id=1, source_target_pairs={{0,4},{1,5},{2,6},{3,7},{4,0},{5,1},{6,2},{7,3},{8,12},{9,13},{10,... | collective-permute-start | bytes 393224 | tf_op jit(solution)/shard_map/ppermute | solution.py:86
  7.1 11.9 %collective-permute-start.9 = (bf16[16,4096]{1,0:T(8,128)(2,1)S(1)}, bf16[16,4096]{1,0:T(8,128)(2,1)S(1)}, u32[]{:S(2)}, u32[]{:S(2)}) collective-permute-start(bf16[16,4096]{1,0:T(8,128)(2,1)S(1)} %get-tuple-element.15), channel_id=1, source_target_pairs={{0,1},{1,0},{2,3},{3,2},{4,5},{5,4},{6,7},{7,6},{8,9},{9,8},{10,11... | collective-permute-start | bytes 393224 | tf_op jit(solution)/shard_map/ppermute | solution.py:86
  10.5 22.0 %copy-start.1 = (s32[32]{0:T(128)}, s32[32]{0:T(128)S(1)}, u32[]{:S(2)}) copy-start(s32[32]{0:T(128)S(1)} %fusion.base_ref) | copy-start | bytes 388
  15.2 14.9 %collective-permute-start.1 = (bf16[32,4096]{1,0:T(8,128)(2,1)S(1)}, bf16[32,4096]{1,0:T(8,128)(2,1)S(1)}, u32[]{:S(2)}, u32[]{:S(2)}) collective-permute-start(bf16[32,4096]{1,0:T(8,128)(2,1)S(1)} %maximum_select_fusion.12), channel_id=1, source_target_pairs={{0,2},{1,3},{2,0},{3,1},{4,6},{5,7},{6,4},{7,5},{8,10},{9,11},{10,... | collective-permute-start | bytes 786440 | tf_op jit(solution)/shard_map/ppermute | solution.py:86
  15.4 17.1 %collective-permute-start.4 = (bf16[32,4096]{1,0:T(8,128)(2,1)S(1)}, bf16[32,4096]{1,0:T(8,128)(2,1)S(1)}, u32[]{:S(2)}, u32[]{:S(2)}) collective-permute-start(bf16[32,4096]{1,0:T(8,128)(2,1)S(1)} %maximum_select_fusion.13), channel_id=1, source_target_pairs={{0,4},{1,5},{2,6},{3,7},{4,0},{5,1},{6,2},{7,3},{8,12},{9,13},{10,... | collective-permute-start | bytes 786440 | tf_op jit(solution)/shard_map/ppermute | solution.py:86
  18.8 22.4 %collective-permute-start.7 = (bf16[32,4096]{1,0:T(8,128)(2,1)S(1)}, bf16[32,4096]{1,0:T(8,128)(2,1)S(1)}, u32[]{:S(2)}, u32[]{:S(2)}) collective-permute-start(bf16[32,4096]{1,0:T(8,128)(2,1)S(1)} %maximum_select_fusion.14), channel_id=1, source_target_pairs={{0,2},{1,3},{2,0},{3,1},{4,6},{5,7},{6,4},{7,5},{8,10},{9,11},{10,... | collective-permute-start | bytes 786440 | tf_op jit(solution)/shard_map/ppermute | solution.py:86
  19.0 24.4 %collective-permute-start.10 = (bf16[32,4096]{1,0:T(8,128)(2,1)S(1)}, bf16[32,4096]{1,0:T(8,128)(2,1)S(1)}, u32[]{:S(2)}, u32[]{:S(2)}) collective-permute-start(bf16[32,4096]{1,0:T(8,128)(2,1)S(1)} %maximum_select_fusion.15), channel_id=1, source_target_pairs={{0,4},{1,5},{2,6},{3,7},{4,0},{5,1},{6,2},{7,3},{8,12},{9,13},{10,... | collective-permute-start | bytes 786440 | tf_op jit(solution)/shard_map/ppermute | solution.py:86
  30.2 13.4 %collective-permute-start.2 = (bf16[64,4096]{1,0:T(8,128)(2,1)S(1)}, bf16[64,4096]{1,0:T(8,128)(2,1)S(1)}, u32[]{:S(2)}, u32[]{:S(2)}) collective-permute-start(bf16[64,4096]{1,0:T(8,128)(2,1)S(1)} %maximum_select_fusion.8), channel_id=1, source_target_pairs={{0,1},{1,0},{2,3},{3,2},{4,5},{5,4},{6,7},{7,6},{8,9},{9,8},{10,11... | collective-permute-start | bytes 1572872 | tf_op jit(solution)/shard_map/ppermute | solution.py:86
  32.5 20.1 %collective-permute-start.5 = (bf16[64,4096]{1,0:T(8,128)(2,1)S(1)}, bf16[64,4096]{1,0:T(8,128)(2,1)S(1)}, u32[]{:S(2)}, u32[]{:S(2)}) collective-permute-start(bf16[64,4096]{1,0:T(8,128)(2,1)S(1)} %maximum_select_fusion.9), channel_id=1, source_target_pairs={{0,2},{1,3},{2,0},{3,1},{4,6},{5,7},{6,4},{7,5},{8,10},{9,11},{10,... | collective-permute-start | bytes 1572872 | tf_op jit(solution)/shard_map/ppermute | solution.py:86
  41.4 11.5 %collective-permute-start.8 = (bf16[64,4096]{1,0:T(8,128)(2,1)S(1)}, bf16[64,4096]{1,0:T(8,128)(2,1)S(1)}, u32[]{:S(2)}, u32[]{:S(2)}) collective-permute-start(bf16[64,4096]{1,0:T(8,128)(2,1)S(1)} %maximum_select_fusion.10), channel_id=1, source_target_pairs={{0,1},{1,0},{2,3},{3,2},{4,5},{5,4},{6,7},{7,6},{8,9},{9,8},{10,11... | collective-permute-start | bytes 1572872 | tf_op jit(solution)/shard_map/ppermute | solution.py:86
  43.5 18.6 %collective-permute-start.11 = (bf16[64,4096]{1,0:T(8,128)(2,1)S(1)}, bf16[64,4096]{1,0:T(8,128)(2,1)S(1)}, u32[]{:S(2)}, u32[]{:S(2)}) collective-permute-start(bf16[64,4096]{1,0:T(8,128)(2,1)S(1)} %maximum_select_fusion.11), channel_id=1, source_target_pairs={{0,2},{1,3},{2,0},{3,1},{4,6},{5,7},{6,4},{7,5},{8,10},{9,11},{10,... | collective-permute-start | bytes 1572872 | tf_op jit(solution)/shard_map/ppermute | solution.py:86
  92.2 27.7 %collective-permute-start.12 = (bf16[128,3328]{1,0:T(8,128)(2,1)}, bf16[128,3328]{1,0:T(8,128)(2,1)}, u32[]{:S(2)}, u32[]{:S(2)}) collective-permute-start(bf16[128,3328]{1,0:T(8,128)(2,1)} %constant_dynamic-slice_fusion.7), channel_id=1, source_target_pairs={{0,8},{8,0},{16,24},{24,16},{1,9},{9,1},{17,25},{25,17},{2,10},{10... | collective-permute-start | bytes 2555912 | tf_op jit(solution)/shard_map/ppermute | solution.py:86
  118.5 4.4 %collective-permute-start.14 = (bf16[128,3328]{1,0:T(8,128)(2,1)S(1)}, bf16[128,3328]{1,0:T(8,128)(2,1)S(1)}, u32[]{:S(2)}, u32[]{:S(2)}) collective-permute-start(bf16[128,3328]{1,0:T(8,128)(2,1)S(1)} %constant_dynamic-slice_fusion.6), channel_id=1, source_target_pairs={{0,8},{8,0},{16,24},{24,16},{1,9},{9,1},{17,25},{25,17},{2,10},{10... | collective-permute-start | bytes 2555912 | tf_op jit(solution)/shard_map/ppermute | solution.py:86
  119.2 4.5 %collective-permute-start.18 = (bf16[128,3328]{1,0:T(8,128)(2,1)S(1)}, bf16[128,3328]{1,0:T(8,128)(2,1)S(1)}, u32[]{:S(2)}, u32[]{:S(2)}) collective-permute-start(bf16[128,3328]{1,0:T(8,128)(2,1)S(1)} %constant_dynamic-slice_fusion.5), channel_id=1, source_target_pairs={{0,8},{8,0},{16,24},{24,16},{1,9},{9,1},{17,25},{25,17},{2,10},{10... | collective-permute-start | bytes 2555912 | tf_op jit(solution)/shard_map/ppermute | solution.py:86
  119.3 6.2 %collective-permute-start.20 = (bf16[128,3328]{1,0:T(8,128)(2,1)S(1)}, bf16[128,3328]{1,0:T(8,128)(2,1)S(1)}, u32[]{:S(2)}, u32[]{:S(2)}) collective-permute-start(bf16[128,3328]{1,0:T(8,128)(2,1)S(1)} %constant_dynamic-slice_fusion.4), channel_id=1, source_target_pairs={{0,8},{8,0},{16,24},{24,16},{1,9},{9,1},{17,25},{25,17},{2,10},{10... | collective-permute-start | bytes 2555912 | tf_op jit(solution)/shard_map/ppermute | solution.py:86
  121.3 12.7 %collective-permute-start.13 = (bf16[64,3328]{1,0:T(8,128)(2,1)S(1)}, bf16[64,3328]{1,0:T(8,128)(2,1)S(1)}, u32[]{:S(2)}, u32[]{:S(2)}) collective-permute-start(bf16[64,3328]{1,0:T(8,128)(2,1)S(1)} %dynamic-slice_convert_fusion.3), channel_id=1, source_target_pairs={{0,16},{8,24},{16,0},{24,8},{1,17},{9,25},{17,1},{25,9},{2,18},{10... | collective-permute-start | bytes 1277960 | tf_op jit(solution)/shard_map/ppermute | solution.py:86
  123.1 20.0 %collective-permute-start.15 = (bf16[64,3328]{1,0:T(8,128)(2,1)S(1)}, bf16[64,3328]{1,0:T(8,128)(2,1)S(1)}, u32[]{:S(2)}, u32[]{:S(2)}) collective-permute-start(bf16[64,3328]{1,0:T(8,128)(2,1)S(1)} %dynamic-slice_convert_fusion.2), channel_id=1, source_target_pairs={{0,16},{8,24},{16,0},{24,8},{1,17},{9,25},{17,1},{25,9},{2,18},{10... | collective-permute-start | bytes 1277960 | tf_op jit(solution)/shard_map/ppermute | solution.py:86
  123.9 28.3 %collective-permute-start.19 = (bf16[64,3328]{1,0:T(8,128)(2,1)S(1)}, bf16[64,3328]{1,0:T(8,128)(2,1)S(1)}, u32[]{:S(2)}, u32[]{:S(2)}) collective-permute-start(bf16[64,3328]{1,0:T(8,128)(2,1)S(1)} %dynamic-slice_convert_fusion.1), channel_id=1, source_target_pairs={{0,16},{8,24},{16,0},{24,8},{1,17},{9,25},{17,1},{25,9},{2,18},{10... | collective-permute-start | bytes 1277960 | tf_op jit(solution)/shard_map/ppermute | solution.py:86
  125.8 35.6 %collective-permute-start.21 = (bf16[64,3328]{1,0:T(8,128)(2,1)S(1)}, bf16[64,3328]{1,0:T(8,128)(2,1)S(1)}, u32[]{:S(2)}, u32[]{:S(2)}) collective-permute-start(bf16[64,3328]{1,0:T(8,128)(2,1)S(1)} %dynamic-slice_convert_fusion), channel_id=1, source_target_pairs={{0,16},{8,24},{16,0},{24,8},{1,17},{9,25},{17,1},{25,9},{2,18},{10... | collective-permute-start | bytes 1277960 | tf_op jit(solution)/shard_map/ppermute | solution.py:86
  143.4 27.1 %collective-permute-start.16 = (bf16[64,3328]{1,0:T(8,128)(2,1)S(1)}, bf16[64,3328]{1,0:T(8,128)(2,1)S(1)}, u32[]{:S(2)}, u32[]{:S(2)}) collective-permute-start(bf16[64,3328]{1,0:T(8,128)(2,1)S(1)} %multiply_convert_fusion.1), channel_id=1, source_target_pairs={{0,16},{8,24},{16,0},{24,8},{1,17},{9,25},{17,1},{25,9},{2,18},{10... | collective-permute-start | bytes 1277960 | tf_op jit(solution)/shard_map/ppermute | solution.py:86
  161.7 17.2 %copy-start = (s32[26,32]{1,0:T(8,128)S(1)}, s32[26,32]{1,0:T(8,128)}, u32[]{:S(2)}) copy-start(s32[26,32]{1,0:T(8,128)} %param.11) | copy-start | bytes 9988
  161.7 17.0 %collective-permute-start.22 = (bf16[64,3328]{1,0:T(8,128)(2,1)S(1)}, bf16[64,3328]{1,0:T(8,128)(2,1)S(1)}, u32[]{:S(2)}, u32[]{:S(2)}) collective-permute-start(bf16[64,3328]{1,0:T(8,128)(2,1)S(1)} %multiply_convert_fusion), channel_id=1, source_target_pairs={{0,16},{8,24},{16,0},{24,8},{1,17},{9,25},{17,1},{25,9},{2,18},{10... | collective-permute-start | bytes 1277960 | tf_op jit(solution)/shard_map/ppermute | solution.py:86
  170.7 9.2 %collective-permute-start.17 = (bf16[128,3328]{1,0:T(8,128)(2,1)S(1)}, bf16[128,3328]{1,0:T(8,128)(2,1)S(1)}, u32[]{:S(2)}, u32[]{:S(2)}) collective-permute-start(bf16[128,3328]{1,0:T(8,128)(2,1)S(1)} %maximum_select_fusion.6), channel_id=1, source_target_pairs={{0,8},{8,0},{16,24},{24,16},{1,9},{9,1},{17,25},{25,17},{2,10},{10... | collective-permute-start | bytes 2555912 | tf_op jit(solution)/shard_map/ppermute | solution.py:86
  178.9 2.4 collective-permute-start.23
  179.2 1.1 copy-start.2
  211.7 16.4 %collective-permute-start.24 = (bf16[64,4096]{1,0:T(8,128)(2,1)S(1)}, bf16[64,4096]{1,0:T(8,128)(2,1)S(1)}, u32[]{:S(2)}, u32[]{:S(2)}) collective-permute-start(bf16[64,4096]{1,0:T(8,128)(2,1)S(1)} %constant_dynamic-slice_fusion.3), channel_id=1, source_target_pairs={{0,1},{1,0},{2,3},{3,2},{4,5},{5,4},{6,7},{7,6},{8,9},{9,8},{10,11... | collective-permute-start | bytes 1572872 | tf_op jit(solution)/shard_map/ppermute | solution.py:86
  215.4 14.9 %collective-permute-start.27 = (bf16[64,4096]{1,0:T(8,128)(2,1)S(1)}, bf16[64,4096]{1,0:T(8,128)(2,1)S(1)}, u32[]{:S(2)}, u32[]{:S(2)}) collective-permute-start(bf16[64,4096]{1,0:T(8,128)(2,1)S(1)} %constant_dynamic-slice_fusion.2), channel_id=1, source_target_pairs={{0,2},{1,3},{2,0},{3,1},{4,6},{5,7},{6,4},{7,5},{8,10},{9,11},{10,... | collective-permute-start | bytes 1572872 | tf_op jit(solution)/shard_map/ppermute | solution.py:86
  215.5 23.2 %collective-permute-start.30 = (bf16[64,4096]{1,0:T(8,128)(2,1)S(1)}, bf16[64,4096]{1,0:T(8,128)(2,1)S(1)}, u32[]{:S(2)}, u32[]{:S(2)}) collective-permute-start(bf16[64,4096]{1,0:T(8,128)(2,1)S(1)} %constant_dynamic-slice_fusion.1), channel_id=1, source_target_pairs={{0,1},{1,0},{2,3},{3,2},{4,5},{5,4},{6,7},{7,6},{8,9},{9,8},{10,11... | collective-permute-start | bytes 1572872 | tf_op jit(solution)/shard_map/ppermute | solution.py:86
  215.7 31.5 %collective-permute-start.33 = (bf16[64,4096]{1,0:T(8,128)(2,1)S(1)}, bf16[64,4096]{1,0:T(8,128)(2,1)S(1)}, u32[]{:S(2)}, u32[]{:S(2)}) collective-permute-start(bf16[64,4096]{1,0:T(8,128)(2,1)S(1)} %constant_dynamic-slice_fusion), channel_id=1, source_target_pairs={{0,2},{1,3},{2,0},{3,1},{4,6},{5,7},{6,4},{7,5},{8,10},{9,11},{10,... | collective-permute-start | bytes 1572872 | tf_op jit(solution)/shard_map/ppermute | solution.py:86
  228.3 30.1 %collective-permute-start.25 = (bf16[32,4096]{1,0:T(8,128)(2,1)S(1)}, bf16[32,4096]{1,0:T(8,128)(2,1)S(1)}, u32[]{:S(2)}, u32[]{:S(2)}) collective-permute-start(bf16[32,4096]{1,0:T(8,128)(2,1)S(1)} %dynamic-slice_convert_fusion.7), channel_id=1, source_target_pairs={{0,2},{1,3},{2,0},{3,1},{4,6},{5,7},{6,4},{7,5},{8,10},{9,11},{10,... | collective-permute-start | bytes 786440 | tf_op jit(solution)/shard_map/ppermute | solution.py:86
  230.5 28.0 %collective-permute-start.28 = (bf16[32,4096]{1,0:T(8,128)(2,1)S(1)}, bf16[32,4096]{1,0:T(8,128)(2,1)S(1)}, u32[]{:S(2)}, u32[]{:S(2)}) collective-permute-start(bf16[32,4096]{1,0:T(8,128)(2,1)S(1)} %dynamic-slice_convert_fusion.6), channel_id=1, source_target_pairs={{0,4},{1,5},{2,6},{3,7},{4,0},{5,1},{6,2},{7,3},{8,12},{9,13},{10,... | collective-permute-start | bytes 786440 | tf_op jit(solution)/shard_map/ppermute | solution.py:86
  238.9 24.0 %collective-permute-start.31 = (bf16[32,4096]{1,0:T(8,128)(2,1)S(1)}, bf16[32,4096]{1,0:T(8,128)(2,1)S(1)}, u32[]{:S(2)}, u32[]{:S(2)}) collective-permute-start(bf16[32,4096]{1,0:T(8,128)(2,1)S(1)} %dynamic-slice_convert_fusion.5), channel_id=1, source_target_pairs={{0,2},{1,3},{2,0},{3,1},{4,6},{5,7},{6,4},{7,5},{8,10},{9,11},{10,... | collective-permute-start | bytes 786440 | tf_op jit(solution)/shard_map/ppermute | solution.py:86
  247.3 22.0 %collective-permute-start.34 = (bf16[32,4096]{1,0:T(8,128)(2,1)S(1)}, bf16[32,4096]{1,0:T(8,128)(2,1)S(1)}, u32[]{:S(2)}, u32[]{:S(2)}) collective-permute-start(bf16[32,4096]{1,0:T(8,128)(2,1)S(1)} %dynamic-slice_convert_fusion.4), channel_id=1, source_target_pairs={{0,4},{1,5},{2,6},{3,7},{4,0},{5,1},{6,2},{7,3},{8,12},{9,13},{10,... | collective-permute-start | bytes 786440 | tf_op jit(solution)/shard_map/ppermute | solution.py:86
  258.4 13.7 %collective-permute-start.26 = (bf16[16,4096]{1,0:T(8,128)(2,1)S(1)}, bf16[16,4096]{1,0:T(8,128)(2,1)S(1)}, u32[]{:S(2)}, u32[]{:S(2)}) collective-permute-start(bf16[16,4096]{1,0:T(8,128)(2,1)S(1)} %dynamic-slice_convert_fusion.11), channel_id=1, source_target_pairs={{0,4},{1,5},{2,6},{3,7},{4,0},{5,1},{6,2},{7,3},{8,12},{9,13},{10,... | collective-permute-start | bytes 393224 | tf_op jit(solution)/shard_map/ppermute | solution.py:86
  258.6 15.6 %collective-permute-start.29 = (bf16[16,4096]{1,0:T(8,128)(2,1)S(1)}, bf16[16,4096]{1,0:T(8,128)(2,1)S(1)}, u32[]{:S(2)}, u32[]{:S(2)}) collective-permute-start(bf16[16,4096]{1,0:T(8,128)(2,1)S(1)} %dynamic-slice_convert_fusion.10), channel_id=1, source_target_pairs={{0,1},{1,0},{2,3},{3,2},{4,5},{5,4},{6,7},{7,6},{8,9},{9,8},{10,11... | collective-permute-start | bytes 393224 | tf_op jit(solution)/shard_map/ppermute | solution.py:86
  262.9 11.2 %collective-permute-start.32 = (bf16[16,4096]{1,0:T(8,128)(2,1)S(1)}, bf16[16,4096]{1,0:T(8,128)(2,1)S(1)}, u32[]{:S(2)}, u32[]{:S(2)}) collective-permute-start(bf16[16,4096]{1,0:T(8,128)(2,1)S(1)} %dynamic-slice_convert_fusion.9), channel_id=1, source_target_pairs={{0,4},{1,5},{2,6},{3,7},{4,0},{5,1},{6,2},{7,3},{8,12},{9,13},{10,... | collective-permute-start | bytes 393224 | tf_op jit(solution)/shard_map/ppermute | solution.py:86
  269.4 5.0 %collective-permute-start.35 = (bf16[16,4096]{1,0:T(8,128)(2,1)S(1)}, bf16[16,4096]{1,0:T(8,128)(2,1)S(1)}, u32[]{:S(2)}, u32[]{:S(2)}) collective-permute-start(bf16[16,4096]{1,0:T(8,128)(2,1)S(1)} %dynamic-slice_convert_fusion.8), channel_id=1, source_target_pairs={{0,1},{1,0},{2,3},{3,2},{4,5},{5,4},{6,7},{7,6},{8,9},{9,8},{10,11... | collective-permute-start | bytes 393224 | tf_op jit(solution)/shard_map/ppermute | solution.py:86

commit v10 on v6

--- a/solution.py
+++ b/solution.py
@@ -117,7 +117,7 @@
     n_col = lax.axis_size("col")
     row_bits = list(range(n_row.bit_length() - 1))
     top = n_col.bit_length() - 1
-    col_orders = [list(range(top - 1, -1, -1)), [0] + list(range(top - 1, 0, -1))]
+    col_orders = [list(range(top - 1, -1, -1)), [top - 1, 0] + list(range(top - 2, 0, -1))]
     quarter = tokens.shape[0] // 4
     orders = col_orders * 2
     token_parts = [tokens[q * quarter:(q + 1) * quarter] for q in range(4)]

time: 268 us -> 264 us (0.985)
  starting transfers between devices: 50.5 us -> 35.1 us
  waiting for transfers between devices: 123 us -> 135 us
    ppermute x36, starting transfers between devices: 50.5 us -> 35.1 us  [exchange(): return lax.ppermute(x, axis, perm=pairs)]
    ppermute x36, waiting for transfers between devices: 123 us -> 135 us  [exchange(): return lax.ppermute(x, axis, perm=pairs)]
  transfers between devices with their start and end apart: 36 -> 36, of which waited for: 21 -> 28; matrix products, arithmetic and copies ran while one was open for 4% -> 4% of each run, Pallas kernels for 0% -> 0%
where the time goes in v10:
time: 264 us; the launch traced here: 263 us
  waiting for transfers between devices  135 us (51%)
  Pallas kernels  69.2 us (26%)
  starting transfers between devices  35.1 us (13%)
  other arithmetic  12.2 us (5%)
  local copies, waits for them, and re-layouts  11.4 us (4%)
    ppermute x36, waiting for transfers between devices, exchange(): return lax.ppermute(x, axis, perm=pairs)  135 us
    pallas_call x2, Pallas kernels, sparse_matmul(): pl.pallas_call(kernel, grid_spec=pltpu.PrefetchScalarGridSpec(num_scalar_...  69.2 us
    ppermute x36, starting transfers between devices, exchange(): return lax.ppermute(x, axis, perm=pairs)  35.1 us
  transfers between devices with their start and end apart: 36, of which 28 were waited for; matrix products, arithmetic and copies ran while one was open for 4% of the time, Pallas kernels for 0%

profile of v10, /device:TPU:0, one launch (start us, length us, event | category | flops | bytes accessed | tf_op | source)
XLA Modules:
  0.0 263.5 jit_solution(14433870128545672187)
XLA Ops:
  0.0 1.1 fusion.6
  1.1 4.1 %collective-permute-start = (bf16[16,4096]{1,0:T(8,128)(2,1)S(1)}, bf16[16,4096]{1,0:T(8,128)(2,1)S(1)}, u32[]{:S(2)}, u32[]{:S(2)}) collective-permute-start(bf16[16,4096]{1,0:T(8,128)(2,1)S(1)} %get-tuple-element.17), channel_id=1, source_target_pairs={{0,4},{1,5},{2,6},{3,7},{4,0},{5,1},{6,2},{7,3},{8,12},{9,13},{10,... | collective-permute-start | bytes 393224 | tf_op jit(solution)/shard_map/ppermute | solution.py:85
  5.3 2.8 %collective-permute-start.6 = (bf16[16,4096]{1,0:T(8,128)(2,1)S(1)}, bf16[16,4096]{1,0:T(8,128)(2,1)S(1)}, u32[]{:S(2)}, u32[]{:S(2)}) collective-permute-start(bf16[16,4096]{1,0:T(8,128)(2,1)S(1)} %get-tuple-element.20), channel_id=1, source_target_pairs={{0,4},{1,5},{2,6},{3,7},{4,0},{5,1},{6,2},{7,3},{8,12},{9,13},{10,... | collective-permute-start | bytes 393224 | tf_op jit(solution)/shard_map/ppermute | solution.py:85
  8.2 0.8 reshape.58
  9.0 0.8 reshape.64
  10.5 0.7 sub.27
  11.4 0.8 subtract_select_fusion
  12.6 0.7 reshape.68.index_ref
  13.6 7.2 %collective-permute-done = bf16[16,4096]{1,0:T(8,128)(2,1)S(1)} collective-permute-done((bf16[16,4096]{1,0:T(8,128)(2,1)S(1)}, bf16[16,4096]{1,0:T(8,128)(2,1)S(1)}, u32[]{:S(2)}, u32[]{:S(2)}) %collective-permute-start) | collective-permute-done | bytes 131104 | tf_op jit(solution)/shard_map/ppermute | solution.py:85
  20.9 2.8 %collective-permute-done.3 = bf16[16,4096]{1,0:T(8,128)(2,1)S(1)} collective-permute-done((bf16[16,4096]{1,0:T(8,128)(2,1)S(1)}, bf16[16,4096]{1,0:T(8,128)(2,1)S(1)}, u32[]{:S(2)}, u32[]{:S(2)}) %collective-permute-start.3) | collective-permute-done | bytes 131104 | tf_op jit(solution)/shard_map/ppermute | solution.py:85
  23.8 1.9 collective-permute-start.4
  25.7 0.9 collective-permute-done.6
  26.6 1.9 collective-permute-done.9
  28.5 1.6 collective-permute-start.10
  30.2 4.0 %collective-permute-done.1 = bf16[32,4096]{1,0:T(8,128)(2,1)S(1)} collective-permute-done((bf16[32,4096]{1,0:T(8,128)(2,1)S(1)}, bf16[32,4096]{1,0:T(8,128)(2,1)S(1)}, u32[]{:S(2)}, u32[]{:S(2)}) %collective-permute-start.1) | collective-permute-done | bytes 262176 | tf_op jit(solution)/shard_map/ppermute | solution.py:85
  34.2 1.6 collective-permute-start.2
  36.0 3.7 %collective-permute-done.7 = bf16[32,4096]{1,0:T(8,128)(2,1)S(1)} collective-permute-done((bf16[32,4096]{1,0:T(8,128)(2,1)S(1)}, bf16[32,4096]{1,0:T(8,128)(2,1)S(1)}, u32[]{:S(2)}, u32[]{:S(2)}) %collective-permute-start.7) | collective-permute-done | bytes 262176 | tf_op jit(solution)/shard_map/ppermute | solution.py:85
  39.8 1.6 collective-permute-start.8
  41.6 7.5 %collective-permute-done.2 = bf16[64,4096]{1,0:T(8,128)(2,1)S(1)} collective-permute-done((bf16[64,4096]{1,0:T(8,128)(2,1)S(1)}, bf16[64,4096]{1,0:T(8,128)(2,1)S(1)}, u32[]{:S(2)}, u32[]{:S(2)}) %collective-permute-start.2) | collective-permute-done | bytes 524320 | tf_op jit(solution)/shard_map/ppermute | solution.py:85
  49.3 1.7 collective-permute-done.5
  51.2 8.1 %collective-permute-done.8 = bf16[64,4096]{1,0:T(8,128)(2,1)S(1)} collective-permute-done((bf16[64,4096]{1,0:T(8,128)(2,1)S(1)}, bf16[64,4096]{1,0:T(8,128)(2,1)S(1)}, u32[]{:S(2)}, u32[]{:S(2)}) %collective-permute-start.8) | collective-permute-done | bytes 524320 | tf_op jit(solution)/shard_map/ppermute | solution.py:85
  59.5 2.6 %collective-permute-done.11 = bf16[64,4096]{1,0:T(8,128)(2,1)S(1)} collective-permute-done((bf16[64,4096]{1,0:T(8,128)(2,1)S(1)}, bf16[64,4096]{1,0:T(8,128)(2,1)S(1)}, u32[]{:S(2)}, u32[]{:S(2)}) %collective-permute-start.11) | collective-permute-done | bytes 524320 | tf_op jit(solution)/shard_map/ppermute | solution.py:85
  62.3 2.5 pad_maximum_fusion.x_ref
  64.8 43.4 %shard_map.64 = (bf16[512,3328]{1,0:T(8,128)(2,1)}, bf16[512,3328]{1,0:T(8,128)(2,1)}) custom-call(s32[32]{0:T(128)} %copy-done.2, s32[832]{0:T(1024)} %reshape.68.index_ref, bf16[512,4096]{1,0:T(8,128)(2,1)} %pad_maximum_fusion.x_ref, bf16[640,128,128]{2,1,0:T(8,128)(2,1)} %refs_3_.1, bf16[640,128,128]{2,1,0:T(8,128)(2,1)} %refs_3_.1, ...), custom_call_target="tpu_custom_call" | custom-call | flops 27917287424 | bytes 65536000 | tf_op jit(solution)/shard_map/pallas_call | solution.py:66
  108.2 2.3 fusion.4
  110.7 0.5 copy-done
  111.6 0.5 collective-permute-start.18
  112.3 0.7 collective-permute-done.12
  113.3 1.6 collective-permute-start.13
  115.2 1.0 collective-permute-start.15
  116.4 1.2 collective-permute-start.19
  117.8 1.0 collective-permute-start.21
  118.8 7.2 %collective-permute-done.13 = bf16[64,3328]{1,0:T(8,128)(2,1)S(1)} collective-permute-done((bf16[64,3328]{1,0:T(8,128)(2,1)S(1)}, bf16[64,3328]{1,0:T(8,128)(2,1)S(1)}, u32[]{:S(2)}, u32[]{:S(2)}) %collective-permute-start.13) | collective-permute-done | bytes 426016 | tf_op jit(solution)/shard_map/ppermute | solution.py:85
  126.0 9.1 %collective-permute-done.15 = bf16[64,3328]{1,0:T(8,128)(2,1)S(1)} collective-permute-done((bf16[64,3328]{1,0:T(8,128)(2,1)S(1)}, bf16[64,3328]{1,0:T(8,128)(2,1)S(1)}, u32[]{:S(2)}, u32[]{:S(2)}) %collective-permute-start.15) | collective-permute-done | bytes 426016 | tf_op jit(solution)/shard_map/ppermute | solution.py:85
  135.5 1.6 collective-permute-start.16
  137.1 7.2 %collective-permute-done.19 = bf16[64,3328]{1,0:T(8,128)(2,1)S(1)} collective-permute-done((bf16[64,3328]{1,0:T(8,128)(2,1)S(1)}, bf16[64,3328]{1,0:T(8,128)(2,1)S(1)}, u32[]{:S(2)}, u32[]{:S(2)}) %collective-permute-start.19) | collective-permute-done | bytes 426016 | tf_op jit(solution)/shard_map/ppermute | solution.py:85
  144.3 9.1 %collective-permute-done.21 = bf16[64,3328]{1,0:T(8,128)(2,1)S(1)} collective-permute-done((bf16[64,3328]{1,0:T(8,128)(2,1)S(1)}, bf16[64,3328]{1,0:T(8,128)(2,1)S(1)}, u32[]{:S(2)}, u32[]{:S(2)}) %collective-permute-start.21) | collective-permute-done | bytes 426016 | tf_op jit(solution)/shard_map/ppermute | solution.py:85
  153.7 1.6 collective-permute-start.22
  155.4 7.2 %collective-permute-done.16 = bf16[64,3328]{1,0:T(8,128)(2,1)S(1)} collective-permute-done((bf16[64,3328]{1,0:T(8,128)(2,1)S(1)}, bf16[64,3328]{1,0:T(8,128)(2,1)S(1)}, u32[]{:S(2)}, u32[]{:S(2)}) %collective-permute-start.16) | collective-permute-done | bytes 426016 | tf_op jit(solution)/shard_map/ppermute | solution.py:85
  162.8 8.1 %collective-permute-done.22 = bf16[64,3328]{1,0:T(8,128)(2,1)S(1)} collective-permute-done((bf16[64,3328]{1,0:T(8,128)(2,1)S(1)}, bf16[64,3328]{1,0:T(8,128)(2,1)S(1)}, u32[]{:S(2)}, u32[]{:S(2)}) %collective-permute-start.22) | collective-permute-done | bytes 426016 | tf_op jit(solution)/shard_map/ppermute | solution.py:85
  171.4 0.7 reshape.63.index_ref
  172.4 1.1 collective-permute-done.23
  173.8 1.9 pad_maximum_fusion.1.x_ref
  175.7 25.8 %shard_map.65 = bf16[512,4096]{1,0:T(8,128)(2,1)} custom-call(s32[26]{0:T(128)} %copy-done.3, s32[832]{0:T(1024)} %reshape.63.index_ref, bf16[512,3328]{1,0:T(8,128)(2,1)} %pad_maximum_fusion.1.x_ref, bf16[640,128,128]{2,1,0:T(8,128)(2,1)} %refs_1_.3, bf16[640,128,128]{2,1,0:T(8,128)(2,1)} %refs_1_.3), custom_call_target="tpu_custom_call" | custom-call | flops 13958643712 | bytes 34865152 | tf_op jit(solution)/shard_map/pallas_call | solution.py:66
  201.5 2.7 %fusion.3 = (bf16[128,4096]{1,0:T(8,128)(2,1)S(1)}, bf16[128,4096]{1,0:T(8,128)(2,1)S(1)}, bf16[128,4096]{1,0:T(8,128)(2,1)S(1)}, bf16[128,4096]{1,0:T(8,128)(2,1)S(1)}) fusion(bf16[512,4096]{1,0:T(8,128)(2,1)} %shard_map.65), kind=kLoop, calls=%fused_computation.70 | loop fusion | bytes 8388608 | tf_op jit(solution)/shard_map/slice | solution.py:136
  204.2 1.4 collective-permute-start.24
  205.8 0.7 collective-permute-start.30
  206.6 2.1 collective-permute-start.33
  208.6 10.4 %collective-permute-done.24 = bf16[64,4096]{1,0:T(8,128)(2,1)S(1)} collective-permute-done((bf16[64,4096]{1,0:T(8,128)(2,1)S(1)}, bf16[64,4096]{1,0:T(8,128)(2,1)S(1)}, u32[]{:S(2)}, u32[]{:S(2)}) %collective-permute-start.24) | collective-permute-done | bytes 524320 | tf_op jit(solution)/shard_map/ppermute | solution.py:85
  219.3 1.3 collective-permute-done.27
  220.7 0.7 collective-permute-start.28
  221.5 8.8 %collective-permute-done.30 = bf16[64,4096]{1,0:T(8,128)(2,1)S(1)} collective-permute-done((bf16[64,4096]{1,0:T(8,128)(2,1)S(1)}, bf16[64,4096]{1,0:T(8,128)(2,1)S(1)}, u32[]{:S(2)}, u32[]{:S(2)}) %collective-permute-start.30) | collective-permute-done | bytes 524320 | tf_op jit(solution)/shard_map/ppermute | solution.py:85
  230.5 1.3 collective-permute-done.33
  232.0 0.7 collective-permute-start.34
  232.7 4.7 %collective-permute-done.25 = bf16[32,4096]{1,0:T(8,128)(2,1)S(1)} collective-permute-done((bf16[32,4096]{1,0:T(8,128)(2,1)S(1)}, bf16[32,4096]{1,0:T(8,128)(2,1)S(1)}, u32[]{:S(2)}, u32[]{:S(2)}) %collective-permute-start.25) | collective-permute-done | bytes 262176 | tf_op jit(solution)/shard_map/ppermute | solution.py:85
  237.5 2.1 collective-permute-start.26
  239.7 0.9 collective-permute-start.29
  240.6 5.0 %collective-permute-done.31 = bf16[32,4096]{1,0:T(8,128)(2,1)S(1)} collective-permute-done((bf16[32,4096]{1,0:T(8,128)(2,1)S(1)}, bf16[32,4096]{1,0:T(8,128)(2,1)S(1)}, u32[]{:S(2)}, u32[]{:S(2)}) %collective-permute-start.31) | collective-permute-done | bytes 262176 | tf_op jit(solution)/shard_map/ppermute | solution.py:85
  245.9 3.0 %collective-permute-start.35 = (bf16[16,4096]{1,0:T(8,128)(2,1)S(1)}, bf16[16,4096]{1,0:T(8,128)(2,1)S(1)}, u32[]{:S(2)}, u32[]{:S(2)}) collective-permute-start(bf16[16,4096]{1,0:T(8,128)(2,1)S(1)} %dynamic-slice_convert_fusion.8), channel_id=1, source_target_pairs={{0,4},{1,5},{2,6},{3,7},{4,0},{5,1},{6,2},{7,3},{8,12},{9,13},{10,... | collective-permute-start | bytes 393224 | tf_op jit(solution)/shard_map/ppermute | solution.py:85
  248.9 7.2 %collective-permute-done.26 = bf16[16,4096]{1,0:T(8,128)(2,1)S(1)} collective-permute-done((bf16[16,4096]{1,0:T(8,128)(2,1)S(1)}, bf16[16,4096]{1,0:T(8,128)(2,1)S(1)}, u32[]{:S(2)}, u32[]{:S(2)}) %collective-permute-start.26) | collective-permute-done | bytes 131104 | tf_op jit(solution)/shard_map/ppermute | solution.py:85
  256.1 2.8 %collective-permute-done.29 = bf16[16,4096]{1,0:T(8,128)(2,1)S(1)} collective-permute-done((bf16[16,4096]{1,0:T(8,128)(2,1)S(1)}, bf16[16,4096]{1,0:T(8,128)(2,1)S(1)}, u32[]{:S(2)}, u32[]{:S(2)}) %collective-permute-start.29) | collective-permute-done | bytes 131104 | tf_op jit(solution)/shard_map/ppermute | solution.py:85
  258.9 2.3 collective-permute-done.32
  261.2 1.4 collective-permute-done.35
  262.6 0.8 pad_maximum_fusion.2
  (103 shorter events, 8.4 us)
Async XLA Ops:
  1.1 19.7 %collective-permute-start = (bf16[16,4096]{1,0:T(8,128)(2,1)S(1)}, bf16[16,4096]{1,0:T(8,128)(2,1)S(1)}, u32[]{:S(2)}, u32[]{:S(2)}) collective-permute-start(bf16[16,4096]{1,0:T(8,128)(2,1)S(1)} %get-tuple-element.17), channel_id=1, source_target_pairs={{0,4},{1,5},{2,6},{3,7},{4,0},{5,1},{6,2},{7,3},{8,12},{9,13},{10,... | collective-permute-start | bytes 393224 | tf_op jit(solution)/shard_map/ppermute | solution.py:85
  5.2 18.5 %collective-permute-start.3 = (bf16[16,4096]{1,0:T(8,128)(2,1)S(1)}, bf16[16,4096]{1,0:T(8,128)(2,1)S(1)}, u32[]{:S(2)}, u32[]{:S(2)}) collective-permute-start(bf16[16,4096]{1,0:T(8,128)(2,1)S(1)} %get-tuple-element.18), channel_id=1, source_target_pairs={{0,4},{1,5},{2,6},{3,7},{4,0},{5,1},{6,2},{7,3},{8,12},{9,13},{10,... | collective-permute-start | bytes 393224 | tf_op jit(solution)/shard_map/ppermute | solution.py:85
  5.3 21.2 %collective-permute-start.6 = (bf16[16,4096]{1,0:T(8,128)(2,1)S(1)}, bf16[16,4096]{1,0:T(8,128)(2,1)S(1)}, u32[]{:S(2)}, u32[]{:S(2)}) collective-permute-start(bf16[16,4096]{1,0:T(8,128)(2,1)S(1)} %get-tuple-element.20), channel_id=1, source_target_pairs={{0,4},{1,5},{2,6},{3,7},{4,0},{5,1},{6,2},{7,3},{8,12},{9,13},{10,... | collective-permute-start | bytes 393224 | tf_op jit(solution)/shard_map/ppermute | solution.py:85
  8.2 20.3 %collective-permute-start.9 = (bf16[16,4096]{1,0:T(8,128)(2,1)S(1)}, bf16[16,4096]{1,0:T(8,128)(2,1)S(1)}, u32[]{:S(2)}, u32[]{:S(2)}) collective-permute-start(bf16[16,4096]{1,0:T(8,128)(2,1)S(1)} %get-tuple-element.19), channel_id=1, source_target_pairs={{0,4},{1,5},{2,6},{3,7},{4,0},{5,1},{6,2},{7,3},{8,12},{9,13},{10,... | collective-permute-start | bytes 393224 | tf_op jit(solution)/shard_map/ppermute | solution.py:85
  11.4 24.5 %copy-start.2 = (s32[32]{0:T(128)}, s32[32]{0:T(128)S(1)}, u32[]{:S(2)}) copy-start(s32[32]{0:T(128)S(1)} %fusion.base_ref) | copy-start | bytes 388
  20.8 13.3 %collective-permute-start.1 = (bf16[32,4096]{1,0:T(8,128)(2,1)S(1)}, bf16[32,4096]{1,0:T(8,128)(2,1)S(1)}, u32[]{:S(2)}, u32[]{:S(2)}) collective-permute-start(bf16[32,4096]{1,0:T(8,128)(2,1)S(1)} %maximum_select_fusion.12), channel_id=1, source_target_pairs={{0,2},{1,3},{2,0},{3,1},{4,6},{5,7},{6,4},{7,5},{8,10},{9,11},{10,... | collective-permute-start | bytes 786440 | tf_op jit(solution)/shard_map/ppermute | solution.py:85
  23.8 12.1 %collective-permute-start.4 = (bf16[32,4096]{1,0:T(8,128)(2,1)S(1)}, bf16[32,4096]{1,0:T(8,128)(2,1)S(1)}, u32[]{:S(2)}, u32[]{:S(2)}) collective-permute-start(bf16[32,4096]{1,0:T(8,128)(2,1)S(1)} %maximum_select_fusion.13), channel_id=1, source_target_pairs={{0,1},{1,0},{2,3},{3,2},{4,5},{5,4},{6,7},{7,6},{8,9},{9,8},{10,11... | collective-permute-start | bytes 786440 | tf_op jit(solution)/shard_map/ppermute | solution.py:85
  26.6 13.2 %collective-permute-start.7 = (bf16[32,4096]{1,0:T(8,128)(2,1)S(1)}, bf16[32,4096]{1,0:T(8,128)(2,1)S(1)}, u32[]{:S(2)}, u32[]{:S(2)}) collective-permute-start(bf16[32,4096]{1,0:T(8,128)(2,1)S(1)} %maximum_select_fusion.14), channel_id=1, source_target_pairs={{0,2},{1,3},{2,0},{3,1},{4,6},{5,7},{6,4},{7,5},{8,10},{9,11},{10,... | collective-permute-start | bytes 786440 | tf_op jit(solution)/shard_map/ppermute | solution.py:85
  28.5 12.9 %collective-permute-start.10 = (bf16[32,4096]{1,0:T(8,128)(2,1)S(1)}, bf16[32,4096]{1,0:T(8,128)(2,1)S(1)}, u32[]{:S(2)}, u32[]{:S(2)}) collective-permute-start(bf16[32,4096]{1,0:T(8,128)(2,1)S(1)} %maximum_select_fusion.15), channel_id=1, source_target_pairs={{0,1},{1,0},{2,3},{3,2},{4,5},{5,4},{6,7},{7,6},{8,9},{9,8},{10,11... | collective-permute-start | bytes 786440 | tf_op jit(solution)/shard_map/ppermute | solution.py:85
  34.2 14.9 %collective-permute-start.2 = (bf16[64,4096]{1,0:T(8,128)(2,1)S(1)}, bf16[64,4096]{1,0:T(8,128)(2,1)S(1)}, u32[]{:S(2)}, u32[]{:S(2)}) collective-permute-start(bf16[64,4096]{1,0:T(8,128)(2,1)S(1)} %maximum_select_fusion.8), channel_id=1, source_target_pairs={{0,1},{1,0},{2,3},{3,2},{4,5},{5,4},{6,7},{7,6},{8,9},{9,8},{10,11... | collective-permute-start | bytes 1572872 | tf_op jit(solution)/shard_map/ppermute | solution.py:85
  35.9 15.0 %collective-permute-start.5 = (bf16[64,4096]{1,0:T(8,128)(2,1)S(1)}, bf16[64,4096]{1,0:T(8,128)(2,1)S(1)}, u32[]{:S(2)}, u32[]{:S(2)}) collective-permute-start(bf16[64,4096]{1,0:T(8,128)(2,1)S(1)} %maximum_select_fusion.9), channel_id=1, source_target_pairs={{0,2},{1,3},{2,0},{3,1},{4,6},{5,7},{6,4},{7,5},{8,10},{9,11},{10,... | collective-permute-start | bytes 1572872 | tf_op jit(solution)/shard_map/ppermute | solution.py:85
  39.8 19.4 %collective-permute-start.8 = (bf16[64,4096]{1,0:T(8,128)(2,1)S(1)}, bf16[64,4096]{1,0:T(8,128)(2,1)S(1)}, u32[]{:S(2)}, u32[]{:S(2)}) collective-permute-start(bf16[64,4096]{1,0:T(8,128)(2,1)S(1)} %maximum_select_fusion.10), channel_id=1, source_target_pairs={{0,1},{1,0},{2,3},{3,2},{4,5},{5,4},{6,7},{7,6},{8,9},{9,8},{10,11... | collective-permute-start | bytes 1572872 | tf_op jit(solution)/shard_map/ppermute | solution.py:85
  41.5 20.6 %collective-permute-start.11 = (bf16[64,4096]{1,0:T(8,128)(2,1)S(1)}, bf16[64,4096]{1,0:T(8,128)(2,1)S(1)}, u32[]{:S(2)}, u32[]{:S(2)}) collective-permute-start(bf16[64,4096]{1,0:T(8,128)(2,1)S(1)} %maximum_select_fusion.11), channel_id=1, source_target_pairs={{0,2},{1,3},{2,0},{3,1},{4,6},{5,7},{6,4},{7,5},{8,10},{9,11},{10,... | collective-permute-start | bytes 1572872 | tf_op jit(solution)/shard_map/ppermute | solution.py:85
  108.2 3.0 %copy-start = (bf16[512,3328]{1,0:T(8,128)(2,1)S(1)}, bf16[512,3328]{1,0:T(8,128)(2,1)}, u32[]{:S(2)}) copy-start(bf16[512,3328]{1,0:T(8,128)(2,1)} %get-tuple-element.8) | copy-start | bytes 10223620
  110.6 2.4 collective-permute-start.12
  111.5 3.4 %collective-permute-start.14 = (bf16[128,3328]{1,0:T(8,128)(2,1)S(1)}, bf16[128,3328]{1,0:T(8,128)(2,1)S(1)}, u32[]{:S(2)}, u32[]{:S(2)}) collective-permute-start(bf16[128,3328]{1,0:T(8,128)(2,1)S(1)} %constant_dynamic-slice_fusion.6), channel_id=1, source_target_pairs={{0,8},{8,0},{16,24},{24,16},{1,9},{9,1},{17,25},{25,17},{2,10},{10... | collective-permute-start | bytes 2555912 | tf_op jit(solution)/shard_map/ppermute | solution.py:85
  111.6 4.5 %collective-permute-start.18 = (bf16[128,3328]{1,0:T(8,128)(2,1)S(1)}, bf16[128,3328]{1,0:T(8,128)(2,1)S(1)}, u32[]{:S(2)}, u32[]{:S(2)}) collective-permute-start(bf16[128,3328]{1,0:T(8,128)(2,1)S(1)} %constant_dynamic-slice_fusion.5), channel_id=1, source_target_pairs={{0,8},{8,0},{16,24},{24,16},{1,9},{9,1},{17,25},{25,17},{2,10},{10... | collective-permute-start | bytes 2555912 | tf_op jit(solution)/shard_map/ppermute | solution.py:85
  112.2 5.3 %collective-permute-start.20 = (bf16[128,3328]{1,0:T(8,128)(2,1)S(1)}, bf16[128,3328]{1,0:T(8,128)(2,1)S(1)}, u32[]{:S(2)}, u32[]{:S(2)}) collective-permute-start(bf16[128,3328]{1,0:T(8,128)(2,1)S(1)} %constant_dynamic-slice_fusion.4), channel_id=1, source_target_pairs={{0,8},{8,0},{16,24},{24,16},{1,9},{9,1},{17,25},{25,17},{2,10},{10... | collective-permute-start | bytes 2555912 | tf_op jit(solution)/shard_map/ppermute | solution.py:85
  113.3 12.7 %collective-permute-start.13 = (bf16[64,3328]{1,0:T(8,128)(2,1)S(1)}, bf16[64,3328]{1,0:T(8,128)(2,1)S(1)}, u32[]{:S(2)}, u32[]{:S(2)}) collective-permute-start(bf16[64,3328]{1,0:T(8,128)(2,1)S(1)} %dynamic-slice_convert_fusion.3), channel_id=1, source_target_pairs={{0,16},{8,24},{16,0},{24,8},{1,17},{9,25},{17,1},{25,9},{2,18},{10... | collective-permute-start | bytes 1277960 | tf_op jit(solution)/shard_map/ppermute | solution.py:85
  115.2 20.0 %collective-permute-start.15 = (bf16[64,3328]{1,0:T(8,128)(2,1)S(1)}, bf16[64,3328]{1,0:T(8,128)(2,1)S(1)}, u32[]{:S(2)}, u32[]{:S(2)}) collective-permute-start(bf16[64,3328]{1,0:T(8,128)(2,1)S(1)} %dynamic-slice_convert_fusion.2), channel_id=1, source_target_pairs={{0,16},{8,24},{16,0},{24,8},{1,17},{9,25},{17,1},{25,9},{2,18},{10... | collective-permute-start | bytes 1277960 | tf_op jit(solution)/shard_map/ppermute | solution.py:85
  116.4 27.9 %collective-permute-start.19 = (bf16[64,3328]{1,0:T(8,128)(2,1)S(1)}, bf16[64,3328]{1,0:T(8,128)(2,1)S(1)}, u32[]{:S(2)}, u32[]{:S(2)}) collective-permute-start(bf16[64,3328]{1,0:T(8,128)(2,1)S(1)} %dynamic-slice_convert_fusion.1), channel_id=1, source_target_pairs={{0,16},{8,24},{16,0},{24,8},{1,17},{9,25},{17,1},{25,9},{2,18},{10... | collective-permute-start | bytes 1277960 | tf_op jit(solution)/shard_map/ppermute | solution.py:85
  117.8 35.6 %collective-permute-start.21 = (bf16[64,3328]{1,0:T(8,128)(2,1)S(1)}, bf16[64,3328]{1,0:T(8,128)(2,1)S(1)}, u32[]{:S(2)}, u32[]{:S(2)}) collective-permute-start(bf16[64,3328]{1,0:T(8,128)(2,1)S(1)} %dynamic-slice_convert_fusion), channel_id=1, source_target_pairs={{0,16},{8,24},{16,0},{24,8},{1,17},{9,25},{17,1},{25,9},{2,18},{10... | collective-permute-start | bytes 1277960 | tf_op jit(solution)/shard_map/ppermute | solution.py:85
  135.5 27.1 %collective-permute-start.16 = (bf16[64,3328]{1,0:T(8,128)(2,1)S(1)}, bf16[64,3328]{1,0:T(8,128)(2,1)S(1)}, u32[]{:S(2)}, u32[]{:S(2)}) collective-permute-start(bf16[64,3328]{1,0:T(8,128)(2,1)S(1)} %multiply_convert_fusion.1), channel_id=1, source_target_pairs={{0,16},{8,24},{16,0},{24,8},{1,17},{9,25},{17,1},{25,9},{2,18},{10... | collective-permute-start | bytes 1277960 | tf_op jit(solution)/shard_map/ppermute | solution.py:85
  153.7 17.4 %copy-start.1 = (s32[26,32]{1,0:T(8,128)S(1)}, s32[26,32]{1,0:T(8,128)}, u32[]{:S(2)}) copy-start(s32[26,32]{1,0:T(8,128)} %param.11) | copy-start | bytes 9988
  153.7 17.1 %collective-permute-start.22 = (bf16[64,3328]{1,0:T(8,128)(2,1)S(1)}, bf16[64,3328]{1,0:T(8,128)(2,1)S(1)}, u32[]{:S(2)}, u32[]{:S(2)}) collective-permute-start(bf16[64,3328]{1,0:T(8,128)(2,1)S(1)} %multiply_convert_fusion), channel_id=1, source_target_pairs={{0,16},{8,24},{16,0},{24,8},{1,17},{9,25},{17,1},{25,9},{2,18},{10... | collective-permute-start | bytes 1277960 | tf_op jit(solution)/shard_map/ppermute | solution.py:85
  162.7 9.3 %collective-permute-start.17 = (bf16[128,3328]{1,0:T(8,128)(2,1)S(1)}, bf16[128,3328]{1,0:T(8,128)(2,1)S(1)}, u32[]{:S(2)}, u32[]{:S(2)}) collective-permute-start(bf16[128,3328]{1,0:T(8,128)(2,1)S(1)} %maximum_select_fusion.6), channel_id=1, source_target_pairs={{0,8},{8,0},{16,24},{24,16},{1,9},{9,1},{17,25},{25,17},{2,10},{10... | collective-permute-start | bytes 2555912 | tf_op jit(solution)/shard_map/ppermute | solution.py:85
  171.0 2.4 collective-permute-start.23
  171.3 1.1 copy-start.3
  204.2 14.9 %collective-permute-start.24 = (bf16[64,4096]{1,0:T(8,128)(2,1)S(1)}, bf16[64,4096]{1,0:T(8,128)(2,1)S(1)}, u32[]{:S(2)}, u32[]{:S(2)}) collective-permute-start(bf16[64,4096]{1,0:T(8,128)(2,1)S(1)} %constant_dynamic-slice_fusion.3), channel_id=1, source_target_pairs={{0,1},{1,0},{2,3},{3,2},{4,5},{5,4},{6,7},{7,6},{8,9},{9,8},{10,11... | collective-permute-start | bytes 1572872 | tf_op jit(solution)/shard_map/ppermute | solution.py:85
  205.7 14.9 %collective-permute-start.27 = (bf16[64,4096]{1,0:T(8,128)(2,1)S(1)}, bf16[64,4096]{1,0:T(8,128)(2,1)S(1)}, u32[]{:S(2)}, u32[]{:S(2)}) collective-permute-start(bf16[64,4096]{1,0:T(8,128)(2,1)S(1)} %constant_dynamic-slice_fusion.2), channel_id=1, source_target_pairs={{0,2},{1,3},{2,0},{3,1},{4,6},{5,7},{6,4},{7,5},{8,10},{9,11},{10,... | collective-permute-start | bytes 1572872 | tf_op jit(solution)/shard_map/ppermute | solution.py:85
  205.8 24.5 %collective-permute-start.30 = (bf16[64,4096]{1,0:T(8,128)(2,1)S(1)}, bf16[64,4096]{1,0:T(8,128)(2,1)S(1)}, u32[]{:S(2)}, u32[]{:S(2)}) collective-permute-start(bf16[64,4096]{1,0:T(8,128)(2,1)S(1)} %constant_dynamic-slice_fusion.1), channel_id=1, source_target_pairs={{0,1},{1,0},{2,3},{3,2},{4,5},{5,4},{6,7},{7,6},{8,9},{9,8},{10,11... | collective-permute-start | bytes 1572872 | tf_op jit(solution)/shard_map/ppermute | solution.py:85
  206.6 25.2 %collective-permute-start.33 = (bf16[64,4096]{1,0:T(8,128)(2,1)S(1)}, bf16[64,4096]{1,0:T(8,128)(2,1)S(1)}, u32[]{:S(2)}, u32[]{:S(2)}) collective-permute-start(bf16[64,4096]{1,0:T(8,128)(2,1)S(1)} %constant_dynamic-slice_fusion), channel_id=1, source_target_pairs={{0,2},{1,3},{2,0},{3,1},{4,6},{5,7},{6,4},{7,5},{8,10},{9,11},{10,... | collective-permute-start | bytes 1572872 | tf_op jit(solution)/shard_map/ppermute | solution.py:85
  219.2 18.2 %collective-permute-start.25 = (bf16[32,4096]{1,0:T(8,128)(2,1)S(1)}, bf16[32,4096]{1,0:T(8,128)(2,1)S(1)}, u32[]{:S(2)}, u32[]{:S(2)}) collective-permute-start(bf16[32,4096]{1,0:T(8,128)(2,1)S(1)} %dynamic-slice_convert_fusion.7), channel_id=1, source_target_pairs={{0,2},{1,3},{2,0},{3,1},{4,6},{5,7},{6,4},{7,5},{8,10},{9,11},{10,... | collective-permute-start | bytes 786440 | tf_op jit(solution)/shard_map/ppermute | solution.py:85
  220.7 18.9 %collective-permute-start.28 = (bf16[32,4096]{1,0:T(8,128)(2,1)S(1)}, bf16[32,4096]{1,0:T(8,128)(2,1)S(1)}, u32[]{:S(2)}, u32[]{:S(2)}) collective-permute-start(bf16[32,4096]{1,0:T(8,128)(2,1)S(1)} %dynamic-slice_convert_fusion.6), channel_id=1, source_target_pairs={{0,1},{1,0},{2,3},{3,2},{4,5},{5,4},{6,7},{7,6},{8,9},{9,8},{10,11... | collective-permute-start | bytes 786440 | tf_op jit(solution)/shard_map/ppermute | solution.py:85
  230.5 15.2 %collective-permute-start.31 = (bf16[32,4096]{1,0:T(8,128)(2,1)S(1)}, bf16[32,4096]{1,0:T(8,128)(2,1)S(1)}, u32[]{:S(2)}, u32[]{:S(2)}) collective-permute-start(bf16[32,4096]{1,0:T(8,128)(2,1)S(1)} %dynamic-slice_convert_fusion.5), channel_id=1, source_target_pairs={{0,2},{1,3},{2,0},{3,1},{4,6},{5,7},{6,4},{7,5},{8,10},{9,11},{10,... | collective-permute-start | bytes 786440 | tf_op jit(solution)/shard_map/ppermute | solution.py:85
  232.0 13.9 %collective-permute-start.34 = (bf16[32,4096]{1,0:T(8,128)(2,1)S(1)}, bf16[32,4096]{1,0:T(8,128)(2,1)S(1)}, u32[]{:S(2)}, u32[]{:S(2)}) collective-permute-start(bf16[32,4096]{1,0:T(8,128)(2,1)S(1)} %dynamic-slice_convert_fusion.4), channel_id=1, source_target_pairs={{0,1},{1,0},{2,3},{3,2},{4,5},{5,4},{6,7},{7,6},{8,9},{9,8},{10,11... | collective-permute-start | bytes 786440 | tf_op jit(solution)/shard_map/ppermute | solution.py:85
  237.5 18.5 %collective-permute-start.26 = (bf16[16,4096]{1,0:T(8,128)(2,1)S(1)}, bf16[16,4096]{1,0:T(8,128)(2,1)S(1)}, u32[]{:S(2)}, u32[]{:S(2)}) collective-permute-start(bf16[16,4096]{1,0:T(8,128)(2,1)S(1)} %dynamic-slice_convert_fusion.11), channel_id=1, source_target_pairs={{0,4},{1,5},{2,6},{3,7},{4,0},{5,1},{6,2},{7,3},{8,12},{9,13},{10,... | collective-permute-start | bytes 393224 | tf_op jit(solution)/shard_map/ppermute | solution.py:85
  239.7 19.1 %collective-permute-start.29 = (bf16[16,4096]{1,0:T(8,128)(2,1)S(1)}, bf16[16,4096]{1,0:T(8,128)(2,1)S(1)}, u32[]{:S(2)}, u32[]{:S(2)}) collective-permute-start(bf16[16,4096]{1,0:T(8,128)(2,1)S(1)} %dynamic-slice_convert_fusion.10), channel_id=1, source_target_pairs={{0,4},{1,5},{2,6},{3,7},{4,0},{5,1},{6,2},{7,3},{8,12},{9,13},{10,... | collective-permute-start | bytes 393224 | tf_op jit(solution)/shard_map/ppermute | solution.py:85
  245.7 15.5 %collective-permute-start.32 = (bf16[16,4096]{1,0:T(8,128)(2,1)S(1)}, bf16[16,4096]{1,0:T(8,128)(2,1)S(1)}, u32[]{:S(2)}, u32[]{:S(2)}) collective-permute-start(bf16[16,4096]{1,0:T(8,128)(2,1)S(1)} %dynamic-slice_convert_fusion.9), channel_id=1, source_target_pairs={{0,4},{1,5},{2,6},{3,7},{4,0},{5,1},{6,2},{7,3},{8,12},{9,13},{10,... | collective-permute-start | bytes 393224 | tf_op jit(solution)/shard_map/ppermute | solution.py:85
  245.9 16.7 %collective-permute-start.35 = (bf16[16,4096]{1,0:T(8,128)(2,1)S(1)}, bf16[16,4096]{1,0:T(8,128)(2,1)S(1)}, u32[]{:S(2)}, u32[]{:S(2)}) collective-permute-start(bf16[16,4096]{1,0:T(8,128)(2,1)S(1)} %dynamic-slice_convert_fusion.8), channel_id=1, source_target_pairs={{0,4},{1,5},{2,6},{3,7},{4,0},{5,1},{6,2},{7,3},{8,12},{9,13},{10,... | collective-permute-start | bytes 393224 | tf_op jit(solution)/shard_map/ppermute | solution.py:85

commit v11 on v10

--- a/solution.py
+++ b/solution.py
@@ -119,7 +119,7 @@
     top = n_col.bit_length() - 1
     col_orders = [list(range(top - 1, -1, -1)), [top - 1, 0] + list(range(top - 2, 0, -1))]
     quarter = tokens.shape[0] // 4
-    orders = col_orders * 2
+    orders = [col_orders[0]] * 3 + [col_orders[1]]
     token_parts = [tokens[q * quarter:(q + 1) * quarter] for q in range(4)]
     segment = jnp.concatenate(doubling_gather(list(zip(token_parts, orders)), "col", n_col), axis=0)
     gate_rows, up_rows = sparse_matmul(segment, [gate_packed, up_packed], gate_keep)

time: 264 us -> 280 us (1.061)
  waiting for transfers between devices: 135 us -> 148 us
    ppermute x36, waiting for transfers between devices: 135 us -> 148 us  [exchange(): return lax.ppermute(x, axis, perm=pairs)]
  transfers between devices with their start and end apart: 36 -> 36, of which waited for: 28 -> 26; matrix products, arithmetic and copies ran while one was open for 4% -> 4% of each run, Pallas kernels for 0% -> 0%
where the time goes in v11:
time: 280 us; the launch traced here: 279 us
  waiting for transfers between devices  148 us (53%)
  Pallas kernels  69.1 us (25%)
  starting transfers between devices  37.5 us (13%)
  other arithmetic  12.2 us (4%)
  local copies, waits for them, and re-layouts  11.4 us (4%)
    ppermute x36, waiting for transfers between devices, exchange(): return lax.ppermute(x, axis, perm=pairs)  148 us
    pallas_call x2, Pallas kernels, sparse_matmul(): pl.pallas_call(kernel, grid_spec=pltpu.PrefetchScalarGridSpec(num_scalar_...  69.1 us
    ppermute x36, starting transfers between devices, exchange(): return lax.ppermute(x, axis, perm=pairs)  37.5 us
  transfers between devices with their start and end apart: 36, of which 26 were waited for; matrix products, arithmetic and copies ran while one was open for 4% of the time, Pallas kernels for 0%

profile of v11, /device:TPU:0, one launch (start us, length us, event | category | flops | bytes accessed | tf_op | source)
XLA Modules:
  0.0 278.8 jit_solution(7388699183956566633)
XLA Ops:
  0.0 1.1 fusion.6
  1.1 4.1 %collective-permute-start = (bf16[16,4096]{1,0:T(8,128)(2,1)S(1)}, bf16[16,4096]{1,0:T(8,128)(2,1)S(1)}, u32[]{:S(2)}, u32[]{:S(2)}) collective-permute-start(bf16[16,4096]{1,0:T(8,128)(2,1)S(1)} %get-tuple-element.17), channel_id=1, source_target_pairs={{0,4},{1,5},{2,6},{3,7},{4,0},{5,1},{6,2},{7,3},{8,12},{9,13},{10,... | collective-permute-start | bytes 393224 | tf_op jit(solution)/shard_map/ppermute | solution.py:85
  5.3 2.8 %collective-permute-start.6 = (bf16[16,4096]{1,0:T(8,128)(2,1)S(1)}, bf16[16,4096]{1,0:T(8,128)(2,1)S(1)}, u32[]{:S(2)}, u32[]{:S(2)}) collective-permute-start(bf16[16,4096]{1,0:T(8,128)(2,1)S(1)} %get-tuple-element.20), channel_id=1, source_target_pairs={{0,4},{1,5},{2,6},{3,7},{4,0},{5,1},{6,2},{7,3},{8,12},{9,13},{10,... | collective-permute-start | bytes 393224 | tf_op jit(solution)/shard_map/ppermute | solution.py:85
  8.2 0.8 reshape.58
  9.0 0.8 reshape.64
  10.5 0.7 sub.27
  11.4 0.8 subtract_select_fusion
  12.6 0.7 reshape.68.index_ref
  13.6 7.2 %collective-permute-done = bf16[16,4096]{1,0:T(8,128)(2,1)S(1)} collective-permute-done((bf16[16,4096]{1,0:T(8,128)(2,1)S(1)}, bf16[16,4096]{1,0:T(8,128)(2,1)S(1)}, u32[]{:S(2)}, u32[]{:S(2)}) %collective-permute-start) | collective-permute-done | bytes 131104 | tf_op jit(solution)/shard_map/ppermute | solution.py:85
  20.9 2.8 collective-permute-done.3
  23.8 2.7 collective-permute-done.6
  26.6 1.9 collective-permute-done.9
  28.5 1.6 collective-permute-start.10
  30.2 4.0 %collective-permute-done.1 = bf16[32,4096]{1,0:T(8,128)(2,1)S(1)} collective-permute-done((bf16[32,4096]{1,0:T(8,128)(2,1)S(1)}, bf16[32,4096]{1,0:T(8,128)(2,1)S(1)}, u32[]{:S(2)}, u32[]{:S(2)}) %collective-permute-start.1) | collective-permute-done | bytes 262176 | tf_op jit(solution)/shard_map/ppermute | solution.py:85
  34.2 1.6 collective-permute-start.2
  35.8 3.9 %collective-permute-done.4 = bf16[32,4096]{1,0:T(8,128)(2,1)S(1)} collective-permute-done((bf16[32,4096]{1,0:T(8,128)(2,1)S(1)}, bf16[32,4096]{1,0:T(8,128)(2,1)S(1)}, u32[]{:S(2)}, u32[]{:S(2)}) %collective-permute-start.4) | collective-permute-done | bytes 262176 | tf_op jit(solution)/shard_map/ppermute | solution.py:85
  39.8 1.6 collective-permute-start.5
  41.4 3.8 %collective-permute-done.7 = bf16[32,4096]{1,0:T(8,128)(2,1)S(1)} collective-permute-done((bf16[32,4096]{1,0:T(8,128)(2,1)S(1)}, bf16[32,4096]{1,0:T(8,128)(2,1)S(1)}, u32[]{:S(2)}, u32[]{:S(2)}) %collective-permute-start.7) | collective-permute-done | bytes 262176 | tf_op jit(solution)/shard_map/ppermute | solution.py:85
  45.3 1.6 collective-permute-start.8
  47.1 1.9 collective-permute-done.2
  49.3 11.0 %collective-permute-done.5 = bf16[64,4096]{1,0:T(8,128)(2,1)S(1)} collective-permute-done((bf16[64,4096]{1,0:T(8,128)(2,1)S(1)}, bf16[64,4096]{1,0:T(8,128)(2,1)S(1)}, u32[]{:S(2)}, u32[]{:S(2)}) %collective-permute-start.5) | collective-permute-done | bytes 524320 | tf_op jit(solution)/shard_map/ppermute | solution.py:85
  60.5 10.0 %collective-permute-done.8 = bf16[64,4096]{1,0:T(8,128)(2,1)S(1)} collective-permute-done((bf16[64,4096]{1,0:T(8,128)(2,1)S(1)}, bf16[64,4096]{1,0:T(8,128)(2,1)S(1)}, u32[]{:S(2)}, u32[]{:S(2)}) %collective-permute-start.8) | collective-permute-done | bytes 524320 | tf_op jit(solution)/shard_map/ppermute | solution.py:85
  70.9 2.5 pad_maximum_fusion.x_ref
  73.4 43.4 %shard_map.64 = (bf16[512,3328]{1,0:T(8,128)(2,1)}, bf16[512,3328]{1,0:T(8,128)(2,1)}) custom-call(s32[32]{0:T(128)} %copy-done.2, s32[832]{0:T(1024)} %reshape.68.index_ref, bf16[512,4096]{1,0:T(8,128)(2,1)} %pad_maximum_fusion.x_ref, bf16[640,128,128]{2,1,0:T(8,128)(2,1)} %refs_3_.1, bf16[640,128,128]{2,1,0:T(8,128)(2,1)} %refs_3_.1, ...), custom_call_target="tpu_custom_call" | custom-call | flops 27917287424 | bytes 65536000 | tf_op jit(solution)/shard_map/pallas_call | solution.py:66
  116.8 2.3 fusion.4
  120.2 0.5 collective-permute-start.18
  120.9 0.7 collective-permute-done.12
  121.9 1.6 collective-permute-start.13
  123.8 1.0 collective-permute-start.15
  125.0 1.2 collective-permute-start.19
  126.4 1.0 collective-permute-start.21
  127.4 7.2 %collective-permute-done.13 = bf16[64,3328]{1,0:T(8,128)(2,1)S(1)} collective-permute-done((bf16[64,3328]{1,0:T(8,128)(2,1)S(1)}, bf16[64,3328]{1,0:T(8,128)(2,1)S(1)}, u32[]{:S(2)}, u32[]{:S(2)}) %collective-permute-start.13) | collective-permute-done | bytes 426016 | tf_op jit(solution)/shard_map/ppermute | solution.py:85
  134.6 9.1 %collective-permute-done.15 = bf16[64,3328]{1,0:T(8,128)(2,1)S(1)} collective-permute-done((bf16[64,3328]{1,0:T(8,128)(2,1)S(1)}, bf16[64,3328]{1,0:T(8,128)(2,1)S(1)}, u32[]{:S(2)}, u32[]{:S(2)}) %collective-permute-start.15) | collective-permute-done | bytes 426016 | tf_op jit(solution)/shard_map/ppermute | solution.py:85
  144.1 1.6 collective-permute-start.16
  145.7 7.2 %collective-permute-done.19 = bf16[64,3328]{1,0:T(8,128)(2,1)S(1)} collective-permute-done((bf16[64,3328]{1,0:T(8,128)(2,1)S(1)}, bf16[64,3328]{1,0:T(8,128)(2,1)S(1)}, u32[]{:S(2)}, u32[]{:S(2)}) %collective-permute-start.19) | collective-permute-done | bytes 426016 | tf_op jit(solution)/shard_map/ppermute | solution.py:85
  152.9 9.1 %collective-permute-done.21 = bf16[64,3328]{1,0:T(8,128)(2,1)S(1)} collective-permute-done((bf16[64,3328]{1,0:T(8,128)(2,1)S(1)}, bf16[64,3328]{1,0:T(8,128)(2,1)S(1)}, u32[]{:S(2)}, u32[]{:S(2)}) %collective-permute-start.21) | collective-permute-done | bytes 426016 | tf_op jit(solution)/shard_map/ppermute | solution.py:85
  162.3 1.6 collective-permute-start.22
  164.0 7.2 %collective-permute-done.16 = bf16[64,3328]{1,0:T(8,128)(2,1)S(1)} collective-permute-done((bf16[64,3328]{1,0:T(8,128)(2,1)S(1)}, bf16[64,3328]{1,0:T(8,128)(2,1)S(1)}, u32[]{:S(2)}, u32[]{:S(2)}) %collective-permute-start.16) | collective-permute-done | bytes 426016 | tf_op jit(solution)/shard_map/ppermute | solution.py:85
  171.4 8.1 %collective-permute-done.22 = bf16[64,3328]{1,0:T(8,128)(2,1)S(1)} collective-permute-done((bf16[64,3328]{1,0:T(8,128)(2,1)S(1)}, bf16[64,3328]{1,0:T(8,128)(2,1)S(1)}, u32[]{:S(2)}, u32[]{:S(2)}) %collective-permute-start.22) | collective-permute-done | bytes 426016 | tf_op jit(solution)/shard_map/ppermute | solution.py:85
  180.0 0.7 reshape.63.index_ref
  181.0 1.1 collective-permute-done.23
  182.4 1.9 pad_maximum_fusion.1.x_ref
  184.3 25.7 %shard_map.65 = bf16[512,4096]{1,0:T(8,128)(2,1)} custom-call(s32[26]{0:T(128)} %copy-done.3, s32[832]{0:T(1024)} %reshape.63.index_ref, bf16[512,3328]{1,0:T(8,128)(2,1)} %pad_maximum_fusion.1.x_ref, bf16[640,128,128]{2,1,0:T(8,128)(2,1)} %refs_1_.3, bf16[640,128,128]{2,1,0:T(8,128)(2,1)} %refs_1_.3), custom_call_target="tpu_custom_call" | custom-call | flops 13958643712 | bytes 34865152 | tf_op jit(solution)/shard_map/pallas_call | solution.py:66
  210.1 2.7 fusion.3
  212.8 1.5 collective-permute-start.24
  214.3 0.7 collective-permute-start.27
  215.0 1.5 collective-permute-start.30
  216.5 0.8 collective-permute-start.33
  217.4 10.3 %collective-permute-done.24 = bf16[64,4096]{1,0:T(8,128)(2,1)S(1)} collective-permute-done((bf16[64,4096]{1,0:T(8,128)(2,1)S(1)}, bf16[64,4096]{1,0:T(8,128)(2,1)S(1)}, u32[]{:S(2)}, u32[]{:S(2)}) %collective-permute-start.24) | collective-permute-done | bytes 524320 | tf_op jit(solution)/shard_map/ppermute | solution.py:85
  227.8 0.7 collective-permute-start.25
  228.5 10.4 %collective-permute-done.27 = bf16[64,4096]{1,0:T(8,128)(2,1)S(1)} collective-permute-done((bf16[64,4096]{1,0:T(8,128)(2,1)S(1)}, bf16[64,4096]{1,0:T(8,128)(2,1)S(1)}, u32[]{:S(2)}, u32[]{:S(2)}) %collective-permute-start.27) | collective-permute-done | bytes 524320 | tf_op jit(solution)/shard_map/ppermute | solution.py:85
  239.0 0.7 collective-permute-start.28
  239.7 9.5 %collective-permute-done.30 = bf16[64,4096]{1,0:T(8,128)(2,1)S(1)} collective-permute-done((bf16[64,4096]{1,0:T(8,128)(2,1)S(1)}, bf16[64,4096]{1,0:T(8,128)(2,1)S(1)}, u32[]{:S(2)}, u32[]{:S(2)}) %collective-permute-start.30) | collective-permute-done | bytes 524320 | tf_op jit(solution)/shard_map/ppermute | solution.py:85
  249.3 0.8 collective-permute-start.31
  250.3 1.6 collective-permute-start.34
  252.0 3.4 %collective-permute-start.26 = (bf16[16,4096]{1,0:T(8,128)(2,1)S(1)}, bf16[16,4096]{1,0:T(8,128)(2,1)S(1)}, u32[]{:S(2)}, u32[]{:S(2)}) collective-permute-start(bf16[16,4096]{1,0:T(8,128)(2,1)S(1)} %dynamic-slice_convert_fusion.11), channel_id=1, source_target_pairs={{0,4},{1,5},{2,6},{3,7},{4,0},{5,1},{6,2},{7,3},{8,12},{9,13},{10,... | collective-permute-start | bytes 393224 | tf_op jit(solution)/shard_map/ppermute | solution.py:85
  255.6 4.3 %collective-permute-done.31 = bf16[32,4096]{1,0:T(8,128)(2,1)S(1)} collective-permute-done((bf16[32,4096]{1,0:T(8,128)(2,1)S(1)}, bf16[32,4096]{1,0:T(8,128)(2,1)S(1)}, u32[]{:S(2)}, u32[]{:S(2)}) %collective-permute-start.31) | collective-permute-done | bytes 262176 | tf_op jit(solution)/shard_map/ppermute | solution.py:85
  259.9 0.9 collective-permute-start.32
  260.9 2.1 collective-permute-start.35
  263.1 7.5 %collective-permute-done.26 = bf16[16,4096]{1,0:T(8,128)(2,1)S(1)} collective-permute-done((bf16[16,4096]{1,0:T(8,128)(2,1)S(1)}, bf16[16,4096]{1,0:T(8,128)(2,1)S(1)}, u32[]{:S(2)}, u32[]{:S(2)}) %collective-permute-start.26) | collective-permute-done | bytes 131104 | tf_op jit(solution)/shard_map/ppermute | solution.py:85
  270.6 2.8 collective-permute-done.29
  273.4 2.8 collective-permute-done.32
  276.2 1.8 collective-permute-done.35
  278.0 0.8 pad_maximum_fusion.2
  (103 shorter events, 8.7 us)
Async XLA Ops:
  1.1 19.7 %collective-permute-start = (bf16[16,4096]{1,0:T(8,128)(2,1)S(1)}, bf16[16,4096]{1,0:T(8,128)(2,1)S(1)}, u32[]{:S(2)}, u32[]{:S(2)}) collective-permute-start(bf16[16,4096]{1,0:T(8,128)(2,1)S(1)} %get-tuple-element.17), channel_id=1, source_target_pairs={{0,4},{1,5},{2,6},{3,7},{4,0},{5,1},{6,2},{7,3},{8,12},{9,13},{10,... | collective-permute-start | bytes 393224 | tf_op jit(solution)/shard_map/ppermute | solution.py:85
  5.2 18.5 %collective-permute-start.3 = (bf16[16,4096]{1,0:T(8,128)(2,1)S(1)}, bf16[16,4096]{1,0:T(8,128)(2,1)S(1)}, u32[]{:S(2)}, u32[]{:S(2)}) collective-permute-start(bf16[16,4096]{1,0:T(8,128)(2,1)S(1)} %get-tuple-element.18), channel_id=1, source_target_pairs={{0,4},{1,5},{2,6},{3,7},{4,0},{5,1},{6,2},{7,3},{8,12},{9,13},{10,... | collective-permute-start | bytes 393224 | tf_op jit(solution)/shard_map/ppermute | solution.py:85
  5.3 21.2 %collective-permute-start.6 = (bf16[16,4096]{1,0:T(8,128)(2,1)S(1)}, bf16[16,4096]{1,0:T(8,128)(2,1)S(1)}, u32[]{:S(2)}, u32[]{:S(2)}) collective-permute-start(bf16[16,4096]{1,0:T(8,128)(2,1)S(1)} %get-tuple-element.20), channel_id=1, source_target_pairs={{0,4},{1,5},{2,6},{3,7},{4,0},{5,1},{6,2},{7,3},{8,12},{9,13},{10,... | collective-permute-start | bytes 393224 | tf_op jit(solution)/shard_map/ppermute | solution.py:85
  8.2 20.3 %collective-permute-start.9 = (bf16[16,4096]{1,0:T(8,128)(2,1)S(1)}, bf16[16,4096]{1,0:T(8,128)(2,1)S(1)}, u32[]{:S(2)}, u32[]{:S(2)}) collective-permute-start(bf16[16,4096]{1,0:T(8,128)(2,1)S(1)} %get-tuple-element.19), channel_id=1, source_target_pairs={{0,4},{1,5},{2,6},{3,7},{4,0},{5,1},{6,2},{7,3},{8,12},{9,13},{10,... | collective-permute-start | bytes 393224 | tf_op jit(solution)/shard_map/ppermute | solution.py:85
  11.4 28.4 %copy-start.2 = (s32[32]{0:T(128)}, s32[32]{0:T(128)S(1)}, u32[]{:S(2)}) copy-start(s32[32]{0:T(128)S(1)} %fusion.base_ref) | copy-start | bytes 388
  20.8 13.3 %collective-permute-start.1 = (bf16[32,4096]{1,0:T(8,128)(2,1)S(1)}, bf16[32,4096]{1,0:T(8,128)(2,1)S(1)}, u32[]{:S(2)}, u32[]{:S(2)}) collective-permute-start(bf16[32,4096]{1,0:T(8,128)(2,1)S(1)} %maximum_select_fusion.12), channel_id=1, source_target_pairs={{0,2},{1,3},{2,0},{3,1},{4,6},{5,7},{6,4},{7,5},{8,10},{9,11},{10,... | collective-permute-start | bytes 786440 | tf_op jit(solution)/shard_map/ppermute | solution.py:85
  23.8 16.0 %collective-permute-start.4 = (bf16[32,4096]{1,0:T(8,128)(2,1)S(1)}, bf16[32,4096]{1,0:T(8,128)(2,1)S(1)}, u32[]{:S(2)}, u32[]{:S(2)}) collective-permute-start(bf16[32,4096]{1,0:T(8,128)(2,1)S(1)} %maximum_select_fusion.13), channel_id=1, source_target_pairs={{0,2},{1,3},{2,0},{3,1},{4,6},{5,7},{6,4},{7,5},{8,10},{9,11},{10,... | collective-permute-start | bytes 786440 | tf_op jit(solution)/shard_map/ppermute | solution.py:85
  26.6 18.7 %collective-permute-start.7 = (bf16[32,4096]{1,0:T(8,128)(2,1)S(1)}, bf16[32,4096]{1,0:T(8,128)(2,1)S(1)}, u32[]{:S(2)}, u32[]{:S(2)}) collective-permute-start(bf16[32,4096]{1,0:T(8,128)(2,1)S(1)} %maximum_select_fusion.14), channel_id=1, source_target_pairs={{0,2},{1,3},{2,0},{3,1},{4,6},{5,7},{6,4},{7,5},{8,10},{9,11},{10,... | collective-permute-start | bytes 786440 | tf_op jit(solution)/shard_map/ppermute | solution.py:85
  28.5 18.4 %collective-permute-start.10 = (bf16[32,4096]{1,0:T(8,128)(2,1)S(1)}, bf16[32,4096]{1,0:T(8,128)(2,1)S(1)}, u32[]{:S(2)}, u32[]{:S(2)}) collective-permute-start(bf16[32,4096]{1,0:T(8,128)(2,1)S(1)} %maximum_select_fusion.15), channel_id=1, source_target_pairs={{0,1},{1,0},{2,3},{3,2},{4,5},{5,4},{6,7},{7,6},{8,9},{9,8},{10,11... | collective-permute-start | bytes 786440 | tf_op jit(solution)/shard_map/ppermute | solution.py:85
  34.2 14.9 %collective-permute-start.2 = (bf16[64,4096]{1,0:T(8,128)(2,1)S(1)}, bf16[64,4096]{1,0:T(8,128)(2,1)S(1)}, u32[]{:S(2)}, u32[]{:S(2)}) collective-permute-start(bf16[64,4096]{1,0:T(8,128)(2,1)S(1)} %maximum_select_fusion.8), channel_id=1, source_target_pairs={{0,1},{1,0},{2,3},{3,2},{4,5},{5,4},{6,7},{7,6},{8,9},{9,8},{10,11... | collective-permute-start | bytes 1572872 | tf_op jit(solution)/shard_map/ppermute | solution.py:85
  39.8 20.5 %collective-permute-start.5 = (bf16[64,4096]{1,0:T(8,128)(2,1)S(1)}, bf16[64,4096]{1,0:T(8,128)(2,1)S(1)}, u32[]{:S(2)}, u32[]{:S(2)}) collective-permute-start(bf16[64,4096]{1,0:T(8,128)(2,1)S(1)} %maximum_select_fusion.9), channel_id=1, source_target_pairs={{0,1},{1,0},{2,3},{3,2},{4,5},{5,4},{6,7},{7,6},{8,9},{9,8},{10,11... | collective-permute-start | bytes 1572872 | tf_op jit(solution)/shard_map/ppermute | solution.py:85
  45.3 25.1 %collective-permute-start.8 = (bf16[64,4096]{1,0:T(8,128)(2,1)S(1)}, bf16[64,4096]{1,0:T(8,128)(2,1)S(1)}, u32[]{:S(2)}, u32[]{:S(2)}) collective-permute-start(bf16[64,4096]{1,0:T(8,128)(2,1)S(1)} %maximum_select_fusion.10), channel_id=1, source_target_pairs={{0,1},{1,0},{2,3},{3,2},{4,5},{5,4},{6,7},{7,6},{8,9},{9,8},{10,11... | collective-permute-start | bytes 1572872 | tf_op jit(solution)/shard_map/ppermute | solution.py:85
  47.0 23.7 %collective-permute-start.11 = (bf16[64,4096]{1,0:T(8,128)(2,1)S(1)}, bf16[64,4096]{1,0:T(8,128)(2,1)S(1)}, u32[]{:S(2)}, u32[]{:S(2)}) collective-permute-start(bf16[64,4096]{1,0:T(8,128)(2,1)S(1)} %maximum_select_fusion.11), channel_id=1, source_target_pairs={{0,2},{1,3},{2,0},{3,1},{4,6},{5,7},{6,4},{7,5},{8,10},{9,11},{10,... | collective-permute-start | bytes 1572872 | tf_op jit(solution)/shard_map/ppermute | solution.py:85
  116.8 3.0 %copy-start = (bf16[512,3328]{1,0:T(8,128)(2,1)S(1)}, bf16[512,3328]{1,0:T(8,128)(2,1)}, u32[]{:S(2)}) copy-start(bf16[512,3328]{1,0:T(8,128)(2,1)} %get-tuple-element.8) | copy-start | bytes 10223620
  119.2 2.4 collective-permute-start.12
  120.1 3.4 %collective-permute-start.14 = (bf16[128,3328]{1,0:T(8,128)(2,1)S(1)}, bf16[128,3328]{1,0:T(8,128)(2,1)S(1)}, u32[]{:S(2)}, u32[]{:S(2)}) collective-permute-start(bf16[128,3328]{1,0:T(8,128)(2,1)S(1)} %constant_dynamic-slice_fusion.6), channel_id=1, source_target_pairs={{0,8},{8,0},{16,24},{24,16},{1,9},{9,1},{17,25},{25,17},{2,10},{10... | collective-permute-start | bytes 2555912 | tf_op jit(solution)/shard_map/ppermute | solution.py:85
  120.2 4.5 %collective-permute-start.18 = (bf16[128,3328]{1,0:T(8,128)(2,1)S(1)}, bf16[128,3328]{1,0:T(8,128)(2,1)S(1)}, u32[]{:S(2)}, u32[]{:S(2)}) collective-permute-start(bf16[128,3328]{1,0:T(8,128)(2,1)S(1)} %constant_dynamic-slice_fusion.5), channel_id=1, source_target_pairs={{0,8},{8,0},{16,24},{24,16},{1,9},{9,1},{17,25},{25,17},{2,10},{10... | collective-permute-start | bytes 2555912 | tf_op jit(solution)/shard_map/ppermute | solution.py:85
  120.8 5.3 %collective-permute-start.20 = (bf16[128,3328]{1,0:T(8,128)(2,1)S(1)}, bf16[128,3328]{1,0:T(8,128)(2,1)S(1)}, u32[]{:S(2)}, u32[]{:S(2)}) collective-permute-start(bf16[128,3328]{1,0:T(8,128)(2,1)S(1)} %constant_dynamic-slice_fusion.4), channel_id=1, source_target_pairs={{0,8},{8,0},{16,24},{24,16},{1,9},{9,1},{17,25},{25,17},{2,10},{10... | collective-permute-start | bytes 2555912 | tf_op jit(solution)/shard_map/ppermute | solution.py:85
  121.9 12.7 %collective-permute-start.13 = (bf16[64,3328]{1,0:T(8,128)(2,1)S(1)}, bf16[64,3328]{1,0:T(8,128)(2,1)S(1)}, u32[]{:S(2)}, u32[]{:S(2)}) collective-permute-start(bf16[64,3328]{1,0:T(8,128)(2,1)S(1)} %dynamic-slice_convert_fusion.3), channel_id=1, source_target_pairs={{0,16},{8,24},{16,0},{24,8},{1,17},{9,25},{17,1},{25,9},{2,18},{10... | collective-permute-start | bytes 1277960 | tf_op jit(solution)/shard_map/ppermute | solution.py:85
  123.8 20.0 %collective-permute-start.15 = (bf16[64,3328]{1,0:T(8,128)(2,1)S(1)}, bf16[64,3328]{1,0:T(8,128)(2,1)S(1)}, u32[]{:S(2)}, u32[]{:S(2)}) collective-permute-start(bf16[64,3328]{1,0:T(8,128)(2,1)S(1)} %dynamic-slice_convert_fusion.2), channel_id=1, source_target_pairs={{0,16},{8,24},{16,0},{24,8},{1,17},{9,25},{17,1},{25,9},{2,18},{10... | collective-permute-start | bytes 1277960 | tf_op jit(solution)/shard_map/ppermute | solution.py:85
  125.0 27.9 %collective-permute-start.19 = (bf16[64,3328]{1,0:T(8,128)(2,1)S(1)}, bf16[64,3328]{1,0:T(8,128)(2,1)S(1)}, u32[]{:S(2)}, u32[]{:S(2)}) collective-permute-start(bf16[64,3328]{1,0:T(8,128)(2,1)S(1)} %dynamic-slice_convert_fusion.1), channel_id=1, source_target_pairs={{0,16},{8,24},{16,0},{24,8},{1,17},{9,25},{17,1},{25,9},{2,18},{10... | collective-permute-start | bytes 1277960 | tf_op jit(solution)/shard_map/ppermute | solution.py:85
  126.4 35.6 %collective-permute-start.21 = (bf16[64,3328]{1,0:T(8,128)(2,1)S(1)}, bf16[64,3328]{1,0:T(8,128)(2,1)S(1)}, u32[]{:S(2)}, u32[]{:S(2)}) collective-permute-start(bf16[64,3328]{1,0:T(8,128)(2,1)S(1)} %dynamic-slice_convert_fusion), channel_id=1, source_target_pairs={{0,16},{8,24},{16,0},{24,8},{1,17},{9,25},{17,1},{25,9},{2,18},{10... | collective-permute-start | bytes 1277960 | tf_op jit(solution)/shard_map/ppermute | solution.py:85
  144.1 27.1 %collective-permute-start.16 = (bf16[64,3328]{1,0:T(8,128)(2,1)S(1)}, bf16[64,3328]{1,0:T(8,128)(2,1)S(1)}, u32[]{:S(2)}, u32[]{:S(2)}) collective-permute-start(bf16[64,3328]{1,0:T(8,128)(2,1)S(1)} %multiply_convert_fusion.1), channel_id=1, source_target_pairs={{0,16},{8,24},{16,0},{24,8},{1,17},{9,25},{17,1},{25,9},{2,18},{10... | collective-permute-start | bytes 1277960 | tf_op jit(solution)/shard_map/ppermute | solution.py:85
  162.3 17.4 %copy-start.1 = (s32[26,32]{1,0:T(8,128)S(1)}, s32[26,32]{1,0:T(8,128)}, u32[]{:S(2)}) copy-start(s32[26,32]{1,0:T(8,128)} %param.11) | copy-start | bytes 9988
  162.3 17.1 %collective-permute-start.22 = (bf16[64,3328]{1,0:T(8,128)(2,1)S(1)}, bf16[64,3328]{1,0:T(8,128)(2,1)S(1)}, u32[]{:S(2)}, u32[]{:S(2)}) collective-permute-start(bf16[64,3328]{1,0:T(8,128)(2,1)S(1)} %multiply_convert_fusion), channel_id=1, source_target_pairs={{0,16},{8,24},{16,0},{24,8},{1,17},{9,25},{17,1},{25,9},{2,18},{10... | collective-permute-start | bytes 1277960 | tf_op jit(solution)/shard_map/ppermute | solution.py:85
  171.3 9.3 %collective-permute-start.17 = (bf16[128,3328]{1,0:T(8,128)(2,1)S(1)}, bf16[128,3328]{1,0:T(8,128)(2,1)S(1)}, u32[]{:S(2)}, u32[]{:S(2)}) collective-permute-start(bf16[128,3328]{1,0:T(8,128)(2,1)S(1)} %maximum_select_fusion.6), channel_id=1, source_target_pairs={{0,8},{8,0},{16,24},{24,16},{1,9},{9,1},{17,25},{25,17},{2,10},{10... | collective-permute-start | bytes 2555912 | tf_op jit(solution)/shard_map/ppermute | solution.py:85
  179.6 2.4 collective-permute-start.23
  179.9 1.1 copy-start.3
  212.8 14.8 %collective-permute-start.24 = (bf16[64,4096]{1,0:T(8,128)(2,1)S(1)}, bf16[64,4096]{1,0:T(8,128)(2,1)S(1)}, u32[]{:S(2)}, u32[]{:S(2)}) collective-permute-start(bf16[64,4096]{1,0:T(8,128)(2,1)S(1)} %constant_dynamic-slice_fusion.3), channel_id=1, source_target_pairs={{0,1},{1,0},{2,3},{3,2},{4,5},{5,4},{6,7},{7,6},{8,9},{9,8},{10,11... | collective-permute-start | bytes 1572872 | tf_op jit(solution)/shard_map/ppermute | solution.py:85
  214.3 24.6 %collective-permute-start.27 = (bf16[64,4096]{1,0:T(8,128)(2,1)S(1)}, bf16[64,4096]{1,0:T(8,128)(2,1)S(1)}, u32[]{:S(2)}, u32[]{:S(2)}) collective-permute-start(bf16[64,4096]{1,0:T(8,128)(2,1)S(1)} %constant_dynamic-slice_fusion.2), channel_id=1, source_target_pairs={{0,1},{1,0},{2,3},{3,2},{4,5},{5,4},{6,7},{7,6},{8,9},{9,8},{10,11... | collective-permute-start | bytes 1572872 | tf_op jit(solution)/shard_map/ppermute | solution.py:85
  215.0 34.2 %collective-permute-start.30 = (bf16[64,4096]{1,0:T(8,128)(2,1)S(1)}, bf16[64,4096]{1,0:T(8,128)(2,1)S(1)}, u32[]{:S(2)}, u32[]{:S(2)}) collective-permute-start(bf16[64,4096]{1,0:T(8,128)(2,1)S(1)} %constant_dynamic-slice_fusion.1), channel_id=1, source_target_pairs={{0,1},{1,0},{2,3},{3,2},{4,5},{5,4},{6,7},{7,6},{8,9},{9,8},{10,11... | collective-permute-start | bytes 1572872 | tf_op jit(solution)/shard_map/ppermute | solution.py:85
  216.5 33.6 %collective-permute-start.33 = (bf16[64,4096]{1,0:T(8,128)(2,1)S(1)}, bf16[64,4096]{1,0:T(8,128)(2,1)S(1)}, u32[]{:S(2)}, u32[]{:S(2)}) collective-permute-start(bf16[64,4096]{1,0:T(8,128)(2,1)S(1)} %constant_dynamic-slice_fusion), channel_id=1, source_target_pairs={{0,2},{1,3},{2,0},{3,1},{4,6},{5,7},{6,4},{7,5},{8,10},{9,11},{10,... | collective-permute-start | bytes 1572872 | tf_op jit(solution)/shard_map/ppermute | solution.py:85
  227.8 24.1 %collective-permute-start.25 = (bf16[32,4096]{1,0:T(8,128)(2,1)S(1)}, bf16[32,4096]{1,0:T(8,128)(2,1)S(1)}, u32[]{:S(2)}, u32[]{:S(2)}) collective-permute-start(bf16[32,4096]{1,0:T(8,128)(2,1)S(1)} %dynamic-slice_convert_fusion.7), channel_id=1, source_target_pairs={{0,2},{1,3},{2,0},{3,1},{4,6},{5,7},{6,4},{7,5},{8,10},{9,11},{10,... | collective-permute-start | bytes 786440 | tf_op jit(solution)/shard_map/ppermute | solution.py:85
  239.0 16.3 %collective-permute-start.28 = (bf16[32,4096]{1,0:T(8,128)(2,1)S(1)}, bf16[32,4096]{1,0:T(8,128)(2,1)S(1)}, u32[]{:S(2)}, u32[]{:S(2)}) collective-permute-start(bf16[32,4096]{1,0:T(8,128)(2,1)S(1)} %dynamic-slice_convert_fusion.6), channel_id=1, source_target_pairs={{0,2},{1,3},{2,0},{3,1},{4,6},{5,7},{6,4},{7,5},{8,10},{9,11},{10,... | collective-permute-start | bytes 786440 | tf_op jit(solution)/shard_map/ppermute | solution.py:85
  249.3 10.5 %collective-permute-start.31 = (bf16[32,4096]{1,0:T(8,128)(2,1)S(1)}, bf16[32,4096]{1,0:T(8,128)(2,1)S(1)}, u32[]{:S(2)}, u32[]{:S(2)}) collective-permute-start(bf16[32,4096]{1,0:T(8,128)(2,1)S(1)} %dynamic-slice_convert_fusion.5), channel_id=1, source_target_pairs={{0,2},{1,3},{2,0},{3,1},{4,6},{5,7},{6,4},{7,5},{8,10},{9,11},{10,... | collective-permute-start | bytes 786440 | tf_op jit(solution)/shard_map/ppermute | solution.py:85
  250.3 10.6 %collective-permute-start.34 = (bf16[32,4096]{1,0:T(8,128)(2,1)S(1)}, bf16[32,4096]{1,0:T(8,128)(2,1)S(1)}, u32[]{:S(2)}, u32[]{:S(2)}) collective-permute-start(bf16[32,4096]{1,0:T(8,128)(2,1)S(1)} %dynamic-slice_convert_fusion.4), channel_id=1, source_target_pairs={{0,1},{1,0},{2,3},{3,2},{4,5},{5,4},{6,7},{7,6},{8,9},{9,8},{10,11... | collective-permute-start | bytes 786440 | tf_op jit(solution)/shard_map/ppermute | solution.py:85
  252.0 18.6 %collective-permute-start.26 = (bf16[16,4096]{1,0:T(8,128)(2,1)S(1)}, bf16[16,4096]{1,0:T(8,128)(2,1)S(1)}, u32[]{:S(2)}, u32[]{:S(2)}) collective-permute-start(bf16[16,4096]{1,0:T(8,128)(2,1)S(1)} %dynamic-slice_convert_fusion.11), channel_id=1, source_target_pairs={{0,4},{1,5},{2,6},{3,7},{4,0},{5,1},{6,2},{7,3},{8,12},{9,13},{10,... | collective-permute-start | bytes 393224 | tf_op jit(solution)/shard_map/ppermute | solution.py:85
  255.5 17.9 %collective-permute-start.29 = (bf16[16,4096]{1,0:T(8,128)(2,1)S(1)}, bf16[16,4096]{1,0:T(8,128)(2,1)S(1)}, u32[]{:S(2)}, u32[]{:S(2)}) collective-permute-start(bf16[16,4096]{1,0:T(8,128)(2,1)S(1)} %dynamic-slice_convert_fusion.10), channel_id=1, source_target_pairs={{0,4},{1,5},{2,6},{3,7},{4,0},{5,1},{6,2},{7,3},{8,12},{9,13},{10,... | collective-permute-start | bytes 393224 | tf_op jit(solution)/shard_map/ppermute | solution.py:85
  259.9 16.3 %collective-permute-start.32 = (bf16[16,4096]{1,0:T(8,128)(2,1)S(1)}, bf16[16,4096]{1,0:T(8,128)(2,1)S(1)}, u32[]{:S(2)}, u32[]{:S(2)}) collective-permute-start(bf16[16,4096]{1,0:T(8,128)(2,1)S(1)} %dynamic-slice_convert_fusion.9), channel_id=1, source_target_pairs={{0,4},{1,5},{2,6},{3,7},{4,0},{5,1},{6,2},{7,3},{8,12},{9,13},{10,... | collective-permute-start | bytes 393224 | tf_op jit(solution)/shard_map/ppermute | solution.py:85
  260.9 17.0 %collective-permute-start.35 = (bf16[16,4096]{1,0:T(8,128)(2,1)S(1)}, bf16[16,4096]{1,0:T(8,128)(2,1)S(1)}, u32[]{:S(2)}, u32[]{:S(2)}) collective-permute-start(bf16[16,4096]{1,0:T(8,128)(2,1)S(1)} %dynamic-slice_convert_fusion.8), channel_id=1, source_target_pairs={{0,4},{1,5},{2,6},{3,7},{4,0},{5,1},{6,2},{7,3},{8,12},{9,13},{10,... | collective-permute-start | bytes 393224 | tf_op jit(solution)/shard_map/ppermute | solution.py:85

commit v12 on v11

--- a/solution.py
+++ b/solution.py
@@ -119,7 +119,8 @@
     top = n_col.bit_length() - 1
     col_orders = [list(range(top - 1, -1, -1)), [top - 1, 0] + list(range(top - 2, 0, -1))]
     quarter = tokens.shape[0] // 4
-    orders = [col_orders[0]] * 3 + [col_orders[1]]
+    rest = list(range(2, top))
+    orders = [[1, 0] + rest, [1] + rest + [0], col_orders[1], col_orders[0]]
     token_parts = [tokens[q * quarter:(q + 1) * quarter] for q in range(4)]
     segment = jnp.concatenate(doubling_gather(list(zip(token_parts, orders)), "col", n_col), axis=0)
     gate_rows, up_rows = sparse_matmul(segment, [gate_packed, up_packed], gate_keep)

time: 280 us -> 257 us (0.918)
  waiting for transfers between devices: 148 us -> 122 us
  starting transfers between devices: 37.5 us -> 40.8 us
    ppermute x36, waiting for transfers between devices: 148 us -> 122 us  [exchange(): return lax.ppermute(x, axis, perm=pairs)]
    ppermute x36, starting transfers between devices: 37.5 us -> 40.8 us  [exchange(): return lax.ppermute(x, axis, perm=pairs)]
  transfers between devices with their start and end apart: 36 -> 36, of which waited for: 26 -> 21; matrix products, arithmetic and copies ran while one was open for 4% -> 4% of each run, Pallas kernels for 0% -> 0%
where the time goes in v12:
time: 257 us; the launch traced here: 256 us
  waiting for transfers between devices  122 us (47%)
  Pallas kernels  69 us (27%)
  starting transfers between devices  40.8 us (16%)
  other arithmetic  12.2 us (5%)
  local copies, waits for them, and re-layouts  11.4 us (4%)
    ppermute x36, waiting for transfers between devices, exchange(): return lax.ppermute(x, axis, perm=pairs)  122 us
    pallas_call x2, Pallas kernels, sparse_matmul(): pl.pallas_call(kernel, grid_spec=pltpu.PrefetchScalarGridSpec(num_scalar_...  69 us
    ppermute x36, starting transfers between devices, exchange(): return lax.ppermute(x, axis, perm=pairs)  40.8 us
  transfers between devices with their start and end apart: 36, of which 21 were waited for; matrix products, arithmetic and copies ran while one was open for 4% of the time, Pallas kernels for 0%

profile of v12, /device:TPU:0, one launch (start us, length us, event | category | flops | bytes accessed | tf_op | source)
XLA Modules:
  0.0 256.3 jit_solution(16194255990575374373)
XLA Ops:
  0.0 1.1 fusion.6
  1.1 3.1 %collective-permute-start.3 = (bf16[16,4096]{1,0:T(8,128)(2,1)S(1)}, bf16[16,4096]{1,0:T(8,128)(2,1)S(1)}, u32[]{:S(2)}, u32[]{:S(2)}) collective-permute-start(bf16[16,4096]{1,0:T(8,128)(2,1)S(1)} %get-tuple-element.18), channel_id=1, source_target_pairs={{0,2},{1,3},{2,0},{3,1},{4,6},{5,7},{6,4},{7,5},{8,10},{9,11},{10,... | collective-permute-start | bytes 393224 | tf_op jit(solution)/shard_map/ppermute | solution.py:85
  4.2 2.6 %collective-permute-start.9 = (bf16[16,4096]{1,0:T(8,128)(2,1)S(1)}, bf16[16,4096]{1,0:T(8,128)(2,1)S(1)}, u32[]{:S(2)}, u32[]{:S(2)}) collective-permute-start(bf16[16,4096]{1,0:T(8,128)(2,1)S(1)} %get-tuple-element.19), channel_id=1, source_target_pairs={{0,4},{1,5},{2,6},{3,7},{4,0},{5,1},{6,2},{7,3},{8,12},{9,13},{10,... | collective-permute-start | bytes 393224 | tf_op jit(solution)/shard_map/ppermute | solution.py:85
  6.8 0.4 collective-permute-start
  7.3 0.8 reshape.58
  8.1 0.8 reshape.64
  9.6 0.7 sub.27
  10.4 0.8 subtract_select_fusion
  11.6 0.7 reshape.68.index_ref
  12.7 3.0 %collective-permute-start.4 = (bf16[32,4096]{1,0:T(8,128)(2,1)S(1)}, bf16[32,4096]{1,0:T(8,128)(2,1)S(1)}, u32[]{:S(2)}, u32[]{:S(2)}) collective-permute-start(bf16[32,4096]{1,0:T(8,128)(2,1)S(1)} %maximum_select_fusion.13), channel_id=1, source_target_pairs={{0,4},{1,5},{2,6},{3,7},{4,0},{5,1},{6,2},{7,3},{8,12},{9,13},{10,... | collective-permute-start | bytes 786440 | tf_op jit(solution)/shard_map/ppermute | solution.py:85
  15.7 1.6 collective-permute-start.10
  17.4 1.6 collective-permute-start.1
  19.0 5.9 %collective-permute-done.6 = bf16[16,4096]{1,0:T(8,128)(2,1)S(1)} collective-permute-done((bf16[16,4096]{1,0:T(8,128)(2,1)S(1)}, bf16[16,4096]{1,0:T(8,128)(2,1)S(1)}, u32[]{:S(2)}, u32[]{:S(2)}) %collective-permute-start.6) | collective-permute-done | bytes 131104 | tf_op jit(solution)/shard_map/ppermute | solution.py:85
  25.0 1.6 collective-permute-start.7
  26.5 3.3 %collective-permute-done.4 = bf16[32,4096]{1,0:T(8,128)(2,1)S(1)} collective-permute-done((bf16[32,4096]{1,0:T(8,128)(2,1)S(1)}, bf16[32,4096]{1,0:T(8,128)(2,1)S(1)}, u32[]{:S(2)}, u32[]{:S(2)}) %collective-permute-start.4) | collective-permute-done | bytes 262176 | tf_op jit(solution)/shard_map/ppermute | solution.py:85
  29.9 1.6 collective-permute-start.5
  31.5 0.6 collective-permute-start.11
  32.4 3.1 %collective-permute-start.8 = (bf16[64,4096]{1,0:T(8,128)(2,1)S(1)}, bf16[64,4096]{1,0:T(8,128)(2,1)S(1)}, u32[]{:S(2)}, u32[]{:S(2)}) collective-permute-start(bf16[64,4096]{1,0:T(8,128)(2,1)S(1)} %maximum_select_fusion.10), channel_id=1, source_target_pairs={{0,2},{1,3},{2,0},{3,1},{4,6},{5,7},{6,4},{7,5},{8,10},{9,11},{10,... | collective-permute-start | bytes 1572872 | tf_op jit(solution)/shard_map/ppermute | solution.py:85
  35.5 9.3 %collective-permute-done.5 = bf16[64,4096]{1,0:T(8,128)(2,1)S(1)} collective-permute-done((bf16[64,4096]{1,0:T(8,128)(2,1)S(1)}, bf16[64,4096]{1,0:T(8,128)(2,1)S(1)}, u32[]{:S(2)}, u32[]{:S(2)}) %collective-permute-start.5) | collective-permute-done | bytes 524320 | tf_op jit(solution)/shard_map/ppermute | solution.py:85
  45.0 9.2 %collective-permute-done.11 = bf16[64,4096]{1,0:T(8,128)(2,1)S(1)} collective-permute-done((bf16[64,4096]{1,0:T(8,128)(2,1)S(1)}, bf16[64,4096]{1,0:T(8,128)(2,1)S(1)}, u32[]{:S(2)}, u32[]{:S(2)}) %collective-permute-start.11) | collective-permute-done | bytes 524320 | tf_op jit(solution)/shard_map/ppermute | solution.py:85
  54.5 2.2 collective-permute-done.2
  57.2 2.5 pad_maximum_fusion.x_ref
  59.7 43.4 %shard_map.64 = (bf16[512,3328]{1,0:T(8,128)(2,1)}, bf16[512,3328]{1,0:T(8,128)(2,1)}) custom-call(s32[32]{0:T(128)} %copy-done.2, s32[832]{0:T(1024)} %reshape.68.index_ref, bf16[512,4096]{1,0:T(8,128)(2,1)} %pad_maximum_fusion.x_ref, bf16[640,128,128]{2,1,0:T(8,128)(2,1)} %refs_3_.1, bf16[640,128,128]{2,1,0:T(8,128)(2,1)} %refs_3_.1, ...), custom_call_target="tpu_custom_call" | custom-call | flops 27917287424 | bytes 65536000 | tf_op jit(solution)/shard_map/pallas_call | solution.py:66
  103.1 2.3 fusion.4
  105.5 0.5 copy-done
  106.5 0.5 collective-permute-start.18
  107.2 0.7 collective-permute-done.12
  108.1 1.6 collective-permute-start.13
  110.0 1.0 collective-permute-start.15
  111.2 1.2 collective-permute-start.19
  112.6 1.0 collective-permute-start.21
  113.6 7.3 %collective-permute-done.13 = bf16[64,3328]{1,0:T(8,128)(2,1)S(1)} collective-permute-done((bf16[64,3328]{1,0:T(8,128)(2,1)S(1)}, bf16[64,3328]{1,0:T(8,128)(2,1)S(1)}, u32[]{:S(2)}, u32[]{:S(2)}) %collective-permute-start.13) | collective-permute-done | bytes 426016 | tf_op jit(solution)/shard_map/ppermute | solution.py:85
  120.9 9.1 %collective-permute-done.15 = bf16[64,3328]{1,0:T(8,128)(2,1)S(1)} collective-permute-done((bf16[64,3328]{1,0:T(8,128)(2,1)S(1)}, bf16[64,3328]{1,0:T(8,128)(2,1)S(1)}, u32[]{:S(2)}, u32[]{:S(2)}) %collective-permute-start.15) | collective-permute-done | bytes 426016 | tf_op jit(solution)/shard_map/ppermute | solution.py:85
  130.0 0.3 multiply_convert_fusion.1
  130.3 1.6 collective-permute-start.16
  131.9 7.2 %collective-permute-done.19 = bf16[64,3328]{1,0:T(8,128)(2,1)S(1)} collective-permute-done((bf16[64,3328]{1,0:T(8,128)(2,1)S(1)}, bf16[64,3328]{1,0:T(8,128)(2,1)S(1)}, u32[]{:S(2)}, u32[]{:S(2)}) %collective-permute-start.19) | collective-permute-done | bytes 426016 | tf_op jit(solution)/shard_map/ppermute | solution.py:85
  139.1 9.1 %collective-permute-done.21 = bf16[64,3328]{1,0:T(8,128)(2,1)S(1)} collective-permute-done((bf16[64,3328]{1,0:T(8,128)(2,1)S(1)}, bf16[64,3328]{1,0:T(8,128)(2,1)S(1)}, u32[]{:S(2)}, u32[]{:S(2)}) %collective-permute-start.21) | collective-permute-done | bytes 426016 | tf_op jit(solution)/shard_map/ppermute | solution.py:85
  148.6 1.6 collective-permute-start.22
  150.2 7.2 %collective-permute-done.16 = bf16[64,3328]{1,0:T(8,128)(2,1)S(1)} collective-permute-done((bf16[64,3328]{1,0:T(8,128)(2,1)S(1)}, bf16[64,3328]{1,0:T(8,128)(2,1)S(1)}, u32[]{:S(2)}, u32[]{:S(2)}) %collective-permute-start.16) | collective-permute-done | bytes 426016 | tf_op jit(solution)/shard_map/ppermute | solution.py:85
  157.6 8.1 %collective-permute-done.22 = bf16[64,3328]{1,0:T(8,128)(2,1)S(1)} collective-permute-done((bf16[64,3328]{1,0:T(8,128)(2,1)S(1)}, bf16[64,3328]{1,0:T(8,128)(2,1)S(1)}, u32[]{:S(2)}, u32[]{:S(2)}) %collective-permute-start.22) | collective-permute-done | bytes 426016 | tf_op jit(solution)/shard_map/ppermute | solution.py:85
  166.2 0.7 reshape.63.index_ref
  166.9 0.3 maximum_select_fusion
  167.2 1.1 collective-permute-done.23
  168.3 0.3 maximum_select_fusion.1
  168.6 1.9 pad_maximum_fusion.1.x_ref
  170.6 25.6 %shard_map.65 = bf16[512,4096]{1,0:T(8,128)(2,1)} custom-call(s32[26]{0:T(128)} %copy-done.3, s32[832]{0:T(1024)} %reshape.63.index_ref, bf16[512,3328]{1,0:T(8,128)(2,1)} %pad_maximum_fusion.1.x_ref, bf16[640,128,128]{2,1,0:T(8,128)(2,1)} %refs_1_.3, bf16[640,128,128]{2,1,0:T(8,128)(2,1)} %refs_1_.3), custom_call_target="tpu_custom_call" | custom-call | flops 13958643712 | bytes 34865152 | tf_op jit(solution)/shard_map/pallas_call | solution.py:66
  196.2 2.7 %fusion.3 = (bf16[128,4096]{1,0:T(8,128)(2,1)S(1)}, bf16[128,4096]{1,0:T(8,128)(2,1)S(1)}, bf16[128,4096]{1,0:T(8,128)(2,1)S(1)}, bf16[128,4096]{1,0:T(8,128)(2,1)S(1)}) fusion(bf16[512,4096]{1,0:T(8,128)(2,1)} %shard_map.65), kind=kLoop, calls=%fused_computation.70 | loop fusion | bytes 8388608 | tf_op jit(solution)/shard_map/slice | solution.py:137
  198.9 0.5 collective-permute-start.24
  199.4 1.3 collective-permute-start.27
  200.8 2.1 collective-permute-start.30
  202.9 0.6 collective-permute-start.33
  203.6 20.7 %collective-permute-done.24 = bf16[64,4096]{1,0:T(8,128)(2,1)S(1)} collective-permute-done((bf16[64,4096]{1,0:T(8,128)(2,1)S(1)}, bf16[64,4096]{1,0:T(8,128)(2,1)S(1)}, u32[]{:S(2)}, u32[]{:S(2)}) %collective-permute-start.24) | collective-permute-done | bytes 524320 | tf_op jit(solution)/shard_map/ppermute | solution.py:85
  224.4 1.6 collective-permute-start.25
  226.4 0.5 collective-permute-start.31
  227.1 2.8 %collective-permute-start.34 = (bf16[32,4096]{1,0:T(8,128)(2,1)S(1)}, bf16[32,4096]{1,0:T(8,128)(2,1)S(1)}, u32[]{:S(2)}, u32[]{:S(2)}) collective-permute-start(bf16[32,4096]{1,0:T(8,128)(2,1)S(1)} %dynamic-slice_convert_fusion.4), channel_id=1, source_target_pairs={{0,2},{1,3},{2,0},{3,1},{4,6},{5,7},{6,4},{7,5},{8,10},{9,11},{10,... | collective-permute-start | bytes 786440 | tf_op jit(solution)/shard_map/ppermute | solution.py:85
  229.9 3.7 %collective-permute-done.25 = bf16[32,4096]{1,0:T(8,128)(2,1)S(1)} collective-permute-done((bf16[32,4096]{1,0:T(8,128)(2,1)S(1)}, bf16[32,4096]{1,0:T(8,128)(2,1)S(1)}, u32[]{:S(2)}, u32[]{:S(2)}) %collective-permute-start.25) | collective-permute-done | bytes 262176 | tf_op jit(solution)/shard_map/ppermute | solution.py:85
  233.8 6.6 %collective-permute-done.28 = bf16[32,4096]{1,0:T(8,128)(2,1)S(1)} collective-permute-done((bf16[32,4096]{1,0:T(8,128)(2,1)S(1)}, bf16[32,4096]{1,0:T(8,128)(2,1)S(1)}, u32[]{:S(2)}, u32[]{:S(2)}) %collective-permute-start.28) | collective-permute-done | bytes 262176 | tf_op jit(solution)/shard_map/ppermute | solution.py:85
  240.6 2.2 collective-permute-start.32
  242.9 0.9 collective-permute-start.35
  243.8 2.8 %collective-permute-done.26 = bf16[16,4096]{1,0:T(8,128)(2,1)S(1)} collective-permute-done((bf16[16,4096]{1,0:T(8,128)(2,1)S(1)}, bf16[16,4096]{1,0:T(8,128)(2,1)S(1)}, u32[]{:S(2)}, u32[]{:S(2)}) %collective-permute-start.26) | collective-permute-done | bytes 131104 | tf_op jit(solution)/shard_map/ppermute | solution.py:85
  246.6 2.0 collective-permute-done.29
  248.6 5.0 %collective-permute-done.32 = bf16[16,4096]{1,0:T(8,128)(2,1)S(1)} collective-permute-done((bf16[16,4096]{1,0:T(8,128)(2,1)S(1)}, bf16[16,4096]{1,0:T(8,128)(2,1)S(1)}, u32[]{:S(2)}, u32[]{:S(2)}) %collective-permute-start.32) | collective-permute-done | bytes 131104 | tf_op jit(solution)/shard_map/ppermute | solution.py:85
  253.6 1.8 collective-permute-done.35
  255.5 0.8 pad_maximum_fusion.2
  (103 shorter events, 7.1 us)
Async XLA Ops:
  1.1 11.5 %collective-permute-start.3 = (bf16[16,4096]{1,0:T(8,128)(2,1)S(1)}, bf16[16,4096]{1,0:T(8,128)(2,1)S(1)}, u32[]{:S(2)}, u32[]{:S(2)}) collective-permute-start(bf16[16,4096]{1,0:T(8,128)(2,1)S(1)} %get-tuple-element.18), channel_id=1, source_target_pairs={{0,2},{1,3},{2,0},{3,1},{4,6},{5,7},{6,4},{7,5},{8,10},{9,11},{10,... | collective-permute-start | bytes 393224 | tf_op jit(solution)/shard_map/ppermute | solution.py:85
  4.2 11.4 %collective-permute-start.9 = (bf16[16,4096]{1,0:T(8,128)(2,1)S(1)}, bf16[16,4096]{1,0:T(8,128)(2,1)S(1)}, u32[]{:S(2)}, u32[]{:S(2)}) collective-permute-start(bf16[16,4096]{1,0:T(8,128)(2,1)S(1)} %get-tuple-element.19), channel_id=1, source_target_pairs={{0,4},{1,5},{2,6},{3,7},{4,0},{5,1},{6,2},{7,3},{8,12},{9,13},{10,... | collective-permute-start | bytes 393224 | tf_op jit(solution)/shard_map/ppermute | solution.py:85
  6.8 10.5 %collective-permute-start = (bf16[16,4096]{1,0:T(8,128)(2,1)S(1)}, bf16[16,4096]{1,0:T(8,128)(2,1)S(1)}, u32[]{:S(2)}, u32[]{:S(2)}) collective-permute-start(bf16[16,4096]{1,0:T(8,128)(2,1)S(1)} %get-tuple-element.17), channel_id=1, source_target_pairs={{0,2},{1,3},{2,0},{3,1},{4,6},{5,7},{6,4},{7,5},{8,10},{9,11},{10,... | collective-permute-start | bytes 393224 | tf_op jit(solution)/shard_map/ppermute | solution.py:85
  7.3 17.6 %collective-permute-start.6 = (bf16[16,4096]{1,0:T(8,128)(2,1)S(1)}, bf16[16,4096]{1,0:T(8,128)(2,1)S(1)}, u32[]{:S(2)}, u32[]{:S(2)}) collective-permute-start(bf16[16,4096]{1,0:T(8,128)(2,1)S(1)} %get-tuple-element.20), channel_id=1, source_target_pairs={{0,4},{1,5},{2,6},{3,7},{4,0},{5,1},{6,2},{7,3},{8,12},{9,13},{10,... | collective-permute-start | bytes 393224 | tf_op jit(solution)/shard_map/ppermute | solution.py:85
  10.4 21.1 %copy-start.2 = (s32[32]{0:T(128)}, s32[32]{0:T(128)S(1)}, u32[]{:S(2)}) copy-start(s32[32]{0:T(128)S(1)} %fusion.base_ref) | copy-start | bytes 388
  12.7 17.1 %collective-permute-start.4 = (bf16[32,4096]{1,0:T(8,128)(2,1)S(1)}, bf16[32,4096]{1,0:T(8,128)(2,1)S(1)}, u32[]{:S(2)}, u32[]{:S(2)}) collective-permute-start(bf16[32,4096]{1,0:T(8,128)(2,1)S(1)} %maximum_select_fusion.13), channel_id=1, source_target_pairs={{0,4},{1,5},{2,6},{3,7},{4,0},{5,1},{6,2},{7,3},{8,12},{9,13},{10,... | collective-permute-start | bytes 786440 | tf_op jit(solution)/shard_map/ppermute | solution.py:85
  15.7 15.7 %collective-permute-start.10 = (bf16[32,4096]{1,0:T(8,128)(2,1)S(1)}, bf16[32,4096]{1,0:T(8,128)(2,1)S(1)}, u32[]{:S(2)}, u32[]{:S(2)}) collective-permute-start(bf16[32,4096]{1,0:T(8,128)(2,1)S(1)} %maximum_select_fusion.15), channel_id=1, source_target_pairs={{0,2},{1,3},{2,0},{3,1},{4,6},{5,7},{6,4},{7,5},{8,10},{9,11},{10,... | collective-permute-start | bytes 786440 | tf_op jit(solution)/shard_map/ppermute | solution.py:85
  17.4 14.7 %collective-permute-start.1 = (bf16[32,4096]{1,0:T(8,128)(2,1)S(1)}, bf16[32,4096]{1,0:T(8,128)(2,1)S(1)}, u32[]{:S(2)}, u32[]{:S(2)}) collective-permute-start(bf16[32,4096]{1,0:T(8,128)(2,1)S(1)} %maximum_select_fusion.12), channel_id=1, source_target_pairs={{0,1},{1,0},{2,3},{3,2},{4,5},{5,4},{6,7},{7,6},{8,9},{9,8},{10,11... | collective-permute-start | bytes 786440 | tf_op jit(solution)/shard_map/ppermute | solution.py:85
  25.0 7.4 %collective-permute-start.7 = (bf16[32,4096]{1,0:T(8,128)(2,1)S(1)}, bf16[32,4096]{1,0:T(8,128)(2,1)S(1)}, u32[]{:S(2)}, u32[]{:S(2)}) collective-permute-start(bf16[32,4096]{1,0:T(8,128)(2,1)S(1)} %maximum_select_fusion.14), channel_id=1, source_target_pairs={{0,1},{1,0},{2,3},{3,2},{4,5},{5,4},{6,7},{7,6},{8,9},{9,8},{10,11... | collective-permute-start | bytes 786440 | tf_op jit(solution)/shard_map/ppermute | solution.py:85
  29.9 14.9 %collective-permute-start.5 = (bf16[64,4096]{1,0:T(8,128)(2,1)S(1)}, bf16[64,4096]{1,0:T(8,128)(2,1)S(1)}, u32[]{:S(2)}, u32[]{:S(2)}) collective-permute-start(bf16[64,4096]{1,0:T(8,128)(2,1)S(1)} %maximum_select_fusion.9), channel_id=1, source_target_pairs={{0,1},{1,0},{2,3},{3,2},{4,5},{5,4},{6,7},{7,6},{8,9},{9,8},{10,11... | collective-permute-start | bytes 1572872 | tf_op jit(solution)/shard_map/ppermute | solution.py:85
  31.5 22.7 %collective-permute-start.11 = (bf16[64,4096]{1,0:T(8,128)(2,1)S(1)}, bf16[64,4096]{1,0:T(8,128)(2,1)S(1)}, u32[]{:S(2)}, u32[]{:S(2)}) collective-permute-start(bf16[64,4096]{1,0:T(8,128)(2,1)S(1)} %maximum_select_fusion.11), channel_id=1, source_target_pairs={{0,1},{1,0},{2,3},{3,2},{4,5},{5,4},{6,7},{7,6},{8,9},{9,8},{10,11... | collective-permute-start | bytes 1572872 | tf_op jit(solution)/shard_map/ppermute | solution.py:85
  32.2 24.4 %collective-permute-start.2 = (bf16[64,4096]{1,0:T(8,128)(2,1)S(1)}, bf16[64,4096]{1,0:T(8,128)(2,1)S(1)}, u32[]{:S(2)}, u32[]{:S(2)}) collective-permute-start(bf16[64,4096]{1,0:T(8,128)(2,1)S(1)} %maximum_select_fusion.8), channel_id=1, source_target_pairs={{0,4},{1,5},{2,6},{3,7},{4,0},{5,1},{6,2},{7,3},{8,12},{9,13},{10,... | collective-permute-start | bytes 1572872 | tf_op jit(solution)/shard_map/ppermute | solution.py:85
  32.4 24.5 %collective-permute-start.8 = (bf16[64,4096]{1,0:T(8,128)(2,1)S(1)}, bf16[64,4096]{1,0:T(8,128)(2,1)S(1)}, u32[]{:S(2)}, u32[]{:S(2)}) collective-permute-start(bf16[64,4096]{1,0:T(8,128)(2,1)S(1)} %maximum_select_fusion.10), channel_id=1, source_target_pairs={{0,2},{1,3},{2,0},{3,1},{4,6},{5,7},{6,4},{7,5},{8,10},{9,11},{10,... | collective-permute-start | bytes 1572872 | tf_op jit(solution)/shard_map/ppermute | solution.py:85
  103.1 3.0 %copy-start = (bf16[512,3328]{1,0:T(8,128)(2,1)S(1)}, bf16[512,3328]{1,0:T(8,128)(2,1)}, u32[]{:S(2)}) copy-start(bf16[512,3328]{1,0:T(8,128)(2,1)} %get-tuple-element.8) | copy-start | bytes 10223620
  105.5 2.4 collective-permute-start.12
  106.3 3.4 %collective-permute-start.14 = (bf16[128,3328]{1,0:T(8,128)(2,1)S(1)}, bf16[128,3328]{1,0:T(8,128)(2,1)S(1)}, u32[]{:S(2)}, u32[]{:S(2)}) collective-permute-start(bf16[128,3328]{1,0:T(8,128)(2,1)S(1)} %constant_dynamic-slice_fusion.6), channel_id=1, source_target_pairs={{0,8},{8,0},{16,24},{24,16},{1,9},{9,1},{17,25},{25,17},{2,10},{10... | collective-permute-start | bytes 2555912 | tf_op jit(solution)/shard_map/ppermute | solution.py:85
  106.5 4.5 %collective-permute-start.18 = (bf16[128,3328]{1,0:T(8,128)(2,1)S(1)}, bf16[128,3328]{1,0:T(8,128)(2,1)S(1)}, u32[]{:S(2)}, u32[]{:S(2)}) collective-permute-start(bf16[128,3328]{1,0:T(8,128)(2,1)S(1)} %constant_dynamic-slice_fusion.5), channel_id=1, source_target_pairs={{0,8},{8,0},{16,24},{24,16},{1,9},{9,1},{17,25},{25,17},{2,10},{10... | collective-permute-start | bytes 2555912 | tf_op jit(solution)/shard_map/ppermute | solution.py:85
  107.1 5.3 %collective-permute-start.20 = (bf16[128,3328]{1,0:T(8,128)(2,1)S(1)}, bf16[128,3328]{1,0:T(8,128)(2,1)S(1)}, u32[]{:S(2)}, u32[]{:S(2)}) collective-permute-start(bf16[128,3328]{1,0:T(8,128)(2,1)S(1)} %constant_dynamic-slice_fusion.4), channel_id=1, source_target_pairs={{0,8},{8,0},{16,24},{24,16},{1,9},{9,1},{17,25},{25,17},{2,10},{10... | collective-permute-start | bytes 2555912 | tf_op jit(solution)/shard_map/ppermute | solution.py:85
  108.1 12.7 %collective-permute-start.13 = (bf16[64,3328]{1,0:T(8,128)(2,1)S(1)}, bf16[64,3328]{1,0:T(8,128)(2,1)S(1)}, u32[]{:S(2)}, u32[]{:S(2)}) collective-permute-start(bf16[64,3328]{1,0:T(8,128)(2,1)S(1)} %dynamic-slice_convert_fusion.3), channel_id=1, source_target_pairs={{0,16},{8,24},{16,0},{24,8},{1,17},{9,25},{17,1},{25,9},{2,18},{10... | collective-permute-start | bytes 1277960 | tf_op jit(solution)/shard_map/ppermute | solution.py:85
  110.0 20.0 %collective-permute-start.15 = (bf16[64,3328]{1,0:T(8,128)(2,1)S(1)}, bf16[64,3328]{1,0:T(8,128)(2,1)S(1)}, u32[]{:S(2)}, u32[]{:S(2)}) collective-permute-start(bf16[64,3328]{1,0:T(8,128)(2,1)S(1)} %dynamic-slice_convert_fusion.2), channel_id=1, source_target_pairs={{0,16},{8,24},{16,0},{24,8},{1,17},{9,25},{17,1},{25,9},{2,18},{10... | collective-permute-start | bytes 1277960 | tf_op jit(solution)/shard_map/ppermute | solution.py:85
  111.2 27.9 %collective-permute-start.19 = (bf16[64,3328]{1,0:T(8,128)(2,1)S(1)}, bf16[64,3328]{1,0:T(8,128)(2,1)S(1)}, u32[]{:S(2)}, u32[]{:S(2)}) collective-permute-start(bf16[64,3328]{1,0:T(8,128)(2,1)S(1)} %dynamic-slice_convert_fusion.1), channel_id=1, source_target_pairs={{0,16},{8,24},{16,0},{24,8},{1,17},{9,25},{17,1},{25,9},{2,18},{10... | collective-permute-start | bytes 1277960 | tf_op jit(solution)/shard_map/ppermute | solution.py:85
  112.6 35.6 %collective-permute-start.21 = (bf16[64,3328]{1,0:T(8,128)(2,1)S(1)}, bf16[64,3328]{1,0:T(8,128)(2,1)S(1)}, u32[]{:S(2)}, u32[]{:S(2)}) collective-permute-start(bf16[64,3328]{1,0:T(8,128)(2,1)S(1)} %dynamic-slice_convert_fusion), channel_id=1, source_target_pairs={{0,16},{8,24},{16,0},{24,8},{1,17},{9,25},{17,1},{25,9},{2,18},{10... | collective-permute-start | bytes 1277960 | tf_op jit(solution)/shard_map/ppermute | solution.py:85
  130.3 27.1 %collective-permute-start.16 = (bf16[64,3328]{1,0:T(8,128)(2,1)S(1)}, bf16[64,3328]{1,0:T(8,128)(2,1)S(1)}, u32[]{:S(2)}, u32[]{:S(2)}) collective-permute-start(bf16[64,3328]{1,0:T(8,128)(2,1)S(1)} %multiply_convert_fusion.1), channel_id=1, source_target_pairs={{0,16},{8,24},{16,0},{24,8},{1,17},{9,25},{17,1},{25,9},{2,18},{10... | collective-permute-start | bytes 1277960 | tf_op jit(solution)/shard_map/ppermute | solution.py:85
  148.6 17.4 %copy-start.1 = (s32[26,32]{1,0:T(8,128)S(1)}, s32[26,32]{1,0:T(8,128)}, u32[]{:S(2)}) copy-start(s32[26,32]{1,0:T(8,128)} %param.11) | copy-start | bytes 9988
  148.6 17.1 %collective-permute-start.22 = (bf16[64,3328]{1,0:T(8,128)(2,1)S(1)}, bf16[64,3328]{1,0:T(8,128)(2,1)S(1)}, u32[]{:S(2)}, u32[]{:S(2)}) collective-permute-start(bf16[64,3328]{1,0:T(8,128)(2,1)S(1)} %multiply_convert_fusion), channel_id=1, source_target_pairs={{0,16},{8,24},{16,0},{24,8},{1,17},{9,25},{17,1},{25,9},{2,18},{10... | collective-permute-start | bytes 1277960 | tf_op jit(solution)/shard_map/ppermute | solution.py:85
  157.6 9.3 %collective-permute-start.17 = (bf16[128,3328]{1,0:T(8,128)(2,1)S(1)}, bf16[128,3328]{1,0:T(8,128)(2,1)S(1)}, u32[]{:S(2)}, u32[]{:S(2)}) collective-permute-start(bf16[128,3328]{1,0:T(8,128)(2,1)S(1)} %maximum_select_fusion.6), channel_id=1, source_target_pairs={{0,8},{8,0},{16,24},{24,16},{1,9},{9,1},{17,25},{25,17},{2,10},{10... | collective-permute-start | bytes 2555912 | tf_op jit(solution)/shard_map/ppermute | solution.py:85
  165.9 2.4 collective-permute-start.23
  166.1 1.1 copy-start.3
  198.9 25.3 %collective-permute-start.24 = (bf16[64,4096]{1,0:T(8,128)(2,1)S(1)}, bf16[64,4096]{1,0:T(8,128)(2,1)S(1)}, u32[]{:S(2)}, u32[]{:S(2)}) collective-permute-start(bf16[64,4096]{1,0:T(8,128)(2,1)S(1)} %constant_dynamic-slice_fusion.3), channel_id=1, source_target_pairs={{0,4},{1,5},{2,6},{3,7},{4,0},{5,1},{6,2},{7,3},{8,12},{9,13},{10,... | collective-permute-start | bytes 1572872 | tf_op jit(solution)/shard_map/ppermute | solution.py:85
  199.4 26.6 %collective-permute-start.27 = (bf16[64,4096]{1,0:T(8,128)(2,1)S(1)}, bf16[64,4096]{1,0:T(8,128)(2,1)S(1)}, u32[]{:S(2)}, u32[]{:S(2)}) collective-permute-start(bf16[64,4096]{1,0:T(8,128)(2,1)S(1)} %constant_dynamic-slice_fusion.2), channel_id=1, source_target_pairs={{0,1},{1,0},{2,3},{3,2},{4,5},{5,4},{6,7},{7,6},{8,9},{9,8},{10,11... | collective-permute-start | bytes 1572872 | tf_op jit(solution)/shard_map/ppermute | solution.py:85
  200.8 25.5 %collective-permute-start.30 = (bf16[64,4096]{1,0:T(8,128)(2,1)S(1)}, bf16[64,4096]{1,0:T(8,128)(2,1)S(1)}, u32[]{:S(2)}, u32[]{:S(2)}) collective-permute-start(bf16[64,4096]{1,0:T(8,128)(2,1)S(1)} %constant_dynamic-slice_fusion.1), channel_id=1, source_target_pairs={{0,2},{1,3},{2,0},{3,1},{4,6},{5,7},{6,4},{7,5},{8,10},{9,11},{10,... | collective-permute-start | bytes 1572872 | tf_op jit(solution)/shard_map/ppermute | solution.py:85
  202.9 24.0 %collective-permute-start.33 = (bf16[64,4096]{1,0:T(8,128)(2,1)S(1)}, bf16[64,4096]{1,0:T(8,128)(2,1)S(1)}, u32[]{:S(2)}, u32[]{:S(2)}) collective-permute-start(bf16[64,4096]{1,0:T(8,128)(2,1)S(1)} %constant_dynamic-slice_fusion), channel_id=1, source_target_pairs={{0,1},{1,0},{2,3},{3,2},{4,5},{5,4},{6,7},{7,6},{8,9},{9,8},{10,11... | collective-permute-start | bytes 1572872 | tf_op jit(solution)/shard_map/ppermute | solution.py:85
  224.4 9.2 %collective-permute-start.25 = (bf16[32,4096]{1,0:T(8,128)(2,1)S(1)}, bf16[32,4096]{1,0:T(8,128)(2,1)S(1)}, u32[]{:S(2)}, u32[]{:S(2)}) collective-permute-start(bf16[32,4096]{1,0:T(8,128)(2,1)S(1)} %dynamic-slice_convert_fusion.7), channel_id=1, source_target_pairs={{0,1},{1,0},{2,3},{3,2},{4,5},{5,4},{6,7},{7,6},{8,9},{9,8},{10,11... | collective-permute-start | bytes 786440 | tf_op jit(solution)/shard_map/ppermute | solution.py:85
  226.2 14.2 %collective-permute-start.28 = (bf16[32,4096]{1,0:T(8,128)(2,1)S(1)}, bf16[32,4096]{1,0:T(8,128)(2,1)S(1)}, u32[]{:S(2)}, u32[]{:S(2)}) collective-permute-start(bf16[32,4096]{1,0:T(8,128)(2,1)S(1)} %dynamic-slice_convert_fusion.6), channel_id=1, source_target_pairs={{0,4},{1,5},{2,6},{3,7},{4,0},{5,1},{6,2},{7,3},{8,12},{9,13},{10,... | collective-permute-start | bytes 786440 | tf_op jit(solution)/shard_map/ppermute | solution.py:85
  226.4 14.1 %collective-permute-start.31 = (bf16[32,4096]{1,0:T(8,128)(2,1)S(1)}, bf16[32,4096]{1,0:T(8,128)(2,1)S(1)}, u32[]{:S(2)}, u32[]{:S(2)}) collective-permute-start(bf16[32,4096]{1,0:T(8,128)(2,1)S(1)} %dynamic-slice_convert_fusion.5), channel_id=1, source_target_pairs={{0,1},{1,0},{2,3},{3,2},{4,5},{5,4},{6,7},{7,6},{8,9},{9,8},{10,11... | collective-permute-start | bytes 786440 | tf_op jit(solution)/shard_map/ppermute | solution.py:85
  227.1 15.7 %collective-permute-start.34 = (bf16[32,4096]{1,0:T(8,128)(2,1)S(1)}, bf16[32,4096]{1,0:T(8,128)(2,1)S(1)}, u32[]{:S(2)}, u32[]{:S(2)}) collective-permute-start(bf16[32,4096]{1,0:T(8,128)(2,1)S(1)} %dynamic-slice_convert_fusion.4), channel_id=1, source_target_pairs={{0,2},{1,3},{2,0},{3,1},{4,6},{5,7},{6,4},{7,5},{8,10},{9,11},{10,... | collective-permute-start | bytes 786440 | tf_op jit(solution)/shard_map/ppermute | solution.py:85
  233.7 12.8 %collective-permute-start.26 = (bf16[16,4096]{1,0:T(8,128)(2,1)S(1)}, bf16[16,4096]{1,0:T(8,128)(2,1)S(1)}, u32[]{:S(2)}, u32[]{:S(2)}) collective-permute-start(bf16[16,4096]{1,0:T(8,128)(2,1)S(1)} %dynamic-slice_convert_fusion.11), channel_id=1, source_target_pairs={{0,2},{1,3},{2,0},{3,1},{4,6},{5,7},{6,4},{7,5},{8,10},{9,11},{10,... | collective-permute-start | bytes 393224 | tf_op jit(solution)/shard_map/ppermute | solution.py:85
  240.5 8.1 %collective-permute-start.29 = (bf16[16,4096]{1,0:T(8,128)(2,1)S(1)}, bf16[16,4096]{1,0:T(8,128)(2,1)S(1)}, u32[]{:S(2)}, u32[]{:S(2)}) collective-permute-start(bf16[16,4096]{1,0:T(8,128)(2,1)S(1)} %dynamic-slice_convert_fusion.10), channel_id=1, source_target_pairs={{0,2},{1,3},{2,0},{3,1},{4,6},{5,7},{6,4},{7,5},{8,10},{9,11},{10,... | collective-permute-start | bytes 393224 | tf_op jit(solution)/shard_map/ppermute | solution.py:85
  240.6 13.0 %collective-permute-start.32 = (bf16[16,4096]{1,0:T(8,128)(2,1)S(1)}, bf16[16,4096]{1,0:T(8,128)(2,1)S(1)}, u32[]{:S(2)}, u32[]{:S(2)}) collective-permute-start(bf16[16,4096]{1,0:T(8,128)(2,1)S(1)} %dynamic-slice_convert_fusion.9), channel_id=1, source_target_pairs={{0,4},{1,5},{2,6},{3,7},{4,0},{5,1},{6,2},{7,3},{8,12},{9,13},{10,... | collective-permute-start | bytes 393224 | tf_op jit(solution)/shard_map/ppermute | solution.py:85
  242.9 12.5 %collective-permute-start.35 = (bf16[16,4096]{1,0:T(8,128)(2,1)S(1)}, bf16[16,4096]{1,0:T(8,128)(2,1)S(1)}, u32[]{:S(2)}, u32[]{:S(2)}) collective-permute-start(bf16[16,4096]{1,0:T(8,128)(2,1)S(1)} %dynamic-slice_convert_fusion.8), channel_id=1, source_target_pairs={{0,4},{1,5},{2,6},{3,7},{4,0},{5,1},{6,2},{7,3},{8,12},{9,13},{10,... | collective-permute-start | bytes 393224 | tf_op jit(solution)/shard_map/ppermute | solution.py:85
